TPU v7x, 128 devices: a whole 4x4x4 slice. The times are simulated.
128 devices in a mesh: seq: 16 (over z, y_hi, core), tp: 8 (over x, y_lo).
Axes of the slice: x: 4, y: 4 (y_hi: 2, y_lo: 2; y = y_hi * 2 + y_lo), z: 4, core: 2. Of those that a mesh axis runs over, the one named last changes fastest.
Arguments:
- trainer_rows: float32 [2, 1024, 12544], P(None, ('seq', 'tp')), as said below
- shard_order: int32 [128], replicated, may hold values from 0 to 127, each once
- residual_in: float32 [16384, 1024], P(('seq', 'tp')), may hold values from -6 to 6
- norm_gains: float32 [2, 2, 1024], replicated, may hold values from 0.25 to 1.75
- prompt_lengths: int32 [16, 4], P('seq'), may hold values from 1 to 512, 1024 in all within a row
- variate_ids: int32 [16384], P('seq'), may hold values from 0 to 7
- variate_bias: float32 [2, 16, 2], replicated, may hold values from -2 to 260
Outputs:
- hidden_states: float32 [16384, 1024], P(('seq', 'tp'))
Inputs may be any that keep to these rules, and one draw needn't show every extreme that they name: shard_order is a permutation of the trainer shards' row blocks. `prompt_lengths`: each row sums to 1024, and one entry of each row is 512. `trainer_rows`: entries of columns up to 9728 are at most 6 / sqrt(1024) in size, later ones at most 6 / sqrt(2816).
All inputs are finite; a program needn't handle non-finite values.
Results may differ from a plain program's by a relative error of at most 0.017.
Values may be sent and summed in bfloat16 or wider, within the bound.
No kernel may reach another device: no remote copies, remote signals or barrier semaphores. Data moves between devices by JAX's collectives and lax.ppermute only.
A program may use at most 128 MiB of HBM per device.

v0:
```python
import jax
import jax.numpy as jnp
from jax import lax
from jax.sharding import PartitionSpec as P

NEGATIVE = -1e30
EPSILON = 1e-05


def rms_scaled(values, gain):
    mean_square = jnp.mean(values * values, axis=-1, keepdims=True)
    return values * lax.rsqrt(mean_square + EPSILON) * gain


def rotate(values, offsets):
    half_width = values.shape[-1] // 2
    frequency = 10000.0 ** (-jnp.arange(half_width, dtype=jnp.float32) / half_width)
    angles = offsets.astype(jnp.float32)[:, None] * frequency[None, :]
    cosine = jnp.cos(angles)[:, None, :]
    sine_part = jnp.sin(angles)[:, None, :]
    front_half = values[..., :half_width]
    back_half = values[..., half_width:]
    return jnp.concatenate(
        [front_half * cosine - back_half * sine_part, front_half * sine_part + back_half * cosine],
        axis=-1,
    )


def prompt_layout(lengths, token_count):
    prompt_ends = jnp.cumsum(lengths)
    prompt_starts = prompt_ends - lengths
    positions = jnp.arange(token_count, dtype=jnp.int32)
    segment = jnp.sum((positions[:, None] >= prompt_ends[None, :]).astype(jnp.int32), axis=1)
    member = segment[:, None] == jnp.arange(lengths.shape[0], dtype=jnp.int32)[None, :]
    offsets = positions - jnp.sum(jnp.where(member, prompt_starts[None, :], 0), axis=1)
    return (segment, offsets)


def project_rows(row_piece, weight):
    return jnp.dot(row_piece, weight, preferred_element_type=jnp.float32)


def gated_units(row_piece, weight):
    gate_up = jnp.dot(row_piece, weight, preferred_element_type=jnp.float32)
    half_width = weight.shape[1] // 2
    return (jax.nn.silu(gate_up[:, :half_width]) * gate_up[:, half_width:]).astype(jnp.bfloat16)


def project_out(source, weight):
    return lax.dot_general(
        source, weight, (((1,), (1,)), ((), ())), preferred_element_type=jnp.float32
    )


def on_device(
    trainer_rows, shard_order, residual_in, norm_gains, prompt_lengths, variate_ids, variate_bias
):
    tp_count = lax.axis_size("tp")
    seq_count = lax.axis_size("seq")
    layer_count, block_rows, total_cols = trainer_rows.shape
    model_width = residual_in.shape[1]
    ff_width = (total_cols - 4 * model_width) // 3
    head_cols = model_width // tp_count
    unit_cols = ff_width // tp_count
    rounded = trainer_rows.astype(jnp.bfloat16)
    part_widths = [model_width] * 4 + [ff_width] * 3
    grouped_parts = []
    column_start = 0
    for part_width in part_widths:
        grouped_parts.append(
            rounded[:, :, column_start : column_start + part_width].reshape(
                layer_count, block_rows, tp_count, part_width // tp_count
            )
        )
        column_start = column_start + part_width
    grouped = jnp.concatenate(grouped_parts, axis=3)
    slot_index = jnp.arange(seq_count * tp_count, dtype=jnp.int32)
    regrouped = lax.all_to_all(grouped, "tp", split_axis=2, concat_axis=1, tiled=True)
    collected = lax.all_gather(regrouped, "seq", axis=1, tiled=True)
    local_cols = collected.shape[3]
    blocks = collected.reshape(layer_count, seq_count * tp_count, block_rows, local_cols)
    placed = jnp.zeros_like(blocks).at[:, shard_order[slot_index]].set(blocks)
    weights = placed.reshape(layer_count, model_width, local_cols)
    token_count = variate_ids.shape[0]
    segment, offsets = prompt_layout(prompt_lengths[0], token_count)
    same_prompt = segment[:, None] == segment[None, :]
    same_variate = variate_ids[:, None] == variate_ids[None, :]
    head_count = variate_bias.shape[1]
    local_heads = head_count // tp_count
    head_size = head_cols // local_heads
    bias_table = lax.dynamic_slice_in_dim(
        variate_bias, lax.axis_index("tp") * local_heads, local_heads, 1
    )
    residual = residual_in
    for layer_index in range(layer_count):
        layer_bias = bias_table[layer_index]
        pair_bias = jnp.where(
            same_variate[None], layer_bias[:, 1][:, None, None], layer_bias[:, 0][:, None, None]
        )
        layer_weights = weights[layer_index]
        qkv_weight = layer_weights[:, : 3 * head_cols]
        out_weight = layer_weights[:, 3 * head_cols : 4 * head_cols]
        gate_up_weight = layer_weights[:, 4 * head_cols : 4 * head_cols + 2 * unit_cols]
        down_weight = layer_weights[:, 4 * head_cols + 2 * unit_cols :]
        normed = rms_scaled(residual, norm_gains[layer_index, 0]).astype(jnp.bfloat16)
        projected = project_rows(
            lax.all_gather(normed, "tp", axis=0, tiled=True), weight=qkv_weight
        )
        queries = rotate(
            projected[:, :head_cols].reshape(token_count, local_heads, head_size), offsets
        ).astype(jnp.bfloat16)
        key_rows = rotate(
            projected[:, head_cols : 2 * head_cols].reshape(token_count, local_heads, head_size),
            offsets,
        ).astype(jnp.bfloat16)
        values = (
            projected[:, 2 * head_cols : 3 * head_cols]
            .reshape(token_count, local_heads, head_size)
            .astype(jnp.bfloat16)
        )
        scores = (
            jnp.einsum("qhd,khd->hqk", queries, key_rows, preferred_element_type=jnp.float32)
            * head_size ** (-0.5)
            + pair_bias
        )
        scores = jnp.where(same_prompt[None], scores, NEGATIVE)
        row_peak = jnp.max(scores, axis=2, keepdims=True)
        weights_exp = jnp.exp(scores - row_peak)
        attn_weights = (weights_exp / jnp.sum(weights_exp, axis=2, keepdims=True)).astype(
            jnp.bfloat16
        )
        mixed_heads = (
            jnp.einsum("hqk,khd->qhd", attn_weights, values, preferred_element_type=jnp.float32)
            .astype(jnp.bfloat16)
            .reshape(token_count, head_cols)
        )
        head_total = lax.psum_scatter(
            project_out(source=mixed_heads, weight=out_weight).astype(jnp.bfloat16),
            "tp",
            scatter_dimension=0,
            tiled=True,
        ).astype(jnp.float32)
        residual = residual + head_total
        normed_mlp = rms_scaled(residual, norm_gains[layer_index, 1]).astype(jnp.bfloat16)
        hidden = gated_units(
            lax.all_gather(normed_mlp, "tp", axis=0, tiled=True), weight=gate_up_weight
        )
        unit_total = lax.psum_scatter(
            project_out(source=hidden, weight=down_weight).astype(jnp.bfloat16),
            "tp",
            scatter_dimension=0,
            tiled=True,
        ).astype(jnp.float32)
        residual = residual + unit_total
    return residual


def solution(mesh):
    return jax.shard_map(
        on_device,
        mesh=mesh,
        in_specs=(
            P(None, ("seq", "tp"), None),
            P(),
            P(("seq", "tp"), None),
            P(),
            P("seq", None),
            P("seq"),
            P(),
        ),
        out_specs=P(("seq", "tp"), None),
        check_vma=False,
    )
```

profile of v0, /device:TPU:0, one launch (start us, length us, event | category | flops | bytes accessed | tf_op | source)
XLA Modules:
  0.0 573.1 jit_solution(13933894712403697919)
XLA Ops:
  8.7 14.0 %all_to_all.18 = bf16[2,8,8,1568]{3,1,0,2:T(8,128)(2,1)S(1)} all-to-all(bf16[2,8,8,1568]{3,1,0,2:T(8,128)(2,1)S(1)} %copy.33), channel_id=1, replica_groups=mesh['seq'=16,'tp'=8] {'tp'}, dimensions={2} | all-to-all | bytes 802816 | tf_op jit(solution)/shard_map/all_to_all | solution.py:78
  29.3 61.4 %all-gather.8.cloned.1.call-done = bf16[2,1024,1,1568]{3,1,0,2:T(8,128)(2,1)} async-done(((bf16[2,64,1,1568]{3,1,0,2:T(8,128)(2,1)}), bf16[2,1024,1,1568]{3,1,0,2:T(8,128)(2,1)}) %all-gather.8.cloned.1.call-update) | async-done | bytes 6422544 | tf_op jit(solution)/shard_map/all_gather | solution.py:79
  90.8 6.3 %copy.35 = bf16[128,2,8,1568]{3,2,1,0:T(8,128)(2,1)} copy(bf16[128,2,8,1568]{3,2,0,1:T(8,128)(2,1)} %bitcast.76) | data formatting | bytes 12845056 | tf_op jit(solution)/shard_map/reshape | solution.py:81
  97.0 3.3 broadcast_in_dim.117
  100.3 22.3 %scatter_fusion = bf16[2,128,8,1568]{3,2,1,0:T(8,128)(2,1)} fusion(bf16[2,128,8,1568]{3,2,1,0:T(8,128)(2,1)} %broadcast_in_dim.117, s32[128]{0:T(128)S(1)} %fusion.44, bf16[128,2,8,1568]{3,2,1,0:T(8,128)(2,1)} %copy.35), kind=kCustom, calls=%fused_computation.1 | custom fusion | bytes 19268096 | tf_op jit(solution)/shard_map/scatter | solution.py:82
  122.7 6.4 %slice_bitcast_fusion.1 = (bf16[1024,1568]{1,0:T(8,128)(2,1)}, bf16[1024,1568]{1,0:T(8,128)(2,1)}) fusion(bf16[2,128,8,1568]{3,2,1,0:T(8,128)(2,1)} %scatter_fusion), kind=kLoop, calls=%fused_computation.27 | loop fusion | bytes 12845056 | tf_op jit(solution)/shard_map/squeeze | solution.py:100
  129.0 12.2 %all-gather.6.cloned.1.call-done = bf16[1024,1024]{1,0:T(8,128)(2,1)} async-done(((bf16[128,1024]{1,0:T(8,128)(2,1)}), bf16[1024,1024]{1,0:T(8,128)(2,1)}) %all-gather.6.cloned.1.call-update) | async-done | bytes 2097168 | tf_op jit(solution)/shard_map/all_gather | solution.py:107
  144.3 8.0 %fusion.64 = (f32[2,1024]{1,0:T(2,128)S(1)}, f32[2,1024,1024]{1,2,0:T(8,128)}) fusion(f32[2]{0:T(128)S(1)} %get-tuple-element.8, f32[2]{0:T(128)S(1)} %get-tuple-element.7, pred[1024,1024]{0,1:T(8,128)(4,1)S(1)} %get-tuple-element.52, pred[1024,1024]{0,1:T(8,128)(4,1)} %get-tuple-element.53, bf16[1024,2,32]{0,2,1:T(8,128)(2,1)S(1)} %get-tuple-element.34, ...), kind=kOutput, calls=%fused_computation.130 | convolution fusion | flops 282067968 | bytes 11018256 | tf_op jit(solution)/shard_map/sub | solution.py:128
  152.2 4.3 fusion.25
  156.5 3.0 convolution_convert_fusion.3
  159.6 51.6 %reduce-scatter.5.cloned.1.call-done = bf16[128,1024]{1,0:T(8,128)(2,1)} async-done(((bf16[1024,1024]{1,0:T(8,128)(2,1)}), bf16[128,1024]{1,0:T(8,128)(2,1)}) %reduce-scatter.5.cloned.1.call-update) | async-done | bytes 262160 | tf_op jit(solution)/shard_map/reduce_scatter | solution.py:137
  214.3 51.9 %all-gather.10.cloned.1.call-done = bf16[1024,1024]{1,0:T(8,128)(2,1)} async-done(((bf16[128,1024]{1,0:T(8,128)(2,1)}), bf16[1024,1024]{1,0:T(8,128)(2,1)}) %all-gather.10.cloned.1.call-update) | async-done | bytes 2097168 | tf_op jit(solution)/shard_map/all_gather | solution.py:146
  266.2 3.8 fusion.20
  270.0 4.1 convolution_convert_fusion.1
  274.2 51.6 %reduce-scatter.7.cloned.1.call-done = bf16[128,1024]{1,0:T(8,128)(2,1)} async-done(((bf16[1024,1024]{1,0:T(8,128)(2,1)}), bf16[128,1024]{1,0:T(8,128)(2,1)}) %reduce-scatter.7.cloned.1.call-update) | async-done | bytes 262160 | tf_op jit(solution)/shard_map/reduce_scatter | solution.py:148
  328.1 52.1 %all-gather.12.cloned.1.call-done = bf16[1024,1024]{1,0:T(8,128)(2,1)} async-done(((bf16[128,1024]{1,0:T(8,128)(2,1)}), bf16[1024,1024]{1,0:T(8,128)(2,1)}) %all-gather.12.cloned.1.call-update) | async-done | bytes 2097168 | tf_op jit(solution)/shard_map/all_gather | solution.py:107
  383.2 8.0 %fusion.65 = (f32[2,1024]{1,0:T(2,128)S(1)}, f32[2,1024,1024]{1,2,0:T(8,128)}) fusion(f32[2]{0:T(128)S(1)} %get-tuple-element.6, f32[2]{0:T(128)S(1)} %get-tuple-element.5, pred[1024,1024]{0,1:T(8,128)(4,1)S(1)} %get-tuple-element.52, pred[1024,1024]{0,1:T(8,128)(4,1)} %get-tuple-element.53, bf16[1024,2,32]{0,2,1:T(8,128)(2,1)S(1)} %get-tuple-element.32, ...), kind=kOutput, calls=%fused_computation.131 | convolution fusion | flops 282067968 | bytes 11018256 | tf_op jit(solution)/shard_map/sub | solution.py:128
  391.2 4.3 fusion.24
  395.5 3.0 convolution_convert_fusion.2
  398.6 51.5 %reduce-scatter.9.cloned.1.call-done = bf16[128,1024]{1,0:T(8,128)(2,1)} async-done(((bf16[1024,1024]{1,0:T(8,128)(2,1)}), bf16[128,1024]{1,0:T(8,128)(2,1)}) %reduce-scatter.9.cloned.1.call-update) | async-done | bytes 262160 | tf_op jit(solution)/shard_map/reduce_scatter | solution.py:137
  453.1 52.1 %all-gather.14.cloned.1.call-done = bf16[1024,1024]{1,0:T(8,128)(2,1)} async-done(((bf16[128,1024]{1,0:T(8,128)(2,1)}), bf16[1024,1024]{1,0:T(8,128)(2,1)}) %all-gather.14.cloned.1.call-update) | async-done | bytes 2097168 | tf_op jit(solution)/shard_map/all_gather | solution.py:146
  505.2 3.8 fusion.18
  509.0 4.1 convolution_convert_fusion
  513.1 51.6 %reduce-scatter.11.cloned.1.call-done = bf16[128,1024]{1,0:T(8,128)(2,1)} async-done(((bf16[1024,1024]{1,0:T(8,128)(2,1)}), bf16[128,1024]{1,0:T(8,128)(2,1)}) %reduce-scatter.11.cloned.1.call-update) | async-done | bytes 262160 | tf_op jit(solution)/shard_map/reduce_scatter | solution.py:148
  (86 shorter events, 25.1 us)
Async XLA Ops:
  6.5 18.5 %copy-start = (s32[128]{0:T(128)S(1)}, s32[128]{0:T(128)}, u32[]{:S(2)}) copy-start(s32[128]{0:T(128)} %param.8) | copy-start | bytes 1540
  6.5 17.1 %copy-start.2 = (f32[128,1024]{1,0:T(8,128)S(1)}, f32[128,1024]{1,0:T(8,128)}, u32[]{:S(2)}) copy-start(f32[128,1024]{1,0:T(8,128)} %param.9) | copy-start | bytes 1572868
  6.5 17.2 %copy-start.6 = (f32[2,2,1024]{2,1,0:T(2,128)S(1)}, f32[2,2,1024]{2,1,0:T(2,128)}, u32[]{:S(2)}) copy-start(f32[2,2,1024]{2,1,0:T(2,128)} %param.10) | copy-start | bytes 49156
  6.5 84.2 %all-gather.8.cloned.1.call-start = ((), (), s32[]{:S(2)}) async-start(), calls=%async_computation.6 | async-start | bytes 7241728 | tf_op jit(solution)/shard_map/all_gather | solution.py:79
  7.8 16.9 %copy-start.8 = (s32[1,4]{1,0:T(1,128)S(1)}, s32[1,4]{1,0:T(1,128)}, u32[]{:S(2)}) copy-start(s32[1,4]{1,0:T(1,128)} %param.11) | copy-start | bytes 52
  7.8 17.0 %copy-start.7 = (f32[2,16,2]{1,2,0:T(2,128)S(1)}, f32[2,16,2]{1,2,0:T(2,128)}, u32[]{:S(2)}) copy-start(f32[2,16,2]{1,2,0:T(2,128)} %param.13) | copy-start | bytes 772
  8.2 19.0 %copy-start.5 = (s32[1024]{0:T(1024)S(1)}, s32[1024]{0:T(1024)}, u32[]{:S(2)}) copy-start(s32[1024]{0:T(1024)} %param.12) | copy-start | bytes 12292
  23.5 117.7 %all-gather.6.cloned.1.call-start = ((), (), s32[]{:S(2)}) async-start(), calls=%async_computation.5 | async-start | bytes 2359296 | tf_op jit(solution)/shard_map/all_gather | solution.py:107
  24.6 186.6 %reduce-scatter.5.cloned.1.call-start = ((), (), s32[]{:S(2)}) async-start(), calls=%async_computation.7 | async-start | bytes 2359296 | tf_op jit(solution)/shard_map/reduce_scatter | solution.py:137
  159.5 106.7 %all-gather.10.cloned.1.call-start = ((), (), s32[]{:S(2)}) async-start(), calls=%async_computation.8 | async-start | bytes 2359296 | tf_op jit(solution)/shard_map/all_gather | solution.py:146
  214.1 111.7 %reduce-scatter.7.cloned.1.call-start = ((), (), s32[]{:S(2)}) async-start(), calls=%async_computation.9 | async-start | bytes 2359296 | tf_op jit(solution)/shard_map/reduce_scatter | solution.py:148
  270.0 55.7 %copy-start.3 = (bf16[128,1024]{1,0:T(8,128)(2,1)S(1)}, bf16[128,1024]{1,0:T(8,128)(2,1)}, u32[]{:S(2)}) copy-start(bf16[128,1024]{1,0:T(8,128)(2,1)} %reduce-scatter.5.cloned.1.call-done) | copy-start | bytes 786436
  274.1 106.0 %all-gather.12.cloned.1.call-start = ((), (), s32[]{:S(2)}) async-start(), calls=%async_computation.10 | async-start | bytes 2359296 | tf_op jit(solution)/shard_map/all_gather | solution.py:107
  327.8 122.3 %reduce-scatter.9.cloned.1.call-start = ((), (), s32[]{:S(2)}) async-start(), calls=%async_computation.11 | async-start | bytes 2359296 | tf_op jit(solution)/shard_map/reduce_scatter | solution.py:137
  398.5 106.7 %all-gather.14.cloned.1.call-start = ((), (), s32[]{:S(2)}) async-start(), calls=%async_computation.12 | async-start | bytes 2359296 | tf_op jit(solution)/shard_map/all_gather | solution.py:146
  453.0 111.7 %reduce-scatter.11.cloned.1.call-start = ((), (), s32[]{:S(2)}) async-start(), calls=%async_computation.13 | async-start | bytes 2359296 | tf_op jit(solution)/shard_map/reduce_scatter | solution.py:148
  509.0 55.7 %copy-start.4 = (bf16[128,1024]{1,0:T(8,128)(2,1)S(1)}, bf16[128,1024]{1,0:T(8,128)(2,1)}, u32[]{:S(2)}) copy-start(bf16[128,1024]{1,0:T(8,128)(2,1)} %reduce-scatter.9.cloned.1.call-done) | copy-start | bytes 786436
  509.0 57.6 %copy-start.1 = (s32[128]{0:T(128)S(1)}, s32[128]{0:T(128)}, u32[]{:S(2)}) copy-start(s32[128]{0:T(128)} %param.8) | copy-start | bytes 1540
Sparse Core Ops, SparseCore 0:
  23.7 67.0 all-gather.7
  92.4 48.7 all-gather.5
  159.7 51.4 reduce-scatter.4
  214.2 51.9 all-gather.9
  274.3 51.4 reduce-scatter.6
  327.9 52.2 all-gather.11
  398.7 51.4 reduce-scatter.8
  453.1 52.0 all-gather.13
  513.3 51.4 reduce-scatter.10
where the time goes:
time: 574 us; the launch traced here: 573 us
  waiting for transfers between devices  436 us (76%)
  matrix products  51.8 us (9%)
  local copies, waits for them, and re-layouts  42 us (7%)
  other arithmetic  15.1 us (3%)
  blocking collectives  14 us (2%)
  between operations  13.5 us (2%)
    all_gather x2, waiting for transfers between devices, on_device(): lax.all_gather(normed_mlp, 'tp', axis=0, tiled=True)  104 us
    reduce_scatter x2, waiting for transfers between devices, on_device(): lax.psum_scatter(project_out(source=hidden, weight=down_weight).astype(jn...  103 us
    reduce_scatter x2, waiting for transfers between devices, on_device(): lax.psum_scatter(project_out(source=mixed_heads, weight=out_weight).astyp...  103 us
    all_gather x2, waiting for transfers between devices, on_device(): lax.all_gather(normed, 'tp', axis=0, tiled=True)  64.3 us
    all_gather x1, waiting for transfers between devices, on_device(): collected = lax.all_gather(regrouped, 'seq', axis=1, tiled=True)  61.4 us
    scatter x1, local copies, waits for them, and re-layouts, on_device(): placed = jnp.zeros_like(blocks).at[:, shard_order[slot_index]].set(blocks)  22.3 us
    sub x2, matrix products, on_device(): weights_exp = jnp.exp(scores - row_peak)  15.9 us
    dot_general x4, matrix products, project_out(): lax.dot_general(source, weight, (((1,), (1,)), ((), ())), preferred_eleme...  14.3 us
  transfers between devices with their start and end apart: 9, of which 9 were waited for; matrix products, arithmetic and copies ran while one was open for 8% of the time, Pallas kernels for 0%

commit v1 on v0

--- a/solution.py
+++ b/solution.py
@@ -52,6 +52,18 @@
     )
 
 
+def gather_tp(values, tp_count):
+    stacked = jnp.broadcast_to(values[None], (tp_count,) + values.shape)
+    gathered = lax.all_to_all(stacked, "tp", 0, 0, tiled=True)
+    return gathered.reshape((tp_count * values.shape[0],) + values.shape[1:])
+
+
+def reduce_tp(products, tp_count):
+    pieces = products.reshape((tp_count, products.shape[0] // tp_count) + products.shape[1:])
+    received = lax.all_to_all(pieces, "tp", 0, 0, tiled=True)
+    return jnp.sum(received.astype(jnp.float32), axis=0)
+
+
 def on_device(
     trainer_rows, shard_order, residual_in, norm_gains, prompt_lengths, variate_ids, variate_bias
 ):
@@ -62,25 +74,38 @@
     ff_width = (total_cols - 4 * model_width) // 3
     head_cols = model_width // tp_count
     unit_cols = ff_width // tp_count
-    rounded = trainer_rows.astype(jnp.bfloat16)
+    block_count = seq_count * tp_count
     part_widths = [model_width] * 4 + [ff_width] * 3
-    grouped_parts = []
-    column_start = 0
-    for part_width in part_widths:
-        grouped_parts.append(
-            rounded[:, :, column_start : column_start + part_width].reshape(
-                layer_count, block_rows, tp_count, part_width // tp_count
+
+    def layer_weights_of(layer_index):
+        rounded = trainer_rows[layer_index].astype(jnp.bfloat16)
+        grouped_parts = []
+        column_start = 0
+        for part_width in part_widths:
+            grouped_parts.append(
+                rounded[:, column_start : column_start + part_width].reshape(
+                    block_rows, tp_count, part_width // tp_count
+                )
             )
-        )
-        column_start = column_start + part_width
-    grouped = jnp.concatenate(grouped_parts, axis=3)
-    slot_index = jnp.arange(seq_count * tp_count, dtype=jnp.int32)
-    regrouped = lax.all_to_all(grouped, "tp", split_axis=2, concat_axis=1, tiled=True)
-    collected = lax.all_gather(regrouped, "seq", axis=1, tiled=True)
-    local_cols = collected.shape[3]
-    blocks = collected.reshape(layer_count, seq_count * tp_count, block_rows, local_cols)
-    placed = jnp.zeros_like(blocks).at[:, shard_order[slot_index]].set(blocks)
-    weights = placed.reshape(layer_count, model_width, local_cols)
+            column_start = column_start + part_width
+        grouped = jnp.concatenate(grouped_parts, axis=2)
+        regrouped = lax.all_to_all(grouped, "tp", split_axis=1, concat_axis=0, tiled=True)
+        collected = lax.all_gather(regrouped, "seq", axis=0, tiled=True)
+        return collected.reshape(block_count * block_rows, collected.shape[2])
+
+    def to_stored(values):
+        blocks = values.reshape(values.shape[:-1] + (block_count, block_rows))
+        return jnp.take(blocks, shard_order, axis=-2).reshape(values.shape)
+
+    inverse_order = jnp.zeros_like(shard_order).at[shard_order].set(
+        jnp.arange(block_count, dtype=shard_order.dtype)
+    )
+
+    def from_stored(values):
+        blocks = values.reshape(values.shape[:-1] + (block_count, block_rows))
+        return jnp.take(blocks, inverse_order, axis=-2).reshape(values.shape)
+
+    gains = to_stored(norm_gains)
     token_count = variate_ids.shape[0]
     segment, offsets = prompt_layout(prompt_lengths[0], token_count)
     same_prompt = segment[:, None] == segment[None, :]
@@ -91,21 +116,19 @@
     bias_table = lax.dynamic_slice_in_dim(
         variate_bias, lax.axis_index("tp") * local_heads, local_heads, 1
     )
-    residual = residual_in
+    residual = to_stored(residual_in)
     for layer_index in range(layer_count):
         layer_bias = bias_table[layer_index]
         pair_bias = jnp.where(
             same_variate[None], layer_bias[:, 1][:, None, None], layer_bias[:, 0][:, None, None]
         )
-        layer_weights = weights[layer_index]
+        layer_weights = layer_weights_of(layer_index)
         qkv_weight = layer_weights[:, : 3 * head_cols]
         out_weight = layer_weights[:, 3 * head_cols : 4 * head_cols]
         gate_up_weight = layer_weights[:, 4 * head_cols : 4 * head_cols + 2 * unit_cols]
         down_weight = layer_weights[:, 4 * head_cols + 2 * unit_cols :]
-        normed = rms_scaled(residual, norm_gains[layer_index, 0]).astype(jnp.bfloat16)
-        projected = project_rows(
-            lax.all_gather(normed, "tp", axis=0, tiled=True), weight=qkv_weight
-        )
+        normed = rms_scaled(residual, gains[layer_index, 0]).astype(jnp.bfloat16)
+        projected = project_rows(gather_tp(normed, tp_count), weight=qkv_weight)
         queries = rotate(
             projected[:, :head_cols].reshape(token_count, local_heads, head_size), offsets
         ).astype(jnp.bfloat16)
@@ -134,25 +157,17 @@
             .astype(jnp.bfloat16)
             .reshape(token_count, head_cols)
         )
-        head_total = lax.psum_scatter(
-            project_out(source=mixed_heads, weight=out_weight).astype(jnp.bfloat16),
-            "tp",
-            scatter_dimension=0,
-            tiled=True,
-        ).astype(jnp.float32)
+        head_total = reduce_tp(
+            project_out(source=mixed_heads, weight=out_weight).astype(jnp.bfloat16), tp_count
+        )
         residual = residual + head_total
-        normed_mlp = rms_scaled(residual, norm_gains[layer_index, 1]).astype(jnp.bfloat16)
-        hidden = gated_units(
-            lax.all_gather(normed_mlp, "tp", axis=0, tiled=True), weight=gate_up_weight
+        normed_mlp = rms_scaled(residual, gains[layer_index, 1]).astype(jnp.bfloat16)
+        hidden = gated_units(gather_tp(normed_mlp, tp_count), weight=gate_up_weight)
+        unit_total = reduce_tp(
+            project_out(source=hidden, weight=down_weight).astype(jnp.bfloat16), tp_count
         )
-        unit_total = lax.psum_scatter(
-            project_out(source=hidden, weight=down_weight).astype(jnp.bfloat16),
-            "tp",
-            scatter_dimension=0,
-            tiled=True,
-        ).astype(jnp.float32)
         residual = residual + unit_total
-    return residual
+    return from_stored(residual)
 
 
 def solution(mesh):

time: 574 us -> 395 us (0.69)
  waiting for transfers between devices: 436 us -> 163 us
  blocking collectives: 14 us -> 97.9 us
  starting transfers between devices: 0.52 us -> 24.3 us
  local copies, waits for them, and re-layouts: 42 us -> 34.5 us
  matrix products: 51.8 us -> 45.9 us
    reduce_scatter x4 -> x0, waiting for transfers between devices: 206 us -> none  [the longest x2 103 us: on_device(): lax.psum_scatter(project_out(source=hidden, weight=down_weight).astype(jn...]
    all_gather x5 -> x2, waiting for transfers between devices: 230 us -> 59 us  [layer_weights_of(): collected = lax.all_gather(regrouped, 'seq', axis=0, tiled=True)]
    all_to_all x0 -> x6, waiting for transfers between devices: none -> 103 us  [the longest x2 52.1 us: reduce_tp(): received = lax.all_to_all(pieces, 'tp', 0, 0, tiled=True)]
    all_to_all x1 -> x4, blocking collectives: 14 us -> 97.9 us  [the longest x2 58.6 us: reduce_tp(): received = lax.all_to_all(pieces, 'tp', 0, 0, tiled=True)]
    all_to_all x0 -> x6, starting transfers between devices: none -> 24.1 us  [the longest x3 12 us: gather_tp(): gathered = lax.all_to_all(stacked, 'tp', 0, 0, tiled=True)]
    scatter x1, local copies, waits for them, and re-layouts: 22.3 us -> 0.98 us  [on_device(): jnp.zeros_like(shard_order).at[shard_order]]
    all_gather x0 -> x2, local copies, waits for them, and re-layouts: none -> 11 us  [layer_weights_of(): collected = lax.all_gather(regrouped, 'seq', axis=0, tiled=True)]
    squeeze x1 -> x0, local copies, waits for them, and re-layouts: 6.37 us -> none  [on_device(): layer_weights = weights[layer_index]]
  transfers between devices with their start and end apart: 9 -> 8, of which waited for: 9 -> 7; matrix products, arithmetic and copies ran while one was open for 8% -> 10% of each run, Pallas kernels for 0% -> 0%
where the time goes in v1:
time: 395 us; the launch traced here: 394 us
  waiting for transfers between devices  163 us (41%)
  blocking collectives  97.9 us (25%)
  matrix products  45.9 us (12%)
  local copies, waits for them, and re-layouts  34.5 us (9%)
  starting transfers between devices  24.3 us (6%)
  other arithmetic  14.4 us (4%)
  between operations  14 us (4%)
    all_gather x2, waiting for transfers between devices, layer_weights_of(): collected = lax.all_gather(regrouped, 'seq', axis=0, tiled=True)  59 us
    all_to_all x2, blocking collectives, reduce_tp(): received = lax.all_to_all(pieces, 'tp', 0, 0, tiled=True)  58.6 us
    all_to_all x2, waiting for transfers between devices, reduce_tp(): received = lax.all_to_all(pieces, 'tp', 0, 0, tiled=True)  52.1 us
    all_to_all x3, waiting for transfers between devices, gather_tp(): gathered = lax.all_to_all(stacked, 'tp', 0, 0, tiled=True)  47 us
    all_to_all x1, blocking collectives, gather_tp(): gathered = lax.all_to_all(stacked, 'tp', 0, 0, tiled=True)  27.3 us
    sub x2, matrix products, on_device(): weights_exp = jnp.exp(scores - row_peak)  18.6 us
    all_to_all x1, blocking collectives, layer_weights_of(): lax.all_to_all(grouped, 'tp', split_axis=1, concat_axis=0, tiled=True)  12.1 us
    all_to_all x3, starting transfers between devices, gather_tp(): gathered = lax.all_to_all(stacked, 'tp', 0, 0, tiled=True)  12 us
  transfers between devices with their start and end apart: 8, of which 7 were waited for; matrix products, arithmetic and copies ran while one was open for 10% of the time, Pallas kernels for 0%

profile of v1, /device:TPU:0, one launch (start us, length us, event | category | flops | bytes accessed | tf_op | source)
XLA Modules:
  0.0 393.7 jit_solution(7004867565954141031)
XLA Ops:
  9.1 12.1 %all_to_all.76 = bf16[8,8,1568]{2,0,1:T(8,128)(2,1)} all-to-all(bf16[8,8,1568]{2,0,1:T(8,128)(2,1)S(1)} %copy.72), channel_id=1, replica_groups=mesh['seq'=16,'tp'=8] {'tp'}, dimensions={1} | all-to-all | bytes 401408 | tf_op jit(solution)/shard_map/all_to_all | solution.py:92
  28.5 3.8 all-to-all-start
  37.0 55.4 %all-gather.3.cloned.1.call-done = bf16[1024,1,1568]{2,0,1:T(8,128)(2,1)} async-done(((bf16[64,1,1568]{2,0,1:T(8,128)(2,1)}), bf16[1024,1,1568]{2,0,1:T(8,128)(2,1)}) %all-gather.3.cloned.1.call-update) | async-done | bytes 3211280 | tf_op jit(solution)/shard_map/all_gather | solution.py:93
  92.4 5.5 %copy.73 = bf16[1024,1,1568]{0,2,1:T(8,128)(2,1)} copy(bf16[1024,1,1568]{2,0,1:T(8,128)(2,1)} %all-gather.3.cloned.1.call-done) | data formatting | bytes 6422528 | tf_op jit(solution)/shard_map/all_gather | solution.py:93
  101.8 9.2 %fusion.67 = (f32[2,1024]{1,0:T(2,128)S(1)}, f32[2,1024,1024]{1,2,0:T(8,128)}) fusion(f32[2]{0:T(128)} %get-tuple-element.9, f32[2]{0:T(128)S(1)} %copy-done.21, pred[1024,1024]{0,1:T(8,128)(4,1)S(1)} %copy-done.4, pred[1024,1024]{0,1:T(8,128)(4,1)} %get-tuple-element.72, bf16[1024,2,32]{0,2,1:T(8,128)(2,1)} %get-tuple-element.34, ...), kind=kOutput, calls=%fused_computation.153 | convolution fusion | flops 282067968 | bytes 11018256 | tf_op jit(solution)/shard_map/sub | solution.py:151
  111.0 4.2 %fusion.25 = bf16[2,64,1024]{2,1,0:T(8,128)(2,1)S(1)} fusion(bf16[1024,2,64]{0,2,1:T(8,128)(2,1)S(1)} %bitcast.163, f32[2,1024,1024]{1,2,0:T(8,128)} %get-tuple-element.59, f32[2,1024]{1,0:T(2,128)S(1)} %get-tuple-element.58), kind=kOutput, calls=%fused_computation.47 | convolution fusion | flops 272760832 | bytes 8921088 | tf_op jit(solution)/shard_map/hqk,khd->qhd/dot_general | solution.py:156
  118.3 4.3 %all-to-all-start.2 = ((bf16[8,128,1024]{2,1,0:T(8,128)(2,1)}), bf16[8,128,1024]{2,1,0:T(8,128)(2,1)S(1)}, u32[]{:S(2)}, u32[]{:S(2)}) async-start(bf16[8,128,1024]{2,1,0:T(8,128)(2,1)} %bitcast.138), calls=%async_computation.2 | async-start | bytes 4194304 | tf_op jit(solution)/shard_map/all_to_all | solution.py:63
  127.7 26.7 %all-to-all-done.2 = bf16[8,128,1024]{2,1,0:T(8,128)(2,1)S(1)} async-done(((bf16[8,128,1024]{2,1,0:T(8,128)(2,1)}), bf16[8,128,1024]{2,1,0:T(8,128)(2,1)S(1)}, u32[]{:S(2)}, u32[]{:S(2)}) %all-to-all-start.2) | async-done | bytes 2097184 | tf_op jit(solution)/shard_map/all_to_all | solution.py:63
  154.4 4.0 %all-to-all-start.6 = ((bf16[8,8,1568]{2,0,1:T(8,128)(2,1)}), bf16[8,8,1568]{2,0,1:T(8,128)(2,1)}, u32[]{:S(2)}, u32[]{:S(2)}) async-start(bf16[8,8,1568]{2,0,1:T(8,128)(2,1)} %copy.79), calls=%async_computation.6 | async-start | bytes 425984 | tf_op jit(solution)/shard_map/all_to_all | solution.py:92
  161.2 4.0 %all-to-all-done.6 = bf16[8,8,1568]{2,0,1:T(8,128)(2,1)} async-done(((bf16[8,8,1568]{2,0,1:T(8,128)(2,1)}), bf16[8,8,1568]{2,0,1:T(8,128)(2,1)}, u32[]{:S(2)}, u32[]{:S(2)}) %all-to-all-start.6) | async-done | bytes 200736 | tf_op jit(solution)/shard_map/all_to_all | solution.py:92
  166.8 3.6 all-to-all-start.3
  171.2 27.7 %all-to-all-done.3 = bf16[8,128,1024]{2,1,0:T(8,128)(2,1)S(1)} async-done(((bf16[8,128,1024]{2,1,0:T(8,128)(2,1)}), bf16[8,128,1024]{2,1,0:T(8,128)(2,1)S(1)}, u32[]{:S(2)}, u32[]{:S(2)}) %all-to-all-start.3) | async-done | bytes 2097184 | tf_op jit(solution)/shard_map/all_to_all | solution.py:57
  198.9 3.1 fusion.22
  204.4 30.9 %all_to_all.77 = bf16[8,128,1024]{2,1,0:T(8,128)(2,1)S(1)} all-to-all(bf16[8,128,1024]{2,1,0:T(8,128)(2,1)S(1)} %bitcast.152), channel_id=1, replica_groups=mesh['seq'=16,'tp'=8] {'tp'}, dimensions={0} | all-to-all | bytes 4194304 | tf_op jit(solution)/shard_map/all_to_all | solution.py:63
  238.9 4.6 %all-to-all-start.5 = ((bf16[8,128,1024]{2,1,0:T(8,128)(2,1)}), bf16[8,128,1024]{2,1,0:T(8,128)(2,1)S(1)}, u32[]{:S(2)}, u32[]{:S(2)}) async-start(bf16[8,128,1024]{2,1,0:T(8,128)(2,1)} %broadcast_in_dim.179), calls=%async_computation.5 | async-start | bytes 4194304 | tf_op jit(solution)/shard_map/all_to_all | solution.py:57
  243.8 3.7 all-gather.5.cloned.1.call-done
  247.4 5.5 %copy.80 = bf16[1024,1,1568]{0,2,1:T(8,128)(2,1)} copy(bf16[1024,1,1568]{2,0,1:T(8,128)(2,1)} %all-gather.5.cloned.1.call-done) | data formatting | bytes 6422528 | tf_op jit(solution)/shard_map/all_gather | solution.py:93
  252.9 19.3 %all-to-all-done.5 = bf16[8,128,1024]{2,1,0:T(8,128)(2,1)S(1)} async-done(((bf16[8,128,1024]{2,1,0:T(8,128)(2,1)}), bf16[8,128,1024]{2,1,0:T(8,128)(2,1)S(1)}, u32[]{:S(2)}, u32[]{:S(2)}) %all-to-all-start.5) | async-done | bytes 2097184 | tf_op jit(solution)/shard_map/all_to_all | solution.py:57
  276.2 9.3 %fusion.68 = (f32[2,1024]{1,0:T(2,128)}, f32[2,1024,1024]{1,2,0:T(8,128)}) fusion(f32[2]{0:T(128)S(1)} %get-tuple-element.7, f32[2]{0:T(128)S(1)} %get-tuple-element.6, pred[1024,1024]{0,1:T(8,128)(4,1)S(1)} %copy-done.5, pred[1024,1024]{0,1:T(8,128)(4,1)S(1)} %copy-done.6, bf16[1024,2,32]{0,2,1:T(8,128)(2,1)} %get-tuple-element.32, ...), kind=kOutput, calls=%fused_computation.154 | convolution fusion | flops 282067968 | bytes 11018256 | tf_op jit(solution)/shard_map/sub | solution.py:151
  285.5 4.2 %fusion.24 = bf16[2,64,1024]{2,1,0:T(8,128)(2,1)S(1)} fusion(bf16[1024,2,64]{0,2,1:T(8,128)(2,1)S(1)} %bitcast.162, f32[2,1024,1024]{1,2,0:T(8,128)} %get-tuple-element.61, f32[2,1024]{1,0:T(2,128)} %get-tuple-element.60), kind=kOutput, calls=%fused_computation.46 | convolution fusion | flops 272760832 | bytes 8921088 | tf_op jit(solution)/shard_map/hqk,khd->qhd/dot_general | solution.py:156
  291.4 27.7 %all_to_all.78 = bf16[8,128,1024]{2,1,0:T(8,128)(2,1)S(1)} all-to-all(bf16[8,128,1024]{2,1,0:T(8,128)(2,1)S(1)} %bitcast.139), channel_id=1, replica_groups=mesh['seq'=16,'tp'=8] {'tp'}, dimensions={0} | all-to-all | bytes 4194304 | tf_op jit(solution)/shard_map/all_to_all | solution.py:63
  320.5 27.3 %all_to_all.79 = bf16[8,128,1024]{2,1,0:T(8,128)(2,1)S(1)} all-to-all(bf16[8,128,1024]{2,1,0:T(8,128)(2,1)S(1)} %broadcast_in_dim.184), channel_id=1, replica_groups=mesh['seq'=16,'tp'=8] {'tp'}, dimensions={0} | all-to-all | bytes 4194304 | tf_op jit(solution)/shard_map/all_to_all | solution.py:57
  352.2 3.7 all-to-all-start.9
  355.9 25.4 %all-to-all-done.9 = bf16[8,128,1024]{2,1,0:T(8,128)(2,1)S(1)} async-done(((bf16[8,128,1024]{2,1,0:T(8,128)(2,1)}), bf16[8,128,1024]{2,1,0:T(8,128)(2,1)S(1)}, u32[]{:S(2)}, u32[]{:S(2)}) %all-to-all-start.9) | async-done | bytes 2097184 | tf_op jit(solution)/shard_map/all_to_all | solution.py:63
  (147 shorter events, 54.5 us)
Async XLA Ops:
  6.5 14.6 %copy-start.12 = (f32[2,2,1024]{2,1,0:T(2,128)S(1)}, f32[2,2,1024]{2,1,0:T(2,128)}, u32[]{:S(2)}) copy-start(f32[2,2,1024]{2,1,0:T(2,128)} %param.12) | copy-start | bytes 49156
  6.5 15.0 %copy-start.18 = (s32[128]{0:T(128)S(1)}, s32[128]{0:T(128)}, u32[]{:S(2)}) copy-start(s32[128]{0:T(128)} %param.10) | copy-start | bytes 1540
  6.5 17.9 %copy-start.7 = (f32[128,1024]{1,0:T(8,128)S(1)}, f32[128,1024]{1,0:T(8,128)}, u32[]{:S(2)}) copy-start(f32[128,1024]{1,0:T(8,128)} %param.11) | copy-start | bytes 1572868
  6.5 85.8 %all-gather.3.cloned.1.call-start = ((), (), s32[]{:S(2)}) async-start(), calls=%async_computation.10 | async-start | bytes 3620864 | tf_op jit(solution)/shard_map/all_gather | solution.py:93
  24.3 2.0 copy-start.13
  26.8 5.5 %copy-start.17 = (f32[2,16,2]{1,2,0:T(2,128)S(1)}, f32[2,16,2]{1,2,0:T(2,128)}, u32[]{:S(2)}) copy-start(f32[2,16,2]{1,2,0:T(2,128)} %param.15) | copy-start | bytes 772
  26.8 6.2 %copy-start.22 = (s32[1,4]{1,0:T(1,128)S(1)}, s32[1,4]{1,0:T(1,128)}, u32[]{:S(2)}) copy-start(s32[1,4]{1,0:T(1,128)} %param.13) | copy-start | bytes 52
  26.8 7.8 %copy-start.10 = (s32[1024]{0:T(1024)S(1)}, s32[1024]{0:T(1024)}, u32[]{:S(2)}) copy-start(s32[1024]{0:T(1024)} %param.14) | copy-start | bytes 12292
  28.5 69.4 %all-to-all-start = ((bf16[8,128,1024]{2,1,0:T(8,128)(2,1)}), bf16[8,128,1024]{2,1,0:T(8,128)(2,1)S(1)}, u32[]{:S(2)}, u32[]{:S(2)}) async-start(bf16[8,128,1024]{2,1,0:T(8,128)(2,1)} %broadcast_in_dim.167), calls=%async_computation | async-start | bytes 4194304 | tf_op jit(solution)/shard_map/all_to_all | solution.py:57
  100.0 1.8 copy-start.4
  101.8 9.2 %copy-start.9 = (bf16[1024,128]{0,1:T(8,128)(2,1)S(1)}, bf16[1024,128]{0,1:T(8,128)(2,1)}, u32[]{:S(2)}) copy-start(bf16[1024,128]{0,1:T(8,128)(2,1)} %slice.325) | copy-start | bytes 786436
  118.3 36.1 %all-to-all-start.2 = ((bf16[8,128,1024]{2,1,0:T(8,128)(2,1)}), bf16[8,128,1024]{2,1,0:T(8,128)(2,1)S(1)}, u32[]{:S(2)}, u32[]{:S(2)}) async-start(bf16[8,128,1024]{2,1,0:T(8,128)(2,1)} %bitcast.138), calls=%async_computation.2 | async-start | bytes 4194304 | tf_op jit(solution)/shard_map/all_to_all | solution.py:63
  122.6 36.4 %copy-start.14 = (pred[128]{0:T(512)(128)(4,1)S(1)}, pred[128]{0:T(512)(128)(4,1)}, u32[]{:S(2)}) copy-start(pred[128]{0:T(512)(128)(4,1)} %copy-done.13) | copy-start | bytes 388
  126.8 32.4 %copy-start.11 = (f32[1,1,1024]{2,1,0:T(1,128)S(1)}, f32[1,1,1024]{2,1,0:T(1,128)}, u32[]{:S(2)}) copy-start(f32[1,1,1024]{2,1,0:T(1,128)} %get-tuple-element.52) | copy-start | bytes 12292
  154.4 10.8 %all-to-all-start.6 = ((bf16[8,8,1568]{2,0,1:T(8,128)(2,1)}), bf16[8,8,1568]{2,0,1:T(8,128)(2,1)}, u32[]{:S(2)}, u32[]{:S(2)}) async-start(bf16[8,8,1568]{2,0,1:T(8,128)(2,1)} %copy.79), calls=%async_computation.6 | async-start | bytes 425984 | tf_op jit(solution)/shard_map/all_to_all | solution.py:92
  166.8 32.1 %all-to-all-start.3 = ((bf16[8,128,1024]{2,1,0:T(8,128)(2,1)}), bf16[8,128,1024]{2,1,0:T(8,128)(2,1)S(1)}, u32[]{:S(2)}, u32[]{:S(2)}) async-start(bf16[8,128,1024]{2,1,0:T(8,128)(2,1)} %broadcast_in_dim.178), calls=%async_computation.3 | async-start | bytes 4194304 | tf_op jit(solution)/shard_map/all_to_all | solution.py:57
  170.4 77.0 %all-gather.5.cloned.1.call-start = ((), (), s32[]{:S(2)}) async-start(), calls=%async_computation.11 | async-start | bytes 3620864 | tf_op jit(solution)/shard_map/all_gather | solution.py:93
  237.2 6.3 %copy-start.15 = (f32[1,2,2]{1,2,0:T(2,128)S(1)}, f32[1,2,2]{1,2,0:T(2,128)}, u32[]{:S(2)}) copy-start(f32[1,2,2]{1,2,0:T(2,128)} %get-tuple-element.56) | copy-start | bytes 52
  238.9 33.4 %all-to-all-start.5 = ((bf16[8,128,1024]{2,1,0:T(8,128)(2,1)}), bf16[8,128,1024]{2,1,0:T(8,128)(2,1)S(1)}, u32[]{:S(2)}, u32[]{:S(2)}) async-start(bf16[8,128,1024]{2,1,0:T(8,128)(2,1)} %broadcast_in_dim.179), calls=%async_computation.5 | async-start | bytes 4194304 | tf_op jit(solution)/shard_map/all_to_all | solution.py:57
  276.2 9.3 %copy-start.8 = (bf16[1024,128]{0,1:T(8,128)(2,1)S(1)}, bf16[1024,128]{0,1:T(8,128)(2,1)}, u32[]{:S(2)}) copy-start(bf16[1024,128]{0,1:T(8,128)(2,1)} %slice.324) | copy-start | bytes 786436
  319.6 28.2 %copy-start = (f32[128,1024]{0,1:T(8,128)}, f32[128,1024]{0,1:T(8,128)S(1)}, u32[]{:S(2)}) copy-start(f32[128,1024]{0,1:T(8,128)S(1)} %copy.83) | copy-start | bytes 1572868
  320.2 27.6 %copy-start.1 = (bf16[1024,1,1568]{0,2,1:T(8,128)(2,1)S(1)}, bf16[1024,1,1568]{0,2,1:T(8,128)(2,1)}, u32[]{:S(2)}) copy-start(bf16[1024,1,1568]{0,2,1:T(8,128)(2,1)} %copy.80) | copy-start | bytes 9633796
  352.2 3.7 copy-start.20
  352.2 29.2 %all-to-all-start.9 = ((bf16[8,128,1024]{2,1,0:T(8,128)(2,1)}), bf16[8,128,1024]{2,1,0:T(8,128)(2,1)S(1)}, u32[]{:S(2)}, u32[]{:S(2)}) async-start(bf16[8,128,1024]{2,1,0:T(8,128)(2,1)} %bitcast.151), calls=%async_computation.9 | async-start | bytes 4194304 | tf_op jit(solution)/shard_map/all_to_all | solution.py:63
  (7 other events, 9.9 us)
Sparse Core Ops, SparseCore 0:
  21.3 71.0 all-gather.2
  173.7 73.6 all-gather.4

commit v2 on v1

--- a/solution.py
+++ b/solution.py
@@ -77,21 +77,25 @@
     block_count = seq_count * tp_count
     part_widths = [model_width] * 4 + [ff_width] * 3
 
-    def layer_weights_of(layer_index):
-        rounded = trainer_rows[layer_index].astype(jnp.bfloat16)
-        grouped_parts = []
-        column_start = 0
-        for part_width in part_widths:
-            grouped_parts.append(
-                rounded[:, column_start : column_start + part_width].reshape(
-                    block_rows, tp_count, part_width // tp_count
-                )
+    rounded = trainer_rows.astype(jnp.bfloat16)
+    grouped_parts = []
+    column_start = 0
+    for part_width in part_widths:
+        grouped_parts.append(
+            rounded[:, :, column_start : column_start + part_width].reshape(
+                layer_count, block_rows, tp_count, part_width // tp_count
             )
-            column_start = column_start + part_width
-        grouped = jnp.concatenate(grouped_parts, axis=2)
-        regrouped = lax.all_to_all(grouped, "tp", split_axis=1, concat_axis=0, tiled=True)
-        collected = lax.all_gather(regrouped, "seq", axis=0, tiled=True)
-        return collected.reshape(block_count * block_rows, collected.shape[2])
+        )
+        column_start = column_start + part_width
+    grouped = jnp.concatenate(grouped_parts, axis=3)
+    regrouped = lax.all_to_all(grouped, "tp", split_axis=2, concat_axis=1, tiled=True)
+
+    def collect(layer_index, first, last):
+        piece = regrouped[layer_index, :, 0, first:last]
+        return lax.all_gather(piece, "seq", axis=0, tiled=True)
+
+    attention_cols = 4 * head_cols
+    local_cols = regrouped.shape[3]
 
     def to_stored(values):
         blocks = values.reshape(values.shape[:-1] + (block_count, block_rows))
@@ -122,11 +126,12 @@
         pair_bias = jnp.where(
             same_variate[None], layer_bias[:, 1][:, None, None], layer_bias[:, 0][:, None, None]
         )
-        layer_weights = layer_weights_of(layer_index)
-        qkv_weight = layer_weights[:, : 3 * head_cols]
-        out_weight = layer_weights[:, 3 * head_cols : 4 * head_cols]
-        gate_up_weight = layer_weights[:, 4 * head_cols : 4 * head_cols + 2 * unit_cols]
-        down_weight = layer_weights[:, 4 * head_cols + 2 * unit_cols :]
+        attention_weights = collect(layer_index, 0, attention_cols)
+        mlp_weights = collect(layer_index, attention_cols, local_cols)
+        qkv_weight = attention_weights[:, : 3 * head_cols]
+        out_weight = attention_weights[:, 3 * head_cols :]
+        gate_up_weight = mlp_weights[:, : 2 * unit_cols]
+        down_weight = mlp_weights[:, 2 * unit_cols :]
         normed = rms_scaled(residual, gains[layer_index, 0]).astype(jnp.bfloat16)
         projected = project_rows(gather_tp(normed, tp_count), weight=qkv_weight)
         queries = rotate(

time: 395 us -> 435 us (1.10)
  waiting for transfers between devices: 163 us -> 280 us
  blocking collectives: 97.9 us -> 0 us
  starting transfers between devices: 24.3 us -> 42.8 us
    all_to_all x4 -> x0, blocking collectives: 97.9 us -> none  [the longest x2 58.6 us: reduce_tp(): received = lax.all_to_all(pieces, 'tp', 0, 0, tiled=True)]
    all_to_all x2 -> x4, waiting for transfers between devices: 52.1 us -> 123 us  [reduce_tp(): received = lax.all_to_all(pieces, 'tp', 0, 0, tiled=True)]
    all_gather x2 -> x4, waiting for transfers between devices: 59 us -> 125 us  [collect(): return lax.all_gather(piece, 'seq', axis=0, tiled=True)]
    all_to_all x3 -> x4, waiting for transfers between devices: 47 us -> 26.8 us  [gather_tp(): gathered = lax.all_to_all(stacked, 'tp', 0, 0, tiled=True)]
    all_to_all x2 -> x4, starting transfers between devices: 8.01 us -> 20.5 us  [reduce_tp(): received = lax.all_to_all(pieces, 'tp', 0, 0, tiled=True)]
    all_gather x2, local copies, waits for them, and re-layouts: 11 us -> 5.91 us  [collect(): return lax.all_gather(piece, 'seq', axis=0, tiled=True)]
    all_to_all x3 -> x4, starting transfers between devices: 12 us -> 16.6 us  [gather_tp(): gathered = lax.all_to_all(stacked, 'tp', 0, 0, tiled=True)]
  transfers between devices with their start and end apart: 8 -> 13, of which waited for: 7 -> 11; matrix products, arithmetic and copies ran while one was open for 10% -> 8% of each run, Pallas kernels for 0% -> 0%
where the time goes in v2:
time: 435 us; the launch traced here: 433 us
  waiting for transfers between devices  280 us (64%)
  matrix products  49.3 us (11%)
  starting transfers between devices  42.8 us (10%)
  local copies, waits for them, and re-layouts  31.4 us (7%)
  other arithmetic  16.2 us (4%)
  between operations  13.7 us (3%)
    all_gather x4, waiting for transfers between devices, collect(): return lax.all_gather(piece, 'seq', axis=0, tiled=True)  125 us
    all_to_all x4, waiting for transfers between devices, reduce_tp(): received = lax.all_to_all(pieces, 'tp', 0, 0, tiled=True)  123 us
    all_to_all x4, waiting for transfers between devices, gather_tp(): gathered = lax.all_to_all(stacked, 'tp', 0, 0, tiled=True)  26.8 us
    all_to_all x4, starting transfers between devices, reduce_tp(): received = lax.all_to_all(pieces, 'tp', 0, 0, tiled=True)  20.5 us
    sub x2, matrix products, on_device(): weights_exp = jnp.exp(scores - row_peak)  18.6 us
    all_to_all x4, starting transfers between devices, gather_tp(): gathered = lax.all_to_all(stacked, 'tp', 0, 0, tiled=True)  16.6 us
    dot_general x4, matrix products, project_out(): lax.dot_general(source, weight, (((1,), (1,)), ((), ())), preferred_eleme...  11.4 us
  transfers between devices with their start and end apart: 13, of which 11 were waited for; matrix products, arithmetic and copies ran while one was open for 8% of the time, Pallas kernels for 0%

profile of v2, /device:TPU:0, one launch (start us, length us, event | category | flops | bytes accessed | tf_op | source)
XLA Modules:
  0.0 433.3 jit_solution(9456925842411469359)
XLA Ops:
  9.4 5.4 %all-to-all-start.1 = ((bf16[2,8,8,1568]{3,1,0,2:T(8,128)(2,1)}), bf16[2,8,8,1568]{3,1,0,2:T(8,128)(2,1)S(1)}, u32[]{:S(2)}, u32[]{:S(2)}) async-start(bf16[2,8,8,1568]{3,1,0,2:T(8,128)(2,1)} %copy.67), calls=%async_computation.1 | async-start | bytes 851968 | tf_op jit(solution)/shard_map/all_to_all | solution.py:91
  19.4 3.8 all-to-all-done.1
  26.8 3.9 all-to-all-start
  35.5 24.9 %all-to-all-done = bf16[8,128,1024]{2,1,0:T(8,128)(2,1)S(1)} async-done(((bf16[8,128,1024]{2,1,0:T(8,128)(2,1)}), bf16[8,128,1024]{2,1,0:T(8,128)(2,1)S(1)}, u32[]{:S(2)}, u32[]{:S(2)}) %all-to-all-start) | async-done | bytes 2097184 | tf_op jit(solution)/shard_map/all_to_all | solution.py:57
  60.4 20.0 %all-gather.9.cloned.1.call-done = bf16[1,1024,1,512]{3,1,0,2:T(8,128)(2,1)} async-done(((bf16[1,64,1,512]{3,1,0,2:T(8,128)(2,1)}), bf16[1,1024,1,512]{3,1,0,2:T(8,128)(2,1)}) %all-gather.9.cloned.1.call-update) | async-done | bytes 1048592 | tf_op jit(solution)/shard_map/all_gather | solution.py:95
  84.3 9.3 %fusion.68 = (f32[2,1024]{1,0:T(2,128)}, f32[2,1024,1024]{1,2,0:T(8,128)}) fusion(f32[2]{0:T(128)} %get-tuple-element.9, f32[2]{0:T(128)} %get-tuple-element.8, pred[1024,1024]{0,1:T(8,128)(4,1)S(1)} %copy-done.6, pred[1024,1024]{0,1:T(8,128)(4,1)S(1)} %copy-done.8, bf16[1024,2,32]{0,2,1:T(8,128)(2,1)} %get-tuple-element.43, ...), kind=kOutput, calls=%fused_computation.145 | convolution fusion | flops 282067968 | bytes 11018256 | tf_op jit(solution)/shard_map/sub | solution.py:156
  93.6 4.2 fusion.25
  100.8 4.3 all-to-all-start.2
  107.9 29.0 %all-to-all-done.2 = bf16[8,128,1024]{2,1,0:T(8,128)(2,1)S(1)} async-done(((bf16[8,128,1024]{2,1,0:T(8,128)(2,1)}), bf16[8,128,1024]{2,1,0:T(8,128)(2,1)S(1)}, u32[]{:S(2)}, u32[]{:S(2)}) %all-to-all-start.2) | async-done | bytes 2097184 | tf_op jit(solution)/shard_map/all_to_all | solution.py:63
  142.6 4.6 %all-to-all-start.3 = ((bf16[8,128,1024]{2,1,0:T(8,128)(2,1)}), bf16[8,128,1024]{2,1,0:T(8,128)(2,1)}, u32[]{:S(2)}, u32[]{:S(2)}) async-start(bf16[8,128,1024]{2,1,0:T(8,128)(2,1)} %broadcast_in_dim.178), calls=%async_computation.3 | async-start | bytes 4194304 | tf_op jit(solution)/shard_map/all_to_all | solution.py:57
  147.2 38.0 %all-gather.11.cloned.1.call-done = bf16[1,1024,1,1056]{3,1,0,2:T(8,128)(2,1)} async-done(((bf16[1,64,1,1056]{3,1,0,2:T(8,128)(2,1)}), bf16[1,1024,1,1056]{3,1,0,2:T(8,128)(2,1)}) %all-gather.11.cloned.1.call-update) | async-done | bytes 2162704 | tf_op jit(solution)/shard_map/all_gather | solution.py:95
  188.2 3.3 fusion.22
  194.2 4.5 %all-to-all-start.4 = ((bf16[8,128,1024]{2,1,0:T(8,128)(2,1)}), bf16[8,128,1024]{2,1,0:T(8,128)(2,1)S(1)}, u32[]{:S(2)}, u32[]{:S(2)}) async-start(bf16[8,128,1024]{2,1,0:T(8,128)(2,1)} %bitcast.125), calls=%async_computation.4 | async-start | bytes 4194304 | tf_op jit(solution)/shard_map/all_to_all | solution.py:63
  199.4 31.1 %all-to-all-done.4 = bf16[8,128,1024]{2,1,0:T(8,128)(2,1)S(1)} async-done(((bf16[8,128,1024]{2,1,0:T(8,128)(2,1)}), bf16[8,128,1024]{2,1,0:T(8,128)(2,1)S(1)}, u32[]{:S(2)}, u32[]{:S(2)}) %all-to-all-start.4) | async-done | bytes 2097184 | tf_op jit(solution)/shard_map/all_to_all | solution.py:63
  234.7 3.7 all-to-all-start.5
  238.7 28.2 %all-gather.13.cloned.1.call-done = bf16[1,1024,1,512]{3,1,0,2:T(8,128)(2,1)} async-done(((bf16[1,64,1,512]{3,1,0,2:T(8,128)(2,1)}), bf16[1,1024,1,512]{3,1,0,2:T(8,128)(2,1)}) %all-gather.13.cloned.1.call-update) | async-done | bytes 1048592 | tf_op jit(solution)/shard_map/all_gather | solution.py:95
  272.7 9.3 %fusion.69 = (f32[2,1024]{1,0:T(2,128)}, f32[2,1024,1024]{1,2,0:T(8,128)}) fusion(f32[2]{0:T(128)S(1)} %get-tuple-element.7, f32[2]{0:T(128)S(1)} %get-tuple-element.6, pred[1024,1024]{0,1:T(8,128)(4,1)S(1)} %copy-done.7, pred[1024,1024]{0,1:T(8,128)(4,1)S(1)} %copy-done.9, bf16[1024,2,32]{0,2,1:T(8,128)(2,1)} %get-tuple-element.41, ...), kind=kOutput, calls=%fused_computation.146 | convolution fusion | flops 282067968 | bytes 11018256 | tf_op jit(solution)/shard_map/sub | solution.py:156
  282.0 4.2 fusion.24
  289.2 6.9 %all-to-all-start.6 = ((bf16[8,128,1024]{2,1,0:T(8,128)(2,1)}), bf16[8,128,1024]{2,1,0:T(8,128)(2,1)S(1)}, u32[]{:S(2)}, u32[]{:S(2)}) async-start(bf16[8,128,1024]{2,1,0:T(8,128)(2,1)} %bitcast.118), calls=%async_computation.6 | async-start | bytes 4194304 | tf_op jit(solution)/shard_map/all_to_all | solution.py:63
  296.7 31.3 %all-to-all-done.6 = bf16[8,128,1024]{2,1,0:T(8,128)(2,1)S(1)} async-done(((bf16[8,128,1024]{2,1,0:T(8,128)(2,1)}), bf16[8,128,1024]{2,1,0:T(8,128)(2,1)S(1)}, u32[]{:S(2)}, u32[]{:S(2)}) %all-to-all-start.6) | async-done | bytes 2097184 | tf_op jit(solution)/shard_map/all_to_all | solution.py:63
  332.4 4.3 %all-to-all-start.7 = ((bf16[8,128,1024]{2,1,0:T(8,128)(2,1)}), bf16[8,128,1024]{2,1,0:T(8,128)(2,1)}, u32[]{:S(2)}, u32[]{:S(2)}) async-start(bf16[8,128,1024]{2,1,0:T(8,128)(2,1)} %broadcast_in_dim.184), calls=%async_computation.7 | async-start | bytes 4194304 | tf_op jit(solution)/shard_map/all_to_all | solution.py:57
  336.8 38.9 %all-gather.15.cloned.1.call-done = bf16[1,1024,1,1056]{3,1,0,2:T(8,128)(2,1)} async-done(((bf16[1,64,1,1056]{3,1,0,2:T(8,128)(2,1)}), bf16[1,1024,1,1056]{3,1,0,2:T(8,128)(2,1)}) %all-gather.15.cloned.1.call-update) | async-done | bytes 2162704 | tf_op jit(solution)/shard_map/all_gather | solution.py:95
  384.6 4.8 %all-to-all-start.8 = ((bf16[8,128,1024]{2,1,0:T(8,128)(2,1)}), bf16[8,128,1024]{2,1,0:T(8,128)(2,1)S(1)}, u32[]{:S(2)}, u32[]{:S(2)}) async-start(bf16[8,128,1024]{2,1,0:T(8,128)(2,1)} %bitcast.126), calls=%async_computation.8 | async-start | bytes 4194304 | tf_op jit(solution)/shard_map/all_to_all | solution.py:63
  389.4 31.8 %all-to-all-done.8 = bf16[8,128,1024]{2,1,0:T(8,128)(2,1)S(1)} async-done(((bf16[8,128,1024]{2,1,0:T(8,128)(2,1)}), bf16[8,128,1024]{2,1,0:T(8,128)(2,1)S(1)}, u32[]{:S(2)}, u32[]{:S(2)}) %all-to-all-start.8) | async-done | bytes 2097184 | tf_op jit(solution)/shard_map/all_to_all | solution.py:63
  (142 shorter events, 69.8 us)
Async XLA Ops:
  7.7 7.1 %copy-start.13 = (f32[2,2,1024]{2,1,0:T(2,128)S(1)}, f32[2,2,1024]{2,1,0:T(2,128)}, u32[]{:S(2)}) copy-start(f32[2,2,1024]{2,1,0:T(2,128)} %param.12) | copy-start | bytes 49156
  7.8 7.5 %copy-start.17 = (s32[128]{0:T(128)S(1)}, s32[128]{0:T(128)}, u32[]{:S(2)}) copy-start(s32[128]{0:T(128)} %param.10) | copy-start | bytes 1540
  8.4 9.8 %copy-start.10 = (f32[128,1024]{1,0:T(8,128)S(1)}, f32[128,1024]{1,0:T(8,128)}, u32[]{:S(2)}) copy-start(f32[128,1024]{1,0:T(8,128)} %param.11) | copy-start | bytes 1572868
  9.4 13.9 %all-to-all-start.1 = ((bf16[2,8,8,1568]{3,1,0,2:T(8,128)(2,1)}), bf16[2,8,8,1568]{3,1,0,2:T(8,128)(2,1)S(1)}, u32[]{:S(2)}, u32[]{:S(2)}) async-start(bf16[2,8,8,1568]{3,1,0,2:T(8,128)(2,1)} %copy.67), calls=%async_computation.1 | async-start | bytes 851968 | tf_op jit(solution)/shard_map/all_to_all | solution.py:91
  14.8 65.6 %all-gather.9.cloned.1.call-start = ((), (), s32[]{:S(2)}) async-start(), calls=%async_computation.9 | async-start | bytes 1114112 | tf_op jit(solution)/shard_map/all_gather | solution.py:95
  26.8 3.9 copy-start.16
  26.8 4.6 %copy-start.20 = (s32[1,4]{1,0:T(1,128)S(1)}, s32[1,4]{1,0:T(1,128)}, u32[]{:S(2)}) copy-start(s32[1,4]{1,0:T(1,128)} %param.13) | copy-start | bytes 52
  26.8 6.3 %copy-start.12 = (s32[1024]{0:T(1024)S(1)}, s32[1024]{0:T(1024)}, u32[]{:S(2)}) copy-start(s32[1024]{0:T(1024)} %param.14) | copy-start | bytes 12292
  26.8 33.6 %all-to-all-start = ((bf16[8,128,1024]{2,1,0:T(8,128)(2,1)}), bf16[8,128,1024]{2,1,0:T(8,128)(2,1)S(1)}, u32[]{:S(2)}, u32[]{:S(2)}) async-start(bf16[8,128,1024]{2,1,0:T(8,128)(2,1)} %broadcast_in_dim.167), calls=%async_computation | async-start | bytes 4194304 | tf_op jit(solution)/shard_map/all_to_all | solution.py:57
  100.8 36.1 %all-to-all-start.2 = ((bf16[8,128,1024]{2,1,0:T(8,128)(2,1)}), bf16[8,128,1024]{2,1,0:T(8,128)(2,1)S(1)}, u32[]{:S(2)}, u32[]{:S(2)}) async-start(bf16[8,128,1024]{2,1,0:T(8,128)(2,1)} %bitcast.117), calls=%async_computation.2 | async-start | bytes 4194304 | tf_op jit(solution)/shard_map/all_to_all | solution.py:63
  105.1 80.2 %all-gather.11.cloned.1.call-start = ((), (), s32[]{:S(2)}) async-start(), calls=%async_computation.10 | async-start | bytes 2506752 | tf_op jit(solution)/shard_map/all_gather | solution.py:95
  142.6 45.6 %all-to-all-start.3 = ((bf16[8,128,1024]{2,1,0:T(8,128)(2,1)}), bf16[8,128,1024]{2,1,0:T(8,128)(2,1)}, u32[]{:S(2)}, u32[]{:S(2)}) async-start(bf16[8,128,1024]{2,1,0:T(8,128)(2,1)} %broadcast_in_dim.178), calls=%async_computation.3 | async-start | bytes 4194304 | tf_op jit(solution)/shard_map/all_to_all | solution.py:57
  194.2 36.3 %all-to-all-start.4 = ((bf16[8,128,1024]{2,1,0:T(8,128)(2,1)}), bf16[8,128,1024]{2,1,0:T(8,128)(2,1)S(1)}, u32[]{:S(2)}, u32[]{:S(2)}) async-start(bf16[8,128,1024]{2,1,0:T(8,128)(2,1)} %bitcast.125), calls=%async_computation.4 | async-start | bytes 4194304 | tf_op jit(solution)/shard_map/all_to_all | solution.py:63
  198.7 68.3 %all-gather.13.cloned.1.call-start = ((), (), s32[]{:S(2)}) async-start(), calls=%async_computation.11 | async-start | bytes 1114112 | tf_op jit(solution)/shard_map/all_gather | solution.py:95
  234.7 3.7 copy-start.14
  234.7 34.1 %all-to-all-start.5 = ((bf16[8,128,1024]{2,1,0:T(8,128)(2,1)}), bf16[8,128,1024]{2,1,0:T(8,128)(2,1)S(1)}, u32[]{:S(2)}, u32[]{:S(2)}) async-start(bf16[8,128,1024]{2,1,0:T(8,128)(2,1)} %broadcast_in_dim.179), calls=%async_computation.5 | async-start | bytes 4194304 | tf_op jit(solution)/shard_map/all_to_all | solution.py:57
  270.9 1.7 copy-start.7
  272.7 9.3 %copy-start.11 = (bf16[1024,128]{0,1:T(8,128)(2,1)S(1)}, bf16[1024,128]{0,1:T(8,128)(2,1)}, u32[]{:S(2)}) copy-start(bf16[1024,128]{0,1:T(8,128)(2,1)} %slice.291) | copy-start | bytes 786436
  289.2 38.7 %all-to-all-start.6 = ((bf16[8,128,1024]{2,1,0:T(8,128)(2,1)}), bf16[8,128,1024]{2,1,0:T(8,128)(2,1)S(1)}, u32[]{:S(2)}, u32[]{:S(2)}) async-start(bf16[8,128,1024]{2,1,0:T(8,128)(2,1)} %bitcast.118), calls=%async_computation.6 | async-start | bytes 4194304 | tf_op jit(solution)/shard_map/all_to_all | solution.py:63
  296.1 79.5 %all-gather.15.cloned.1.call-start = ((), (), s32[]{:S(2)}) async-start(), calls=%async_computation.12 | async-start | bytes 2506752 | tf_op jit(solution)/shard_map/all_gather | solution.py:95
  330.4 2.0 copy-start.1
  332.4 46.2 %all-to-all-start.7 = ((bf16[8,128,1024]{2,1,0:T(8,128)(2,1)}), bf16[8,128,1024]{2,1,0:T(8,128)(2,1)}, u32[]{:S(2)}, u32[]{:S(2)}) async-start(bf16[8,128,1024]{2,1,0:T(8,128)(2,1)} %broadcast_in_dim.184), calls=%async_computation.7 | async-start | bytes 4194304 | tf_op jit(solution)/shard_map/all_to_all | solution.py:57
  384.6 4.8 %copy-start.19 = (s32[128]{0:T(128)S(1)}, s32[128]{0:T(128)}, u32[]{:S(2)}) copy-start(s32[128]{0:T(128)} %copy-done.18) | copy-start | bytes 1540
  384.6 36.7 %all-to-all-start.8 = ((bf16[8,128,1024]{2,1,0:T(8,128)(2,1)}), bf16[8,128,1024]{2,1,0:T(8,128)(2,1)S(1)}, u32[]{:S(2)}, u32[]{:S(2)}) async-start(bf16[8,128,1024]{2,1,0:T(8,128)(2,1)} %bitcast.126), calls=%async_computation.8 | async-start | bytes 4194304 | tf_op jit(solution)/shard_map/all_to_all | solution.py:63
  (10 other events, 12.1 us)
Sparse Core Ops, SparseCore 0:
  24.8 55.4 all-gather.8
  108.4 76.8 all-gather.10
  201.9 64.9 all-gather.12
  299.1 76.4 all-gather.14

commit v3 on v2

--- a/solution.py
+++ b/solution.py
@@ -1,10 +1,13 @@
 import jax
 import jax.numpy as jnp
 from jax import lax
+from jax.sharding import Mesh
 from jax.sharding import PartitionSpec as P
 
 NEGATIVE = -1e30
 EPSILON = 1e-05
+CHIP_AXES = "chip"
+SEQ_AXES = ("chip", "core")
 
 
 def rms_scaled(values, gain):
@@ -68,7 +71,7 @@
     trainer_rows, shard_order, residual_in, norm_gains, prompt_lengths, variate_ids, variate_bias
 ):
     tp_count = lax.axis_size("tp")
-    seq_count = lax.axis_size("seq")
+    seq_count = lax.axis_size(SEQ_AXES)
     layer_count, block_rows, total_cols = trainer_rows.shape
     model_width = residual_in.shape[1]
     ff_width = (total_cols - 4 * model_width) // 3
@@ -89,21 +92,37 @@
         column_start = column_start + part_width
     grouped = jnp.concatenate(grouped_parts, axis=3)
     regrouped = lax.all_to_all(grouped, "tp", split_axis=2, concat_axis=1, tiled=True)
-
-    def collect(layer_index, first, last):
-        piece = regrouped[layer_index, :, 0, first:last]
-        return lax.all_gather(piece, "seq", axis=0, tiled=True)
-
-    attention_cols = 4 * head_cols
-    local_cols = regrouped.shape[3]
+    chip_count = lax.axis_size(CHIP_AXES)
+    core = lax.axis_index("core")
+    core_swap = [(0, 1), (1, 0)]
+
+    def join_cores(half):
+        other = lax.ppermute(half, "core", core_swap)
+        return jnp.concatenate([half, other], axis=0)
+
+    def collect(layer_index):
+        piece = regrouped[layer_index, :, 0, :]
+        if layer_index == 0:
+            stacked = jnp.broadcast_to(piece[None], (chip_count,) + piece.shape)
+            half = lax.all_to_all(stacked, CHIP_AXES, 0, 0, tiled=True).reshape(
+                chip_count * piece.shape[0], piece.shape[1]
+            )
+        else:
+            half = lax.all_gather(piece, CHIP_AXES, axis=0, tiled=True)
+        return join_cores(half)
+
+    block_index = jnp.arange(block_count, dtype=jnp.int32)
+    half_blocks = block_count // 2
+    core_of_block = jnp.where(block_index < half_blocks, core, 1 - core)
+    within = block_index % half_blocks
+    shard_of_block = ((within // tp_count) * 2 + core_of_block) * tp_count + within % tp_count
+    stored_order = shard_order[shard_of_block]
 
     def to_stored(values):
         blocks = values.reshape(values.shape[:-1] + (block_count, block_rows))
-        return jnp.take(blocks, shard_order, axis=-2).reshape(values.shape)
-
-    inverse_order = jnp.zeros_like(shard_order).at[shard_order].set(
-        jnp.arange(block_count, dtype=shard_order.dtype)
-    )
+        return jnp.take(blocks, stored_order, axis=-2).reshape(values.shape)
+
+    inverse_order = jnp.zeros_like(stored_order).at[stored_order].set(block_index)
 
     def from_stored(values):
         blocks = values.reshape(values.shape[:-1] + (block_count, block_rows))
@@ -126,12 +145,11 @@
         pair_bias = jnp.where(
             same_variate[None], layer_bias[:, 1][:, None, None], layer_bias[:, 0][:, None, None]
         )
-        attention_weights = collect(layer_index, 0, attention_cols)
-        mlp_weights = collect(layer_index, attention_cols, local_cols)
-        qkv_weight = attention_weights[:, : 3 * head_cols]
-        out_weight = attention_weights[:, 3 * head_cols :]
-        gate_up_weight = mlp_weights[:, : 2 * unit_cols]
-        down_weight = mlp_weights[:, 2 * unit_cols :]
+        layer_weights = collect(layer_index)
+        qkv_weight = layer_weights[:, : 3 * head_cols]
+        out_weight = layer_weights[:, 3 * head_cols : 4 * head_cols]
+        gate_up_weight = layer_weights[:, 4 * head_cols : 4 * head_cols + 2 * unit_cols]
+        down_weight = layer_weights[:, 4 * head_cols + 2 * unit_cols :]
         normed = rms_scaled(residual, gains[layer_index, 0]).astype(jnp.bfloat16)
         projected = project_rows(gather_tp(normed, tp_count), weight=qkv_weight)
         queries = rotate(
@@ -176,18 +194,24 @@
 
 
 def solution(mesh):
+    seq_size = mesh.shape["seq"]
+    chip_mesh = Mesh(
+        mesh.devices.reshape((seq_size // 2, 2) + mesh.devices.shape[1:]),
+        ("chip", "core", "tp"),
+    )
+    rows = SEQ_AXES + ("tp",)
     return jax.shard_map(
         on_device,
-        mesh=mesh,
+        mesh=chip_mesh,
         in_specs=(
-            P(None, ("seq", "tp"), None),
+            P(None, rows, None),
             P(),
-            P(("seq", "tp"), None),
+            P(rows, None),
             P(),
-            P("seq", None),
-            P("seq"),
+            P(SEQ_AXES, None),
+            P(SEQ_AXES),
             P(),
         ),
-        out_specs=P(("seq", "tp"), None),
+        out_specs=P(rows, None),
         check_vma=False,
     )

time: 435 us -> 407 us (0.936)
  waiting for transfers between devices: 280 us -> 171 us
  blocking collectives: 0 us -> 88.2 us
  starting transfers between devices: 42.8 us -> 32.7 us
  matrix products: 49.3 us -> 42.5 us
  other arithmetic: 16.2 us -> 21 us
  local copies, waits for them, and re-layouts: 31.4 us -> 36 us
    all_to_all x0 -> x3, blocking collectives: none -> 88.2 us  [the longest x2 56.7 us: gather_tp(): gathered = lax.all_to_all(stacked, 'tp', 0, 0, tiled=True)]
    all_gather x4 -> x1, waiting for transfers between devices: 125 us -> 41.5 us  [collect(): half = lax.all_gather(piece, CHIP_AXES, axis=0, tiled=True)]
    all_to_all x4 -> x3, waiting for transfers between devices: 123 us -> 82.4 us  [reduce_tp(): received = lax.all_to_all(pieces, 'tp', 0, 0, tiled=True)]
    all_to_all x0 -> x1, waiting for transfers between devices: none -> 21.4 us  [collect(): lax.all_to_all(stacked, CHIP_AXES, 0, 0, tiled=True)]
    all_to_all x4 -> x2, waiting for transfers between devices: 26.8 us -> 17.7 us  [gather_tp(): gathered = lax.all_to_all(stacked, 'tp', 0, 0, tiled=True)]
    all_to_all x4 -> x3, starting transfers between devices: 20.5 us -> 11.7 us  [reduce_tp(): received = lax.all_to_all(pieces, 'tp', 0, 0, tiled=True)]
    all_to_all x4 -> x2, starting transfers between devices: 16.6 us -> 7.95 us  [gather_tp(): gathered = lax.all_to_all(stacked, 'tp', 0, 0, tiled=True)]
    all_to_all x0 -> x1, starting transfers between devices: none -> 7.65 us  [collect(): lax.all_to_all(stacked, CHIP_AXES, 0, 0, tiled=True)]
  transfers between devices with their start and end apart: 13 -> 10, of which waited for: 11 -> 8; matrix products, arithmetic and copies ran while one was open for 8% -> 7% of each run, Pallas kernels for 0% -> 0%
where the time goes in v3:
time: 407 us; the launch traced here: 405 us
  waiting for transfers between devices  171 us (42%)
  blocking collectives  88.2 us (22%)
  matrix products  42.5 us (10%)
  local copies, waits for them, and re-layouts  36 us (9%)
  starting transfers between devices  32.7 us (8%)
  other arithmetic  21 us (5%)
  between operations  14.1 us (3%)
    all_to_all x3, waiting for transfers between devices, reduce_tp(): received = lax.all_to_all(pieces, 'tp', 0, 0, tiled=True)  82.4 us
    all_to_all x2, blocking collectives, gather_tp(): gathered = lax.all_to_all(stacked, 'tp', 0, 0, tiled=True)  56.7 us
    all_gather x1, waiting for transfers between devices, collect(): half = lax.all_gather(piece, CHIP_AXES, axis=0, tiled=True)  41.5 us
    all_to_all x1, blocking collectives, reduce_tp(): received = lax.all_to_all(pieces, 'tp', 0, 0, tiled=True)  31.5 us
    all_to_all x1, waiting for transfers between devices, collect(): lax.all_to_all(stacked, CHIP_AXES, 0, 0, tiled=True)  21.4 us
    all_to_all x2, waiting for transfers between devices, gather_tp(): gathered = lax.all_to_all(stacked, 'tp', 0, 0, tiled=True)  17.7 us
    sub x2, matrix products, on_device(): weights_exp = jnp.exp(scores - row_peak)  16.8 us
    all_to_all x3, starting transfers between devices, reduce_tp(): received = lax.all_to_all(pieces, 'tp', 0, 0, tiled=True)  11.7 us
  transfers between devices with their start and end apart: 10, of which 8 were waited for; matrix products, arithmetic and copies ran while one was open for 7% of the time, Pallas kernels for 0%

profile of v3, /device:TPU:0, one launch (start us, length us, event | category | flops | bytes accessed | tf_op | source)
XLA Modules:
  0.0 405.4 jit_solution(6814599049663593879)
XLA Ops:
  9.4 5.4 %all-to-all-start.1 = ((bf16[2,8,8,1568]{3,1,0,2:T(8,128)(2,1)}), bf16[2,8,8,1568]{3,1,0,2:T(8,128)(2,1)S(1)}, u32[]{:S(2)}, u32[]{:S(2)}) async-start(bf16[2,8,8,1568]{3,1,0,2:T(8,128)(2,1)} %copy.85), calls=%async_computation.1 | async-start | bytes 851968 | tf_op jit(solution)/shard_map/all_to_all | solution.py:94
  19.6 3.6 all-to-all-done.1
  25.4 7.7 %all-to-all-start.2 = ((bf16[8,64,1568]{2,1,0:T(8,128)(2,1)}), bf16[8,64,1568]{2,1,0:T(8,128)(2,1)S(1)}, u32[]{:S(2)}, u32[]{:S(2)}) async-start(bf16[8,64,1568]{2,1,0:T(8,128)(2,1)} %broadcast_in_dim.184), calls=%async_computation.2 | async-start | bytes 3407872 | tf_op jit(solution)/shard_map/all_to_all | solution.py:107
  34.6 21.4 %all-to-all-done.2 = bf16[8,64,1568]{2,1,0:T(8,128)(2,1)S(1)} async-done(((bf16[8,64,1568]{2,1,0:T(8,128)(2,1)}), bf16[8,64,1568]{2,1,0:T(8,128)(2,1)S(1)}, u32[]{:S(2)}, u32[]{:S(2)}) %all-to-all-start.2) | async-done | bytes 1605664 | tf_op jit(solution)/shard_map/all_to_all | solution.py:107
  57.6 4.3 %all-to-all-start = ((bf16[8,128,1024]{2,1,0:T(8,128)(2,1)}), bf16[8,128,1024]{2,1,0:T(8,128)(2,1)}, u32[]{:S(2)}, u32[]{:S(2)}) async-start(bf16[8,128,1024]{2,1,0:T(8,128)(2,1)} %broadcast_in_dim.182), calls=%async_computation | async-start | bytes 4194304 | tf_op jit(solution)/shard_map/all_to_all | solution.py:60
  69.0 3.6 copy.88
  72.6 17.7 %all-to-all-done = bf16[8,128,1024]{2,1,0:T(8,128)(2,1)} async-done(((bf16[8,128,1024]{2,1,0:T(8,128)(2,1)}), bf16[8,128,1024]{2,1,0:T(8,128)(2,1)}, u32[]{:S(2)}, u32[]{:S(2)}) %all-to-all-start) | async-done | bytes 2097184 | tf_op jit(solution)/shard_map/all_to_all | solution.py:60
  93.9 10.0 %fusion.90 = (f32[2,1024]{1,0:T(2,128)}, f32[2,1024,1024]{1,2,0:T(8,128)}) fusion(f32[2]{0:T(128)} %get-tuple-element.9, f32[2]{0:T(128)S(1)} %copy-done.22, pred[1024,1024]{0,1:T(8,128)(4,1)} %get-tuple-element.61, pred[1024,1024]{0,1:T(8,128)(4,1)} %get-tuple-element.62, bf16[1024,2,32]{0,2,1:T(8,128)(2,1)} %get-tuple-element.41, ...), kind=kOutput, calls=%fused_computation.183 | convolution fusion | flops 282067968 | bytes 11018256 | tf_op jit(solution)/shard_map/sub | solution.py:174
  103.9 4.4 %fusion.29 = bf16[2,64,1024]{2,1,0:T(8,128)(2,1)S(1)} fusion(bf16[1024,2,64]{0,2,1:T(8,128)(2,1)S(1)} %bitcast.143, f32[2,1024,1024]{1,2,0:T(8,128)} %get-tuple-element.52, f32[2,1024]{1,0:T(2,128)} %get-tuple-element.51), kind=kOutput, calls=%fused_computation.52 | convolution fusion | flops 272760832 | bytes 8921088 | tf_op jit(solution)/shard_map/hqk,khd->qhd/dot_general | solution.py:179
  110.3 4.3 %all-to-all-start.3 = ((bf16[8,128,1024]{2,1,0:T(8,128)(2,1)}), bf16[8,128,1024]{2,1,0:T(8,128)(2,1)}, u32[]{:S(2)}, u32[]{:S(2)}) async-start(bf16[8,128,1024]{2,1,0:T(8,128)(2,1)} %bitcast.128), calls=%async_computation.3 | async-start | bytes 4194304 | tf_op jit(solution)/shard_map/all_to_all | solution.py:66
  115.7 27.6 %all-to-all-done.3 = bf16[8,128,1024]{2,1,0:T(8,128)(2,1)} async-done(((bf16[8,128,1024]{2,1,0:T(8,128)(2,1)}), bf16[8,128,1024]{2,1,0:T(8,128)(2,1)}, u32[]{:S(2)}, u32[]{:S(2)}) %all-to-all-start.3) | async-done | bytes 2097184 | tf_op jit(solution)/shard_map/all_to_all | solution.py:66
  150.0 27.7 %all_to_all.60 = bf16[8,128,1024]{2,1,0:T(8,128)(2,1)S(1)} all-to-all(bf16[8,128,1024]{2,1,0:T(8,128)(2,1)S(1)} %broadcast_in_dim.195), channel_id=1, replica_groups=mesh['chip'=8,'core'=2,'tp'=8] {'tp'}, dimensions={0} | all-to-all | bytes 4194304 | tf_op jit(solution)/shard_map/all_to_all | solution.py:60
  182.4 3.6 all-to-all-start.5
  186.7 26.6 %all-to-all-done.5 = bf16[8,128,1024]{2,1,0:T(8,128)(2,1)S(1)} async-done(((bf16[8,128,1024]{2,1,0:T(8,128)(2,1)}), bf16[8,128,1024]{2,1,0:T(8,128)(2,1)S(1)}, u32[]{:S(2)}, u32[]{:S(2)}) %all-to-all-start.5) | async-done | bytes 2097184 | tf_op jit(solution)/shard_map/all_to_all | solution.py:66
  217.6 3.6 all-to-all-start.6
  221.2 41.5 %all-gather.2.cloned.1.call-done = bf16[512,1568]{1,0:T(8,128)(2,1)} async-done(((bf16[64,1568]{1,0:T(8,128)(2,1)}), bf16[512,1568]{1,0:T(8,128)(2,1)}) %all-gather.2.cloned.1.call-update) | async-done | bytes 1605648 | tf_op jit(solution)/shard_map/all_gather | solution.py:111
  262.7 3.6 copy.94
  270.1 3.5 copy.95
  277.5 6.9 %fusion.91 = (f32[2,1024]{1,0:T(2,128)S(1)}, f32[2,1024,1024]{1,2,0:T(8,128)}) fusion(f32[2]{0:T(128)S(1)} %get-tuple-element.7, f32[2]{0:T(128)S(1)} %get-tuple-element.6, pred[1024,1024]{0,1:T(8,128)(4,1)S(1)} %copy-done.10, pred[1024,1024]{0,1:T(8,128)(4,1)S(1)} %copy-done.11, bf16[1024,2,32]{0,2,1:T(8,128)(2,1)S(1)} %get-tuple-element.39, ...), kind=kOutput, calls=%fused_computation.184 | convolution fusion | flops 282067968 | bytes 11018256 | tf_op jit(solution)/shard_map/sub | solution.py:174
  284.3 4.5 %fusion.28 = bf16[2,64,1024]{2,1,0:T(8,128)(2,1)S(1)} fusion(bf16[1024,2,64]{0,2,1:T(8,128)(2,1)} %bitcast.142, f32[2,1024,1024]{1,2,0:T(8,128)} %get-tuple-element.54, f32[2,1024]{1,0:T(2,128)S(1)} %get-tuple-element.53), kind=kOutput, calls=%fused_computation.51 | convolution fusion | flops 272760832 | bytes 8921088 | tf_op jit(solution)/shard_map/hqk,khd->qhd/dot_general | solution.py:179
  289.6 31.5 %all_to_all.61 = bf16[8,128,1024]{2,1,0:T(8,128)(2,1)S(1)} all-to-all(bf16[8,128,1024]{2,1,0:T(8,128)(2,1)S(1)} %bitcast.129), channel_id=1, replica_groups=mesh['chip'=8,'core'=2,'tp'=8] {'tp'}, dimensions={0} | all-to-all | bytes 4194304 | tf_op jit(solution)/shard_map/all_to_all | solution.py:66
  327.3 29.0 %all_to_all.62 = bf16[8,128,1024]{2,1,0:T(8,128)(2,1)S(1)} all-to-all(bf16[8,128,1024]{2,1,0:T(8,128)(2,1)S(1)} %broadcast_in_dim.201), channel_id=1, replica_groups=mesh['chip'=8,'core'=2,'tp'=8] {'tp'}, dimensions={0} | all-to-all | bytes 4194304 | tf_op jit(solution)/shard_map/all_to_all | solution.py:60
  360.9 3.7 all-to-all-start.9
  364.7 28.2 %all-to-all-done.9 = bf16[8,128,1024]{2,1,0:T(8,128)(2,1)S(1)} async-done(((bf16[8,128,1024]{2,1,0:T(8,128)(2,1)}), bf16[8,128,1024]{2,1,0:T(8,128)(2,1)S(1)}, u32[]{:S(2)}, u32[]{:S(2)}) %all-to-all-start.9) | async-done | bytes 2097184 | tf_op jit(solution)/shard_map/all_to_all | solution.py:66
  (149 shorter events, 67.3 us)
Async XLA Ops:
  6.5 8.3 %copy-start = (s32[128]{0:T(128)S(1)}, s32[128]{0:T(128)}, u32[]{:S(2)}) copy-start(s32[128]{0:T(128)} %param.10) | copy-start | bytes 1540
  7.8 10.1 %copy-start.14 = (f32[2,2,1024]{2,1,0:T(2,128)S(1)}, f32[2,2,1024]{2,1,0:T(2,128)}, u32[]{:S(2)}) copy-start(f32[2,2,1024]{2,1,0:T(2,128)} %param.12) | copy-start | bytes 49156
  8.6 10.8 %copy-start.12 = (f32[128,1024]{1,0:T(8,128)S(1)}, f32[128,1024]{1,0:T(8,128)}, u32[]{:S(2)}) copy-start(f32[128,1024]{1,0:T(8,128)} %param.11) | copy-start | bytes 1572868
  9.4 13.9 %all-to-all-start.1 = ((bf16[2,8,8,1568]{3,1,0,2:T(8,128)(2,1)}), bf16[2,8,8,1568]{3,1,0,2:T(8,128)(2,1)S(1)}, u32[]{:S(2)}, u32[]{:S(2)}) async-start(bf16[2,8,8,1568]{3,1,0,2:T(8,128)(2,1)} %copy.85), calls=%async_computation.1 | async-start | bytes 851968 | tf_op jit(solution)/shard_map/all_to_all | solution.py:94
  17.7 16.4 %copy-start.15 = (pred[128]{0:T(512)(128)(4,1)}, pred[128]{0:T(512)(128)(4,1)S(1)}, u32[]{:S(2)}) copy-start(pred[128]{0:T(512)(128)(4,1)S(1)} %get-tuple-element.60) | copy-start | bytes 388
  25.4 30.6 %all-to-all-start.2 = ((bf16[8,64,1568]{2,1,0:T(8,128)(2,1)}), bf16[8,64,1568]{2,1,0:T(8,128)(2,1)S(1)}, u32[]{:S(2)}, u32[]{:S(2)}) async-start(bf16[8,64,1568]{2,1,0:T(8,128)(2,1)} %broadcast_in_dim.184), calls=%async_computation.2 | async-start | bytes 3407872 | tf_op jit(solution)/shard_map/all_to_all | solution.py:107
  57.6 32.7 %all-to-all-start = ((bf16[8,128,1024]{2,1,0:T(8,128)(2,1)}), bf16[8,128,1024]{2,1,0:T(8,128)(2,1)}, u32[]{:S(2)}, u32[]{:S(2)}) async-start(bf16[8,128,1024]{2,1,0:T(8,128)(2,1)} %broadcast_in_dim.182), calls=%async_computation | async-start | bytes 4194304 | tf_op jit(solution)/shard_map/all_to_all | solution.py:60
  62.0 4.7 %copy-start.13 = (s32[1024]{0:T(1024)S(1)}, s32[1024]{0:T(1024)}, u32[]{:S(2)}) copy-start(s32[1024]{0:T(1024)} %param.14) | copy-start | bytes 12292
  64.3 4.7 %collective-permute-start = (bf16[512,1568]{0,1:T(8,128)(2,1)}, bf16[512,1568]{0,1:T(8,128)(2,1)}, u32[]{:S(2)}, u32[]{:S(2)}) collective-permute-start(bf16[512,1568]{0,1:T(8,128)(2,1)} %copy.87), channel_id=1, source_target_pairs={{0,8},{8,0},{1,9},{9,1},{2,10},{10,2},{3,11},{11,3},{4,12},{12,4},... | collective-permute-start | bytes 4816904 | tf_op jit(solution)/shard_map/ppermute | solution.py:100
  103.9 4.4 %copy-start.3 = (bf16[512,1568]{1,0:T(8,128)(2,1)S(1)}, bf16[512,1568]{1,0:T(8,128)(2,1)}, u32[]{:S(2)}) copy-start(bf16[512,1568]{1,0:T(8,128)(2,1)} %copy.88) | copy-start | bytes 4816900
  110.3 33.0 %all-to-all-start.3 = ((bf16[8,128,1024]{2,1,0:T(8,128)(2,1)}), bf16[8,128,1024]{2,1,0:T(8,128)(2,1)}, u32[]{:S(2)}, u32[]{:S(2)}) async-start(bf16[8,128,1024]{2,1,0:T(8,128)(2,1)} %bitcast.128), calls=%async_computation.3 | async-start | bytes 4194304 | tf_op jit(solution)/shard_map/all_to_all | solution.py:66
  115.7 30.7 %copy-start.16 = (pred[128]{0:T(512)(128)(4,1)S(1)}, pred[128]{0:T(512)(128)(4,1)}, u32[]{:S(2)}) copy-start(pred[128]{0:T(512)(128)(4,1)} %copy-done.15) | copy-start | bytes 388
  147.6 66.2 %copy-start.6 = (f32[128,128,8]{0,2,1:T(8,128)}, f32[128,128,8]{0,2,1:T(8,128)S(1)}, u32[]{:S(2)}) copy-start(f32[128,128,8]{0,2,1:T(8,128)S(1)} %get-tuple-element.15) | copy-start | bytes 1572868
  150.0 27.8 %copy-start.4 = (bf16[512,1568]{1,0:T(8,128)(2,1)S(1)}, bf16[512,1568]{1,0:T(8,128)(2,1)}, u32[]{:S(2)}) copy-start(bf16[512,1568]{1,0:T(8,128)(2,1)} %copy.88) | copy-start | bytes 4816900
  182.4 30.9 %all-to-all-start.5 = ((bf16[8,128,1024]{2,1,0:T(8,128)(2,1)}), bf16[8,128,1024]{2,1,0:T(8,128)(2,1)S(1)}, u32[]{:S(2)}, u32[]{:S(2)}) async-start(bf16[8,128,1024]{2,1,0:T(8,128)(2,1)} %bitcast.130), calls=%async_computation.5 | async-start | bytes 4194304 | tf_op jit(solution)/shard_map/all_to_all | solution.py:66
  186.0 76.7 %all-gather.2.cloned.1.call-start = ((), (), s32[]{:S(2)}) async-start(), calls=%async_computation.10 | async-start | bytes 1916928 | tf_op jit(solution)/shard_map/all_gather | solution.py:111
  217.6 56.0 %all-to-all-start.6 = ((bf16[8,128,1024]{2,1,0:T(8,128)(2,1)}), bf16[8,128,1024]{2,1,0:T(8,128)(2,1)S(1)}, u32[]{:S(2)}, u32[]{:S(2)}) async-start(bf16[8,128,1024]{2,1,0:T(8,128)(2,1)} %broadcast_in_dim.196), calls=%async_computation.6 | async-start | bytes 4194304 | tf_op jit(solution)/shard_map/all_to_all | solution.py:60
  221.2 45.1 %copy-start.17 = (f32[1,2,2]{1,2,0:T(2,128)S(1)}, f32[1,2,2]{1,2,0:T(2,128)}, u32[]{:S(2)}) copy-start(f32[1,2,2]{1,2,0:T(2,128)} %get-tuple-element.49) | copy-start | bytes 52
  266.3 3.8 collective-permute-start.1
  284.3 4.5 %copy-start.2 = (bf16[512,1568]{1,0:T(8,128)(2,1)S(1)}, bf16[512,1568]{1,0:T(8,128)(2,1)}, u32[]{:S(2)}) copy-start(bf16[512,1568]{1,0:T(8,128)(2,1)} %all-gather.2.cloned.1.call-done) | copy-start | bytes 4816900
  284.3 4.5 %copy-start.5 = (bf16[512,1568]{1,0:T(8,128)(2,1)S(1)}, bf16[512,1568]{1,0:T(8,128)(2,1)}, u32[]{:S(2)}) copy-start(bf16[512,1568]{1,0:T(8,128)(2,1)} %copy.95) | copy-start | bytes 4816900
  360.9 32.0 %all-to-all-start.9 = ((bf16[8,128,1024]{2,1,0:T(8,128)(2,1)}), bf16[8,128,1024]{2,1,0:T(8,128)(2,1)S(1)}, u32[]{:S(2)}, u32[]{:S(2)}) async-start(bf16[8,128,1024]{2,1,0:T(8,128)(2,1)} %bitcast.131), calls=%async_computation.9 | async-start | bytes 4194304 | tf_op jit(solution)/shard_map/all_to_all | solution.py:66
  364.7 30.7 %copy-start.7 = (f32[128,128,8]{0,2,1:T(8,128)S(1)}, f32[128,128,8]{0,2,1:T(8,128)}, u32[]{:S(2)}) copy-start(f32[128,128,8]{0,2,1:T(8,128)} %copy-done.6) | copy-start | bytes 1572868
  364.7 30.7 %copy-start.9 = (f32[128,1024]{0,1:T(8,128)S(1)}, f32[128,1024]{0,1:T(8,128)}, u32[]{:S(2)}) copy-start(f32[128,1024]{0,1:T(8,128)} %copy-done.8) | copy-start | bytes 1572868
  (10 other events, 20.4 us)
Sparse Core Ops, SparseCore 0:
  189.1 73.5 all-gather.1

commit v4 on v3

--- a/solution.py
+++ b/solution.py
@@ -107,28 +107,24 @@
             half = lax.all_to_all(stacked, CHIP_AXES, 0, 0, tiled=True).reshape(
                 chip_count * piece.shape[0], piece.shape[1]
             )
-        else:
-            half = lax.all_gather(piece, CHIP_AXES, axis=0, tiled=True)
-        return join_cores(half)
+            return join_cores(half)
+        return lax.all_gather(piece, SEQ_AXES, axis=0, tiled=True)
 
     block_index = jnp.arange(block_count, dtype=jnp.int32)
     half_blocks = block_count // 2
     core_of_block = jnp.where(block_index < half_blocks, core, 1 - core)
     within = block_index % half_blocks
     shard_of_block = ((within // tp_count) * 2 + core_of_block) * tp_count + within % tp_count
-    stored_order = shard_order[shard_of_block]
-
-    def to_stored(values):
+    block_of_shard = jnp.zeros_like(shard_of_block).at[shard_of_block].set(block_index)
+    stored_orders = [shard_order[shard_of_block]] + [shard_order] * (layer_count - 1)
+
+    def reorder(values, order):
         blocks = values.reshape(values.shape[:-1] + (block_count, block_rows))
-        return jnp.take(blocks, stored_order, axis=-2).reshape(values.shape)
-
-    inverse_order = jnp.zeros_like(stored_order).at[stored_order].set(block_index)
-
-    def from_stored(values):
-        blocks = values.reshape(values.shape[:-1] + (block_count, block_rows))
-        return jnp.take(blocks, inverse_order, axis=-2).reshape(values.shape)
-
-    gains = to_stored(norm_gains)
+        return jnp.take(blocks, order, axis=-2).reshape(values.shape)
+
+    inverse_order = jnp.zeros_like(shard_order).at[shard_order].set(block_index)
+
+    gains = [reorder(norm_gains[i], stored_orders[i]) for i in range(layer_count)]
     token_count = variate_ids.shape[0]
     segment, offsets = prompt_layout(prompt_lengths[0], token_count)
     same_prompt = segment[:, None] == segment[None, :]
@@ -139,18 +135,20 @@
     bias_table = lax.dynamic_slice_in_dim(
         variate_bias, lax.axis_index("tp") * local_heads, local_heads, 1
     )
-    residual = to_stored(residual_in)
+    residual = reorder(residual_in, stored_orders[0])
     for layer_index in range(layer_count):
         layer_bias = bias_table[layer_index]
         pair_bias = jnp.where(
             same_variate[None], layer_bias[:, 1][:, None, None], layer_bias[:, 0][:, None, None]
         )
+        if layer_index == 1:
+            residual = reorder(residual, block_of_shard)
         layer_weights = collect(layer_index)
         qkv_weight = layer_weights[:, : 3 * head_cols]
         out_weight = layer_weights[:, 3 * head_cols : 4 * head_cols]
         gate_up_weight = layer_weights[:, 4 * head_cols : 4 * head_cols + 2 * unit_cols]
         down_weight = layer_weights[:, 4 * head_cols + 2 * unit_cols :]
-        normed = rms_scaled(residual, gains[layer_index, 0]).astype(jnp.bfloat16)
+        normed = rms_scaled(residual, gains[layer_index][0]).astype(jnp.bfloat16)
         projected = project_rows(gather_tp(normed, tp_count), weight=qkv_weight)
         queries = rotate(
             projected[:, :head_cols].reshape(token_count, local_heads, head_size), offsets
@@ -184,13 +182,13 @@
             project_out(source=mixed_heads, weight=out_weight).astype(jnp.bfloat16), tp_count
         )
         residual = residual + head_total
-        normed_mlp = rms_scaled(residual, gains[layer_index, 1]).astype(jnp.bfloat16)
+        normed_mlp = rms_scaled(residual, gains[layer_index][1]).astype(jnp.bfloat16)
         hidden = gated_units(gather_tp(normed_mlp, tp_count), weight=gate_up_weight)
         unit_total = reduce_tp(
             project_out(source=hidden, weight=down_weight).astype(jnp.bfloat16), tp_count
         )
         residual = residual + unit_total
-    return from_stored(residual)
+    return reorder(residual, inverse_order)
 
 
 def solution(mesh):

time: 407 us -> 396 us (0.973)
  blocking collectives: 88.2 us -> 28.3 us
  waiting for transfers between devices: 171 us -> 212 us
  starting transfers between devices: 32.7 us -> 42 us
  matrix products: 42.5 us -> 48.6 us
  other arithmetic: 21 us -> 15.2 us
    all_to_all x2 -> x3, waiting for transfers between devices: 17.7 us -> 73 us  [gather_tp(): gathered = lax.all_to_all(stacked, 'tp', 0, 0, tiled=True)]
    all_gather x1, waiting for transfers between devices: 41.5 us -> 4.4 us  [collect(): return lax.all_gather(piece, SEQ_AXES, axis=0, tiled=True)]
    all_to_all x1 -> x0, blocking collectives: 31.5 us -> none  [reduce_tp(): received = lax.all_to_all(pieces, 'tp', 0, 0, tiled=True)]
    all_to_all x2 -> x1, blocking collectives: 56.7 us -> 28.3 us  [gather_tp(): gathered = lax.all_to_all(stacked, 'tp', 0, 0, tiled=True)]
    all_to_all x3 -> x4, waiting for transfers between devices: 82.4 us -> 110 us  [reduce_tp(): received = lax.all_to_all(pieces, 'tp', 0, 0, tiled=True)]
    all_to_all x2 -> x3, starting transfers between devices: 7.95 us -> 12.9 us  [gather_tp(): gathered = lax.all_to_all(stacked, 'tp', 0, 0, tiled=True)]
    all_to_all x3 -> x4, starting transfers between devices: 11.7 us -> 15.7 us  [reduce_tp(): received = lax.all_to_all(pieces, 'tp', 0, 0, tiled=True)]
  transfers between devices with their start and end apart: 10 -> 11, of which waited for: 8 -> 10; matrix products, arithmetic and copies ran while one was open for 7% -> 9% of each run, Pallas kernels for 0% -> 0%
where the time goes in v4:
time: 396 us; the launch traced here: 393 us
  waiting for transfers between devices  212 us (54%)
  matrix products  48.6 us (12%)
  starting transfers between devices  42 us (11%)
  local copies, waits for them, and re-layouts  32.9 us (8%)
  blocking collectives  28.3 us (7%)
  other arithmetic  15.2 us (4%)
  between operations  14.2 us (4%)
    all_to_all x4, waiting for transfers between devices, reduce_tp(): received = lax.all_to_all(pieces, 'tp', 0, 0, tiled=True)  110 us
    all_to_all x3, waiting for transfers between devices, gather_tp(): gathered = lax.all_to_all(stacked, 'tp', 0, 0, tiled=True)  73 us
    all_to_all x1, blocking collectives, gather_tp(): gathered = lax.all_to_all(stacked, 'tp', 0, 0, tiled=True)  28.3 us
    all_to_all x1, waiting for transfers between devices, collect(): lax.all_to_all(stacked, CHIP_AXES, 0, 0, tiled=True)  19.4 us
    sub x2, matrix products, on_device(): weights_exp = jnp.exp(scores - row_peak)  19.1 us
    all_to_all x4, starting transfers between devices, reduce_tp(): received = lax.all_to_all(pieces, 'tp', 0, 0, tiled=True)  15.7 us
    all_to_all x3, starting transfers between devices, gather_tp(): gathered = lax.all_to_all(stacked, 'tp', 0, 0, tiled=True)  12.9 us
    dot_general x4, matrix products, project_out(): lax.dot_general(source, weight, (((1,), (1,)), ((), ())), preferred_eleme...  10.8 us
  transfers between devices with their start and end apart: 11, of which 10 were waited for; matrix products, arithmetic and copies ran while one was open for 9% of the time, Pallas kernels for 0%

profile of v4, /device:TPU:0, one launch (start us, length us, event | category | flops | bytes accessed | tf_op | source)
XLA Modules:
  0.0 393.2 jit_solution(3459460521746365691)
XLA Ops:
  9.4 5.4 %all-to-all-start.1 = ((bf16[2,8,8,1568]{3,1,0,2:T(8,128)(2,1)}), bf16[2,8,8,1568]{3,1,0,2:T(8,128)(2,1)S(1)}, u32[]{:S(2)}, u32[]{:S(2)}) async-start(bf16[2,8,8,1568]{3,1,0,2:T(8,128)(2,1)} %copy.84), calls=%async_computation.1 | async-start | bytes 851968 | tf_op jit(solution)/shard_map/all_to_all | solution.py:94
  18.1 5.1 %all-to-all-done.1 = bf16[2,8,8,1568]{3,1,0,2:T(8,128)(2,1)S(1)} async-done(((bf16[2,8,8,1568]{3,1,0,2:T(8,128)(2,1)}), bf16[2,8,8,1568]{3,1,0,2:T(8,128)(2,1)S(1)}, u32[]{:S(2)}, u32[]{:S(2)}) %all-to-all-start.1) | async-done | bytes 401440 | tf_op jit(solution)/shard_map/all_to_all | solution.py:94
  25.3 7.8 %all-to-all-start.2 = ((bf16[8,64,1568]{2,1,0:T(8,128)(2,1)}), bf16[8,64,1568]{2,1,0:T(8,128)(2,1)S(1)}, u32[]{:S(2)}, u32[]{:S(2)}) async-start(bf16[8,64,1568]{2,1,0:T(8,128)(2,1)} %broadcast_in_dim.178), calls=%async_computation.2 | async-start | bytes 3407872 | tf_op jit(solution)/shard_map/all_to_all | solution.py:107
  36.7 19.4 %all-to-all-done.2 = bf16[8,64,1568]{2,1,0:T(8,128)(2,1)S(1)} async-done(((bf16[8,64,1568]{2,1,0:T(8,128)(2,1)}), bf16[8,64,1568]{2,1,0:T(8,128)(2,1)S(1)}, u32[]{:S(2)}, u32[]{:S(2)}) %all-to-all-start.2) | async-done | bytes 1605664 | tf_op jit(solution)/shard_map/all_to_all | solution.py:107
  57.7 4.3 %all-to-all-start = ((bf16[8,128,1024]{2,1,0:T(8,128)(2,1)}), bf16[8,128,1024]{2,1,0:T(8,128)(2,1)}, u32[]{:S(2)}, u32[]{:S(2)}) async-start(bf16[8,128,1024]{2,1,0:T(8,128)(2,1)} %broadcast_in_dim.176), calls=%async_computation | async-start | bytes 4194304 | tf_op jit(solution)/shard_map/all_to_all | solution.py:60
  72.0 18.3 %all-to-all-done = bf16[8,128,1024]{2,1,0:T(8,128)(2,1)} async-done(((bf16[8,128,1024]{2,1,0:T(8,128)(2,1)}), bf16[8,128,1024]{2,1,0:T(8,128)(2,1)}, u32[]{:S(2)}, u32[]{:S(2)}) %all-to-all-start) | async-done | bytes 2097184 | tf_op jit(solution)/shard_map/all_to_all | solution.py:60
  94.0 10.0 %fusion.82 = (f32[2,1024]{1,0:T(2,128)}, f32[2,1024,1024]{1,2,0:T(8,128)}) fusion(f32[2]{0:T(128)S(1)} %copy-done.22, f32[2]{0:T(128)S(1)} %copy-done.21, pred[1024,1024]{0,1:T(8,128)(4,1)} %get-tuple-element.62, pred[1024,1024]{0,1:T(8,128)(4,1)} %get-tuple-element.63, bf16[1024,2,32]{0,2,1:T(8,128)(2,1)} %get-tuple-element.42, ...), kind=kOutput, calls=%fused_computation.187 | convolution fusion | flops 282067968 | bytes 11018256 | tf_op jit(solution)/shard_map/sub | solution.py:172
  104.0 4.4 %fusion.27 = bf16[2,64,1024]{2,1,0:T(8,128)(2,1)S(1)} fusion(bf16[1024,2,64]{0,2,1:T(8,128)(2,1)S(1)} %bitcast.145, f32[2,1024,1024]{1,2,0:T(8,128)} %get-tuple-element.51, f32[2,1024]{1,0:T(2,128)} %get-tuple-element.50), kind=kOutput, calls=%fused_computation.53 | convolution fusion | flops 272760832 | bytes 8921088 | tf_op jit(solution)/shard_map/hqk,khd->qhd/dot_general | solution.py:177
  110.4 4.5 %all-to-all-start.3 = ((bf16[8,128,1024]{2,1,0:T(8,128)(2,1)}), bf16[8,128,1024]{2,1,0:T(8,128)(2,1)}, u32[]{:S(2)}, u32[]{:S(2)}) async-start(bf16[8,128,1024]{2,1,0:T(8,128)(2,1)} %bitcast.132), calls=%async_computation.3 | async-start | bytes 4194304 | tf_op jit(solution)/shard_map/all_to_all | solution.py:66
  115.9 27.5 %all-to-all-done.3 = bf16[8,128,1024]{2,1,0:T(8,128)(2,1)} async-done(((bf16[8,128,1024]{2,1,0:T(8,128)(2,1)}), bf16[8,128,1024]{2,1,0:T(8,128)(2,1)}, u32[]{:S(2)}, u32[]{:S(2)}) %all-to-all-start.3) | async-done | bytes 2097184 | tf_op jit(solution)/shard_map/all_to_all | solution.py:66
  148.6 4.3 %all-to-all-start.4 = ((bf16[8,128,1024]{2,1,0:T(8,128)(2,1)}), bf16[8,128,1024]{2,1,0:T(8,128)(2,1)}, u32[]{:S(2)}, u32[]{:S(2)}) async-start(bf16[8,128,1024]{2,1,0:T(8,128)(2,1)} %broadcast_in_dim.189), calls=%async_computation.4 | async-start | bytes 4194304 | tf_op jit(solution)/shard_map/all_to_all | solution.py:60
  153.7 28.0 %all-to-all-done.4 = bf16[8,128,1024]{2,1,0:T(8,128)(2,1)} async-done(((bf16[8,128,1024]{2,1,0:T(8,128)(2,1)}), bf16[8,128,1024]{2,1,0:T(8,128)(2,1)}, u32[]{:S(2)}, u32[]{:S(2)}) %all-to-all-start.4) | async-done | bytes 2097184 | tf_op jit(solution)/shard_map/all_to_all | solution.py:60
  188.2 3.7 all-to-all-start.5
  194.9 26.1 %all-to-all-done.5 = bf16[8,128,1024]{2,1,0:T(8,128)(2,1)S(1)} async-done(((bf16[8,128,1024]{2,1,0:T(8,128)(2,1)}), bf16[8,128,1024]{2,1,0:T(8,128)(2,1)S(1)}, u32[]{:S(2)}, u32[]{:S(2)}) %all-to-all-start.5) | async-done | bytes 2097184 | tf_op jit(solution)/shard_map/all_to_all | solution.py:66
  226.6 4.2 %all-to-all-start.6 = ((bf16[8,128,1024]{2,1,0:T(8,128)(2,1)}), bf16[8,128,1024]{2,1,0:T(8,128)(2,1)S(1)}, u32[]{:S(2)}, u32[]{:S(2)}) async-start(bf16[8,128,1024]{2,1,0:T(8,128)(2,1)} %broadcast_in_dim.190), calls=%async_computation.6 | async-start | bytes 4194304 | tf_op jit(solution)/shard_map/all_to_all | solution.py:60
  231.2 4.4 %all-gather.2.cloned.1.call-done = bf16[1024,1568]{1,0:T(8,128)(2,1)} async-done(((bf16[64,1568]{1,0:T(8,128)(2,1)}), bf16[1024,1568]{1,0:T(8,128)(2,1)}) %all-gather.2.cloned.1.call-update) | async-done | bytes 3211280 | tf_op jit(solution)/shard_map/all_gather | solution.py:111
  235.6 26.7 %all-to-all-done.6 = bf16[8,128,1024]{2,1,0:T(8,128)(2,1)S(1)} async-done(((bf16[8,128,1024]{2,1,0:T(8,128)(2,1)}), bf16[8,128,1024]{2,1,0:T(8,128)(2,1)S(1)}, u32[]{:S(2)}, u32[]{:S(2)}) %all-to-all-start.6) | async-done | bytes 2097184 | tf_op jit(solution)/shard_map/all_to_all | solution.py:60
  266.1 9.1 %fusion.83 = (f32[2,1024]{1,0:T(2,128)S(1)}, f32[2,1024,1024]{1,2,0:T(8,128)}) fusion(f32[2]{0:T(128)S(1)} %get-tuple-element.12, f32[2]{0:T(128)S(1)} %get-tuple-element.11, pred[1024,1024]{0,1:T(8,128)(4,1)S(1)} %copy-done.6, pred[1024,1024]{0,1:T(8,128)(4,1)} %get-tuple-element.63, bf16[1024,2,32]{0,2,1:T(8,128)(2,1)} %get-tuple-element.40, ...), kind=kOutput, calls=%fused_computation.188 | convolution fusion | flops 282067968 | bytes 11018256 | tf_op jit(solution)/shard_map/sub | solution.py:172
  275.2 4.2 %fusion.26 = bf16[2,64,1024]{2,1,0:T(8,128)(2,1)S(1)} fusion(bf16[1024,2,64]{0,2,1:T(8,128)(2,1)S(1)} %bitcast.144, f32[2,1024,1024]{1,2,0:T(8,128)} %get-tuple-element.53, f32[2,1024]{1,0:T(2,128)S(1)} %get-tuple-element.52), kind=kOutput, calls=%fused_computation.52 | convolution fusion | flops 272760832 | bytes 8921088 | tf_op jit(solution)/shard_map/hqk,khd->qhd/dot_general | solution.py:177
  282.5 3.7 all-to-all-start.7
  287.4 28.8 %all-to-all-done.7 = bf16[8,128,1024]{2,1,0:T(8,128)(2,1)S(1)} async-done(((bf16[8,128,1024]{2,1,0:T(8,128)(2,1)}), bf16[8,128,1024]{2,1,0:T(8,128)(2,1)S(1)}, u32[]{:S(2)}, u32[]{:S(2)}) %all-to-all-start.7) | async-done | bytes 2097184 | tf_op jit(solution)/shard_map/all_to_all | solution.py:66
  318.0 28.3 %all_to_all.60 = bf16[8,128,1024]{2,1,0:T(8,128)(2,1)S(1)} all-to-all(bf16[8,128,1024]{2,1,0:T(8,128)(2,1)S(1)} %broadcast_in_dim.195), channel_id=1, replica_groups=mesh['chip'=8,'core'=2,'tp'=8] {'tp'}, dimensions={0} | all-to-all | bytes 4194304 | tf_op jit(solution)/shard_map/all_to_all | solution.py:60
  350.9 3.7 all-to-all-start.9
  354.7 27.1 %all-to-all-done.9 = bf16[8,128,1024]{2,1,0:T(8,128)(2,1)S(1)} async-done(((bf16[8,128,1024]{2,1,0:T(8,128)(2,1)}), bf16[8,128,1024]{2,1,0:T(8,128)(2,1)S(1)}, u32[]{:S(2)}, u32[]{:S(2)}) %all-to-all-start.9) | async-done | bytes 2097184 | tf_op jit(solution)/shard_map/all_to_all | solution.py:66
  (162 shorter events, 69.8 us)
Async XLA Ops:
  7.7 7.1 %copy-start = (s32[128]{0:T(128)S(1)}, s32[128]{0:T(128)}, u32[]{:S(2)}) copy-start(s32[128]{0:T(128)} %param.12) | copy-start | bytes 1540
  7.8 8.3 %copy-start.14 = (f32[2,2,1024]{2,1,0:T(2,128)S(1)}, f32[2,2,1024]{2,1,0:T(2,128)}, u32[]{:S(2)}) copy-start(f32[2,2,1024]{2,1,0:T(2,128)} %param.14) | copy-start | bytes 49156
  9.4 13.9 %all-to-all-start.1 = ((bf16[2,8,8,1568]{3,1,0,2:T(8,128)(2,1)}), bf16[2,8,8,1568]{3,1,0,2:T(8,128)(2,1)S(1)}, u32[]{:S(2)}, u32[]{:S(2)}) async-start(bf16[2,8,8,1568]{3,1,0,2:T(8,128)(2,1)} %copy.84), calls=%async_computation.1 | async-start | bytes 851968 | tf_op jit(solution)/shard_map/all_to_all | solution.py:94
  14.8 10.5 %copy-start.17 = (s32[128]{0:T(128)}, s32[128]{0:T(128)S(1)}, u32[]{:S(2)}) copy-start(s32[128]{0:T(128)S(1)} %compare_select_fusion.3) | copy-start | bytes 1540
  25.3 9.6 %copy-start.7 = (f32[128,1024]{1,0:T(8,128)S(1)}, f32[128,1024]{1,0:T(8,128)}, u32[]{:S(2)}) copy-start(f32[128,1024]{1,0:T(8,128)} %param.13) | copy-start | bytes 1572868
  25.3 30.8 %all-to-all-start.2 = ((bf16[8,64,1568]{2,1,0:T(8,128)(2,1)}), bf16[8,64,1568]{2,1,0:T(8,128)(2,1)S(1)}, u32[]{:S(2)}, u32[]{:S(2)}) async-start(bf16[8,64,1568]{2,1,0:T(8,128)(2,1)} %broadcast_in_dim.178), calls=%async_computation.2 | async-start | bytes 3407872 | tf_op jit(solution)/shard_map/all_to_all | solution.py:107
  57.7 32.7 %all-to-all-start = ((bf16[8,128,1024]{2,1,0:T(8,128)(2,1)}), bf16[8,128,1024]{2,1,0:T(8,128)(2,1)}, u32[]{:S(2)}, u32[]{:S(2)}) async-start(bf16[8,128,1024]{2,1,0:T(8,128)(2,1)} %broadcast_in_dim.176), calls=%async_computation | async-start | bytes 4194304 | tf_op jit(solution)/shard_map/all_to_all | solution.py:60
  62.0 4.2 %copy-start.13 = (s32[1024]{0:T(1024)S(1)}, s32[1024]{0:T(1024)}, u32[]{:S(2)}) copy-start(s32[1024]{0:T(1024)} %param.16) | copy-start | bytes 12292
  64.3 4.2 %collective-permute-start = (bf16[512,1568]{0,1:T(8,128)(2,1)}, bf16[512,1568]{0,1:T(8,128)(2,1)}, u32[]{:S(2)}, u32[]{:S(2)}) collective-permute-start(bf16[512,1568]{0,1:T(8,128)(2,1)} %copy.86), channel_id=1, source_target_pairs={{0,8},{8,0},{1,9},{9,1},{2,10},{10,2},{3,11},{11,3},{4,12},{12,4},... | collective-permute-start | bytes 4816904 | tf_op jit(solution)/shard_map/ppermute | solution.py:100
  104.0 4.4 %copy-start.1 = (bf16[512,1568]{1,0:T(8,128)(2,1)S(1)}, bf16[512,1568]{1,0:T(8,128)(2,1)}, u32[]{:S(2)}) copy-start(bf16[512,1568]{1,0:T(8,128)(2,1)} %copy.87) | copy-start | bytes 4816900
  110.4 5.5 %copy-start.11 = (f32[128,8]{1,0:T(8,128)S(1)}, f32[128,8]{1,0:T(8,128)}, u32[]{:S(2)}) copy-start(f32[128,8]{1,0:T(8,128)} %get-tuple-element.59) | copy-start | bytes 12292
  110.4 33.1 %all-to-all-start.3 = ((bf16[8,128,1024]{2,1,0:T(8,128)(2,1)}), bf16[8,128,1024]{2,1,0:T(8,128)(2,1)}, u32[]{:S(2)}, u32[]{:S(2)}) async-start(bf16[8,128,1024]{2,1,0:T(8,128)(2,1)} %bitcast.132), calls=%async_computation.3 | async-start | bytes 4194304 | tf_op jit(solution)/shard_map/all_to_all | solution.py:66
  148.6 33.1 %all-to-all-start.4 = ((bf16[8,128,1024]{2,1,0:T(8,128)(2,1)}), bf16[8,128,1024]{2,1,0:T(8,128)(2,1)}, u32[]{:S(2)}, u32[]{:S(2)}) async-start(bf16[8,128,1024]{2,1,0:T(8,128)(2,1)} %broadcast_in_dim.189), calls=%async_computation.4 | async-start | bytes 4194304 | tf_op jit(solution)/shard_map/all_to_all | solution.py:60
  153.0 82.6 %all-gather.2.cloned.1.call-start = ((), (), s32[]{:S(2)}) async-start(), calls=%async_computation.10 | async-start | bytes 3620864 | tf_op jit(solution)/shard_map/all_gather | solution.py:111
  188.2 6.0 %copy-start.10 = (f32[128,8]{1,0:T(8,128)S(1)}, f32[128,8]{1,0:T(8,128)}, u32[]{:S(2)}) copy-start(f32[128,8]{1,0:T(8,128)} %get-tuple-element.8) | copy-start | bytes 12292
  188.2 32.7 %all-to-all-start.5 = ((bf16[8,128,1024]{2,1,0:T(8,128)(2,1)}), bf16[8,128,1024]{2,1,0:T(8,128)(2,1)S(1)}, u32[]{:S(2)}, u32[]{:S(2)}) async-start(bf16[8,128,1024]{2,1,0:T(8,128)(2,1)} %bitcast.133), calls=%async_computation.5 | async-start | bytes 4194304 | tf_op jit(solution)/shard_map/all_to_all | solution.py:66
  194.2 29.3 %copy-start.19 = (s32[128]{0:T(128)}, s32[128]{0:T(128)S(1)}, u32[]{:S(2)}) copy-start(s32[128]{0:T(128)S(1)} %scatter_custom_fusion.1) | copy-start | bytes 1540
  226.6 35.6 %all-to-all-start.6 = ((bf16[8,128,1024]{2,1,0:T(8,128)(2,1)}), bf16[8,128,1024]{2,1,0:T(8,128)(2,1)S(1)}, u32[]{:S(2)}, u32[]{:S(2)}) async-start(bf16[8,128,1024]{2,1,0:T(8,128)(2,1)} %broadcast_in_dim.190), calls=%async_computation.6 | async-start | bytes 4194304 | tf_op jit(solution)/shard_map/all_to_all | solution.py:60
  266.1 9.1 %copy-start.8 = (bf16[1024,128]{0,1:T(8,128)(2,1)S(1)}, bf16[1024,128]{0,1:T(8,128)(2,1)}, u32[]{:S(2)}) copy-start(bf16[1024,128]{0,1:T(8,128)(2,1)} %slice.295) | copy-start | bytes 786436
  282.5 3.7 copy-start.9
  282.5 33.7 %all-to-all-start.7 = ((bf16[8,128,1024]{2,1,0:T(8,128)(2,1)}), bf16[8,128,1024]{2,1,0:T(8,128)(2,1)S(1)}, u32[]{:S(2)}, u32[]{:S(2)}) async-start(bf16[8,128,1024]{2,1,0:T(8,128)(2,1)} %bitcast.131), calls=%async_computation.7 | async-start | bytes 4194304 | tf_op jit(solution)/shard_map/all_to_all | solution.py:66
  318.0 28.3 %copy-start.12 = (bf16[1024,1568]{1,0:T(8,128)(2,1)S(1)}, bf16[1024,1568]{1,0:T(8,128)(2,1)}, u32[]{:S(2)}) copy-start(bf16[1024,1568]{1,0:T(8,128)(2,1)} %all-gather.2.cloned.1.call-done) | copy-start | bytes 9633796
  350.9 30.9 %all-to-all-start.9 = ((bf16[8,128,1024]{2,1,0:T(8,128)(2,1)}), bf16[8,128,1024]{2,1,0:T(8,128)(2,1)S(1)}, u32[]{:S(2)}, u32[]{:S(2)}) async-start(bf16[8,128,1024]{2,1,0:T(8,128)(2,1)} %bitcast.135), calls=%async_computation.9 | async-start | bytes 4194304 | tf_op jit(solution)/shard_map/all_to_all | solution.py:66
  354.7 29.5 %copy-start.4 = (f32[128,1024]{0,1:T(8,128)S(1)}, f32[128,1024]{0,1:T(8,128)}, u32[]{:S(2)}) copy-start(f32[128,1024]{0,1:T(8,128)} %copy-done.3) | copy-start | bytes 1572868
  (11 other events, 20.1 us)
Sparse Core Ops, SparseCore 0:
  156.3 79.2 all-gather.1

commit v5 on v4

--- a/solution.py
+++ b/solution.py
@@ -91,7 +91,7 @@
         )
         column_start = column_start + part_width
     grouped = jnp.concatenate(grouped_parts, axis=3)
-    regrouped = lax.all_to_all(grouped, "tp", split_axis=2, concat_axis=1, tiled=True)
+    weight_payload = jnp.moveaxis(grouped, 2, 0).reshape(tp_count, -1)
     chip_count = lax.axis_size(CHIP_AXES)
     core = lax.axis_index("core")
     core_swap = [(0, 1), (1, 0)]
@@ -100,8 +100,8 @@
         other = lax.ppermute(half, "core", core_swap)
         return jnp.concatenate([half, other], axis=0)
 
-    def collect(layer_index):
-        piece = regrouped[layer_index, :, 0, :]
+    def collect(layer_index, regrouped):
+        piece = regrouped[layer_index]
         if layer_index == 0:
             stacked = jnp.broadcast_to(piece[None], (chip_count,) + piece.shape)
             half = lax.all_to_all(stacked, CHIP_AXES, 0, 0, tiled=True).reshape(
@@ -143,13 +143,24 @@
         )
         if layer_index == 1:
             residual = reorder(residual, block_of_shard)
-        layer_weights = collect(layer_index)
+        normed = rms_scaled(residual, gains[layer_index][0]).astype(jnp.bfloat16)
+        if layer_index == 0:
+            token_payload = jnp.broadcast_to(normed.reshape(1, -1), (tp_count, normed.size))
+            received = lax.all_to_all(
+                jnp.concatenate([token_payload, weight_payload], axis=1), "tp", 0, 0, tiled=True
+            )
+            gathered = received[:, : normed.size].reshape(tp_count * normed.shape[0], model_width)
+            regrouped = jnp.moveaxis(
+                received[:, normed.size :].reshape(tp_count, layer_count, block_rows, -1), 0, 1
+            ).reshape(layer_count, tp_count * block_rows, -1)
+        else:
+            gathered = gather_tp(normed, tp_count)
+        layer_weights = collect(layer_index, regrouped)
         qkv_weight = layer_weights[:, : 3 * head_cols]
         out_weight = layer_weights[:, 3 * head_cols : 4 * head_cols]
         gate_up_weight = layer_weights[:, 4 * head_cols : 4 * head_cols + 2 * unit_cols]
         down_weight = layer_weights[:, 4 * head_cols + 2 * unit_cols :]
-        normed = rms_scaled(residual, gains[layer_index][0]).astype(jnp.bfloat16)
-        projected = project_rows(gather_tp(normed, tp_count), weight=qkv_weight)
+        projected = project_rows(gathered, weight=qkv_weight)
         queries = rotate(
             projected[:, :head_cols].reshape(token_count, local_heads, head_size), offsets
         ).astype(jnp.bfloat16)

time: 396 us -> 470 us (1.19)
  local copies, waits for them, and re-layouts: 32.9 us -> 71 us
  blocking collectives: 28.3 us -> 64.9 us
  other arithmetic: 15.2 us -> 32 us
  waiting for transfers between devices: 212 us -> 199 us
  starting transfers between devices: 42 us -> 34.2 us
    all_to_all x0 -> x1, blocking collectives: none -> 36.8 us  [on_device(): lax.all_to_all(jnp.concatenate([token_payload, weight_payload], axis=1),...]
    unnamed x50 -> x42, local copies, waits for them, and re-layouts: 0.9 us -> 18.1 us
    all_to_all x0 -> x2, other arithmetic: none -> 13.7 us  [on_device(): lax.all_to_all(jnp.concatenate([token_payload, weight_payload], axis=1),...]
    all_to_all x3 -> x2, waiting for transfers between devices: 73 us -> 60 us  [gather_tp(): gathered = lax.all_to_all(stacked, 'tp', 0, 0, tiled=True)]
    select_n x0 -> x1, local copies, waits for them, and re-layouts: none -> 7.54 us  [reorder(): return jnp.take(blocks, order, axis=-2).reshape(values.shape)]
    all_to_all x4, waiting for transfers between devices: 110 us -> 116 us  [reduce_tp(): received = lax.all_to_all(pieces, 'tp', 0, 0, tiled=True)]
    reshape x0 -> x3, local copies, waits for them, and re-layouts: none -> 5.73 us  [the longest x1 3.89 us: on_device(): received[:, :normed.size].reshape(tp_count * normed.shape[0], model_width)]
    reshape x3 -> x4, local copies, waits for them, and re-layouts: 2.99 us -> 8.56 us  [reorder(): return jnp.take(blocks, order, axis=-2).reshape(values.shape)]
  transfers between devices with their start and end apart: 11 -> 9, of which waited for: 10 -> 7; matrix products, arithmetic and copies ran while one was open for 9% -> 6% of each run, Pallas kernels for 0% -> 0%
where the time goes in v5:
time: 470 us; the launch traced here: 465 us
  waiting for transfers between devices  199 us (42%)
  local copies, waits for them, and re-layouts  71 us (15%)
  blocking collectives  64.9 us (14%)
  matrix products  49.1 us (10%)
  starting transfers between devices  34.2 us (7%)
  other arithmetic  32 us (7%)
  between operations  14.4 us (3%)
    all_to_all x4, waiting for transfers between devices, reduce_tp(): received = lax.all_to_all(pieces, 'tp', 0, 0, tiled=True)  116 us
    all_to_all x2, waiting for transfers between devices, gather_tp(): gathered = lax.all_to_all(stacked, 'tp', 0, 0, tiled=True)  60 us
    all_to_all x1, blocking collectives, on_device(): lax.all_to_all(jnp.concatenate([token_payload, weight_payload], axis=1),...  36.8 us
    all_to_all x1, blocking collectives, gather_tp(): gathered = lax.all_to_all(stacked, 'tp', 0, 0, tiled=True)  28.1 us
    all_to_all x1, waiting for transfers between devices, collect(): lax.all_to_all(stacked, CHIP_AXES, 0, 0, tiled=True)  22.7 us
    sub x2, matrix products, on_device(): weights_exp = jnp.exp(scores - row_peak)  19.1 us
    unnamed x42, local copies, waits for them, and re-layouts  18.1 us
    all_to_all x4, starting transfers between devices, reduce_tp(): received = lax.all_to_all(pieces, 'tp', 0, 0, tiled=True)  17.4 us
  transfers between devices with their start and end apart: 9, of which 7 were waited for; matrix products, arithmetic and copies ran while one was open for 6% of the time, Pallas kernels for 0%

profile of v5, /device:TPU:0, one launch (start us, length us, event | category | flops | bytes accessed | tf_op | source)
XLA Modules:
  0.0 464.9 jit_solution(3156824785561542370)
XLA Ops:
  15.9 7.5 %copy.86 = f32[128,128,8]{2,1,0:T(8,128)} copy(f32[128,128,8]{0,2,1:T(8,128)S(1)} %get-tuple-element.18) | data formatting | bytes 1048576 | tf_op jit(solution)/shard_map/jit(_take)/select_n | solution.py:123
  23.5 6.4 %reshape.540 = f32[131072]{0:T(1024)S(1)} reshape(f32[128,128,8]{2,1,0:T(8,128)} %copy.86) | data formatting | bytes 1048576 | tf_op jit(solution)/shard_map/reshape | solution.py:123
  34.5 9.1 %maximum_bitcast_fusion = bf16[8,1,156160]{2,0,1:T(8,128)(2,1)} fusion(bf16[8,25088]{1,0:T(8,128)(2,1)S(1)} %copy-done.3, bf16[156160]{0:T(1024)(128)(2,1)S(1)} %pad.10.clone), kind=kLoop, calls=%fused_computation.36 | loop fusion | flops 4997120 | bytes 3212288 | tf_op jit(solution)/shard_map/all_to_all | solution.py:149
  44.1 4.7 %reduce.28 = bf16[8,156160]{1,0:T(8,128)(2,1)} reduce(bf16[8,1,156160]{2,0,1:T(8,128)(2,1)} %maximum_bitcast_fusion, bf16[]{:T(256)} %broadcast.509), dimensions={1}, to_apply=%copy.95.reduce_sub_computation | reduce | bytes 4997122 | tf_op jit(solution)/shard_map/all_to_all | solution.py:149
  52.5 36.8 %all_to_all.52 = bf16[8,2,78080]{2,1,0:T(2,128)(2,1)} all-to-all(bf16[8,2,78080]{2,1,0:T(2,128)(2,1)} %reshape.681), channel_id=1, replica_groups=mesh['chip'=8,'core'=2,'tp'=8] {'tp'}, dimensions={0} | all-to-all | bytes 4997120 | tf_op jit(solution)/shard_map/all_to_all | solution.py:149
  89.3 8.3 %reshape.682 = bf16[8,1,156160]{2,1,0:T(2,128)(2,1)} reshape(bf16[8,2,78080]{2,1,0:T(2,128)(2,1)} %all_to_all.52) | data formatting | bytes 4997120
  104.9 7.9 %all-to-all-start.1 = ((bf16[8,64,1568]{2,1,0:T(8,128)(2,1)}), bf16[8,64,1568]{2,1,0:T(8,128)(2,1)S(1)}, u32[]{:S(2)}, u32[]{:S(2)}) async-start(bf16[8,64,1568]{2,1,0:T(8,128)(2,1)} %broadcast_in_dim.177), calls=%async_computation.1 | async-start | bytes 3407872 | tf_op jit(solution)/shard_map/all_to_all | solution.py:107
  112.8 22.7 %all-to-all-done.1 = bf16[8,64,1568]{2,1,0:T(8,128)(2,1)S(1)} async-done(((bf16[8,64,1568]{2,1,0:T(8,128)(2,1)}), bf16[8,64,1568]{2,1,0:T(8,128)(2,1)S(1)}, u32[]{:S(2)}, u32[]{:S(2)}) %all-to-all-start.1) | async-done | bytes 1605664 | tf_op jit(solution)/shard_map/all_to_all | solution.py:107
  156.0 10.0 %fusion.81 = (f32[2,1024]{1,0:T(2,128)}, f32[2,1024,1024]{1,2,0:T(8,128)}) fusion(f32[2]{0:T(128)} %get-tuple-element.14, f32[2]{0:T(128)S(1)} %copy-done.15, pred[1024,1024]{0,1:T(8,128)(4,1)} %get-tuple-element.58, pred[1024,1024]{0,1:T(8,128)(4,1)} %get-tuple-element.59, bf16[1024,2,32]{0,2,1:T(8,128)(2,1)} %get-tuple-element.42, ...), kind=kOutput, calls=%fused_computation.186 | convolution fusion | flops 282067968 | bytes 11018256 | tf_op jit(solution)/shard_map/sub | solution.py:183
  166.0 4.4 fusion.27
  172.4 4.9 %all-to-all-start.2 = ((bf16[8,128,1024]{2,1,0:T(8,128)(2,1)}), bf16[8,128,1024]{2,1,0:T(8,128)(2,1)}, u32[]{:S(2)}, u32[]{:S(2)}) async-start(bf16[8,128,1024]{2,1,0:T(8,128)(2,1)} %bitcast.120), calls=%async_computation.2 | async-start | bytes 4194304 | tf_op jit(solution)/shard_map/all_to_all | solution.py:66
  178.6 31.1 %all-to-all-done.2 = bf16[8,128,1024]{2,1,0:T(8,128)(2,1)} async-done(((bf16[8,128,1024]{2,1,0:T(8,128)(2,1)}), bf16[8,128,1024]{2,1,0:T(8,128)(2,1)}, u32[]{:S(2)}, u32[]{:S(2)}) %all-to-all-start.2) | async-done | bytes 2097184 | tf_op jit(solution)/shard_map/all_to_all | solution.py:66
  214.7 4.3 all-to-all-start.3
  219.8 30.8 %all-to-all-done.3 = bf16[8,128,1024]{2,1,0:T(8,128)(2,1)} async-done(((bf16[8,128,1024]{2,1,0:T(8,128)(2,1)}), bf16[8,128,1024]{2,1,0:T(8,128)(2,1)}, u32[]{:S(2)}, u32[]{:S(2)}) %all-to-all-start.3) | async-done | bytes 2097184 | tf_op jit(solution)/shard_map/all_to_all | solution.py:60
  263.1 28.3 %all-to-all-done.4 = bf16[8,128,1024]{2,1,0:T(8,128)(2,1)S(1)} async-done(((bf16[8,128,1024]{2,1,0:T(8,128)(2,1)}), bf16[8,128,1024]{2,1,0:T(8,128)(2,1)S(1)}, u32[]{:S(2)}, u32[]{:S(2)}) %all-to-all-start.4) | async-done | bytes 2097184 | tf_op jit(solution)/shard_map/all_to_all | solution.py:66
  296.9 4.5 all-to-all-start.5
  302.2 29.3 %all-to-all-done.5 = bf16[8,128,1024]{2,1,0:T(8,128)(2,1)} async-done(((bf16[8,128,1024]{2,1,0:T(8,128)(2,1)}), bf16[8,128,1024]{2,1,0:T(8,128)(2,1)}, u32[]{:S(2)}, u32[]{:S(2)}) %all-to-all-start.5) | async-done | bytes 2097184 | tf_op jit(solution)/shard_map/all_to_all | solution.py:60
  335.9 9.1 %fusion.82 = (f32[2,1024]{1,0:T(2,128)S(1)}, f32[2,1024,1024]{1,2,0:T(8,128)}) fusion(f32[2]{0:T(128)} %get-tuple-element.12, f32[2]{0:T(128)S(1)} %get-tuple-element.11, pred[1024,1024]{0,1:T(8,128)(4,1)S(1)} %copy-done.4, pred[1024,1024]{0,1:T(8,128)(4,1)} %get-tuple-element.59, bf16[1024,2,32]{0,2,1:T(8,128)(2,1)} %get-tuple-element.40, ...), kind=kOutput, calls=%fused_computation.187 | convolution fusion | flops 282067968 | bytes 11018256 | tf_op jit(solution)/shard_map/sub | solution.py:183
  345.1 4.2 fusion.26
  352.3 4.5 all-to-all-start.6
  357.1 29.1 %all-to-all-done.6 = bf16[8,128,1024]{2,1,0:T(8,128)(2,1)} async-done(((bf16[8,128,1024]{2,1,0:T(8,128)(2,1)}), bf16[8,128,1024]{2,1,0:T(8,128)(2,1)}, u32[]{:S(2)}, u32[]{:S(2)}) %all-to-all-start.6) | async-done | bytes 2097184 | tf_op jit(solution)/shard_map/all_to_all | solution.py:66
  389.1 28.1 %all_to_all.53 = bf16[8,128,1024]{2,1,0:T(8,128)(2,1)S(1)} all-to-all(bf16[8,128,1024]{2,1,0:T(8,128)(2,1)S(1)} %broadcast_in_dim.194), channel_id=1, replica_groups=mesh['chip'=8,'core'=2,'tp'=8] {'tp'}, dimensions={0} | all-to-all | bytes 4194304 | tf_op jit(solution)/shard_map/all_to_all | solution.py:60
  421.7 4.3 all-to-all-start.8
  426.1 27.4 %all-to-all-done.8 = bf16[8,128,1024]{2,1,0:T(8,128)(2,1)} async-done(((bf16[8,128,1024]{2,1,0:T(8,128)(2,1)}), bf16[8,128,1024]{2,1,0:T(8,128)(2,1)}, u32[]{:S(2)}, u32[]{:S(2)}) %all-to-all-start.8) | async-done | bytes 2097184 | tf_op jit(solution)/shard_map/all_to_all | solution.py:66
  (165 shorter events, 93.0 us)
Async XLA Ops:
  6.5 4.2 copy-start.12
  8.8 5.7 %copy-start.14 = (s32[128]{0:T(128)}, s32[128]{0:T(128)S(1)}, u32[]{:S(2)}) copy-start(s32[128]{0:T(128)S(1)} %compare_select_fusion.3) | copy-start | bytes 1540
  10.7 4.0 copy-start.5
  100.7 1.5 copy-start.2
  104.9 30.6 %all-to-all-start.1 = ((bf16[8,64,1568]{2,1,0:T(8,128)(2,1)}), bf16[8,64,1568]{2,1,0:T(8,128)(2,1)S(1)}, u32[]{:S(2)}, u32[]{:S(2)}) async-start(bf16[8,64,1568]{2,1,0:T(8,128)(2,1)} %broadcast_in_dim.177), calls=%async_computation.1 | async-start | bytes 3407872 | tf_op jit(solution)/shard_map/all_to_all | solution.py:107
  112.8 24.9 %copy-start.13 = (f32[2,16,2]{1,2,0:T(2,128)S(1)}, f32[2,16,2]{1,2,0:T(2,128)}, u32[]{:S(2)}) copy-start(f32[2,16,2]{1,2,0:T(2,128)} %param.17) | copy-start | bytes 772
  112.8 25.0 %copy-start.16 = (s32[1,4]{1,0:T(1,128)S(1)}, s32[1,4]{1,0:T(1,128)}, u32[]{:S(2)}) copy-start(s32[1,4]{1,0:T(1,128)} %param.15) | copy-start | bytes 52
  112.8 26.8 %copy-start.11 = (s32[1024]{0:T(1024)S(1)}, s32[1024]{0:T(1024)}, u32[]{:S(2)}) copy-start(s32[1024]{0:T(1024)} %param.16) | copy-start | bytes 12292
  137.7 11.1 %collective-permute-start = (bf16[512,1568]{0,1:T(8,128)(2,1)}, bf16[512,1568]{0,1:T(8,128)(2,1)}, u32[]{:S(2)}, u32[]{:S(2)}) collective-permute-start(bf16[512,1568]{0,1:T(8,128)(2,1)} %copy.96), channel_id=1, source_target_pairs={{0,8},{8,0},{1,9},{9,1},{2,10},{10,2},{3,11},{11,3},{4,12},{12,4},... | collective-permute-start | bytes 4816904 | tf_op jit(solution)/shard_map/ppermute | solution.py:100
  166.0 4.4 copy-start
  172.4 4.9 %copy-start.9 = (f32[128,8]{1,0:T(8,128)S(1)}, f32[128,8]{1,0:T(8,128)}, u32[]{:S(2)}) copy-start(f32[128,8]{1,0:T(8,128)} %get-tuple-element.55) | copy-start | bytes 12292
  172.4 37.3 %all-to-all-start.2 = ((bf16[8,128,1024]{2,1,0:T(8,128)(2,1)}), bf16[8,128,1024]{2,1,0:T(8,128)(2,1)}, u32[]{:S(2)}, u32[]{:S(2)}) async-start(bf16[8,128,1024]{2,1,0:T(8,128)(2,1)} %bitcast.120), calls=%async_computation.2 | async-start | bytes 4194304 | tf_op jit(solution)/shard_map/all_to_all | solution.py:66
  214.7 35.9 %all-to-all-start.3 = ((bf16[8,128,1024]{2,1,0:T(8,128)(2,1)}), bf16[8,128,1024]{2,1,0:T(8,128)(2,1)}, u32[]{:S(2)}, u32[]{:S(2)}) async-start(bf16[8,128,1024]{2,1,0:T(8,128)(2,1)} %broadcast_in_dim.188), calls=%async_computation.3 | async-start | bytes 4194304 | tf_op jit(solution)/shard_map/all_to_all | solution.py:60
  219.1 83.1 %all-gather.2.cloned.1.call-start = ((), (), s32[]{:S(2)}) async-start(), calls=%async_computation.9 | async-start | bytes 3620864 | tf_op jit(solution)/shard_map/all_gather | solution.py:111
  250.6 3.6 copy-start.1
  257.1 5.9 %copy-start.8 = (f32[128,8]{1,0:T(8,128)S(1)}, f32[128,8]{1,0:T(8,128)}, u32[]{:S(2)}) copy-start(f32[128,8]{1,0:T(8,128)} %get-tuple-element.8) | copy-start | bytes 12292
  257.1 34.3 %all-to-all-start.4 = ((bf16[8,128,1024]{2,1,0:T(8,128)(2,1)}), bf16[8,128,1024]{2,1,0:T(8,128)(2,1)S(1)}, u32[]{:S(2)}, u32[]{:S(2)}) async-start(bf16[8,128,1024]{2,1,0:T(8,128)(2,1)} %bitcast.123), calls=%async_computation.4 | async-start | bytes 4194304 | tf_op jit(solution)/shard_map/all_to_all | solution.py:66
  296.9 34.5 %all-to-all-start.5 = ((bf16[8,128,1024]{2,1,0:T(8,128)(2,1)}), bf16[8,128,1024]{2,1,0:T(8,128)(2,1)}, u32[]{:S(2)}, u32[]{:S(2)}) async-start(bf16[8,128,1024]{2,1,0:T(8,128)(2,1)} %broadcast_in_dim.189), calls=%async_computation.5 | async-start | bytes 4194304 | tf_op jit(solution)/shard_map/all_to_all | solution.py:60
  334.2 1.7 copy-start.4
  335.9 9.1 %copy-start.6 = (bf16[1024,128]{0,1:T(8,128)(2,1)S(1)}, bf16[1024,128]{0,1:T(8,128)(2,1)}, u32[]{:S(2)}) copy-start(bf16[1024,128]{0,1:T(8,128)(2,1)} %slice.305) | copy-start | bytes 786436
  352.3 4.5 copy-start.7
  352.3 33.9 %all-to-all-start.6 = ((bf16[8,128,1024]{2,1,0:T(8,128)(2,1)}), bf16[8,128,1024]{2,1,0:T(8,128)(2,1)}, u32[]{:S(2)}, u32[]{:S(2)}) async-start(bf16[8,128,1024]{2,1,0:T(8,128)(2,1)} %bitcast.119), calls=%async_computation.6 | async-start | bytes 4194304 | tf_op jit(solution)/shard_map/all_to_all | solution.py:66
  389.0 28.2 %copy-start.10 = (bf16[1024,1568]{1,0:T(8,128)(2,1)S(1)}, bf16[1024,1568]{1,0:T(8,128)(2,1)}, u32[]{:S(2)}) copy-start(bf16[1024,1568]{1,0:T(8,128)(2,1)} %all-gather.2.cloned.1.call-done) | copy-start | bytes 9633796
  421.7 31.7 %all-to-all-start.8 = ((bf16[8,128,1024]{2,1,0:T(8,128)(2,1)}), bf16[8,128,1024]{2,1,0:T(8,128)(2,1)}, u32[]{:S(2)}, u32[]{:S(2)}) async-start(bf16[8,128,1024]{2,1,0:T(8,128)(2,1)} %bitcast.124), calls=%async_computation.8 | async-start | bytes 4194304 | tf_op jit(solution)/shard_map/all_to_all | solution.py:66
  (2 other events, 2.0 us)
Sparse Core Ops, SparseCore 0:
  222.4 77.3 all-gather.1

commit v6 on v4

--- a/solution.py
+++ b/solution.py
@@ -103,18 +103,21 @@
     def collect(layer_index):
         piece = regrouped[layer_index, :, 0, :]
         if layer_index == 0:
-            stacked = jnp.broadcast_to(piece[None], (chip_count,) + piece.shape)
-            half = lax.all_to_all(stacked, CHIP_AXES, 0, 0, tiled=True).reshape(
-                chip_count * piece.shape[0], piece.shape[1]
-            )
-            return join_cores(half)
+            shifted = [piece] + [
+                lax.ppermute(
+                    piece, CHIP_AXES, [(i, (i + shift) % chip_count) for i in range(chip_count)]
+                )
+                for shift in range(1, chip_count)
+            ]
+            return join_cores(jnp.concatenate(shifted, axis=0))
         return lax.all_gather(piece, SEQ_AXES, axis=0, tiled=True)
 
     block_index = jnp.arange(block_count, dtype=jnp.int32)
     half_blocks = block_count // 2
     core_of_block = jnp.where(block_index < half_blocks, core, 1 - core)
     within = block_index % half_blocks
-    shard_of_block = ((within // tp_count) * 2 + core_of_block) * tp_count + within % tp_count
+    source_chip = (lax.axis_index(CHIP_AXES) - within // tp_count) % chip_count
+    shard_of_block = (source_chip * 2 + core_of_block) * tp_count + within % tp_count
     block_of_shard = jnp.zeros_like(shard_of_block).at[shard_of_block].set(block_index)
     stored_orders = [shard_order[shard_of_block]] + [shard_order] * (layer_count - 1)
 

time: 396 us -> 414 us (1.045)
  the two profiles are of different devices: /device:TPU:0 before, /device:TPU:16 now
where the time goes in v6:
time: 414 us; the launch traced here: 405 us
  waiting for transfers between devices  162 us (39%)
  starting transfers between devices  62.6 us (15%)
  blocking collectives  55.8 us (13%)
  local copies, waits for them, and re-layouts  48.7 us (12%)
  matrix products  47.8 us (12%)
  between operations  14.5 us (4%)
  other arithmetic  13.5 us (3%)
    all_to_all x3, waiting for transfers between devices, reduce_tp(): received = lax.all_to_all(pieces, 'tp', 0, 0, tiled=True)  86.5 us
    all_to_all x3, waiting for transfers between devices, gather_tp(): gathered = lax.all_to_all(stacked, 'tp', 0, 0, tiled=True)  48.7 us
    all_to_all x1, blocking collectives, gather_tp(): gathered = lax.all_to_all(stacked, 'tp', 0, 0, tiled=True)  28.3 us
    all_to_all x1, blocking collectives, reduce_tp(): received = lax.all_to_all(pieces, 'tp', 0, 0, tiled=True)  27.4 us
    ppermute x7, waiting for transfers between devices, collect(): lax.ppermute(piece, CHIP_AXES, [(i, (i + shift) % chip_count) for i in ra...  25.7 us
    sub x2, matrix products, on_device(): weights_exp = jnp.exp(scores - row_peak)  18.3 us
    ppermute x7, starting transfers between devices, collect(): lax.ppermute(piece, CHIP_AXES, [(i, (i + shift) % chip_count) for i in ra...  17.6 us
    all_to_all x3, starting transfers between devices, reduce_tp(): received = lax.all_to_all(pieces, 'tp', 0, 0, tiled=True)  14.7 us
  transfers between devices with their start and end apart: 16, of which 10 were waited for; matrix products, arithmetic and copies ran while one was open for 13% of the time, Pallas kernels for 0%

profile of v6, /device:TPU:16, one launch (start us, length us, event | category | flops | bytes accessed | tf_op | source)
XLA Modules:
  0.0 405.3 jit_solution(6660843506996328694)
XLA Ops:
  9.4 5.0 %all-to-all-start.1 = ((bf16[2,8,8,1568]{3,1,0,2:T(8,128)(2,1)}), bf16[2,8,8,1568]{3,1,0,2:T(8,128)(2,1)S(1)}, u32[]{:S(2)}, u32[]{:S(2)}) async-start(bf16[2,8,8,1568]{3,1,0,2:T(8,128)(2,1)} %copy.72), calls=%async_computation.1 | async-start | bytes 851968 | tf_op jit(solution)/shard_map/all_to_all | solution.py:94
  24.4 4.3 %all-to-all-start = ((bf16[8,128,1024]{2,1,0:T(8,128)(2,1)}), bf16[8,128,1024]{2,1,0:T(8,128)(2,1)}, u32[]{:S(2)}, u32[]{:S(2)}) async-start(bf16[8,128,1024]{2,1,0:T(8,128)(2,1)} %broadcast_in_dim.169), calls=%async_computation | async-start | bytes 4194304 | tf_op jit(solution)/shard_map/all_to_all | solution.py:60
  33.5 4.6 %collective-permute-start.2 = (bf16[64,1568]{1,0:T(8,128)(2,1)S(1)}, bf16[64,1568]{1,0:T(8,128)(2,1)S(1)}, u32[]{:S(2)}, u32[]{:S(2)}) collective-permute-start(bf16[64,1568]{1,0:T(8,128)(2,1)S(1)} %get-tuple-element.31), channel_id=1, source_target_pairs={{0,48},{16,64},{32,80},{48,96},{64,112},{80,0},{96,16},{112,32},{1... | collective-permute-start | bytes 602120 | tf_op jit(solution)/shard_map/ppermute | solution.py:107
  40.3 17.4 %collective-permute-done = bf16[64,1568]{1,0:T(8,128)(2,1)S(1)} collective-permute-done((bf16[64,1568]{1,0:T(8,128)(2,1)S(1)}, bf16[64,1568]{1,0:T(8,128)(2,1)S(1)}, u32[]{:S(2)}, u32[]{:S(2)}) %collective-permute-start) | collective-permute-done | bytes 200736 | tf_op jit(solution)/shard_map/ppermute | solution.py:107
  57.7 4.0 collective-permute-start.5
  66.0 4.2 %collective-permute-done.4 = bf16[64,1568]{1,0:T(8,128)(2,1)S(1)} collective-permute-done((bf16[64,1568]{1,0:T(8,128)(2,1)S(1)}, bf16[64,1568]{1,0:T(8,128)(2,1)S(1)}, u32[]{:S(2)}, u32[]{:S(2)}) %collective-permute-start.4) | collective-permute-done | bytes 200736 | tf_op jit(solution)/shard_map/ppermute | solution.py:107
  94.4 6.5 %concatenate.28 = bf16[1024,1568]{0,1:T(8,128)(2,1)} concatenate(bf16[64,1568]{0,1:T(8,128)(2,1)S(1)} %copy.75, bf16[64,1568]{0,1:T(8,128)(2,1)S(1)} %copy.76, bf16[64,1568]{0,1:T(8,128)(2,1)} %copy.77, bf16[64,1568]{0,1:T(8,128)(2,1)} %copy.78, bf16[64,1568]{0,1:T(8,128)(2,1)} %copy.79, bf16[64,1568]{0,1:T(8,128)(2,1)} %copy.80, bf16[64,1568]{0,1:T(8,128)(2,1)} %copy.81, ...), dimensions={0} | concatenate | bytes 6422528 | tf_op jit(solution)/shard_map/concatenate | solution.py:101
  105.7 9.1 %fusion.74 = (f32[2,1024]{1,0:T(2,128)S(1)}, f32[2,1024,1024]{1,2,0:T(8,128)}) fusion(f32[2]{0:T(128)S(1)} %copy-done.29, f32[2]{0:T(128)S(1)} %copy-done.28, pred[1024,1024]{0,1:T(8,128)(4,1)S(1)} %copy-done.6, pred[1024,1024]{0,1:T(8,128)(4,1)} %get-tuple-element.65, bf16[1024,2,32]{0,2,1:T(8,128)(2,1)} %get-tuple-element.42, ...), kind=kOutput, calls=%fused_computation.189 | convolution fusion | flops 282067968 | bytes 11018256 | tf_op jit(solution)/shard_map/sub | solution.py:175
  114.8 4.2 %fusion.25 = bf16[2,64,1024]{2,1,0:T(8,128)(2,1)S(1)} fusion(bf16[1024,2,64]{0,2,1:T(8,128)(2,1)S(1)} %bitcast.143, f32[2,1024,1024]{1,2,0:T(8,128)} %get-tuple-element.51, f32[2,1024]{1,0:T(2,128)S(1)} %get-tuple-element.50), kind=kOutput, calls=%fused_computation.51 | convolution fusion | flops 272760832 | bytes 8921088 | tf_op jit(solution)/shard_map/hqk,khd->qhd/dot_general | solution.py:180
  122.1 7.2 %all-to-all-start.2 = ((bf16[8,128,1024]{2,1,0:T(8,128)(2,1)}), bf16[8,128,1024]{2,1,0:T(8,128)(2,1)S(1)}, u32[]{:S(2)}, u32[]{:S(2)}) async-start(bf16[8,128,1024]{2,1,0:T(8,128)(2,1)} %bitcast.128), calls=%async_computation.2 | async-start | bytes 4194304 | tf_op jit(solution)/shard_map/all_to_all | solution.py:66
  130.4 31.0 %all-to-all-done.2 = bf16[8,128,1024]{2,1,0:T(8,128)(2,1)S(1)} async-done(((bf16[8,128,1024]{2,1,0:T(8,128)(2,1)}), bf16[8,128,1024]{2,1,0:T(8,128)(2,1)S(1)}, u32[]{:S(2)}, u32[]{:S(2)}) %all-to-all-start.2) | async-done | bytes 2097184 | tf_op jit(solution)/shard_map/all_to_all | solution.py:66
  168.5 13.1 %all-gather.2.cloned.1.call-start = ((), (), s32[]{:S(2)}) async-start(), calls=%async_computation.9 | async-start | bytes 3620864 | tf_op jit(solution)/shard_map/all_gather | solution.py:113
  181.6 17.7 %all-to-all-done.3 = bf16[8,128,1024]{2,1,0:T(8,128)(2,1)S(1)} async-done(((bf16[8,128,1024]{2,1,0:T(8,128)(2,1)}), bf16[8,128,1024]{2,1,0:T(8,128)(2,1)S(1)}, u32[]{:S(2)}, u32[]{:S(2)}) %all-to-all-start.3) | async-done | bytes 2097184 | tf_op jit(solution)/shard_map/all_to_all | solution.py:60
  202.4 3.8 convolution_convert_fusion.1
  206.2 3.7 all-to-all-start.4
  212.9 26.7 %all-to-all-done.4 = bf16[8,128,1024]{2,1,0:T(8,128)(2,1)S(1)} async-done(((bf16[8,128,1024]{2,1,0:T(8,128)(2,1)}), bf16[8,128,1024]{2,1,0:T(8,128)(2,1)S(1)}, u32[]{:S(2)}, u32[]{:S(2)}) %all-to-all-start.4) | async-done | bytes 2097184 | tf_op jit(solution)/shard_map/all_to_all | solution.py:66
  245.4 4.1 %all-to-all-start.5 = ((bf16[8,128,1024]{2,1,0:T(8,128)(2,1)}), bf16[8,128,1024]{2,1,0:T(8,128)(2,1)S(1)}, u32[]{:S(2)}, u32[]{:S(2)}) async-start(bf16[8,128,1024]{2,1,0:T(8,128)(2,1)} %broadcast_in_dim.181), calls=%async_computation.5 | async-start | bytes 4194304 | tf_op jit(solution)/shard_map/all_to_all | solution.py:60
  249.7 31.1 %all-to-all-done.5 = bf16[8,128,1024]{2,1,0:T(8,128)(2,1)S(1)} async-done(((bf16[8,128,1024]{2,1,0:T(8,128)(2,1)}), bf16[8,128,1024]{2,1,0:T(8,128)(2,1)S(1)}, u32[]{:S(2)}, u32[]{:S(2)}) %all-to-all-start.5) | async-done | bytes 2097184 | tf_op jit(solution)/shard_map/all_to_all | solution.py:60
  284.7 9.1 %fusion.75 = (f32[2,1024]{1,0:T(2,128)S(1)}, f32[2,1024,1024]{1,2,0:T(8,128)}) fusion(f32[2]{0:T(128)S(1)} %get-tuple-element.12, f32[2]{0:T(128)S(1)} %get-tuple-element.11, pred[1024,1024]{0,1:T(8,128)(4,1)S(1)} %copy-done.7, pred[1024,1024]{0,1:T(8,128)(4,1)} %get-tuple-element.65, bf16[1024,2,32]{0,2,1:T(8,128)(2,1)} %get-tuple-element.40, ...), kind=kOutput, calls=%fused_computation.190 | convolution fusion | flops 282067968 | bytes 11018256 | tf_op jit(solution)/shard_map/sub | solution.py:175
  293.8 4.2 %fusion.24 = bf16[2,64,1024]{2,1,0:T(8,128)(2,1)S(1)} fusion(bf16[1024,2,64]{0,2,1:T(8,128)(2,1)S(1)} %bitcast.142, f32[2,1024,1024]{1,2,0:T(8,128)} %get-tuple-element.53, f32[2,1024]{1,0:T(2,128)S(1)} %get-tuple-element.52), kind=kOutput, calls=%fused_computation.50 | convolution fusion | flops 272760832 | bytes 8921088 | tf_op jit(solution)/shard_map/hqk,khd->qhd/dot_general | solution.py:180
  301.1 3.7 all-to-all-start.6
  305.9 28.8 %all-to-all-done.6 = bf16[8,128,1024]{2,1,0:T(8,128)(2,1)S(1)} async-done(((bf16[8,128,1024]{2,1,0:T(8,128)(2,1)}), bf16[8,128,1024]{2,1,0:T(8,128)(2,1)S(1)}, u32[]{:S(2)}, u32[]{:S(2)}) %all-to-all-start.6) | async-done | bytes 2097184 | tf_op jit(solution)/shard_map/all_to_all | solution.py:66
  336.5 28.3 %all_to_all.55 = bf16[8,128,1024]{2,1,0:T(8,128)(2,1)S(1)} all-to-all(bf16[8,128,1024]{2,1,0:T(8,128)(2,1)S(1)} %broadcast_in_dim.186), channel_id=1, replica_groups=mesh['chip'=8,'core'=2,'tp'=8] {'tp'}, dimensions={0} | all-to-all | bytes 4194304 | tf_op jit(solution)/shard_map/all_to_all | solution.py:60
  368.1 27.4 %all_to_all.56 = bf16[8,128,1024]{2,1,0:T(8,128)(2,1)S(1)} all-to-all(bf16[8,128,1024]{2,1,0:T(8,128)(2,1)S(1)} %bitcast.134), channel_id=1, replica_groups=mesh['chip'=8,'core'=2,'tp'=8] {'tp'}, dimensions={0} | all-to-all | bytes 4194304 | tf_op jit(solution)/shard_map/all_to_all | solution.py:66
  (201 shorter events, 91.5 us)
Async XLA Ops:
  7.8 8.0 %copy-start.23 = (f32[2,2,1024]{2,1,0:T(2,128)S(1)}, f32[2,2,1024]{2,1,0:T(2,128)}, u32[]{:S(2)}) copy-start(f32[2,2,1024]{2,1,0:T(2,128)} %param.14) | copy-start | bytes 49156
  9.4 13.5 %all-to-all-start.1 = ((bf16[2,8,8,1568]{3,1,0,2:T(8,128)(2,1)}), bf16[2,8,8,1568]{3,1,0,2:T(8,128)(2,1)S(1)}, u32[]{:S(2)}, u32[]{:S(2)}) async-start(bf16[2,8,8,1568]{3,1,0,2:T(8,128)(2,1)} %copy.72), calls=%async_computation.1 | async-start | bytes 851968 | tf_op jit(solution)/shard_map/all_to_all | solution.py:94
  24.4 76.5 %all-to-all-start = ((bf16[8,128,1024]{2,1,0:T(8,128)(2,1)}), bf16[8,128,1024]{2,1,0:T(8,128)(2,1)}, u32[]{:S(2)}, u32[]{:S(2)}) async-start(bf16[8,128,1024]{2,1,0:T(8,128)(2,1)} %broadcast_in_dim.169), calls=%async_computation | async-start | bytes 4194304 | tf_op jit(solution)/shard_map/all_to_all | solution.py:60
  29.6 28.2 %collective-permute-start = (bf16[64,1568]{1,0:T(8,128)(2,1)S(1)}, bf16[64,1568]{1,0:T(8,128)(2,1)S(1)}, u32[]{:S(2)}, u32[]{:S(2)}) collective-permute-start(bf16[64,1568]{1,0:T(8,128)(2,1)S(1)} %get-tuple-element.31), channel_id=1, source_target_pairs={{0,16},{16,32},{32,48},{48,64},{64,80},{80,96},{96,112},{112,0},{1... | collective-permute-start | bytes 602120 | tf_op jit(solution)/shard_map/ppermute | solution.py:107
  31.6 30.2 %collective-permute-start.1 = (bf16[64,1568]{1,0:T(8,128)(2,1)S(1)}, bf16[64,1568]{1,0:T(8,128)(2,1)S(1)}, u32[]{:S(2)}, u32[]{:S(2)}) collective-permute-start(bf16[64,1568]{1,0:T(8,128)(2,1)S(1)} %get-tuple-element.31), channel_id=1, source_target_pairs={{0,32},{16,48},{32,64},{48,80},{64,96},{80,112},{96,0},{112,16},{1... | collective-permute-start | bytes 602120 | tf_op jit(solution)/shard_map/ppermute | solution.py:107
  33.5 32.4 %collective-permute-start.2 = (bf16[64,1568]{1,0:T(8,128)(2,1)S(1)}, bf16[64,1568]{1,0:T(8,128)(2,1)S(1)}, u32[]{:S(2)}, u32[]{:S(2)}) collective-permute-start(bf16[64,1568]{1,0:T(8,128)(2,1)S(1)} %get-tuple-element.31), channel_id=1, source_target_pairs={{0,48},{16,64},{32,80},{48,96},{64,112},{80,0},{96,16},{112,32},{1... | collective-permute-start | bytes 602120 | tf_op jit(solution)/shard_map/ppermute | solution.py:107
  38.1 27.8 %collective-permute-start.3 = (bf16[64,1568]{1,0:T(8,128)(2,1)S(1)}, bf16[64,1568]{1,0:T(8,128)(2,1)S(1)}, u32[]{:S(2)}, u32[]{:S(2)}) collective-permute-start(bf16[64,1568]{1,0:T(8,128)(2,1)S(1)} %get-tuple-element.31), channel_id=1, source_target_pairs={{0,64},{16,80},{32,96},{48,112},{64,0},{80,16},{96,32},{112,48},{1... | collective-permute-start | bytes 602120 | tf_op jit(solution)/shard_map/ppermute | solution.py:107
  38.1 32.0 %collective-permute-start.4 = (bf16[64,1568]{1,0:T(8,128)(2,1)S(1)}, bf16[64,1568]{1,0:T(8,128)(2,1)S(1)}, u32[]{:S(2)}, u32[]{:S(2)}) collective-permute-start(bf16[64,1568]{1,0:T(8,128)(2,1)S(1)} %get-tuple-element.31), channel_id=1, source_target_pairs={{0,80},{16,96},{32,112},{48,0},{64,16},{80,32},{96,48},{112,64},{1... | collective-permute-start | bytes 602120 | tf_op jit(solution)/shard_map/ppermute | solution.py:107
  57.7 19.0 %copy-start.8 = (bf16[64,1568]{1,0:T(8,128)(2,1)}, bf16[64,1568]{1,0:T(8,128)(2,1)S(1)}, u32[]{:S(2)}) copy-start(bf16[64,1568]{1,0:T(8,128)(2,1)S(1)} %collective-permute-done) | copy-start | bytes 602116
  57.7 15.4 %collective-permute-start.5 = (bf16[64,1568]{1,0:T(8,128)(2,1)S(1)}, bf16[64,1568]{1,0:T(8,128)(2,1)S(1)}, u32[]{:S(2)}, u32[]{:S(2)}) collective-permute-start(bf16[64,1568]{1,0:T(8,128)(2,1)S(1)} %get-tuple-element.31), channel_id=1, source_target_pairs={{0,96},{16,112},{32,0},{48,16},{64,32},{80,48},{96,64},{112,80},{1... | collective-permute-start | bytes 602120 | tf_op jit(solution)/shard_map/ppermute | solution.py:107
  61.8 11.3 %copy-start.9 = (bf16[64,1568]{1,0:T(8,128)(2,1)}, bf16[64,1568]{1,0:T(8,128)(2,1)S(1)}, u32[]{:S(2)}) copy-start(bf16[64,1568]{1,0:T(8,128)(2,1)S(1)} %collective-permute-done.1) | copy-start | bytes 602116
  61.8 11.3 %collective-permute-start.6 = (bf16[64,1568]{1,0:T(8,128)(2,1)S(1)}, bf16[64,1568]{1,0:T(8,128)(2,1)S(1)}, u32[]{:S(2)}, u32[]{:S(2)}) collective-permute-start(bf16[64,1568]{1,0:T(8,128)(2,1)S(1)} %get-tuple-element.31), channel_id=1, source_target_pairs={{0,112},{16,0},{32,16},{48,32},{64,48},{80,64},{96,80},{112,96},{1... | collective-permute-start | bytes 602120 | tf_op jit(solution)/shard_map/ppermute | solution.py:107
  76.7 17.7 %collective-permute-start.7 = (bf16[512,1568]{0,1:T(8,128)(2,1)}, bf16[512,1568]{0,1:T(8,128)(2,1)S(1)}, u32[]{:S(2)}, u32[]{:S(2)}) collective-permute-start(bf16[512,1568]{0,1:T(8,128)(2,1)} %copy.74), channel_id=1, source_target_pairs={{0,8},{8,0},{1,9},{9,1},{2,10},{10,2},{3,11},{11,3},{4,12},{12,4},... | collective-permute-start | bytes 4816904 | tf_op jit(solution)/shard_map/ppermute | solution.py:100
  105.6 9.2 %copy-start.17 = (bf16[1024,128]{0,1:T(8,128)(2,1)S(1)}, bf16[1024,128]{0,1:T(8,128)(2,1)}, u32[]{:S(2)}) copy-start(bf16[1024,128]{0,1:T(8,128)(2,1)} %slice.310) | copy-start | bytes 786436
  122.1 8.2 %copy-start.20 = (f32[128,8]{1,0:T(8,128)S(1)}, f32[128,8]{1,0:T(8,128)}, u32[]{:S(2)}) copy-start(f32[128,8]{1,0:T(8,128)} %get-tuple-element.59) | copy-start | bytes 12292
  122.1 39.3 %all-to-all-start.2 = ((bf16[8,128,1024]{2,1,0:T(8,128)(2,1)}), bf16[8,128,1024]{2,1,0:T(8,128)(2,1)S(1)}, u32[]{:S(2)}, u32[]{:S(2)}) async-start(bf16[8,128,1024]{2,1,0:T(8,128)(2,1)} %bitcast.128), calls=%async_computation.2 | async-start | bytes 4194304 | tf_op jit(solution)/shard_map/all_to_all | solution.py:66
  164.9 34.4 %all-to-all-start.3 = ((bf16[8,128,1024]{2,1,0:T(8,128)(2,1)}), bf16[8,128,1024]{2,1,0:T(8,128)(2,1)S(1)}, u32[]{:S(2)}, u32[]{:S(2)}) async-start(bf16[8,128,1024]{2,1,0:T(8,128)(2,1)} %broadcast_in_dim.180), calls=%async_computation.3 | async-start | bytes 4194304 | tf_op jit(solution)/shard_map/all_to_all | solution.py:60
  168.5 81.2 %all-gather.2.cloned.1.call-start = ((), (), s32[]{:S(2)}) async-start(), calls=%async_computation.9 | async-start | bytes 3620864 | tf_op jit(solution)/shard_map/all_gather | solution.py:113
  206.2 33.4 %all-to-all-start.4 = ((bf16[8,128,1024]{2,1,0:T(8,128)(2,1)}), bf16[8,128,1024]{2,1,0:T(8,128)(2,1)S(1)}, u32[]{:S(2)}, u32[]{:S(2)}) async-start(bf16[8,128,1024]{2,1,0:T(8,128)(2,1)} %bitcast.131), calls=%async_computation.4 | async-start | bytes 4194304 | tf_op jit(solution)/shard_map/all_to_all | solution.py:66
  209.9 32.1 %copy-start.2 = (f32[128,1024]{0,1:T(8,128)S(1)}, f32[128,1024]{0,1:T(8,128)}, u32[]{:S(2)}) copy-start(f32[128,1024]{0,1:T(8,128)} %copy-done.1) | copy-start | bytes 1572868
  245.4 35.4 %all-to-all-start.5 = ((bf16[8,128,1024]{2,1,0:T(8,128)(2,1)}), bf16[8,128,1024]{2,1,0:T(8,128)(2,1)S(1)}, u32[]{:S(2)}, u32[]{:S(2)}) async-start(bf16[8,128,1024]{2,1,0:T(8,128)(2,1)} %broadcast_in_dim.181), calls=%async_computation.5 | async-start | bytes 4194304 | tf_op jit(solution)/shard_map/all_to_all | solution.py:60
  284.7 9.2 %copy-start.16 = (bf16[1024,128]{0,1:T(8,128)(2,1)S(1)}, bf16[1024,128]{0,1:T(8,128)(2,1)}, u32[]{:S(2)}) copy-start(bf16[1024,128]{0,1:T(8,128)(2,1)} %slice.309) | copy-start | bytes 786436
  301.1 33.7 %all-to-all-start.6 = ((bf16[8,128,1024]{2,1,0:T(8,128)(2,1)}), bf16[8,128,1024]{2,1,0:T(8,128)(2,1)S(1)}, u32[]{:S(2)}, u32[]{:S(2)}) async-start(bf16[8,128,1024]{2,1,0:T(8,128)(2,1)} %bitcast.127), calls=%async_computation.6 | async-start | bytes 4194304 | tf_op jit(solution)/shard_map/all_to_all | solution.py:66
  336.5 28.3 %copy-start.21 = (bf16[1024,1568]{1,0:T(8,128)(2,1)S(1)}, bf16[1024,1568]{1,0:T(8,128)(2,1)}, u32[]{:S(2)}) copy-start(bf16[1024,1568]{1,0:T(8,128)(2,1)} %all-gather.2.cloned.1.call-done) | copy-start | bytes 9633796
  (23 other events, 79.9 us)
Sparse Core Ops, SparseCore 0:
  181.8 66.6 all-gather.1

commit v7 on v4

--- a/solution.py
+++ b/solution.py
@@ -65,6 +65,17 @@
     pieces = products.reshape((tp_count, products.shape[0] // tp_count) + products.shape[1:])
     received = lax.all_to_all(pieces, "tp", 0, 0, tiled=True)
     return jnp.sum(received.astype(jnp.float32), axis=0)
+
+
+def project_owned(mixed_heads, out_weight, tp_count):
+    own_rows = mixed_heads.shape[0] // tp_count
+    pieces = mixed_heads.reshape(tp_count, own_rows, mixed_heads.shape[1])
+    received = lax.all_to_all(pieces, "tp", 0, 0, tiled=True)
+    group_weight = out_weight.reshape(out_weight.shape[0], tp_count, mixed_heads.shape[1])
+    products = jnp.einsum(
+        "gtc,rgc->gtr", received, group_weight, preferred_element_type=jnp.float32
+    ).astype(jnp.bfloat16)
+    return jnp.sum(products.astype(jnp.float32), axis=0)
 
 
 def on_device(
@@ -83,12 +94,13 @@
     rounded = trainer_rows.astype(jnp.bfloat16)
     grouped_parts = []
     column_start = 0
-    for part_width in part_widths:
-        grouped_parts.append(
-            rounded[:, :, column_start : column_start + part_width].reshape(
-                layer_count, block_rows, tp_count, part_width // tp_count
-            )
-        )
+    for part_index, part_width in enumerate(part_widths):
+        part = rounded[:, :, column_start : column_start + part_width]
+        if part_index == 3:
+            part = jnp.broadcast_to(part[:, :, None, :], (layer_count, block_rows, tp_count, part_width))
+        else:
+            part = part.reshape(layer_count, block_rows, tp_count, part_width // tp_count)
+        grouped_parts.append(part)
         column_start = column_start + part_width
     grouped = jnp.concatenate(grouped_parts, axis=3)
     regrouped = lax.all_to_all(grouped, "tp", split_axis=2, concat_axis=1, tiled=True)
@@ -145,9 +157,10 @@
             residual = reorder(residual, block_of_shard)
         layer_weights = collect(layer_index)
         qkv_weight = layer_weights[:, : 3 * head_cols]
-        out_weight = layer_weights[:, 3 * head_cols : 4 * head_cols]
-        gate_up_weight = layer_weights[:, 4 * head_cols : 4 * head_cols + 2 * unit_cols]
-        down_weight = layer_weights[:, 4 * head_cols + 2 * unit_cols :]
+        mlp_start = 3 * head_cols + model_width
+        out_weight = layer_weights[:, 3 * head_cols : mlp_start]
+        gate_up_weight = layer_weights[:, mlp_start : mlp_start + 2 * unit_cols]
+        down_weight = layer_weights[:, mlp_start + 2 * unit_cols :]
         normed = rms_scaled(residual, gains[layer_index][0]).astype(jnp.bfloat16)
         projected = project_rows(gather_tp(normed, tp_count), weight=qkv_weight)
         queries = rotate(
@@ -178,9 +191,7 @@
             .astype(jnp.bfloat16)
             .reshape(token_count, head_cols)
         )
-        head_total = reduce_tp(
-            project_out(source=mixed_heads, weight=out_weight).astype(jnp.bfloat16), tp_count
-        )
+        head_total = project_owned(mixed_heads, out_weight, tp_count)
         residual = residual + head_total
         normed_mlp = rms_scaled(residual, gains[layer_index][1]).astype(jnp.bfloat16)
         hidden = gated_units(gather_tp(normed_mlp, tp_count), weight=gate_up_weight)

time: 396 us -> 378 us (0.955)
  waiting for transfers between devices: 212 us -> 130 us
  blocking collectives: 28.3 us -> 78.4 us
  local copies, waits for them, and re-layouts: 32.9 us -> 53.5 us
  starting transfers between devices: 42 us -> 30.8 us
  other arithmetic: 15.2 us -> 19.8 us
    all_to_all x4 -> x2, waiting for transfers between devices: 110 us -> 50.4 us  [reduce_tp(): received = lax.all_to_all(pieces, 'tp', 0, 0, tiled=True)]
    all_to_all x1 -> x2, blocking collectives: 28.3 us -> 61.9 us  [gather_tp(): gathered = lax.all_to_all(stacked, 'tp', 0, 0, tiled=True)]
    all_to_all x3 -> x2, waiting for transfers between devices: 73 us -> 51.7 us  [gather_tp(): gathered = lax.all_to_all(stacked, 'tp', 0, 0, tiled=True)]
    all_to_all x0 -> x1, blocking collectives: none -> 16.5 us  [on_device(): lax.all_to_all(grouped, 'tp', split_axis=2, concat_axis=1, tiled=True)]
    slice x1 -> x5, local copies, waits for them, and re-layouts: 0.02 us -> 9.99 us  [the longest x3 9.95 us: on_device(): out_weight = layer_weights[:, 3 * head_cols:mlp_start]]
    all_to_all x1, waiting for transfers between devices: 19.4 us -> 28.2 us  [collect(): lax.all_to_all(stacked, CHIP_AXES, 0, 0, tiled=True)]
    all_to_all x4 -> x2, starting transfers between devices: 15.7 us -> 7.2 us  [reduce_tp(): received = lax.all_to_all(pieces, 'tp', 0, 0, tiled=True)]
    all_to_all x1 -> x2, waiting for transfers between devices: 5.13 us -> 0.01 us  [project_owned(): received = lax.all_to_all(pieces, 'tp', 0, 0, tiled=True)]
  transfers between devices with their start and end apart: 11 -> 9, of which waited for: 10 -> 5; matrix products, arithmetic and copies ran while one was open for 9% -> 21% of each run, Pallas kernels for 0% -> 0%
where the time goes in v7:
time: 378 us; the launch traced here: 376 us
  waiting for transfers between devices  130 us (34%)
  blocking collectives  78.4 us (21%)
  local copies, waits for them, and re-layouts  53.5 us (14%)
  matrix products  49.4 us (13%)
  starting transfers between devices  30.8 us (8%)
  other arithmetic  19.8 us (5%)
  between operations  14.1 us (4%)
    all_to_all x2, blocking collectives, gather_tp(): gathered = lax.all_to_all(stacked, 'tp', 0, 0, tiled=True)  61.9 us
    all_to_all x2, waiting for transfers between devices, gather_tp(): gathered = lax.all_to_all(stacked, 'tp', 0, 0, tiled=True)  51.7 us
    all_to_all x2, waiting for transfers between devices, reduce_tp(): received = lax.all_to_all(pieces, 'tp', 0, 0, tiled=True)  50.4 us
    all_to_all x1, waiting for transfers between devices, collect(): lax.all_to_all(stacked, CHIP_AXES, 0, 0, tiled=True)  28.2 us
    sub x2, matrix products, on_device(): weights_exp = jnp.exp(scores - row_peak)  19.5 us
    all_to_all x1, blocking collectives, on_device(): lax.all_to_all(grouped, 'tp', split_axis=2, concat_axis=1, tiled=True)  16.5 us
    slice x3, local copies, waits for them, and re-layouts, on_device(): out_weight = layer_weights[:, 3 * head_cols:mlp_start]  9.95 us
    dot_general x2, matrix products, on_device(): jnp.einsum('hqk,khd->qhd', attn_weights, values, preferred_element_type=j...  8.51 us
  transfers between devices with their start and end apart: 9, of which 5 were waited for; matrix products, arithmetic and copies ran while one was open for 21% of the time, Pallas kernels for 0%

profile of v7, /device:TPU:0, one launch (start us, length us, event | category | flops | bytes accessed | tf_op | source)
XLA Modules:
  0.0 376.3 jit_solution(3615781920992408555)
XLA Ops:
  8.8 16.5 %all_to_all.60 = bf16[2,8,8,2464]{3,1,0,2:T(8,128)(2,1)S(1)} all-to-all(bf16[2,8,8,2464]{3,1,0,2:T(8,128)(2,1)S(1)} %concatenate.22), channel_id=1, replica_groups=mesh['chip'=8,'core'=2,'tp'=8] {'tp'}, dimensions={2} | all-to-all | bytes 1261568 | tf_op jit(solution)/shard_map/all_to_all | solution.py:106
  27.8 7.8 %all-to-all-start.2 = ((bf16[8,64,2464]{2,1,0:T(8,128)(2,1)}), bf16[8,64,2464]{2,1,0:T(8,128)(2,1)S(1)}, u32[]{:S(2)}, u32[]{:S(2)}) async-start(bf16[8,64,2464]{2,1,0:T(8,128)(2,1)} %broadcast_in_dim.185), calls=%async_computation.2 | async-start | bytes 5242880 | tf_op jit(solution)/shard_map/all_to_all | solution.py:119
  39.9 28.2 %all-to-all-done.2 = bf16[8,64,2464]{2,1,0:T(8,128)(2,1)S(1)} async-done(((bf16[8,64,2464]{2,1,0:T(8,128)(2,1)}), bf16[8,64,2464]{2,1,0:T(8,128)(2,1)S(1)}, u32[]{:S(2)}, u32[]{:S(2)}) %all-to-all-start.2) | async-done | bytes 2523168 | tf_op jit(solution)/shard_map/all_to_all | solution.py:119
  77.6 4.5 %all-to-all-start = ((bf16[8,128,1024]{2,1,0:T(8,128)(2,1)}), bf16[8,128,1024]{2,1,0:T(8,128)(2,1)}, u32[]{:S(2)}, u32[]{:S(2)}) async-start(bf16[8,128,1024]{2,1,0:T(8,128)(2,1)} %broadcast_in_dim.182), calls=%async_computation | async-start | bytes 4194304 | tf_op jit(solution)/shard_map/all_to_all | solution.py:60
  86.6 4.5 %copy.126 = bf16[512,2464]{1,0:T(8,128)(2,1)} copy(bf16[512,2464]{0,1:T(8,128)(2,1)} %collective-permute-done) | data formatting | bytes 5046272 | tf_op jit(solution)/shard_map/ppermute | solution.py:112
  91.1 23.5 %all-to-all-done = bf16[8,128,1024]{2,1,0:T(8,128)(2,1)} async-done(((bf16[8,128,1024]{2,1,0:T(8,128)(2,1)}), bf16[8,128,1024]{2,1,0:T(8,128)(2,1)}, u32[]{:S(2)}, u32[]{:S(2)}) %all-to-all-start) | async-done | bytes 2097184 | tf_op jit(solution)/shard_map/all_to_all | solution.py:60
  119.1 10.3 %fusion.78 = (f32[2,1024]{1,0:T(2,128)}, f32[2,1024,1024]{1,2,0:T(8,128)}) fusion(f32[2]{0:T(128)} %get-tuple-element.14, f32[2]{0:T(128)S(1)} %copy-done.12, pred[1024,1024]{0,1:T(8,128)(4,1)} %get-tuple-element.60, pred[1024,1024]{0,1:T(8,128)(4,1)} %get-tuple-element.61, bf16[1024,2,32]{0,2,1:T(8,128)(2,1)} %get-tuple-element.42, ...), kind=kOutput, calls=%fused_computation.182 | convolution fusion | flops 282067968 | bytes 11018256 | tf_op jit(solution)/shard_map/sub | solution.py:185
  129.3 4.3 %fusion.27 = bf16[2,64,1024]{2,1,0:T(8,128)(2,1)S(1)} fusion(bf16[1024,2,64]{0,2,1:T(8,128)(2,1)} %bitcast.143, f32[2,1024,1024]{1,2,0:T(8,128)} %get-tuple-element.51, f32[2,1024]{1,0:T(2,128)} %get-tuple-element.50), kind=kOutput, calls=%fused_computation.54 | convolution fusion | flops 272760832 | bytes 8921088 | tf_op jit(solution)/shard_map/hqk,khd->qhd/dot_general | solution.py:190
  136.2 4.0 %all-to-all-start.3 = ((bf16[8,128,128]{2,1,0:T(8,128)(2,1)}), bf16[8,128,128]{2,1,0:T(8,128)(2,1)}, u32[]{:S(2)}, u32[]{:S(2)}) async-start(bf16[8,128,128]{2,1,0:T(8,128)(2,1)} %copy.129), calls=%async_computation.3 | async-start | bytes 524288 | tf_op jit(solution)/shard_map/all_to_all | solution.py:73
  146.1 4.0 %copy.130 = bf16[1024,1024]{0,1:T(8,128)(2,1)} copy(bf16[1024,1024]{1,0:T(8,128)(2,1)} %fusion.18) | data formatting | bytes 4194304 | tf_op jit(solution)/shard_map/slice | solution.py:161
  150.0 3.2 convert_reduce_fusion.3
  158.2 31.9 %all_to_all.61 = bf16[8,128,1024]{2,1,0:T(8,128)(2,1)S(1)} all-to-all(bf16[8,128,1024]{2,1,0:T(8,128)(2,1)S(1)} %broadcast_in_dim.196), channel_id=1, replica_groups=mesh['chip'=8,'core'=2,'tp'=8] {'tp'}, dimensions={0} | all-to-all | bytes 4194304 | tf_op jit(solution)/shard_map/all_to_all | solution.py:60
  194.7 3.6 all-to-all-start.5
  202.3 24.3 %all-to-all-done.5 = bf16[8,128,1024]{2,1,0:T(8,128)(2,1)S(1)} async-done(((bf16[8,128,1024]{2,1,0:T(8,128)(2,1)}), bf16[8,128,1024]{2,1,0:T(8,128)(2,1)S(1)}, u32[]{:S(2)}, u32[]{:S(2)}) %all-to-all-start.5) | async-done | bytes 2097184 | tf_op jit(solution)/shard_map/all_to_all | solution.py:66
  232.3 3.6 all-to-all-start.6
  236.2 28.3 %all-to-all-done.6 = bf16[8,128,1024]{2,1,0:T(8,128)(2,1)S(1)} async-done(((bf16[8,128,1024]{2,1,0:T(8,128)(2,1)}), bf16[8,128,1024]{2,1,0:T(8,128)(2,1)S(1)}, u32[]{:S(2)}, u32[]{:S(2)}) %all-to-all-start.6) | async-done | bytes 2097184 | tf_op jit(solution)/shard_map/all_to_all | solution.py:60
  268.4 9.2 %fusion.79 = (f32[2,1024]{1,0:T(2,128)S(1)}, f32[2,1024,1024]{1,2,0:T(8,128)}) fusion(f32[2]{0:T(128)S(1)} %get-tuple-element.12, f32[2]{0:T(128)S(1)} %get-tuple-element.11, pred[1024,1024]{0,1:T(8,128)(4,1)S(1)} %copy-done.5, pred[1024,1024]{0,1:T(8,128)(4,1)} %get-tuple-element.61, bf16[1024,2,32]{0,2,1:T(8,128)(2,1)} %get-tuple-element.40, ...), kind=kOutput, calls=%fused_computation.183 | convolution fusion | flops 282067968 | bytes 11018256 | tf_op jit(solution)/shard_map/sub | solution.py:185
  277.7 4.2 %fusion.26 = bf16[2,64,1024]{2,1,0:T(8,128)(2,1)S(1)} fusion(bf16[1024,2,64]{0,2,1:T(8,128)(2,1)S(1)} %bitcast.142, f32[2,1024,1024]{1,2,0:T(8,128)} %get-tuple-element.53, f32[2,1024]{1,0:T(2,128)S(1)} %get-tuple-element.52), kind=kOutput, calls=%fused_computation.53 | convolution fusion | flops 272760832 | bytes 8921088 | tf_op jit(solution)/shard_map/hqk,khd->qhd/dot_general | solution.py:190
  282.9 3.4 all-to-all-start.7
  297.9 30.0 %all_to_all.62 = bf16[8,128,1024]{2,1,0:T(8,128)(2,1)S(1)} all-to-all(bf16[8,128,1024]{2,1,0:T(8,128)(2,1)S(1)} %broadcast_in_dim.202), channel_id=1, replica_groups=mesh['chip'=8,'core'=2,'tp'=8] {'tp'}, dimensions={0} | all-to-all | bytes 4194304 | tf_op jit(solution)/shard_map/all_to_all | solution.py:60
  327.9 3.1 fusion.22
  331.1 4.1 %convolution_convert_fusion = bf16[1024,1024]{1,0:T(8,128)(2,1)} fusion(bf16[1024,2464]{1,0:T(8,128)(2,1)} %all-gather.2.cloned.1.call-done, f32[1024,704]{0,1:T(8,128)S(1)} %fusion.22), kind=kOutput, calls=%fused_computation.43 | convolution fusion | flops 741408768 | bytes 5767168 | tf_op jit(solution)/shard_map/dot_general | solution.py:53
  335.1 3.6 all-to-all-start.9
  338.8 26.2 %all-to-all-done.9 = bf16[8,128,1024]{2,1,0:T(8,128)(2,1)S(1)} async-done(((bf16[8,128,1024]{2,1,0:T(8,128)(2,1)}), bf16[8,128,1024]{2,1,0:T(8,128)(2,1)S(1)}, u32[]{:S(2)}, u32[]{:S(2)}) %all-to-all-start.9) | async-done | bytes 2097184 | tf_op jit(solution)/shard_map/all_to_all | solution.py:66
  (149 shorter events, 76.0 us)
Async XLA Ops:
  27.8 7.8 %copy-start.9 = (f32[2,2,1024]{2,1,0:T(2,128)S(1)}, f32[2,2,1024]{2,1,0:T(2,128)}, u32[]{:S(2)}) copy-start(f32[2,2,1024]{2,1,0:T(2,128)} %param.14) | copy-start | bytes 49156
  27.8 8.3 %copy-start = (s32[128]{0:T(128)S(1)}, s32[128]{0:T(128)}, u32[]{:S(2)}) copy-start(s32[128]{0:T(128)} %param.12) | copy-start | bytes 1540
  27.8 40.3 %all-to-all-start.2 = ((bf16[8,64,2464]{2,1,0:T(8,128)(2,1)}), bf16[8,64,2464]{2,1,0:T(8,128)(2,1)S(1)}, u32[]{:S(2)}, u32[]{:S(2)}) async-start(bf16[8,64,2464]{2,1,0:T(8,128)(2,1)} %broadcast_in_dim.185), calls=%async_computation.2 | async-start | bytes 5242880 | tf_op jit(solution)/shard_map/all_to_all | solution.py:119
  38.2 0.6 copy-start.11
  68.1 4.5 %copy-start.1 = (bf16[8,64,2464]{2,1,0:T(8,128)(2,1)}, bf16[8,64,2464]{2,1,0:T(8,128)(2,1)S(1)}, u32[]{:S(2)}) copy-start(bf16[8,64,2464]{2,1,0:T(8,128)(2,1)S(1)} %all-to-all-done.2) | copy-start | bytes 7569412
  68.2 5.4 %copy-start.6 = (f32[128,1024]{1,0:T(8,128)S(1)}, f32[128,1024]{1,0:T(8,128)}, u32[]{:S(2)}) copy-start(f32[128,1024]{1,0:T(8,128)} %param.13) | copy-start | bytes 1572868
  71.3 15.3 %collective-permute-start = (bf16[512,2464]{0,1:T(8,128)(2,1)}, bf16[512,2464]{0,1:T(8,128)(2,1)}, u32[]{:S(2)}, u32[]{:S(2)}) collective-permute-start(bf16[512,2464]{0,1:T(8,128)(2,1)} %copy.125), channel_id=1, source_target_pairs={{0,8},{8,0},{1,9},{9,1},{2,10},{10,2},{3,11},{11,3},{4,12},{12,4},... | collective-permute-start | bytes 7569416 | tf_op jit(solution)/shard_map/ppermute | solution.py:112
  77.6 4.7 %copy-start.13 = (s32[1,4]{1,0:T(1,128)S(1)}, s32[1,4]{1,0:T(1,128)}, u32[]{:S(2)}) copy-start(s32[1,4]{1,0:T(1,128)} %param.15) | copy-start | bytes 52
  77.6 4.9 %copy-start.10 = (f32[2,16,2]{1,2,0:T(2,128)S(1)}, f32[2,16,2]{1,2,0:T(2,128)}, u32[]{:S(2)}) copy-start(f32[2,16,2]{1,2,0:T(2,128)} %param.17) | copy-start | bytes 772
  77.6 6.6 %copy-start.8 = (s32[1024]{0:T(1024)S(1)}, s32[1024]{0:T(1024)}, u32[]{:S(2)}) copy-start(s32[1024]{0:T(1024)} %param.16) | copy-start | bytes 12292
  77.6 36.9 %all-to-all-start = ((bf16[8,128,1024]{2,1,0:T(8,128)(2,1)}), bf16[8,128,1024]{2,1,0:T(8,128)(2,1)}, u32[]{:S(2)}, u32[]{:S(2)}) async-start(bf16[8,128,1024]{2,1,0:T(8,128)(2,1)} %broadcast_in_dim.182), calls=%async_computation | async-start | bytes 4194304 | tf_op jit(solution)/shard_map/all_to_all | solution.py:60
  82.1 154.1 %all-gather.2.cloned.1.call-start = ((), (), s32[]{:S(2)}) async-start(), calls=%async_computation.10 | async-start | bytes 5570560 | tf_op jit(solution)/shard_map/all_gather | solution.py:123
  86.5 28.0 %copy-start.2 = (bf16[8,64,2464]{2,1,0:T(8,128)(2,1)S(1)}, bf16[8,64,2464]{2,1,0:T(8,128)(2,1)}, u32[]{:S(2)}) copy-start(bf16[8,64,2464]{2,1,0:T(8,128)(2,1)} %copy-done.1) | copy-start | bytes 7569412
  117.2 1.8 copy-start.12
  136.2 13.8 %all-to-all-start.3 = ((bf16[8,128,128]{2,1,0:T(8,128)(2,1)}), bf16[8,128,128]{2,1,0:T(8,128)(2,1)}, u32[]{:S(2)}, u32[]{:S(2)}) async-start(bf16[8,128,128]{2,1,0:T(8,128)(2,1)} %copy.129), calls=%async_computation.3 | async-start | bytes 524288 | tf_op jit(solution)/shard_map/all_to_all | solution.py:73
  158.1 31.9 %copy-start.3 = (bf16[512,2464]{1,0:T(8,128)(2,1)S(1)}, bf16[512,2464]{1,0:T(8,128)(2,1)}, u32[]{:S(2)}) copy-start(bf16[512,2464]{1,0:T(8,128)(2,1)} %copy.126) | copy-start | bytes 7569412
  194.7 31.9 %all-to-all-start.5 = ((bf16[8,128,1024]{2,1,0:T(8,128)(2,1)}), bf16[8,128,1024]{2,1,0:T(8,128)(2,1)S(1)}, u32[]{:S(2)}, u32[]{:S(2)}) async-start(bf16[8,128,1024]{2,1,0:T(8,128)(2,1)} %bitcast.131), calls=%async_computation.5 | async-start | bytes 4194304 | tf_op jit(solution)/shard_map/all_to_all | solution.py:66
  198.3 30.7 %copy-start.4 = (f32[128,1024]{0,1:T(8,128)S(1)}, f32[128,1024]{0,1:T(8,128)}, u32[]{:S(2)}) copy-start(f32[128,1024]{0,1:T(8,128)} %copy.132) | copy-start | bytes 1572868
  232.3 32.2 %all-to-all-start.6 = ((bf16[8,128,1024]{2,1,0:T(8,128)(2,1)}), bf16[8,128,1024]{2,1,0:T(8,128)(2,1)S(1)}, u32[]{:S(2)}, u32[]{:S(2)}) async-start(bf16[8,128,1024]{2,1,0:T(8,128)(2,1)} %broadcast_in_dim.197), calls=%async_computation.6 | async-start | bytes 4194304 | tf_op jit(solution)/shard_map/all_to_all | solution.py:60
  266.6 1.8 copy-start.5
  268.4 9.2 %copy-start.7 = (bf16[1024,128]{0,1:T(8,128)(2,1)S(1)}, bf16[1024,128]{0,1:T(8,128)(2,1)}, u32[]{:S(2)}) copy-start(bf16[1024,128]{0,1:T(8,128)(2,1)} %slice.310) | copy-start | bytes 786436
  282.9 10.5 %all-to-all-start.7 = ((bf16[8,128,128]{2,1,0:T(8,128)(2,1)}), bf16[8,128,128]{2,1,0:T(8,128)(2,1)S(1)}, u32[]{:S(2)}, u32[]{:S(2)}) async-start(bf16[8,128,128]{2,1,0:T(8,128)(2,1)} %copy.139), calls=%async_computation.7 | async-start | bytes 524288 | tf_op jit(solution)/shard_map/all_to_all | solution.py:73
  335.1 29.8 %all-to-all-start.9 = ((bf16[8,128,1024]{2,1,0:T(8,128)(2,1)}), bf16[8,128,1024]{2,1,0:T(8,128)(2,1)S(1)}, u32[]{:S(2)}, u32[]{:S(2)}) async-start(bf16[8,128,1024]{2,1,0:T(8,128)(2,1)} %bitcast.133), calls=%async_computation.9 | async-start | bytes 4194304 | tf_op jit(solution)/shard_map/all_to_all | solution.py:66
Sparse Core Ops, SparseCore 0:
  86.7 69.4 all-gather.1

commit v8 on v7

--- a/solution.py
+++ b/solution.py
@@ -112,23 +112,21 @@
         other = lax.ppermute(half, "core", core_swap)
         return jnp.concatenate([half, other], axis=0)
 
-    def collect(layer_index):
-        piece = regrouped[layer_index, :, 0, :]
-        if layer_index == 0:
-            stacked = jnp.broadcast_to(piece[None], (chip_count,) + piece.shape)
-            half = lax.all_to_all(stacked, CHIP_AXES, 0, 0, tiled=True).reshape(
-                chip_count * piece.shape[0], piece.shape[1]
-            )
-            return join_cores(half)
+    def gather_seq(piece):
         return lax.all_gather(piece, SEQ_AXES, axis=0, tiled=True)
+
+    def gather_chips(piece):
+        stacked = jnp.broadcast_to(piece[None], (chip_count,) + piece.shape)
+        half = lax.all_to_all(stacked, CHIP_AXES, 0, 0, tiled=True).reshape(
+            chip_count * piece.shape[0], piece.shape[1]
+        )
+        return join_cores(half)
 
     block_index = jnp.arange(block_count, dtype=jnp.int32)
     half_blocks = block_count // 2
     core_of_block = jnp.where(block_index < half_blocks, core, 1 - core)
     within = block_index % half_blocks
     shard_of_block = ((within // tp_count) * 2 + core_of_block) * tp_count + within % tp_count
-    block_of_shard = jnp.zeros_like(shard_of_block).at[shard_of_block].set(block_index)
-    stored_orders = [shard_order[shard_of_block]] + [shard_order] * (layer_count - 1)
 
     def reorder(values, order):
         blocks = values.reshape(values.shape[:-1] + (block_count, block_rows))
@@ -136,7 +134,7 @@
 
     inverse_order = jnp.zeros_like(shard_order).at[shard_order].set(block_index)
 
-    gains = [reorder(norm_gains[i], stored_orders[i]) for i in range(layer_count)]
+    gains = [reorder(norm_gains[i], shard_order) for i in range(layer_count)]
     token_count = variate_ids.shape[0]
     segment, offsets = prompt_layout(prompt_lengths[0], token_count)
     same_prompt = segment[:, None] == segment[None, :]
@@ -147,21 +145,25 @@
     bias_table = lax.dynamic_slice_in_dim(
         variate_bias, lax.axis_index("tp") * local_heads, local_heads, 1
     )
-    residual = reorder(residual_in, stored_orders[0])
+    residual = reorder(residual_in, shard_order)
     for layer_index in range(layer_count):
         layer_bias = bias_table[layer_index]
         pair_bias = jnp.where(
             same_variate[None], layer_bias[:, 1][:, None, None], layer_bias[:, 0][:, None, None]
         )
-        if layer_index == 1:
-            residual = reorder(residual, block_of_shard)
-        layer_weights = collect(layer_index)
-        qkv_weight = layer_weights[:, : 3 * head_cols]
-        mlp_start = 3 * head_cols + model_width
-        out_weight = layer_weights[:, 3 * head_cols : mlp_start]
-        gate_up_weight = layer_weights[:, mlp_start : mlp_start + 2 * unit_cols]
-        down_weight = layer_weights[:, mlp_start + 2 * unit_cols :]
         normed = rms_scaled(residual, gains[layer_index][0]).astype(jnp.bfloat16)
+        piece = regrouped[layer_index, :, 0, :]
+        if layer_index == 0:
+            qkv_weight = gather_chips(piece[:, : 3 * head_cols])
+            normed = reorder(normed, shard_of_block)
+            layer_weights = gather_seq(piece[:, 3 * head_cols :])
+        else:
+            layer_weights = gather_seq(piece)
+            qkv_weight = layer_weights[:, : 3 * head_cols]
+            layer_weights = layer_weights[:, 3 * head_cols :]
+        out_weight = layer_weights[:, :model_width]
+        gate_up_weight = layer_weights[:, model_width : model_width + 2 * unit_cols]
+        down_weight = layer_weights[:, model_width + 2 * unit_cols :]
         projected = project_rows(gather_tp(normed, tp_count), weight=qkv_weight)
         queries = rotate(
             projected[:, :head_cols].reshape(token_count, local_heads, head_size), offsets

time: 378 us -> 347 us (0.918)
  local copies, waits for them, and re-layouts: 53.5 us -> 37.4 us
  waiting for transfers between devices: 130 us -> 118 us
  other arithmetic: 19.8 us -> 15.7 us
    all_to_all x1, waiting for transfers between devices: 28.2 us -> 8.9 us  [gather_chips(): lax.all_to_all(stacked, CHIP_AXES, 0, 0, tiled=True)]
    ppermute x1 -> x0, local copies, waits for them, and re-layouts: 4.54 us -> none  [join_cores(): other = lax.ppermute(half, 'core', core_swap)]
    all_to_all x2, waiting for transfers between devices: 50.4 us -> 54.9 us  [reduce_tp(): received = lax.all_to_all(pieces, 'tp', 0, 0, tiled=True)]
    slice x4 -> x7, local copies, waits for them, and re-layouts: 9.96 us -> 12.7 us  [the longest x4 11.9 us: on_device(): out_weight = layer_weights[:, :model_width]]
  transfers between devices with their start and end apart: 9 -> 10, of which waited for: 5 -> 7; matrix products, arithmetic and copies ran while one was open for 21% -> 18% of each run, Pallas kernels for 0% -> 0%
where the time goes in v8:
time: 347 us; the launch traced here: 346 us
  waiting for transfers between devices  118 us (34%)
  blocking collectives  79.4 us (23%)
  matrix products  48.2 us (14%)
  local copies, waits for them, and re-layouts  37.4 us (11%)
  starting transfers between devices  32.5 us (9%)
  other arithmetic  15.7 us (5%)
  between operations  14.1 us (4%)
    all_to_all x2, blocking collectives, gather_tp(): gathered = lax.all_to_all(stacked, 'tp', 0, 0, tiled=True)  62.7 us
    all_to_all x2, waiting for transfers between devices, reduce_tp(): received = lax.all_to_all(pieces, 'tp', 0, 0, tiled=True)  54.9 us
    all_to_all x2, waiting for transfers between devices, gather_tp(): gathered = lax.all_to_all(stacked, 'tp', 0, 0, tiled=True)  53.8 us
    sub x2, matrix products, on_device(): weights_exp = jnp.exp(scores - row_peak)  18 us
    all_to_all x1, blocking collectives, on_device(): lax.all_to_all(grouped, 'tp', split_axis=2, concat_axis=1, tiled=True)  16.6 us
    slice x4, local copies, waits for them, and re-layouts, on_device(): out_weight = layer_weights[:, :model_width]  11.9 us
    all_to_all x1, waiting for transfers between devices, gather_chips(): lax.all_to_all(stacked, CHIP_AXES, 0, 0, tiled=True)  8.9 us
    all_to_all x2, starting transfers between devices, reduce_tp(): received = lax.all_to_all(pieces, 'tp', 0, 0, tiled=True)  8.68 us
  transfers between devices with their start and end apart: 10, of which 7 were waited for; matrix products, arithmetic and copies ran while one was open for 18% of the time, Pallas kernels for 0%

profile of v8, /device:TPU:0, one launch (start us, length us, event | category | flops | bytes accessed | tf_op | source)
XLA Modules:
  0.0 345.5 jit_solution(767735261711812030)
XLA Ops:
  8.8 16.6 %all_to_all.60 = bf16[2,8,8,2464]{3,1,0,2:T(8,128)(2,1)S(1)} all-to-all(bf16[2,8,8,2464]{3,1,0,2:T(8,128)(2,1)S(1)} %concatenate.22), channel_id=1, replica_groups=mesh['chip'=8,'core'=2,'tp'=8] {'tp'}, dimensions={2} | all-to-all | bytes 1261568 | tf_op jit(solution)/shard_map/all_to_all | solution.py:106
  33.9 7.7 %all-to-all-start.2 = ((bf16[8,64,384]{2,1,0:T(8,128)(2,1)}), bf16[8,64,384]{2,1,0:T(8,128)(2,1)S(1)}, u32[]{:S(2)}, u32[]{:S(2)}) async-start(bf16[8,64,384]{2,1,0:T(8,128)(2,1)} %broadcast_in_dim.204), calls=%async_computation.2 | async-start | bytes 786432 | tf_op jit(solution)/shard_map/all_to_all | solution.py:120
  42.7 8.9 %all-to-all-done.2 = bf16[8,64,384]{2,1,0:T(8,128)(2,1)S(1)} async-done(((bf16[8,64,384]{2,1,0:T(8,128)(2,1)}), bf16[8,64,384]{2,1,0:T(8,128)(2,1)S(1)}, u32[]{:S(2)}, u32[]{:S(2)}) %all-to-all-start.2) | async-done | bytes 393248 | tf_op jit(solution)/shard_map/all_to_all | solution.py:120
  53.2 4.4 %all-to-all-start = ((bf16[8,128,1024]{2,1,0:T(8,128)(2,1)}), bf16[8,128,1024]{2,1,0:T(8,128)(2,1)S(1)}, u32[]{:S(2)}, u32[]{:S(2)}) async-start(bf16[8,128,1024]{2,1,0:T(8,128)(2,1)} %broadcast_in_dim.202), calls=%async_computation | async-start | bytes 4194304 | tf_op jit(solution)/shard_map/all_to_all | solution.py:60
  62.2 25.2 %all-to-all-done = bf16[8,128,1024]{2,1,0:T(8,128)(2,1)S(1)} async-done(((bf16[8,128,1024]{2,1,0:T(8,128)(2,1)}), bf16[8,128,1024]{2,1,0:T(8,128)(2,1)S(1)}, u32[]{:S(2)}, u32[]{:S(2)}) %all-to-all-start) | async-done | bytes 2097184 | tf_op jit(solution)/shard_map/all_to_all | solution.py:60
  91.0 9.2 %fusion.75 = (f32[2,1024]{1,0:T(2,128)}, f32[2,1024,1024]{1,2,0:T(8,128)}) fusion(f32[2]{0:T(128)} %get-tuple-element.12, f32[2]{0:T(128)} %get-tuple-element.11, pred[1024,1024]{0,1:T(8,128)(4,1)S(1)} %copy-done.3, pred[1024,1024]{0,1:T(8,128)(4,1)S(1)} %copy-done.5, bf16[1024,2,32]{0,2,1:T(8,128)(2,1)} %get-tuple-element.42, ...), kind=kOutput, calls=%fused_computation.175 | convolution fusion | flops 282067968 | bytes 11018256 | tf_op jit(solution)/shard_map/sub | solution.py:187
  100.3 4.2 %fusion.25 = bf16[2,64,1024]{2,1,0:T(8,128)(2,1)S(1)} fusion(bf16[1024,2,64]{0,2,1:T(8,128)(2,1)S(1)} %bitcast.139, f32[2,1024,1024]{1,2,0:T(8,128)} %get-tuple-element.55, f32[2,1024]{1,0:T(2,128)} %get-tuple-element.54), kind=kOutput, calls=%fused_computation.47 | convolution fusion | flops 272760832 | bytes 8921088 | tf_op jit(solution)/shard_map/hqk,khd->qhd/dot_general | solution.py:192
  105.5 4.2 %all-to-all-start.3 = ((bf16[8,128,128]{2,1,0:T(8,128)(2,1)}), bf16[8,128,128]{2,1,0:T(8,128)(2,1)S(1)}, u32[]{:S(2)}, u32[]{:S(2)}) async-start(bf16[8,128,128]{2,1,0:T(8,128)(2,1)} %copy.119), calls=%async_computation.3 | async-start | bytes 524288 | tf_op jit(solution)/shard_map/all_to_all | solution.py:73
  110.9 3.1 slice.232
  121.9 33.4 %all_to_all.61 = bf16[8,128,1024]{2,1,0:T(8,128)(2,1)S(1)} all-to-all(bf16[8,128,1024]{2,1,0:T(8,128)(2,1)S(1)} %broadcast_in_dim.215), channel_id=1, replica_groups=mesh['chip'=8,'core'=2,'tp'=8] {'tp'}, dimensions={0} | all-to-all | bytes 4194304 | tf_op jit(solution)/shard_map/all_to_all | solution.py:60
  155.3 3.2 fusion.20
  158.5 4.0 %convolution_convert_fusion.1 = bf16[1024,1024]{1,0:T(8,128)(2,1)} fusion(bf16[1024,2080]{1,0:T(8,128)(2,1)} %all-gather.3.cloned.1.call-done, f32[1024,704]{0,1:T(8,128)S(1)} %fusion.20), kind=kOutput, calls=%fused_computation.37 | convolution fusion | flops 741408768 | bytes 5767168 | tf_op jit(solution)/shard_map/dot_general | solution.py:53
  162.5 4.9 %all-to-all-start.5 = ((bf16[8,128,1024]{2,1,0:T(8,128)(2,1)}), bf16[8,128,1024]{2,1,0:T(8,128)(2,1)S(1)}, u32[]{:S(2)}, u32[]{:S(2)}) async-start(bf16[8,128,1024]{2,1,0:T(8,128)(2,1)} %bitcast.127), calls=%async_computation.5 | async-start | bytes 4194304 | tf_op jit(solution)/shard_map/all_to_all | solution.py:66
  167.5 29.0 %all-to-all-done.5 = bf16[8,128,1024]{2,1,0:T(8,128)(2,1)S(1)} async-done(((bf16[8,128,1024]{2,1,0:T(8,128)(2,1)}), bf16[8,128,1024]{2,1,0:T(8,128)(2,1)S(1)}, u32[]{:S(2)}, u32[]{:S(2)}) %all-to-all-start.5) | async-done | bytes 2097184 | tf_op jit(solution)/shard_map/all_to_all | solution.py:66
  202.7 3.6 %all-to-all-start.6 = ((bf16[8,128,1024]{2,1,0:T(8,128)(2,1)}), bf16[8,128,1024]{2,1,0:T(8,128)(2,1)S(1)}, u32[]{:S(2)}, u32[]{:S(2)}) async-start(bf16[8,128,1024]{2,1,0:T(8,128)(2,1)} %broadcast_in_dim.216), calls=%async_computation.6 | async-start | bytes 4194304 | tf_op jit(solution)/shard_map/all_to_all | solution.py:60
  206.6 28.6 %all-to-all-done.6 = bf16[8,128,1024]{2,1,0:T(8,128)(2,1)S(1)} async-done(((bf16[8,128,1024]{2,1,0:T(8,128)(2,1)}), bf16[8,128,1024]{2,1,0:T(8,128)(2,1)S(1)}, u32[]{:S(2)}, u32[]{:S(2)}) %all-to-all-start.6) | async-done | bytes 2097184 | tf_op jit(solution)/shard_map/all_to_all | solution.py:60
  239.2 8.8 %fusion.76 = (f32[2,1024]{1,0:T(2,128)S(1)}, f32[2,1024,1024]{1,2,0:T(8,128)}) fusion(f32[2]{0:T(128)S(1)} %get-tuple-element.10, f32[2]{0:T(128)S(1)} %get-tuple-element.9, pred[1024,1024]{0,1:T(8,128)(4,1)S(1)} %copy-done.4, pred[1024,1024]{0,1:T(8,128)(4,1)S(1)} %copy-done.6, bf16[1024,2,32]{0,2,1:T(8,128)(2,1)} %get-tuple-element.40, ...), kind=kOutput, calls=%fused_computation.176 | convolution fusion | flops 282067968 | bytes 11018256 | tf_op jit(solution)/shard_map/sub | solution.py:187
  248.0 4.2 %fusion.24 = bf16[2,64,1024]{2,1,0:T(8,128)(2,1)S(1)} fusion(bf16[1024,2,64]{0,2,1:T(8,128)(2,1)S(1)} %bitcast.138, f32[2,1024,1024]{1,2,0:T(8,128)} %get-tuple-element.57, f32[2,1024]{1,0:T(2,128)S(1)} %get-tuple-element.56), kind=kOutput, calls=%fused_computation.46 | convolution fusion | flops 272760832 | bytes 8921088 | tf_op jit(solution)/shard_map/hqk,khd->qhd/dot_general | solution.py:192
  253.2 3.7 %all-to-all-start.7 = ((bf16[8,128,128]{2,1,0:T(8,128)(2,1)}), bf16[8,128,128]{2,1,0:T(8,128)(2,1)S(1)}, u32[]{:S(2)}, u32[]{:S(2)}) async-start(bf16[8,128,128]{2,1,0:T(8,128)(2,1)} %copy.128), calls=%async_computation.7 | async-start | bytes 524288 | tf_op jit(solution)/shard_map/all_to_all | solution.py:73
  266.9 29.4 %all_to_all.62 = bf16[8,128,1024]{2,1,0:T(8,128)(2,1)S(1)} all-to-all(bf16[8,128,1024]{2,1,0:T(8,128)(2,1)S(1)} %broadcast_in_dim.221), channel_id=1, replica_groups=mesh['chip'=8,'core'=2,'tp'=8] {'tp'}, dimensions={0} | all-to-all | bytes 4194304 | tf_op jit(solution)/shard_map/all_to_all | solution.py:60
  296.2 3.2 fusion.18
  299.4 4.0 %convolution_convert_fusion = bf16[1024,1024]{1,0:T(8,128)(2,1)} fusion(bf16[1024,2464]{1,0:T(8,128)(2,1)} %all-gather.5.cloned.1.call-done, f32[1024,704]{0,1:T(8,128)S(1)} %fusion.18), kind=kOutput, calls=%fused_computation.36 | convolution fusion | flops 741408768 | bytes 5767168 | tf_op jit(solution)/shard_map/dot_general | solution.py:53
  303.5 3.7 %all-to-all-start.9 = ((bf16[8,128,1024]{2,1,0:T(8,128)(2,1)}), bf16[8,128,1024]{2,1,0:T(8,128)(2,1)S(1)}, u32[]{:S(2)}, u32[]{:S(2)}) async-start(bf16[8,128,1024]{2,1,0:T(8,128)(2,1)} %bitcast.126), calls=%async_computation.9 | async-start | bytes 4194304 | tf_op jit(solution)/shard_map/all_to_all | solution.py:66
  307.2 25.9 %all-to-all-done.9 = bf16[8,128,1024]{2,1,0:T(8,128)(2,1)S(1)} async-done(((bf16[8,128,1024]{2,1,0:T(8,128)(2,1)}), bf16[8,128,1024]{2,1,0:T(8,128)(2,1)S(1)}, u32[]{:S(2)}, u32[]{:S(2)}) %all-to-all-start.9) | async-done | bytes 2097184 | tf_op jit(solution)/shard_map/all_to_all | solution.py:66
  (149 shorter events, 58.2 us)
Async XLA Ops:
  6.5 104.3 %all-gather.3.cloned.1.call-start = ((), (), s32[]{:S(2)}) async-start(), calls=%async_computation.10 | async-start | bytes 4734976 | tf_op jit(solution)/shard_map/all_gather | solution.py:116
  8.4 18.6 %copy-start.11 = (f32[2,2,1024]{2,1,0:T(2,128)S(1)}, f32[2,2,1024]{2,1,0:T(2,128)}, u32[]{:S(2)}) copy-start(f32[2,2,1024]{2,1,0:T(2,128)} %param.14) | copy-start | bytes 49156
  8.8 18.7 %copy-start.15 = (s32[128]{0:T(128)S(1)}, s32[128]{0:T(128)}, u32[]{:S(2)}) copy-start(s32[128]{0:T(128)} %param.12) | copy-start | bytes 1540
  8.8 20.2 %copy-start.8 = (f32[128,1024]{1,0:T(8,128)S(1)}, f32[128,1024]{1,0:T(8,128)}, u32[]{:S(2)}) copy-start(f32[128,1024]{1,0:T(8,128)} %param.13) | copy-start | bytes 1572868
  33.9 17.6 %all-to-all-start.2 = ((bf16[8,64,384]{2,1,0:T(8,128)(2,1)}), bf16[8,64,384]{2,1,0:T(8,128)(2,1)S(1)}, u32[]{:S(2)}, u32[]{:S(2)}) async-start(bf16[8,64,384]{2,1,0:T(8,128)(2,1)} %broadcast_in_dim.204), calls=%async_computation.2 | async-start | bytes 786432 | tf_op jit(solution)/shard_map/all_to_all | solution.py:120
  42.6 15.0 %copy-start.12 = (f32[2,16,2]{1,2,0:T(2,128)S(1)}, f32[2,16,2]{1,2,0:T(2,128)}, u32[]{:S(2)}) copy-start(f32[2,16,2]{1,2,0:T(2,128)} %param.17) | copy-start | bytes 772
  42.7 15.2 %copy-start.16 = (s32[1,4]{1,0:T(1,128)S(1)}, s32[1,4]{1,0:T(1,128)}, u32[]{:S(2)}) copy-start(s32[1,4]{1,0:T(1,128)} %param.15) | copy-start | bytes 52
  53.2 6.6 %copy-start.10 = (s32[1024]{0:T(1024)S(1)}, s32[1024]{0:T(1024)}, u32[]{:S(2)}) copy-start(s32[1024]{0:T(1024)} %param.16) | copy-start | bytes 12292
  53.2 34.2 %all-to-all-start = ((bf16[8,128,1024]{2,1,0:T(8,128)(2,1)}), bf16[8,128,1024]{2,1,0:T(8,128)(2,1)S(1)}, u32[]{:S(2)}, u32[]{:S(2)}) async-start(bf16[8,128,1024]{2,1,0:T(8,128)(2,1)} %broadcast_in_dim.202), calls=%async_computation | async-start | bytes 4194304 | tf_op jit(solution)/shard_map/all_to_all | solution.py:60
  57.6 149.1 %all-gather.5.cloned.1.call-start = ((), (), s32[]{:S(2)}) async-start(), calls=%async_computation.11 | async-start | bytes 5570560 | tf_op jit(solution)/shard_map/all_gather | solution.py:116
  59.6 2.6 collective-permute-start
  89.4 1.6 copy-start.5
  105.5 11.4 %all-to-all-start.3 = ((bf16[8,128,128]{2,1,0:T(8,128)(2,1)}), bf16[8,128,128]{2,1,0:T(8,128)(2,1)S(1)}, u32[]{:S(2)}, u32[]{:S(2)}) async-start(bf16[8,128,128]{2,1,0:T(8,128)(2,1)} %copy.119), calls=%async_computation.3 | async-start | bytes 524288 | tf_op jit(solution)/shard_map/all_to_all | solution.py:73
  162.5 34.0 %all-to-all-start.5 = ((bf16[8,128,1024]{2,1,0:T(8,128)(2,1)}), bf16[8,128,1024]{2,1,0:T(8,128)(2,1)S(1)}, u32[]{:S(2)}, u32[]{:S(2)}) async-start(bf16[8,128,1024]{2,1,0:T(8,128)(2,1)} %bitcast.127), calls=%async_computation.5 | async-start | bytes 4194304 | tf_op jit(solution)/shard_map/all_to_all | solution.py:66
  202.7 32.5 %all-to-all-start.6 = ((bf16[8,128,1024]{2,1,0:T(8,128)(2,1)}), bf16[8,128,1024]{2,1,0:T(8,128)(2,1)S(1)}, u32[]{:S(2)}, u32[]{:S(2)}) async-start(bf16[8,128,1024]{2,1,0:T(8,128)(2,1)} %broadcast_in_dim.216), calls=%async_computation.6 | async-start | bytes 4194304 | tf_op jit(solution)/shard_map/all_to_all | solution.py:60
  237.4 1.8 copy-start.4
  237.4 1.8 copy-start.6
  239.2 8.8 %copy-start.9 = (bf16[1024,128]{0,1:T(8,128)(2,1)S(1)}, bf16[1024,128]{0,1:T(8,128)(2,1)}, u32[]{:S(2)}) copy-start(bf16[1024,128]{0,1:T(8,128)(2,1)} %slice.306) | copy-start | bytes 786436
  253.2 10.3 %all-to-all-start.7 = ((bf16[8,128,128]{2,1,0:T(8,128)(2,1)}), bf16[8,128,128]{2,1,0:T(8,128)(2,1)S(1)}, u32[]{:S(2)}, u32[]{:S(2)}) async-start(bf16[8,128,128]{2,1,0:T(8,128)(2,1)} %copy.128), calls=%async_computation.7 | async-start | bytes 524288 | tf_op jit(solution)/shard_map/all_to_all | solution.py:73
  265.0 1.5 copy-start.1
  265.0 1.5 copy-start.2
  266.3 29.9 %copy-start = (f32[128,1024]{0,1:T(8,128)}, f32[128,1024]{0,1:T(8,128)S(1)}, u32[]{:S(2)}) copy-start(f32[128,1024]{0,1:T(8,128)S(1)} %copy.131) | copy-start | bytes 1572868
  303.4 3.7 %copy-start.14 = (s32[128]{0:T(128)S(1)}, s32[128]{0:T(128)}, u32[]{:S(2)}) copy-start(s32[128]{0:T(128)} %copy-done.13) | copy-start | bytes 1540
  303.5 29.7 %all-to-all-start.9 = ((bf16[8,128,1024]{2,1,0:T(8,128)(2,1)}), bf16[8,128,1024]{2,1,0:T(8,128)(2,1)S(1)}, u32[]{:S(2)}, u32[]{:S(2)}) async-start(bf16[8,128,1024]{2,1,0:T(8,128)(2,1)} %bitcast.126), calls=%async_computation.9 | async-start | bytes 4194304 | tf_op jit(solution)/shard_map/all_to_all | solution.py:66
  (3 other events, 2.5 us)
Sparse Core Ops, SparseCore 0:
  27.2 72.4 all-gather.2
  102.2 70.4 all-gather.4

commit v9 on v8

--- a/solution.py
+++ b/solution.py
@@ -103,7 +103,9 @@
         grouped_parts.append(part)
         column_start = column_start + part_width
     grouped = jnp.concatenate(grouped_parts, axis=3)
-    regrouped = lax.all_to_all(grouped, "tp", split_axis=2, concat_axis=1, tiled=True)
+    attention_cols = 3 * head_cols + model_width
+    grouped = jnp.concatenate([grouped[0], grouped[1, :, :, :attention_cols]], axis=2)
+    regrouped = lax.all_to_all(grouped, "tp", split_axis=1, concat_axis=0, tiled=True)
     chip_count = lax.axis_size(CHIP_AXES)
     core = lax.axis_index("core")
     core_swap = [(0, 1), (1, 0)]
@@ -152,7 +154,8 @@
             same_variate[None], layer_bias[:, 1][:, None, None], layer_bias[:, 0][:, None, None]
         )
         normed = rms_scaled(residual, gains[layer_index][0]).astype(jnp.bfloat16)
-        piece = regrouped[layer_index, :, 0, :]
+        first_cols = regrouped.shape[2] - attention_cols
+        piece = regrouped[:, 0, :first_cols] if layer_index == 0 else regrouped[:, 0, first_cols:]
         if layer_index == 0:
             qkv_weight = gather_chips(piece[:, : 3 * head_cols])
             normed = reorder(normed, shard_of_block)
@@ -161,6 +164,9 @@
             layer_weights = gather_seq(piece)
             qkv_weight = layer_weights[:, : 3 * head_cols]
             layer_weights = layer_weights[:, 3 * head_cols :]
+            full_mlp = lax.all_gather(
+                rounded[layer_index, :, 4 * model_width :], SEQ_AXES + ("tp",), axis=0, tiled=True
+            )
         out_weight = layer_weights[:, :model_width]
         gate_up_weight = layer_weights[:, model_width : model_width + 2 * unit_cols]
         down_weight = layer_weights[:, model_width + 2 * unit_cols :]
@@ -196,10 +202,21 @@
         head_total = project_owned(mixed_heads, out_weight, tp_count)
         residual = residual + head_total
         normed_mlp = rms_scaled(residual, gains[layer_index][1]).astype(jnp.bfloat16)
-        hidden = gated_units(gather_tp(normed_mlp, tp_count), weight=gate_up_weight)
-        unit_total = reduce_tp(
-            project_out(source=hidden, weight=down_weight).astype(jnp.bfloat16), tp_count
-        )
+        if layer_index == 0:
+            hidden = gated_units(gather_tp(normed_mlp, tp_count), weight=gate_up_weight)
+            unit_total = reduce_tp(
+                project_out(source=hidden, weight=down_weight).astype(jnp.bfloat16), tp_count
+            )
+        else:
+            hidden = gated_units(normed_mlp, weight=full_mlp[:, : 2 * ff_width])
+            group_weight = full_mlp[:, 2 * ff_width :].reshape(model_width, tp_count, unit_cols)
+            products = jnp.einsum(
+                "tgu,rgu->gtr",
+                hidden.reshape(hidden.shape[0], tp_count, unit_cols),
+                group_weight,
+                preferred_element_type=jnp.float32,
+            ).astype(jnp.bfloat16)
+            unit_total = jnp.sum(products.astype(jnp.float32), axis=0)
         residual = residual + unit_total
     return reorder(residual, inverse_order)
 

time: 347 us -> 559 us (1.61)
  waiting for transfers between devices: 118 us -> 346 us
  blocking collectives: 79.4 us -> 48.9 us
  local copies, waits for them, and re-layouts: 37.4 us -> 52.1 us
    all_gather x0 -> x1, waiting for transfers between devices: none -> 252 us  [on_device(): lax.all_gather(rounded[layer_index, :, 4 * model_width:], SEQ_AXES + ('tp...]
    all_to_all x2 -> x1, blocking collectives: 62.7 us -> 34 us  [gather_tp(): gathered = lax.all_to_all(stacked, 'tp', 0, 0, tiled=True)]
    all_to_all x2 -> x1, waiting for transfers between devices: 54.9 us -> 31.2 us  [reduce_tp(): received = lax.all_to_all(pieces, 'tp', 0, 0, tiled=True)]
    slice x0 -> x6, local copies, waits for them, and re-layouts: none -> 21.3 us  [the longest x2 13.9 us: on_device(): full_mlp[:, 2 * ff_width:].reshape(model_width, tp_count, unit_cols)]
    slice x4 -> x2, local copies, waits for them, and re-layouts: 11.9 us -> 5.98 us  [on_device(): out_weight = layer_weights[:, :model_width]]
  transfers between devices with their start and end apart: 10 -> 10, of which waited for: 7 -> 8; matrix products, arithmetic and copies ran while one was open for 18% -> 15% of each run, Pallas kernels for 0% -> 0%
where the time goes in v9:
time: 559 us; the launch traced here: 555 us
  waiting for transfers between devices  346 us (62%)
  local copies, waits for them, and re-layouts  52.1 us (9%)
  matrix products  51.1 us (9%)
  blocking collectives  48.9 us (9%)
  starting transfers between devices  28.5 us (5%)
  other arithmetic  14.7 us (3%)
  between operations  13.8 us (2%)
    all_gather x1, waiting for transfers between devices, on_device(): lax.all_gather(rounded[layer_index, :, 4 * model_width:], SEQ_AXES + ('tp...  252 us
    all_to_all x2, waiting for transfers between devices, gather_tp(): gathered = lax.all_to_all(stacked, 'tp', 0, 0, tiled=True)  52.4 us
    all_to_all x1, blocking collectives, gather_tp(): gathered = lax.all_to_all(stacked, 'tp', 0, 0, tiled=True)  34 us
    all_to_all x1, waiting for transfers between devices, reduce_tp(): received = lax.all_to_all(pieces, 'tp', 0, 0, tiled=True)  31.2 us
    sub x2, matrix products, on_device(): weights_exp = jnp.exp(scores - row_peak)  18.7 us
    all_to_all x1, blocking collectives, on_device(): lax.all_to_all(grouped, 'tp', split_axis=1, concat_axis=0, tiled=True)  14.9 us
    slice x2, local copies, waits for them, and re-layouts, on_device(): full_mlp[:, 2 * ff_width:].reshape(model_width, tp_count, unit_cols)  13.9 us
  transfers between devices with their start and end apart: 10, of which 8 were waited for; matrix products, arithmetic and copies ran while one was open for 15% of the time, Pallas kernels for 0%

profile of v9, /device:TPU:0, one launch (start us, length us, event | category | flops | bytes accessed | tf_op | source)
XLA Modules:
  0.0 555.2 jit_solution(10029087035308725874)
XLA Ops:
  9.0 14.9 %all_to_all.53 = bf16[8,8,3872]{2,0,1:T(8,128)(2,1)S(1)} all-to-all(bf16[8,8,3872]{2,0,1:T(8,128)(2,1)S(1)} %pad_maximum_fusion), channel_id=1, replica_groups=mesh['chip'=8,'core'=2,'tp'=8] {'tp'}, dimensions={1} | all-to-all | bytes 991232 | tf_op jit(solution)/shard_map/all_to_all | solution.py:108
  33.2 7.7 %all-to-all-start.2 = ((bf16[8,64,384]{2,1,0:T(8,128)(2,1)}), bf16[8,64,384]{2,1,0:T(8,128)(2,1)S(1)}, u32[]{:S(2)}, u32[]{:S(2)}) async-start(bf16[8,64,384]{2,1,0:T(8,128)(2,1)} %broadcast_in_dim.198), calls=%async_computation.2 | async-start | bytes 786432 | tf_op jit(solution)/shard_map/all_to_all | solution.py:122
  42.0 9.2 %all-to-all-done.2 = bf16[8,64,384]{2,1,0:T(8,128)(2,1)S(1)} async-done(((bf16[8,64,384]{2,1,0:T(8,128)(2,1)}), bf16[8,64,384]{2,1,0:T(8,128)(2,1)S(1)}, u32[]{:S(2)}, u32[]{:S(2)}) %all-to-all-start.2) | async-done | bytes 393248 | tf_op jit(solution)/shard_map/all_to_all | solution.py:122
  52.8 3.7 all-to-all-start
  61.2 23.7 %all-to-all-done = bf16[8,128,1024]{2,1,0:T(8,128)(2,1)S(1)} async-done(((bf16[8,128,1024]{2,1,0:T(8,128)(2,1)}), bf16[8,128,1024]{2,1,0:T(8,128)(2,1)S(1)}, u32[]{:S(2)}, u32[]{:S(2)}) %all-to-all-start) | async-done | bytes 2097184 | tf_op jit(solution)/shard_map/all_to_all | solution.py:60
  88.5 9.3 %fusion.73 = (f32[2,1024]{1,0:T(2,128)}, f32[2,1024,1024]{1,2,0:T(8,128)}) fusion(f32[2]{0:T(128)} %get-tuple-element.12, f32[2]{0:T(128)} %get-tuple-element.11, pred[1024,1024]{0,1:T(8,128)(4,1)S(1)} %copy-done.1, pred[1024,1024]{0,1:T(8,128)(4,1)S(1)} %copy-done.3, bf16[1024,2,32]{0,2,1:T(8,128)(2,1)} %get-tuple-element.40, ...), kind=kOutput, calls=%fused_computation.173 | convolution fusion | flops 282067968 | bytes 11018256 | tf_op jit(solution)/shard_map/sub | solution.py:193
  97.8 4.3 fusion.25
  103.1 4.3 all-to-all-start.3
  108.6 3.1 slice.240
  119.7 34.0 %all_to_all.54 = bf16[8,128,1024]{2,1,0:T(8,128)(2,1)S(1)} all-to-all(bf16[8,128,1024]{2,1,0:T(8,128)(2,1)S(1)} %broadcast_in_dim.209), channel_id=1, replica_groups=mesh['chip'=8,'core'=2,'tp'=8] {'tp'}, dimensions={0} | all-to-all | bytes 4194304 | tf_op jit(solution)/shard_map/all_to_all | solution.py:60
  153.7 3.2 fusion.20
  156.8 4.0 convolution_convert_fusion
  160.9 5.1 all-to-all-start.5
  166.1 31.2 %all-to-all-done.5 = bf16[8,128,1024]{2,1,0:T(8,128)(2,1)S(1)} async-done(((bf16[8,128,1024]{2,1,0:T(8,128)(2,1)}), bf16[8,128,1024]{2,1,0:T(8,128)(2,1)S(1)}, u32[]{:S(2)}, u32[]{:S(2)}) %all-to-all-start.5) | async-done | bytes 2097184 | tf_op jit(solution)/shard_map/all_to_all | solution.py:66
  203.6 3.6 all-to-all-start.6
  207.6 28.8 %all-to-all-done.6 = bf16[8,128,1024]{2,1,0:T(8,128)(2,1)S(1)} async-done(((bf16[8,128,1024]{2,1,0:T(8,128)(2,1)}), bf16[8,128,1024]{2,1,0:T(8,128)(2,1)S(1)}, u32[]{:S(2)}, u32[]{:S(2)}) %all-to-all-start.6) | async-done | bytes 2097184 | tf_op jit(solution)/shard_map/all_to_all | solution.py:60
  240.2 9.4 %fusion.74 = (f32[2,1024]{1,0:T(2,128)}, f32[2,1024,1024]{1,2,0:T(8,128)}) fusion(f32[2]{0:T(128)S(1)} %get-tuple-element.10, f32[2]{0:T(128)S(1)} %get-tuple-element.9, pred[1024,1024]{0,1:T(8,128)(4,1)S(1)} %copy-done.2, pred[1024,1024]{0,1:T(8,128)(4,1)S(1)} %copy-done.4, bf16[1024,2,32]{0,2,1:T(8,128)(2,1)} %get-tuple-element.38, ...), kind=kOutput, calls=%fused_computation.174 | convolution fusion | flops 282067968 | bytes 11018256 | tf_op jit(solution)/shard_map/sub | solution.py:193
  249.6 4.3 fusion.24
  254.9 3.7 all-to-all-start.7
  268.4 252.1 %all-gather.10.cloned.1.call-done = bf16[1,1024,8448]{2,1,0:T(8,128)(2,1)} async-done(((bf16[1,8,8448]{2,1,0:T(8,128)(2,1)}), bf16[1,1024,8448]{2,1,0:T(8,128)(2,1)}) %all-gather.10.cloned.1.call-update) | async-done | bytes 17301520 | tf_op jit(solution)/shard_map/all_gather | solution.py:167
  520.5 5.6 %slice.262 = bf16[1024,2816]{1,0:T(8,128)(2,1)} slice(bf16[1024,8448]{1,0:T(8,128)(2,1)} %bitcast.133), slice={[0:1024], [5632:8448]} | slice | bytes 11534336 | tf_op jit(solution)/shard_map/slice | solution.py:212
  526.1 5.3 fusion.2
  534.2 8.3 %copy.110 = bf16[1024,2816]{0,1:T(8,128)(2,1)} copy(bf16[1024,2816]{1,0:T(8,128)(2,1)} %slice.262) | data formatting | bytes 11534336 | tf_op jit(solution)/shard_map/slice | solution.py:212
  542.4 4.0 convert_reduce_fusion
  (150 shorter events, 58.7 us)
Async XLA Ops:
  6.5 102.1 %all-gather.6.cloned.1.call-start = ((), (), s32[]{:S(2)}) async-start(), calls=%async_computation.8 | async-start | bytes 4734976 | tf_op jit(solution)/shard_map/all_gather | solution.py:118
  8.8 17.5 %copy-start.10 = (f32[2,2,1024]{2,1,0:T(2,128)S(1)}, f32[2,2,1024]{2,1,0:T(2,128)}, u32[]{:S(2)}) copy-start(f32[2,2,1024]{2,1,0:T(2,128)} %param.14) | copy-start | bytes 49156
  8.8 17.9 %copy-start.14 = (s32[128]{0:T(128)S(1)}, s32[128]{0:T(128)}, u32[]{:S(2)}) copy-start(s32[128]{0:T(128)} %param.12) | copy-start | bytes 1540
  8.8 19.4 %copy-start.6 = (f32[128,1024]{1,0:T(8,128)S(1)}, f32[128,1024]{1,0:T(8,128)}, u32[]{:S(2)}) copy-start(f32[128,1024]{1,0:T(8,128)} %param.13) | copy-start | bytes 1572868
  24.7 182.9 %all-gather.8.cloned.1.call-start = ((), (), s32[]{:S(2)}) async-start(), calls=%async_computation.9 | async-start | bytes 3063808 | tf_op jit(solution)/shard_map/all_gather | solution.py:118
  25.5 495.0 %all-gather.10.cloned.1.call-start = ((), (), s32[]{:S(2)}) async-start(), calls=%async_computation.10 | async-start | bytes 17436672 | tf_op jit(solution)/shard_map/all_gather | solution.py:167
  33.2 18.0 %all-to-all-start.2 = ((bf16[8,64,384]{2,1,0:T(8,128)(2,1)}), bf16[8,64,384]{2,1,0:T(8,128)(2,1)S(1)}, u32[]{:S(2)}, u32[]{:S(2)}) async-start(bf16[8,64,384]{2,1,0:T(8,128)(2,1)} %broadcast_in_dim.198), calls=%async_computation.2 | async-start | bytes 786432 | tf_op jit(solution)/shard_map/all_to_all | solution.py:122
  41.9 14.6 %copy-start.15 = (s32[1,4]{1,0:T(1,128)S(1)}, s32[1,4]{1,0:T(1,128)}, u32[]{:S(2)}) copy-start(s32[1,4]{1,0:T(1,128)} %param.15) | copy-start | bytes 52
  42.0 14.8 %copy-start.11 = (f32[2,16,2]{1,2,0:T(2,128)S(1)}, f32[2,16,2]{1,2,0:T(2,128)}, u32[]{:S(2)}) copy-start(f32[2,16,2]{1,2,0:T(2,128)} %param.17) | copy-start | bytes 772
  52.8 6.0 %copy-start.9 = (s32[1024]{0:T(1024)S(1)}, s32[1024]{0:T(1024)}, u32[]{:S(2)}) copy-start(s32[1024]{0:T(1024)} %param.16) | copy-start | bytes 12292
  52.8 32.0 %all-to-all-start = ((bf16[8,128,1024]{2,1,0:T(8,128)(2,1)}), bf16[8,128,1024]{2,1,0:T(8,128)(2,1)S(1)}, u32[]{:S(2)}, u32[]{:S(2)}) async-start(bf16[8,128,1024]{2,1,0:T(8,128)(2,1)} %broadcast_in_dim.196), calls=%async_computation | async-start | bytes 4194304 | tf_op jit(solution)/shard_map/all_to_all | solution.py:60
  58.5 2.7 collective-permute-start
  86.9 1.2 copy-start.1
  86.9 1.6 copy-start.3
  103.1 11.6 %all-to-all-start.3 = ((bf16[8,128,128]{2,1,0:T(8,128)(2,1)}), bf16[8,128,128]{2,1,0:T(8,128)(2,1)S(1)}, u32[]{:S(2)}, u32[]{:S(2)}) async-start(bf16[8,128,128]{2,1,0:T(8,128)(2,1)} %copy.96), calls=%async_computation.3 | async-start | bytes 524288 | tf_op jit(solution)/shard_map/all_to_all | solution.py:73
  160.9 36.4 %all-to-all-start.5 = ((bf16[8,128,1024]{2,1,0:T(8,128)(2,1)}), bf16[8,128,1024]{2,1,0:T(8,128)(2,1)S(1)}, u32[]{:S(2)}, u32[]{:S(2)}) async-start(bf16[8,128,1024]{2,1,0:T(8,128)(2,1)} %bitcast.125), calls=%async_computation.5 | async-start | bytes 4194304 | tf_op jit(solution)/shard_map/all_to_all | solution.py:66
  203.6 32.8 %all-to-all-start.6 = ((bf16[8,128,1024]{2,1,0:T(8,128)(2,1)}), bf16[8,128,1024]{2,1,0:T(8,128)(2,1)S(1)}, u32[]{:S(2)}, u32[]{:S(2)}) async-start(bf16[8,128,1024]{2,1,0:T(8,128)(2,1)} %broadcast_in_dim.210), calls=%async_computation.6 | async-start | bytes 4194304 | tf_op jit(solution)/shard_map/all_to_all | solution.py:60
  238.5 1.7 copy-start.2
  238.5 1.7 copy-start.4
  240.2 9.4 %copy-start.8 = (bf16[1024,128]{0,1:T(8,128)(2,1)S(1)}, bf16[1024,128]{0,1:T(8,128)(2,1)}, u32[]{:S(2)}) copy-start(bf16[1024,128]{0,1:T(8,128)(2,1)} %slice.311) | copy-start | bytes 786436
  249.6 9.0 %copy-start.13 = (s32[128]{0:T(128)S(1)}, s32[128]{0:T(128)}, u32[]{:S(2)}) copy-start(s32[128]{0:T(128)} %copy-done.12) | copy-start | bytes 1540
  254.9 10.6 %all-to-all-start.7 = ((bf16[8,128,128]{2,1,0:T(8,128)(2,1)}), bf16[8,128,128]{2,1,0:T(8,128)(2,1)S(1)}, u32[]{:S(2)}, u32[]{:S(2)}) async-start(bf16[8,128,128]{2,1,0:T(8,128)(2,1)} %copy.105), calls=%async_computation.7 | async-start | bytes 524288 | tf_op jit(solution)/shard_map/all_to_all | solution.py:73
  520.5 5.6 %copy-start = (f32[128,1024]{1,0:T(8,128)S(1)}, f32[128,1024]{1,0:T(8,128)}, u32[]{:S(2)}) copy-start(f32[128,1024]{1,0:T(8,128)} %convert_reduce_fusion.1) | copy-start | bytes 1572868
  520.5 5.6 %copy-start.7 = (f32[128,1024]{1,0:T(8,128)S(1)}, f32[128,1024]{1,0:T(8,128)}, u32[]{:S(2)}) copy-start(f32[128,1024]{1,0:T(8,128)} %get-tuple-element.14) | copy-start | bytes 1572868
  (2 other events, 1.3 us)
Sparse Core Ops, SparseCore 0:
  24.8 74.4 all-gather.5
  101.8 62.2 all-gather.7
  165.8 354.6 all-gather.9

commit v10 on v8

--- a/solution.py
+++ b/solution.py
@@ -76,6 +76,25 @@
         "gtc,rgc->gtr", received, group_weight, preferred_element_type=jnp.float32
     ).astype(jnp.bfloat16)
     return jnp.sum(products.astype(jnp.float32), axis=0)
+
+
+def owned_qkv(normed, qkv_weight, own_offsets, tp_count, head_count, head_size):
+    own_rows, model_width = normed.shape
+    projected = project_rows(normed, weight=qkv_weight)
+    queries = rotate(projected[:, :model_width].reshape(own_rows, head_count, head_size), own_offsets)
+    key_rows = rotate(
+        projected[:, model_width : 2 * model_width].reshape(own_rows, head_count, head_size),
+        own_offsets,
+    )
+    values = projected[:, 2 * model_width :].reshape(own_rows, head_count, head_size)
+    local_heads = head_count // tp_count
+    stacked = jnp.stack([queries, key_rows, values], axis=0).astype(jnp.bfloat16)
+    pieces = jnp.moveaxis(
+        stacked.reshape(3, own_rows, tp_count, local_heads, head_size), 2, 0
+    )
+    received = lax.all_to_all(pieces, "tp", 0, 0, tiled=True)
+    gathered = jnp.moveaxis(received, 1, 0).reshape(3, tp_count * own_rows, local_heads, head_size)
+    return gathered[0], gathered[1], gathered[2]
 
 
 def on_device(
@@ -93,17 +112,19 @@
 
     rounded = trainer_rows.astype(jnp.bfloat16)
     grouped_parts = []
-    column_start = 0
-    for part_index, part_width in enumerate(part_widths):
-        part = rounded[:, :, column_start : column_start + part_width]
-        if part_index == 3:
-            part = jnp.broadcast_to(part[:, :, None, :], (layer_count, block_rows, tp_count, part_width))
-        else:
-            part = part.reshape(layer_count, block_rows, tp_count, part_width // tp_count)
-        grouped_parts.append(part)
-        column_start = column_start + part_width
-    grouped = jnp.concatenate(grouped_parts, axis=3)
-    regrouped = lax.all_to_all(grouped, "tp", split_axis=2, concat_axis=1, tiled=True)
+    for layer_index in range(layer_count):
+        column_start = 0
+        for part_index, part_width in enumerate(part_widths):
+            part = rounded[layer_index, :, column_start : column_start + part_width]
+            if part_index == 3 or (part_index < 3 and layer_index > 0):
+                part = jnp.broadcast_to(part[:, None, :], (block_rows, tp_count, part_width))
+            else:
+                part = part.reshape(block_rows, tp_count, part_width // tp_count)
+            grouped_parts.append(part)
+            column_start = column_start + part_width
+    grouped = jnp.concatenate(grouped_parts, axis=2)
+    first_cols = 3 * head_cols + model_width + 3 * unit_cols
+    regrouped = lax.all_to_all(grouped, "tp", split_axis=1, concat_axis=0, tiled=True)
     chip_count = lax.axis_size(CHIP_AXES)
     core = lax.axis_index("core")
     core_swap = [(0, 1), (1, 0)]
@@ -146,37 +167,43 @@
         variate_bias, lax.axis_index("tp") * local_heads, local_heads, 1
     )
     residual = reorder(residual_in, shard_order)
+    own_offsets = lax.dynamic_slice_in_dim(
+        offsets, lax.axis_index("tp") * residual.shape[0], residual.shape[0]
+    )
     for layer_index in range(layer_count):
         layer_bias = bias_table[layer_index]
         pair_bias = jnp.where(
             same_variate[None], layer_bias[:, 1][:, None, None], layer_bias[:, 0][:, None, None]
         )
         normed = rms_scaled(residual, gains[layer_index][0]).astype(jnp.bfloat16)
-        piece = regrouped[layer_index, :, 0, :]
         if layer_index == 0:
+            piece = regrouped[:, 0, :first_cols]
             qkv_weight = gather_chips(piece[:, : 3 * head_cols])
             normed = reorder(normed, shard_of_block)
             layer_weights = gather_seq(piece[:, 3 * head_cols :])
+            projected = project_rows(gather_tp(normed, tp_count), weight=qkv_weight)
+            queries = rotate(
+                projected[:, :head_cols].reshape(token_count, local_heads, head_size), offsets
+            ).astype(jnp.bfloat16)
+            key_rows = rotate(
+                projected[:, head_cols : 2 * head_cols].reshape(token_count, local_heads, head_size),
+                offsets,
+            ).astype(jnp.bfloat16)
+            values = (
+                projected[:, 2 * head_cols : 3 * head_cols]
+                .reshape(token_count, local_heads, head_size)
+                .astype(jnp.bfloat16)
+            )
         else:
-            layer_weights = gather_seq(piece)
-            qkv_weight = layer_weights[:, : 3 * head_cols]
-            layer_weights = layer_weights[:, 3 * head_cols :]
+            layer_weights = gather_seq(regrouped[:, 0, first_cols:])
+            qkv_weight = layer_weights[:, : 3 * model_width]
+            layer_weights = layer_weights[:, 3 * model_width :]
+            queries, key_rows, values = owned_qkv(
+                normed, qkv_weight, own_offsets, tp_count, head_count, head_size
+            )
         out_weight = layer_weights[:, :model_width]
         gate_up_weight = layer_weights[:, model_width : model_width + 2 * unit_cols]
         down_weight = layer_weights[:, model_width + 2 * unit_cols :]
-        projected = project_rows(gather_tp(normed, tp_count), weight=qkv_weight)
-        queries = rotate(
-            projected[:, :head_cols].reshape(token_count, local_heads, head_size), offsets
-        ).astype(jnp.bfloat16)
-        key_rows = rotate(
-            projected[:, head_cols : 2 * head_cols].reshape(token_count, local_heads, head_size),
-            offsets,
-        ).astype(jnp.bfloat16)
-        values = (
-            projected[:, 2 * head_cols : 3 * head_cols]
-            .reshape(token_count, local_heads, head_size)
-            .astype(jnp.bfloat16)
-        )
         scores = (
             jnp.einsum("qhd,khd->hqk", queries, key_rows, preferred_element_type=jnp.float32)
             * head_size ** (-0.5)

time: 347 us -> 364 us (1.049)
  local copies, waits for them, and re-layouts: 37.4 us -> 47.7 us
  waiting for transfers between devices: 118 us -> 124 us
    all_to_all x2 -> x1, waiting for transfers between devices: 53.8 us -> 24.4 us  [gather_tp(): gathered = lax.all_to_all(stacked, 'tp', 0, 0, tiled=True)]
    all_gather x2, waiting for transfers between devices: 0.01 us -> 16.5 us  [gather_seq(): return lax.all_gather(piece, SEQ_AXES, axis=0, tiled=True)]
    all_gather x0 -> x1, local copies, waits for them, and re-layouts: none -> 14.4 us  [gather_seq(): return lax.all_gather(piece, SEQ_AXES, axis=0, tiled=True)]
    all_to_all x0 -> x1, waiting for transfers between devices: none -> 12.6 us  [owned_qkv(): received = lax.all_to_all(pieces, 'tp', 0, 0, tiled=True)]
    all_to_all x0 -> x1, starting transfers between devices: none -> 4.95 us  [owned_qkv(): received = lax.all_to_all(pieces, 'tp', 0, 0, tiled=True)]
    all_to_all x2 -> x1, starting transfers between devices: 7.99 us -> 3.73 us  [gather_tp(): gathered = lax.all_to_all(stacked, 'tp', 0, 0, tiled=True)]
    slice x4 -> x3, local copies, waits for them, and re-layouts: 11.9 us -> 7.72 us  [on_device(): out_weight = layer_weights[:, :model_width]]
    all_to_all x2, waiting for transfers between devices: 0.63 us -> 4.83 us  [project_owned(): received = lax.all_to_all(pieces, 'tp', 0, 0, tiled=True)]
  transfers between devices with their start and end apart: 10 -> 10, of which waited for: 7 -> 8; matrix products, arithmetic and copies ran while one was open for 18% -> 15% of each run, Pallas kernels for 0% -> 0%
where the time goes in v10:
time: 364 us; the launch traced here: 362 us
  waiting for transfers between devices  124 us (34%)
  blocking collectives  79.3 us (22%)
  matrix products  48.5 us (13%)
  local copies, waits for them, and re-layouts  47.7 us (13%)
  starting transfers between devices  33.9 us (9%)
  between operations  14.3 us (4%)
  other arithmetic  14.2 us (4%)
    all_to_all x2, blocking collectives, gather_tp(): gathered = lax.all_to_all(stacked, 'tp', 0, 0, tiled=True)  59.4 us
    all_to_all x2, waiting for transfers between devices, reduce_tp(): received = lax.all_to_all(pieces, 'tp', 0, 0, tiled=True)  55.9 us
    all_to_all x1, waiting for transfers between devices, gather_tp(): gathered = lax.all_to_all(stacked, 'tp', 0, 0, tiled=True)  24.4 us
    all_to_all x1, blocking collectives, on_device(): lax.all_to_all(grouped, 'tp', split_axis=1, concat_axis=0, tiled=True)  19.9 us
    sub x2, matrix products, on_device(): weights_exp = jnp.exp(scores - row_peak)  16.7 us
    all_gather x2, waiting for transfers between devices, gather_seq(): return lax.all_gather(piece, SEQ_AXES, axis=0, tiled=True)  16.5 us
    all_gather x1, local copies, waits for them, and re-layouts, gather_seq(): return lax.all_gather(piece, SEQ_AXES, axis=0, tiled=True)  14.4 us
    all_to_all x1, waiting for transfers between devices, owned_qkv(): received = lax.all_to_all(pieces, 'tp', 0, 0, tiled=True)  12.6 us
  transfers between devices with their start and end apart: 10, of which 8 were waited for; matrix products, arithmetic and copies ran while one was open for 15% of the time, Pallas kernels for 0%

profile of v10, /device:TPU:0, one launch (start us, length us, event | category | flops | bytes accessed | tf_op | source)
XLA Modules:
  0.0 361.8 jit_solution(14654539612038334331)
XLA Ops:
  9.4 19.9 %all_to_all.63 = bf16[8,8,7616]{2,0,1:T(8,128)(2,1)S(1)} all-to-all(bf16[8,8,7616]{2,0,1:T(8,128)(2,1)S(1)} %concatenate.24), channel_id=1, replica_groups=mesh['chip'=8,'core'=2,'tp'=8] {'tp'}, dimensions={1} | all-to-all | bytes 1949696 | tf_op jit(solution)/shard_map/all_to_all | solution.py:127
  37.9 7.7 %all-to-all-start.2 = ((bf16[8,64,384]{2,1,0:T(8,128)(2,1)}), bf16[8,64,384]{2,1,0:T(8,128)(2,1)S(1)}, u32[]{:S(2)}, u32[]{:S(2)}) async-start(bf16[8,64,384]{2,1,0:T(8,128)(2,1)} %broadcast_in_dim.236), calls=%async_computation.2 | async-start | bytes 786432 | tf_op jit(solution)/shard_map/all_to_all | solution.py:141
  46.7 9.4 %all-to-all-done.2 = bf16[8,64,384]{2,1,0:T(8,128)(2,1)S(1)} async-done(((bf16[8,64,384]{2,1,0:T(8,128)(2,1)}), bf16[8,64,384]{2,1,0:T(8,128)(2,1)S(1)}, u32[]{:S(2)}, u32[]{:S(2)}) %all-to-all-start.2) | async-done | bytes 393248 | tf_op jit(solution)/shard_map/all_to_all | solution.py:141
  57.7 3.7 %all-to-all-start = ((bf16[8,128,1024]{2,1,0:T(8,128)(2,1)}), bf16[8,128,1024]{2,1,0:T(8,128)(2,1)S(1)}, u32[]{:S(2)}, u32[]{:S(2)}) async-start(bf16[8,128,1024]{2,1,0:T(8,128)(2,1)} %broadcast_in_dim.225), calls=%async_computation | async-start | bytes 4194304 | tf_op jit(solution)/shard_map/all_to_all | solution.py:60
  66.0 24.4 %all-to-all-done = bf16[8,128,1024]{2,1,0:T(8,128)(2,1)S(1)} async-done(((bf16[8,128,1024]{2,1,0:T(8,128)(2,1)}), bf16[8,128,1024]{2,1,0:T(8,128)(2,1)S(1)}, u32[]{:S(2)}, u32[]{:S(2)}) %all-to-all-start) | async-done | bytes 2097184 | tf_op jit(solution)/shard_map/all_to_all | solution.py:60
  94.2 8.8 %fusion.74 = (f32[2,1024]{1,0:T(2,128)S(1)}, f32[2,1024,1024]{1,2,0:T(8,128)}) fusion(f32[2]{0:T(128)} %get-tuple-element.12, f32[2]{0:T(128)} %get-tuple-element.11, pred[1024,1024]{0,1:T(8,128)(4,1)S(1)} %copy-done.5, pred[1024,1024]{0,1:T(8,128)(4,1)S(1)} %copy-done.7, bf16[1024,2,32]{0,2,1:T(8,128)(2,1)} %get-tuple-element.46, ...), kind=kOutput, calls=%fused_computation.180 | convolution fusion | flops 282067968 | bytes 11018256 | tf_op jit(solution)/shard_map/sub | solution.py:214
  103.0 4.2 %fusion.27 = bf16[2,64,1024]{2,1,0:T(8,128)(2,1)S(1)} fusion(bf16[1024,2,64]{0,2,1:T(8,128)(2,1)S(1)} %bitcast.167, f32[2,1024,1024]{1,2,0:T(8,128)} %get-tuple-element.65, f32[2,1024]{1,0:T(2,128)S(1)} %get-tuple-element.64), kind=kOutput, calls=%fused_computation.49 | convolution fusion | flops 272760832 | bytes 8921088 | tf_op jit(solution)/shard_map/hqk,khd->qhd/dot_general | solution.py:219
  108.2 4.3 %all-to-all-start.3 = ((bf16[8,128,128]{2,1,0:T(8,128)(2,1)}), bf16[8,128,128]{2,1,0:T(8,128)(2,1)S(1)}, u32[]{:S(2)}, u32[]{:S(2)}) async-start(bf16[8,128,128]{2,1,0:T(8,128)(2,1)} %copy.116), calls=%async_computation.3 | async-start | bytes 524288 | tf_op jit(solution)/shard_map/all_to_all | solution.py:73
  124.0 31.5 %all_to_all.64 = bf16[8,128,1024]{2,1,0:T(8,128)(2,1)S(1)} all-to-all(bf16[8,128,1024]{2,1,0:T(8,128)(2,1)S(1)} %broadcast_in_dim.247), channel_id=1, replica_groups=mesh['chip'=8,'core'=2,'tp'=8] {'tp'}, dimensions={0} | all-to-all | bytes 4194304 | tf_op jit(solution)/shard_map/all_to_all | solution.py:60
  158.7 4.0 %convolution_convert_fusion.1 = bf16[1024,1024]{1,0:T(8,128)(2,1)} fusion(bf16[1024,2080]{1,0:T(8,128)(2,1)} %all-gather.4.cloned.1.call-done, f32[1024,704]{0,1:T(8,128)S(1)} %fusion.20), kind=kOutput, calls=%fused_computation.39 | convolution fusion | flops 741408768 | bytes 5767168 | tf_op jit(solution)/shard_map/dot_general | solution.py:53
  162.7 5.6 %all-to-all-start.5 = ((bf16[8,128,1024]{2,1,0:T(8,128)(2,1)}), bf16[8,128,1024]{2,1,0:T(8,128)(2,1)S(1)}, u32[]{:S(2)}, u32[]{:S(2)}) async-start(bf16[8,128,1024]{2,1,0:T(8,128)(2,1)} %bitcast.154), calls=%async_computation.5 | async-start | bytes 4194304 | tf_op jit(solution)/shard_map/all_to_all | solution.py:66
  169.4 29.2 %all-to-all-done.5 = bf16[8,128,1024]{2,1,0:T(8,128)(2,1)S(1)} async-done(((bf16[8,128,1024]{2,1,0:T(8,128)(2,1)}), bf16[8,128,1024]{2,1,0:T(8,128)(2,1)S(1)}, u32[]{:S(2)}, u32[]{:S(2)}) %all-to-all-start.5) | async-done | bytes 2097184 | tf_op jit(solution)/shard_map/all_to_all | solution.py:66
  200.5 16.5 %all-gather.6.cloned.1.call-done = bf16[1024,1,5152]{2,0,1:T(8,128)(2,1)} async-done(((bf16[64,1,5152]{2,0,1:T(8,128)(2,1)}), bf16[1024,1,5152]{2,0,1:T(8,128)(2,1)}) %all-gather.6.cloned.1.call-update) | async-done | bytes 10551312 | tf_op jit(solution)/shard_map/all_gather | solution.py:137
  217.0 14.4 %copy.123 = bf16[1024,1,5152]{0,2,1:T(8,128)(2,1)} copy(bf16[1024,1,5152]{2,0,1:T(8,128)(2,1)} %all-gather.6.cloned.1.call-done) | data formatting | bytes 21102592 | tf_op jit(solution)/shard_map/all_gather | solution.py:137
  231.5 5.0 %fusion.2 = f32[128,3072]{1,0:T(8,128)S(1)} fusion(bf16[1024,5152]{0,1:T(8,128)(2,1)} %bitcast.142, f32[128,1024]{1,0:T(8,128)S(1)} %add.239, f32[1024]{0:T(1024)S(1)} %mul.361, f32[128]{0:T(128)S(1)} %add_rsqrt_fusion.1), kind=kOutput, calls=%fused_computation.14 | convolution fusion | flops 805699584 | bytes 8393216 | tf_op jit(solution)/shard_map/dot_general | solution.py:43
  238.4 5.0 %all-to-all-start.6 = ((bf16[8,3,128,2,64]{2,4,3,1,0:T(8,128)(2,1)}), bf16[8,3,128,2,64]{2,4,3,1,0:T(8,128)(2,1)S(1)}, u32[]{:S(2)}, u32[]{:S(2)}) async-start(bf16[8,3,128,2,64]{2,4,3,1,0:T(8,128)(2,1)} %copy.127), calls=%async_computation.6 | async-start | bytes 1572864 | tf_op jit(solution)/shard_map/all_to_all | solution.py:95
  243.6 12.6 %all-to-all-done.6 = bf16[8,3,128,2,64]{2,4,3,1,0:T(8,128)(2,1)S(1)} async-done(((bf16[8,3,128,2,64]{2,4,3,1,0:T(8,128)(2,1)}), bf16[8,3,128,2,64]{2,4,3,1,0:T(8,128)(2,1)S(1)}, u32[]{:S(2)}, u32[]{:S(2)}) %all-to-all-start.6) | async-done | bytes 786464 | tf_op jit(solution)/shard_map/all_to_all | solution.py:95
  257.3 8.0 %fusion.75 = (f32[2,1024]{1,0:T(2,128)S(1)}, f32[2,1024,1024]{1,2,0:T(8,128)}) fusion(f32[2]{0:T(128)S(1)} %get-tuple-element.10, f32[2]{0:T(128)S(1)} %get-tuple-element.9, pred[1024,1024]{0,1:T(8,128)(4,1)S(1)} %copy-done.6, pred[1024,1024]{0,1:T(8,128)(4,1)} %get-tuple-element.71, bf16[1024,2,64]{0,2,1:T(8,128)(2,1)S(1)} %squeeze.26, ...), kind=kOutput, calls=%fused_computation.181 | convolution fusion | flops 281019392 | bytes 11018256 | tf_op jit(solution)/shard_map/sub | solution.py:214
  265.2 4.3 %fusion.26 = bf16[2,64,1024]{2,1,0:T(8,128)(2,1)S(1)} fusion(bf16[1024,2,64]{0,2,1:T(8,128)(2,1)S(1)} %squeeze.25, f32[2,1024,1024]{1,2,0:T(8,128)} %get-tuple-element.67, f32[2,1024]{1,0:T(2,128)S(1)} %get-tuple-element.66), kind=kOutput, calls=%fused_computation.48 | convolution fusion | flops 272760832 | bytes 8921088 | tf_op jit(solution)/shard_map/hqk,khd->qhd/dot_general | solution.py:219
  276.0 4.7 %all-to-all-done.7 = bf16[8,128,128]{2,1,0:T(8,128)(2,1)S(1)} async-done(((bf16[8,128,128]{2,1,0:T(8,128)(2,1)}), bf16[8,128,128]{2,1,0:T(8,128)(2,1)S(1)}, u32[]{:S(2)}, u32[]{:S(2)}) %all-to-all-start.7) | async-done | bytes 262176 | tf_op jit(solution)/shard_map/all_to_all | solution.py:73
  284.1 27.9 %all_to_all.65 = bf16[8,128,1024]{2,1,0:T(8,128)(2,1)S(1)} all-to-all(bf16[8,128,1024]{2,1,0:T(8,128)(2,1)S(1)} %broadcast_in_dim.252), channel_id=1, replica_groups=mesh['chip'=8,'core'=2,'tp'=8] {'tp'}, dimensions={0} | all-to-all | bytes 4194304 | tf_op jit(solution)/shard_map/all_to_all | solution.py:60
  315.1 3.8 %convolution_convert_fusion = bf16[1024,1024]{1,0:T(8,128)(2,1)} fusion(f32[1024,704]{0,1:T(8,128)S(1)} %fusion.23, bf16[1024,5152]{0,1:T(8,128)(2,1)} %bitcast.145), kind=kOutput, calls=%fused_computation.38 | convolution fusion | flops 741408768 | bytes 5701632 | tf_op jit(solution)/shard_map/dot_general | solution.py:53
  318.9 3.7 %all-to-all-start.9 = ((bf16[8,128,1024]{2,1,0:T(8,128)(2,1)}), bf16[8,128,1024]{2,1,0:T(8,128)(2,1)S(1)}, u32[]{:S(2)}, u32[]{:S(2)}) async-start(bf16[8,128,1024]{2,1,0:T(8,128)(2,1)} %bitcast.155), calls=%async_computation.9 | async-start | bytes 4194304 | tf_op jit(solution)/shard_map/all_to_all | solution.py:66
  322.7 26.7 %all-to-all-done.9 = bf16[8,128,1024]{2,1,0:T(8,128)(2,1)S(1)} async-done(((bf16[8,128,1024]{2,1,0:T(8,128)(2,1)}), bf16[8,128,1024]{2,1,0:T(8,128)(2,1)S(1)}, u32[]{:S(2)}, u32[]{:S(2)}) %all-to-all-start.9) | async-done | bytes 2097184 | tf_op jit(solution)/shard_map/all_to_all | solution.py:66
  (181 shorter events, 62.1 us)
Async XLA Ops:
  6.5 107.2 %all-gather.4.cloned.1.call-start = ((), (), s32[]{:S(2)}) async-start(), calls=%async_computation.10 | async-start | bytes 4734976 | tf_op jit(solution)/shard_map/all_gather | solution.py:137
  9.4 22.0 %copy-start.12 = (f32[2,2,1024]{2,1,0:T(2,128)S(1)}, f32[2,2,1024]{2,1,0:T(2,128)}, u32[]{:S(2)}) copy-start(f32[2,2,1024]{2,1,0:T(2,128)} %param.14) | copy-start | bytes 49156
  9.4 22.4 %copy-start.17 = (s32[128]{0:T(128)S(1)}, s32[128]{0:T(128)}, u32[]{:S(2)}) copy-start(s32[128]{0:T(128)} %param.12) | copy-start | bytes 1540
  29.4 4.0 %copy-start.8 = (f32[128,1024]{1,0:T(8,128)S(1)}, f32[128,1024]{1,0:T(8,128)}, u32[]{:S(2)}) copy-start(f32[128,1024]{1,0:T(8,128)} %param.13) | copy-start | bytes 1572868
  30.1 186.9 %all-gather.6.cloned.1.call-start = ((), (), s32[]{:S(2)}) async-start(), calls=%async_computation.11 | async-start | bytes 11419648 | tf_op jit(solution)/shard_map/all_gather | solution.py:137
  35.6 10.7 %copy-start.18 = (s32[128]{0:T(128)}, s32[128]{0:T(128)S(1)}, u32[]{:S(2)}) copy-start(s32[128]{0:T(128)S(1)} %scatter_custom_fusion) | copy-start | bytes 1540
  37.9 18.1 %all-to-all-start.2 = ((bf16[8,64,384]{2,1,0:T(8,128)(2,1)}), bf16[8,64,384]{2,1,0:T(8,128)(2,1)S(1)}, u32[]{:S(2)}, u32[]{:S(2)}) async-start(bf16[8,64,384]{2,1,0:T(8,128)(2,1)} %broadcast_in_dim.236), calls=%async_computation.2 | async-start | bytes 786432 | tf_op jit(solution)/shard_map/all_to_all | solution.py:141
  46.7 14.8 %copy-start.16 = (f32[2,16,2]{1,2,0:T(2,128)S(1)}, f32[2,16,2]{1,2,0:T(2,128)}, u32[]{:S(2)}) copy-start(f32[2,16,2]{1,2,0:T(2,128)} %param.17) | copy-start | bytes 772
  46.7 15.0 %copy-start.20 = (s32[1,4]{1,0:T(1,128)S(1)}, s32[1,4]{1,0:T(1,128)}, u32[]{:S(2)}) copy-start(s32[1,4]{1,0:T(1,128)} %param.15) | copy-start | bytes 52
  57.7 6.0 %copy-start.11 = (s32[1024]{0:T(1024)S(1)}, s32[1024]{0:T(1024)}, u32[]{:S(2)}) copy-start(s32[1024]{0:T(1024)} %param.16) | copy-start | bytes 12292
  57.7 32.8 %all-to-all-start = ((bf16[8,128,1024]{2,1,0:T(8,128)(2,1)}), bf16[8,128,1024]{2,1,0:T(8,128)(2,1)S(1)}, u32[]{:S(2)}, u32[]{:S(2)}) async-start(bf16[8,128,1024]{2,1,0:T(8,128)(2,1)} %broadcast_in_dim.225), calls=%async_computation | async-start | bytes 4194304 | tf_op jit(solution)/shard_map/all_to_all | solution.py:60
  61.9 30.7 %copy-start.13 = (f32[32]{0:T(128)}, f32[32]{0:T(128)S(1)}, u32[]{:S(2)}) copy-start(f32[32]{0:T(128)S(1)} %multiply_power_fusion) | copy-start | bytes 388
  63.4 2.6 collective-permute-start
  108.2 11.6 %all-to-all-start.3 = ((bf16[8,128,128]{2,1,0:T(8,128)(2,1)}), bf16[8,128,128]{2,1,0:T(8,128)(2,1)S(1)}, u32[]{:S(2)}, u32[]{:S(2)}) async-start(bf16[8,128,128]{2,1,0:T(8,128)(2,1)} %copy.116), calls=%async_computation.3 | async-start | bytes 524288 | tf_op jit(solution)/shard_map/all_to_all | solution.py:73
  162.7 6.6 %copy-start.14 = (f32[32]{0:T(128)S(1)}, f32[32]{0:T(128)}, u32[]{:S(2)}) copy-start(f32[32]{0:T(128)} %copy-done.13) | copy-start | bytes 388
  162.7 36.0 %all-to-all-start.5 = ((bf16[8,128,1024]{2,1,0:T(8,128)(2,1)}), bf16[8,128,1024]{2,1,0:T(8,128)(2,1)S(1)}, u32[]{:S(2)}, u32[]{:S(2)}) async-start(bf16[8,128,1024]{2,1,0:T(8,128)(2,1)} %bitcast.154), calls=%async_computation.5 | async-start | bytes 4194304 | tf_op jit(solution)/shard_map/all_to_all | solution.py:66
  200.3 31.1 %copy-start.3 = (f32[128,1024]{1,0:T(8,128)}, f32[128,1024]{1,0:T(8,128)S(1)}, u32[]{:S(2)}) copy-start(f32[128,1024]{1,0:T(8,128)S(1)} %add.239) | copy-start | bytes 1572868
  238.4 18.9 %copy-start.6 = (pred[1024,1024]{0,1:T(8,128)(4,1)S(1)}, pred[1024,1024]{0,1:T(8,128)(4,1)}, u32[]{:S(2)}) copy-start(pred[1024,1024]{0,1:T(8,128)(4,1)} %get-tuple-element.70) | copy-start | bytes 3145732
  238.4 17.9 %all-to-all-start.6 = ((bf16[8,3,128,2,64]{2,4,3,1,0:T(8,128)(2,1)}), bf16[8,3,128,2,64]{2,4,3,1,0:T(8,128)(2,1)S(1)}, u32[]{:S(2)}, u32[]{:S(2)}) async-start(bf16[8,3,128,2,64]{2,4,3,1,0:T(8,128)(2,1)} %copy.127), calls=%async_computation.6 | async-start | bytes 1572864 | tf_op jit(solution)/shard_map/all_to_all | solution.py:95
  265.2 8.9 %copy-start.10 = (f32[128,8]{1,0:T(8,128)S(1)}, f32[128,8]{1,0:T(8,128)}, u32[]{:S(2)}) copy-start(f32[128,8]{1,0:T(8,128)} %get-tuple-element.6) | copy-start | bytes 12292
  270.5 10.3 %all-to-all-start.7 = ((bf16[8,128,128]{2,1,0:T(8,128)(2,1)}), bf16[8,128,128]{2,1,0:T(8,128)(2,1)S(1)}, u32[]{:S(2)}, u32[]{:S(2)}) async-start(bf16[8,128,128]{2,1,0:T(8,128)(2,1)} %copy.133), calls=%async_computation.7 | async-start | bytes 524288 | tf_op jit(solution)/shard_map/all_to_all | solution.py:73
  283.5 28.5 %copy-start = (f32[128,1024]{0,1:T(8,128)}, f32[128,1024]{0,1:T(8,128)S(1)}, u32[]{:S(2)}) copy-start(f32[128,1024]{0,1:T(8,128)S(1)} %copy.135) | copy-start | bytes 1572868
  318.9 3.7 %copy-start.19 = (s32[128]{0:T(128)S(1)}, s32[128]{0:T(128)}, u32[]{:S(2)}) copy-start(s32[128]{0:T(128)} %copy-done.18) | copy-start | bytes 1540
  318.9 30.5 %all-to-all-start.9 = ((bf16[8,128,1024]{2,1,0:T(8,128)(2,1)}), bf16[8,128,1024]{2,1,0:T(8,128)(2,1)S(1)}, u32[]{:S(2)}, u32[]{:S(2)}) async-start(bf16[8,128,1024]{2,1,0:T(8,128)(2,1)} %bitcast.155), calls=%async_computation.9 | async-start | bytes 4194304 | tf_op jit(solution)/shard_map/all_to_all | solution.py:66
  (7 other events, 9.1 us)
Sparse Core Ops, SparseCore 0:
  30.3 73.7 all-gather.3
  106.5 110.5 all-gather.5

commit v11 on v8

--- a/solution.py
+++ b/solution.py
@@ -76,6 +76,33 @@
         "gtc,rgc->gtr", received, group_weight, preferred_element_type=jnp.float32
     ).astype(jnp.bfloat16)
     return jnp.sum(products.astype(jnp.float32), axis=0)
+
+
+def core_pair_mlp(normed_mlp, pair_mlp, shard_of_block, block_of_shard, core_swap, tp_count):
+    own_rows, model_width = normed_mlp.shape
+    block_count = shard_of_block.shape[0]
+
+    def reorder(values, order):
+        blocks = values.reshape(values.shape[:-1] + (block_count, model_width // block_count))
+        return jnp.take(blocks, order, axis=-2).reshape(values.shape)
+
+    partner = lax.ppermute(normed_mlp, "core", core_swap)
+    tokens = reorder(jnp.concatenate([normed_mlp, partner], axis=0), shard_of_block)
+    half_units = pair_mlp.shape[2]
+    gate_up = jnp.dot(
+        tokens, pair_mlp[:, :2].reshape(model_width, 2 * half_units), preferred_element_type=jnp.float32
+    )
+    hidden = (jax.nn.silu(gate_up[:, :half_units]) * gate_up[:, half_units:]).astype(jnp.bfloat16)
+    group_count = tp_count // 2
+    group_width = half_units // group_count
+    products = jnp.einsum(
+        "tgu,rgu->gtr",
+        hidden.reshape(hidden.shape[0], group_count, group_width),
+        pair_mlp[:, 2].reshape(model_width, group_count, group_width),
+        preferred_element_type=jnp.float32,
+    ).astype(jnp.bfloat16)
+    partial = reorder(jnp.sum(products.astype(jnp.float32), axis=0), block_of_shard)
+    return partial[:own_rows] + lax.ppermute(partial[own_rows:], "core", core_swap)
 
 
 def on_device(
@@ -93,20 +120,36 @@
 
     rounded = trainer_rows.astype(jnp.bfloat16)
     grouped_parts = []
-    column_start = 0
-    for part_index, part_width in enumerate(part_widths):
-        part = rounded[:, :, column_start : column_start + part_width]
-        if part_index == 3:
-            part = jnp.broadcast_to(part[:, :, None, :], (layer_count, block_rows, tp_count, part_width))
-        else:
-            part = part.reshape(layer_count, block_rows, tp_count, part_width // tp_count)
-        grouped_parts.append(part)
-        column_start = column_start + part_width
-    grouped = jnp.concatenate(grouped_parts, axis=3)
-    regrouped = lax.all_to_all(grouped, "tp", split_axis=2, concat_axis=1, tiled=True)
-    chip_count = lax.axis_size(CHIP_AXES)
+    for layer_index in range(layer_count):
+        column_start = 0
+        for part_index, part_width in enumerate(part_widths):
+            part = rounded[layer_index, :, column_start : column_start + part_width]
+            column_start = column_start + part_width
+            if part_index > 3 and layer_index > 0:
+                continue
+            if part_index == 3:
+                part = jnp.broadcast_to(part[:, None, :], (block_rows, tp_count, part_width))
+            else:
+                part = part.reshape(block_rows, tp_count, part_width // tp_count)
+            grouped_parts.append(part)
+    grouped = jnp.concatenate(grouped_parts, axis=2)
+    regrouped = lax.all_to_all(grouped, "tp", split_axis=1, concat_axis=0, tiled=True)
+    first_cols = 3 * head_cols + model_width + 3 * unit_cols
     core = lax.axis_index("core")
     core_swap = [(0, 1), (1, 0)]
+    mlp_rows = jnp.broadcast_to(
+        rounded[1, :, 4 * model_width :][:, None, :], (block_rows, tp_count, 3 * ff_width)
+    )
+    mlp_chip_rows = lax.all_gather(
+        lax.all_to_all(mlp_rows, "tp", split_axis=1, concat_axis=0, tiled=True)[:, 0, :],
+        CHIP_AXES,
+        axis=0,
+        tiled=True,
+    ).reshape(block_count // 2 * block_rows, 3, 2, ff_width // 2)
+    own_units = lax.dynamic_index_in_dim(mlp_chip_rows, core, axis=2, keepdims=False)
+    other_units = lax.dynamic_index_in_dim(mlp_chip_rows, 1 - core, axis=2, keepdims=False)
+    pair_mlp = jnp.concatenate([own_units, lax.ppermute(other_units, "core", core_swap)], axis=0)
+    chip_count = lax.axis_size(CHIP_AXES)
 
     def join_cores(half):
         other = lax.ppermute(half, "core", core_swap)
@@ -133,6 +176,7 @@
         return jnp.take(blocks, order, axis=-2).reshape(values.shape)
 
     inverse_order = jnp.zeros_like(shard_order).at[shard_order].set(block_index)
+    block_of_shard = jnp.zeros_like(shard_of_block).at[shard_of_block].set(block_index)
 
     gains = [reorder(norm_gains[i], shard_order) for i in range(layer_count)]
     token_count = variate_ids.shape[0]
@@ -152,13 +196,13 @@
             same_variate[None], layer_bias[:, 1][:, None, None], layer_bias[:, 0][:, None, None]
         )
         normed = rms_scaled(residual, gains[layer_index][0]).astype(jnp.bfloat16)
-        piece = regrouped[layer_index, :, 0, :]
         if layer_index == 0:
+            piece = regrouped[:, 0, :first_cols]
             qkv_weight = gather_chips(piece[:, : 3 * head_cols])
             normed = reorder(normed, shard_of_block)
             layer_weights = gather_seq(piece[:, 3 * head_cols :])
         else:
-            layer_weights = gather_seq(piece)
+            layer_weights = gather_seq(regrouped[:, 0, first_cols:])
             qkv_weight = layer_weights[:, : 3 * head_cols]
             layer_weights = layer_weights[:, 3 * head_cols :]
         out_weight = layer_weights[:, :model_width]
@@ -196,10 +240,15 @@
         head_total = project_owned(mixed_heads, out_weight, tp_count)
         residual = residual + head_total
         normed_mlp = rms_scaled(residual, gains[layer_index][1]).astype(jnp.bfloat16)
-        hidden = gated_units(gather_tp(normed_mlp, tp_count), weight=gate_up_weight)
-        unit_total = reduce_tp(
-            project_out(source=hidden, weight=down_weight).astype(jnp.bfloat16), tp_count
-        )
+        if layer_index == 0:
+            hidden = gated_units(gather_tp(normed_mlp, tp_count), weight=gate_up_weight)
+            unit_total = reduce_tp(
+                project_out(source=hidden, weight=down_weight).astype(jnp.bfloat16), tp_count
+            )
+        else:
+            unit_total = core_pair_mlp(
+                normed_mlp, pair_mlp, shard_of_block, block_of_shard, core_swap, tp_count
+            )
         residual = residual + unit_total
     return reorder(residual, inverse_order)
 

time: 347 us -> 390 us (1.12); the launches traced: 346 us -> 382 us
  waiting for transfers between devices: 118 us -> 173 us
  blocking collectives: 79.4 us -> 33.2 us
  local copies, waits for them, and re-layouts: 37.4 us -> 63.4 us
  other arithmetic: 15.7 us -> 20.2 us
  matrix products: 48.2 us -> 44.2 us
    all_gather x0 -> x1, waiting for transfers between devices: none -> 50 us  [on_device(): lax.all_gather(lax.all_to_all(mlp_rows, 'tp', split_axis=1, concat_axis=0...]
    all_to_all x3 -> x2, blocking collectives: 79.4 us -> 33.2 us  [the longest x1 18.3 us: on_device(): lax.all_to_all(mlp_rows, 'tp', split_axis=1, concat_axis=0, tiled=True)]
    all_gather x2, waiting for transfers between devices: 0.01 us -> 31.6 us  [gather_seq(): return lax.all_gather(piece, SEQ_AXES, axis=0, tiled=True)]
    all_to_all x2 -> x1, waiting for transfers between devices: 54.9 us -> 30.9 us  [reduce_tp(): received = lax.all_to_all(pieces, 'tp', 0, 0, tiled=True)]
    all_gather x0 -> x1, local copies, waits for them, and re-layouts: none -> 12.3 us  [on_device(): lax.all_gather(lax.all_to_all(mlp_rows, 'tp', split_axis=1, concat_axis=0...]
    slice x2 -> x7, local copies, waits for them, and re-layouts: 0.03 us -> 8.2 us  [the longest x2 6.02 us: on_device(): layer_weights = layer_weights[:, 3 * head_cols:]]
    squeeze x1 -> x2, local copies, waits for them, and re-layouts: 0.78 us -> 8.27 us  [the longest x1 8.25 us: on_device(): lax.dynamic_index_in_dim(mlp_chip_rows, 1 - core, axis=2, keepdims=False)]
    slice x4 -> x2, local copies, waits for them, and re-layouts: 11.9 us -> 5.95 us  [on_device(): out_weight = layer_weights[:, :model_width]]
  transfers between devices with their start and end apart: 10 -> 14, of which waited for: 7 -> 10; matrix products, arithmetic and copies ran while one was open for 18% -> 28% of each run, Pallas kernels for 0% -> 0%
where the time goes in v11:
time: 390 us; the launch traced here: 382 us
  waiting for transfers between devices  173 us (44%)
  local copies, waits for them, and re-layouts  63.4 us (16%)
  matrix products  44.2 us (11%)
  starting transfers between devices  34.2 us (9%)
  blocking collectives  33.2 us (9%)
  other arithmetic  20.2 us (5%)
  between operations  14.3 us (4%)
    all_gather x1, waiting for transfers between devices, on_device(): lax.all_gather(lax.all_to_all(mlp_rows, 'tp', split_axis=1, concat_axis=0...  50 us
    all_to_all x3, waiting for transfers between devices, gather_tp(): gathered = lax.all_to_all(stacked, 'tp', 0, 0, tiled=True)  49.9 us
    all_gather x2, waiting for transfers between devices, gather_seq(): return lax.all_gather(piece, SEQ_AXES, axis=0, tiled=True)  31.6 us
    all_to_all x1, waiting for transfers between devices, reduce_tp(): received = lax.all_to_all(pieces, 'tp', 0, 0, tiled=True)  30.9 us
    all_to_all x1, blocking collectives, on_device(): lax.all_to_all(mlp_rows, 'tp', split_axis=1, concat_axis=0, tiled=True)  18.3 us
    sub x2, matrix products, on_device(): weights_exp = jnp.exp(scores - row_peak)  18 us
    all_to_all x1, blocking collectives, on_device(): lax.all_to_all(grouped, 'tp', split_axis=1, concat_axis=0, tiled=True)  14.9 us
    all_to_all x3, starting transfers between devices, gather_tp(): gathered = lax.all_to_all(stacked, 'tp', 0, 0, tiled=True)  12.8 us
  transfers between devices with their start and end apart: 14, of which 10 were waited for; matrix products, arithmetic and copies ran while one was open for 28% of the time, Pallas kernels for 0%

profile of v11, /device:TPU:0, one launch (start us, length us, event | category | flops | bytes accessed | tf_op | source)
XLA Modules:
  0.0 382.0 jit_solution(17736765379853198471)
XLA Ops:
  8.5 14.9 %all_to_all.68 = bf16[8,8,3872]{2,0,1:T(8,128)(2,1)S(1)} all-to-all(bf16[8,8,3872]{2,0,1:T(8,128)(2,1)S(1)} %concatenate.28), channel_id=1, replica_groups=mesh['chip'=8,'core'=2,'tp'=8] {'tp'}, dimensions={1} | all-to-all | bytes 991232 | tf_op jit(solution)/shard_map/all_to_all | solution.py:136
  25.2 18.3 %all_to_all.69 = bf16[8,8,8448]{2,0,1:T(8,128)(2,1)} all-to-all(bf16[8,8,8448]{2,0,1:T(8,128)(2,1)S(1)} %broadcast_in_dim.260), channel_id=1, replica_groups=mesh['chip'=8,'core'=2,'tp'=8] {'tp'}, dimensions={1} | all-to-all | bytes 2162688 | tf_op jit(solution)/shard_map/all_to_all | solution.py:144
  49.5 7.7 %all-to-all-start.2 = ((bf16[8,64,384]{2,1,0:T(8,128)(2,1)}), bf16[8,64,384]{2,1,0:T(8,128)(2,1)S(1)}, u32[]{:S(2)}, u32[]{:S(2)}) async-start(bf16[8,64,384]{2,1,0:T(8,128)(2,1)} %broadcast_in_dim.239), calls=%async_computation.2 | async-start | bytes 786432 | tf_op jit(solution)/shard_map/all_to_all | solution.py:163
  58.3 8.4 %all-to-all-done.2 = bf16[8,64,384]{2,1,0:T(8,128)(2,1)S(1)} async-done(((bf16[8,64,384]{2,1,0:T(8,128)(2,1)}), bf16[8,64,384]{2,1,0:T(8,128)(2,1)S(1)}, u32[]{:S(2)}, u32[]{:S(2)}) %all-to-all-start.2) | async-done | bytes 393248 | tf_op jit(solution)/shard_map/all_to_all | solution.py:163
  68.3 3.6 all-to-all-start
  76.8 21.2 %all-to-all-done = bf16[8,128,1024]{2,1,0:T(8,128)(2,1)S(1)} async-done(((bf16[8,128,1024]{2,1,0:T(8,128)(2,1)}), bf16[8,128,1024]{2,1,0:T(8,128)(2,1)S(1)}, u32[]{:S(2)}, u32[]{:S(2)}) %all-to-all-start) | async-done | bytes 2097184 | tf_op jit(solution)/shard_map/all_to_all | solution.py:60
  101.8 9.3 %fusion.79 = (f32[2,1024]{1,0:T(2,128)}, f32[2,1024,1024]{1,2,0:T(8,128)}) fusion(f32[2]{0:T(128)} %get-tuple-element.12, f32[2]{0:T(128)} %get-tuple-element.11, pred[1024,1024]{0,1:T(8,128)(4,1)S(1)} %copy-done.4, pred[1024,1024]{0,1:T(8,128)(4,1)S(1)} %copy-done.6, bf16[1024,2,32]{0,2,1:T(8,128)(2,1)} %get-tuple-element.50, ...), kind=kOutput, calls=%fused_computation.194 | convolution fusion | flops 282067968 | bytes 11018256 | tf_op jit(solution)/shard_map/sub | solution.py:231
  111.1 4.2 %fusion.24 = bf16[2,64,1024]{2,1,0:T(8,128)(2,1)S(1)} fusion(bf16[1024,2,64]{0,2,1:T(8,128)(2,1)S(1)} %bitcast.173, f32[2,1024,1024]{1,2,0:T(8,128)} %get-tuple-element.63, f32[2,1024]{1,0:T(2,128)} %get-tuple-element.62), kind=kOutput, calls=%fused_computation.53 | convolution fusion | flops 272760832 | bytes 8921088 | tf_op jit(solution)/shard_map/hqk,khd->qhd/dot_general | solution.py:236
  116.3 4.3 %all-to-all-start.3 = ((bf16[8,128,128]{2,1,0:T(8,128)(2,1)}), bf16[8,128,128]{2,1,0:T(8,128)(2,1)S(1)}, u32[]{:S(2)}, u32[]{:S(2)}) async-start(bf16[8,128,128]{2,1,0:T(8,128)(2,1)} %copy.99), calls=%async_computation.3 | async-start | bytes 524288 | tf_op jit(solution)/shard_map/all_to_all | solution.py:73
  135.0 5.6 %all-to-all-start.4 = ((bf16[8,128,1024]{2,1,0:T(8,128)(2,1)}), bf16[8,128,1024]{2,1,0:T(8,128)(2,1)S(1)}, u32[]{:S(2)}, u32[]{:S(2)}) async-start(bf16[8,128,1024]{2,1,0:T(8,128)(2,1)} %broadcast_in_dim.250), calls=%async_computation.4 | async-start | bytes 4194304 | tf_op jit(solution)/shard_map/all_to_all | solution.py:60
  142.6 28.7 %all-to-all-done.4 = bf16[8,128,1024]{2,1,0:T(8,128)(2,1)S(1)} async-done(((bf16[8,128,1024]{2,1,0:T(8,128)(2,1)}), bf16[8,128,1024]{2,1,0:T(8,128)(2,1)S(1)}, u32[]{:S(2)}, u32[]{:S(2)}) %all-to-all-start.4) | async-done | bytes 2097184 | tf_op jit(solution)/shard_map/all_to_all | solution.py:60
  171.3 3.1 fusion.19
  174.4 4.0 %convolution_convert_fusion = bf16[1024,1024]{1,0:T(8,128)(2,1)} fusion(bf16[1024,2080]{1,0:T(8,128)(2,1)} %all-gather.5.cloned.1.call-done, f32[1024,704]{0,1:T(8,128)S(1)} %fusion.19), kind=kOutput, calls=%fused_computation.45 | convolution fusion | flops 741408768 | bytes 5767168 | tf_op jit(solution)/shard_map/dot_general | solution.py:53
  178.4 3.6 all-to-all-start.5
  182.1 30.9 %all-to-all-done.5 = bf16[8,128,1024]{2,1,0:T(8,128)(2,1)S(1)} async-done(((bf16[8,128,1024]{2,1,0:T(8,128)(2,1)}), bf16[8,128,1024]{2,1,0:T(8,128)(2,1)S(1)}, u32[]{:S(2)}, u32[]{:S(2)}) %all-to-all-start.5) | async-done | bytes 2097184 | tf_op jit(solution)/shard_map/all_to_all | solution.py:66
  217.3 3.6 all-to-all-start.6
  221.0 50.0 %all-gather.7.cloned.1.call-done = bf16[512,8448]{1,0:T(8,128)(2,1)} async-done(((bf16[64,8448]{1,0:T(8,128)(2,1)}), bf16[512,8448]{1,0:T(8,128)(2,1)}) %all-gather.7.cloned.1.call-update) | async-done | bytes 8650768 | tf_op jit(solution)/shard_map/all_gather | solution.py:143
  271.0 12.3 %copy.113 = bf16[512,8448]{0,1:T(8,128)(2,1)} copy(bf16[512,8448]{1,0:T(8,128)(2,1)} %all-gather.7.cloned.1.call-done) | data formatting | bytes 17301504 | tf_op jit(solution)/shard_map/all_gather | solution.py:143
  283.3 8.2 %dynamic-slice_bitcast_fusion = (bf16[512,3,1408]{0,2,1:T(8,128)(2,1)}, bf16[512,3,1408]{0,2,1:T(8,128)(2,1)}) fusion(bf16[512,3,2,1408]{0,3,2,1:T(8,128)(2,1)} %bitcast.149, s32[]{:T(128)S(6)} %select_n.180, s32[]{:T(128)S(6)} %select_n.179), kind=kLoop, calls=%fused_computation.22 | loop fusion | bytes 17301512 | tf_op jit(solution)/shard_map/jit(dynamic_index_in_dim)/squeeze | solution.py:150
  291.9 31.6 %all-gather.9.cloned.1.call-done = bf16[1024,1,1408]{2,0,1:T(8,128)(2,1)} async-done(((bf16[64,1,1408]{2,0,1:T(8,128)(2,1)}), bf16[1024,1,1408]{2,0,1:T(8,128)(2,1)}) %all-gather.9.cloned.1.call-update) | async-done | bytes 2883600 | tf_op jit(solution)/shard_map/all_gather | solution.py:159
  327.3 8.8 %fusion.80 = (f32[2,1024]{1,0:T(2,128)S(1)}, f32[2,1024,1024]{1,2,0:T(8,128)}) fusion(f32[2]{0:T(128)S(1)} %get-tuple-element.10, f32[2]{0:T(128)S(1)} %get-tuple-element.9, pred[1024,1024]{0,1:T(8,128)(4,1)S(1)} %copy-done.5, pred[1024,1024]{0,1:T(8,128)(4,1)S(1)} %copy-done.7, bf16[1024,2,32]{0,2,1:T(8,128)(2,1)} %get-tuple-element.48, ...), kind=kOutput, calls=%fused_computation.195 | convolution fusion | flops 282067968 | bytes 11018256 | tf_op jit(solution)/shard_map/sub | solution.py:231
  336.1 4.2 %fusion.23 = bf16[2,64,1024]{2,1,0:T(8,128)(2,1)S(1)} fusion(bf16[1024,2,64]{0,2,1:T(8,128)(2,1)S(1)} %bitcast.172, f32[2,1024,1024]{1,2,0:T(8,128)} %get-tuple-element.65, f32[2,1024]{1,0:T(2,128)S(1)} %get-tuple-element.64), kind=kOutput, calls=%fused_computation.52 | convolution fusion | flops 272760832 | bytes 8921088 | tf_op jit(solution)/shard_map/hqk,khd->qhd/dot_general | solution.py:236
  341.2 4.3 %all-to-all-start.7 = ((bf16[8,128,128]{2,1,0:T(8,128)(2,1)}), bf16[8,128,128]{2,1,0:T(8,128)(2,1)S(1)}, u32[]{:S(2)}, u32[]{:S(2)}) async-start(bf16[8,128,128]{2,1,0:T(8,128)(2,1)} %copy.108), calls=%async_computation.7 | async-start | bytes 524288 | tf_op jit(solution)/shard_map/all_to_all | solution.py:73
  359.6 3.5 fusion.2
  (180 shorter events, 73.4 us)
Async XLA Ops:
  6.5 115.2 %all-gather.5.cloned.1.call-start = ((), (), s32[]{:S(2)}) async-start(), calls=%async_computation.9 | async-start | bytes 4734976 | tf_op jit(solution)/shard_map/all_gather | solution.py:159
  8.2 35.3 %copy-start.11 = (f32[2,2,1024]{2,1,0:T(2,128)S(1)}, f32[2,2,1024]{2,1,0:T(2,128)}, u32[]{:S(2)}) copy-start(f32[2,2,1024]{2,1,0:T(2,128)} %param.14) | copy-start | bytes 49156
  8.5 35.4 %copy-start.17 = (s32[128]{0:T(128)S(1)}, s32[128]{0:T(128)}, u32[]{:S(2)}) copy-start(s32[128]{0:T(128)} %param.12) | copy-start | bytes 1540
  8.5 37.5 %copy-start.9 = (f32[128,1024]{1,0:T(8,128)S(1)}, f32[128,1024]{1,0:T(8,128)}, u32[]{:S(2)}) copy-start(f32[128,1024]{1,0:T(8,128)} %param.13) | copy-start | bytes 1572868
  25.0 246.0 %all-gather.7.cloned.1.call-start = ((), (), s32[]{:S(2)}) async-start(), calls=%async_computation.10 | async-start | bytes 9732096 | tf_op jit(solution)/shard_map/all_gather | solution.py:143
  47.2 10.0 %copy-start.16 = (s32[128]{0:T(128)}, s32[128]{0:T(128)S(1)}, u32[]{:S(2)}) copy-start(s32[128]{0:T(128)S(1)} %fusion.54) | copy-start | bytes 1540
  49.5 17.2 %all-to-all-start.2 = ((bf16[8,64,384]{2,1,0:T(8,128)(2,1)}), bf16[8,64,384]{2,1,0:T(8,128)(2,1)S(1)}, u32[]{:S(2)}, u32[]{:S(2)}) async-start(bf16[8,64,384]{2,1,0:T(8,128)(2,1)} %broadcast_in_dim.239), calls=%async_computation.2 | async-start | bytes 786432 | tf_op jit(solution)/shard_map/all_to_all | solution.py:163
  57.9 14.0 %copy-start.12 = (f32[2,16,2]{1,2,0:T(2,128)S(1)}, f32[2,16,2]{1,2,0:T(2,128)}, u32[]{:S(2)}) copy-start(f32[2,16,2]{1,2,0:T(2,128)} %param.17) | copy-start | bytes 772
  57.9 14.2 %copy-start.18 = (s32[1,4]{1,0:T(1,128)S(1)}, s32[1,4]{1,0:T(1,128)}, u32[]{:S(2)}) copy-start(s32[1,4]{1,0:T(1,128)} %param.15) | copy-start | bytes 52
  57.9 16.6 %copy-start.10 = (s32[1024]{0:T(1024)S(1)}, s32[1024]{0:T(1024)}, u32[]{:S(2)}) copy-start(s32[1024]{0:T(1024)} %param.16) | copy-start | bytes 12292
  68.3 29.7 %all-to-all-start = ((bf16[8,128,1024]{2,1,0:T(8,128)(2,1)}), bf16[8,128,1024]{2,1,0:T(8,128)(2,1)S(1)}, u32[]{:S(2)}, u32[]{:S(2)}) async-start(bf16[8,128,1024]{2,1,0:T(8,128)(2,1)} %broadcast_in_dim.234), calls=%async_computation | async-start | bytes 4194304 | tf_op jit(solution)/shard_map/all_to_all | solution.py:60
  73.9 2.9 collective-permute-start
  116.3 11.5 %all-to-all-start.3 = ((bf16[8,128,128]{2,1,0:T(8,128)(2,1)}), bf16[8,128,128]{2,1,0:T(8,128)(2,1)S(1)}, u32[]{:S(2)}, u32[]{:S(2)}) async-start(bf16[8,128,128]{2,1,0:T(8,128)(2,1)} %copy.99), calls=%async_computation.3 | async-start | bytes 524288 | tf_op jit(solution)/shard_map/all_to_all | solution.py:73
  135.0 36.3 %all-to-all-start.4 = ((bf16[8,128,1024]{2,1,0:T(8,128)(2,1)}), bf16[8,128,1024]{2,1,0:T(8,128)(2,1)S(1)}, u32[]{:S(2)}, u32[]{:S(2)}) async-start(bf16[8,128,1024]{2,1,0:T(8,128)(2,1)} %broadcast_in_dim.250), calls=%async_computation.4 | async-start | bytes 4194304 | tf_op jit(solution)/shard_map/all_to_all | solution.py:60
  140.6 182.9 %all-gather.9.cloned.1.call-start = ((), (), s32[]{:S(2)}) async-start(), calls=%async_computation.11 | async-start | bytes 3063808 | tf_op jit(solution)/shard_map/all_gather | solution.py:159
  178.4 34.6 %all-to-all-start.5 = ((bf16[8,128,1024]{2,1,0:T(8,128)(2,1)}), bf16[8,128,1024]{2,1,0:T(8,128)(2,1)S(1)}, u32[]{:S(2)}, u32[]{:S(2)}) async-start(bf16[8,128,1024]{2,1,0:T(8,128)(2,1)} %bitcast.158), calls=%async_computation.5 | async-start | bytes 4194304 | tf_op jit(solution)/shard_map/all_to_all | solution.py:66
  213.6 3.7 copy-start
  217.3 106.2 %all-to-all-start.6 = ((bf16[8,128,1024]{2,1,0:T(8,128)(2,1)}), bf16[8,128,1024]{2,1,0:T(8,128)(2,1)S(1)}, u32[]{:S(2)}, u32[]{:S(2)}) async-start(bf16[8,128,1024]{2,1,0:T(8,128)(2,1)} %broadcast_in_dim.251), calls=%async_computation.6 | async-start | bytes 4194304 | tf_op jit(solution)/shard_map/all_to_all | solution.py:60
  291.5 68.1 %collective-permute-start.2 = (bf16[512,3,1408]{0,2,1:T(8,128)(2,1)}, bf16[512,3,1408]{0,2,1:T(8,128)(2,1)}, u32[]{:S(2)}, u32[]{:S(2)}) collective-permute-start(bf16[512,3,1408]{0,2,1:T(8,128)(2,1)} %get-tuple-element.21), channel_id=1, source_target_pairs={{0,8},{8,0},{1,9},{9,1},{2,10},{10,2},{3,11},{11,3},{4,12},{12,4},... | collective-permute-start | bytes 12976136 | tf_op jit(solution)/shard_map/ppermute | solution.py:151
  341.2 11.6 %all-to-all-start.7 = ((bf16[8,128,128]{2,1,0:T(8,128)(2,1)}), bf16[8,128,128]{2,1,0:T(8,128)(2,1)S(1)}, u32[]{:S(2)}, u32[]{:S(2)}) async-start(bf16[8,128,128]{2,1,0:T(8,128)(2,1)} %copy.108), calls=%async_computation.7 | async-start | bytes 524288 | tf_op jit(solution)/shard_map/all_to_all | solution.py:73
  349.9 5.7 %copy-start.1 = (f32[128,1024]{0,1:T(8,128)S(1)}, f32[128,1024]{0,1:T(8,128)}, u32[]{:S(2)}) copy-start(f32[128,1024]{0,1:T(8,128)} %copy-done) | copy-start | bytes 1572868
  357.1 1.6 collective-permute-start.1
  359.6 3.6 copy-start.14
  370.9 2.0 collective-permute-start.3
  (9 other events, 9.4 us)
Sparse Core Ops, SparseCore 0:
  25.1 83.2 all-gather.4
  110.7 160.2 all-gather.6
  273.5 49.9 all-gather.8

commit v12 on v8

--- a/solution.py
+++ b/solution.py
@@ -137,8 +137,24 @@
     gains = [reorder(norm_gains[i], shard_order) for i in range(layer_count)]
     token_count = variate_ids.shape[0]
     segment, offsets = prompt_layout(prompt_lengths[0], token_count)
-    same_prompt = segment[:, None] == segment[None, :]
-    same_variate = variate_ids[:, None] == variate_ids[None, :]
+    half_count = token_count // 2
+    lengths = prompt_lengths[0]
+    long_start = (jnp.cumsum(lengths) - lengths)[jnp.argmax(lengths)]
+    position = jnp.arange(token_count, dtype=jnp.int32)
+    half_order = jnp.where(
+        position < half_count,
+        long_start + position,
+        jnp.where(position - half_count < long_start, position - half_count, position),
+    )
+    token_place = jnp.where(
+        (position >= long_start) & (position < long_start + half_count),
+        position - long_start,
+        jnp.where(position < long_start, position + half_count, position),
+    )
+    half_segment = jnp.take(segment, half_order).reshape(2, half_count)
+    half_variate = jnp.take(variate_ids, half_order).reshape(2, half_count)
+    same_prompt = half_segment[:, :, None] == half_segment[:, None, :]
+    same_variate = half_variate[:, :, None] == half_variate[:, None, :]
     head_count = variate_bias.shape[1]
     local_heads = head_count // tp_count
     head_size = head_cols // local_heads
@@ -149,7 +165,9 @@
     for layer_index in range(layer_count):
         layer_bias = bias_table[layer_index]
         pair_bias = jnp.where(
-            same_variate[None], layer_bias[:, 1][:, None, None], layer_bias[:, 0][:, None, None]
+            same_variate[:, None],
+            layer_bias[:, 1][None, :, None, None],
+            layer_bias[:, 0][None, :, None, None],
         )
         normed = rms_scaled(residual, gains[layer_index][0]).astype(jnp.bfloat16)
         piece = regrouped[layer_index, :, 0, :]
@@ -177,22 +195,33 @@
             .reshape(token_count, local_heads, head_size)
             .astype(jnp.bfloat16)
         )
+        def halves(rows):
+            return jnp.take(rows, half_order, axis=0).reshape(
+                (2, half_count) + rows.shape[1:]
+            )
+
         scores = (
-            jnp.einsum("qhd,khd->hqk", queries, key_rows, preferred_element_type=jnp.float32)
+            jnp.einsum(
+                "bqhd,bkhd->bhqk",
+                halves(queries),
+                halves(key_rows),
+                preferred_element_type=jnp.float32,
+            )
             * head_size ** (-0.5)
             + pair_bias
         )
-        scores = jnp.where(same_prompt[None], scores, NEGATIVE)
-        row_peak = jnp.max(scores, axis=2, keepdims=True)
+        scores = jnp.where(same_prompt[:, None], scores, NEGATIVE)
+        row_peak = jnp.max(scores, axis=3, keepdims=True)
         weights_exp = jnp.exp(scores - row_peak)
-        attn_weights = (weights_exp / jnp.sum(weights_exp, axis=2, keepdims=True)).astype(
+        attn_weights = (weights_exp / jnp.sum(weights_exp, axis=3, keepdims=True)).astype(
             jnp.bfloat16
         )
-        mixed_heads = (
-            jnp.einsum("hqk,khd->qhd", attn_weights, values, preferred_element_type=jnp.float32)
-            .astype(jnp.bfloat16)
-            .reshape(token_count, head_cols)
-        )
+        mixed_halves = jnp.einsum(
+            "bhqk,bkhd->bqhd", attn_weights, halves(values), preferred_element_type=jnp.float32
+        ).astype(jnp.bfloat16)
+        mixed_heads = jnp.take(
+            mixed_halves.reshape(token_count, local_heads, head_size), token_place, axis=0
+        ).reshape(token_count, head_cols)
         head_total = project_owned(mixed_heads, out_weight, tp_count)
         residual = residual + head_total
         normed_mlp = rms_scaled(residual, gains[layer_index][1]).astype(jnp.bfloat16)

time: 347 us -> 428 us (1.23)
  local copies, waits for them, and re-layouts: 37.4 us -> 96 us
  other arithmetic: 15.7 us -> 50.8 us
  waiting for transfers between devices: 118 us -> 105 us
  matrix products: 48.2 us -> 38.2 us
  starting transfers between devices: 32.5 us -> 38.7 us
    gather x0 -> x10, local copies, waits for them, and re-layouts: none -> 38.7 us  [the longest x6 22.2 us: halves(): jnp.take(rows, half_order, axis=0).reshape((2, half_count) + rows.shape[1:])]
    select_n x0 -> x6, other arithmetic: none -> 19.2 us  [the longest x2 10.6 us: halves(): jnp.take(rows, half_order, axis=0).reshape((2, half_count) + rows.shape[1:])]
    unnamed x37 -> x75, local copies, waits for them, and re-layouts: 2.17 us -> 15.3 us
    all_to_all x1, waiting for transfers between devices: 8.9 us -> 0.01 us  [gather_chips(): lax.all_to_all(stacked, CHIP_AXES, 0, 0, tiled=True)]
    all_to_all x2, starting transfers between devices: 7.99 us -> 16.7 us  [gather_tp(): gathered = lax.all_to_all(stacked, 'tp', 0, 0, tiled=True)]
    another operation x3 -> x4, other arithmetic: 1.98 us -> 9.67 us
    sub x2, matrix products: 18 us -> 11.3 us  [on_device(): weights_exp = jnp.exp(scores - row_peak)]
    concatenate x0 -> x4, other arithmetic: none -> 5.68 us  [rotate(): jnp.concatenate([front_half * cosine - back_half * sine_part, front_half...]
  transfers between devices with their start and end apart: 10 -> 10, of which waited for: 7 -> 5; matrix products, arithmetic and copies ran while one was open for 18% -> 26% of each run, Pallas kernels for 0% -> 0%
where the time goes in v12:
time: 428 us; the launch traced here: 423 us
  waiting for transfers between devices  105 us (25%)
  local copies, waits for them, and re-layouts  96 us (22%)
  blocking collectives  76.6 us (18%)
  other arithmetic  50.8 us (12%)
  starting transfers between devices  38.7 us (9%)
  matrix products  38.2 us (9%)
  between operations  17.1 us (4%)
    all_to_all x2, blocking collectives, gather_tp(): gathered = lax.all_to_all(stacked, 'tp', 0, 0, tiled=True)  60.1 us
    all_to_all x2, waiting for transfers between devices, reduce_tp(): received = lax.all_to_all(pieces, 'tp', 0, 0, tiled=True)  53.8 us
    all_to_all x2, waiting for transfers between devices, gather_tp(): gathered = lax.all_to_all(stacked, 'tp', 0, 0, tiled=True)  50.6 us
    gather x6, local copies, waits for them, and re-layouts, halves(): jnp.take(rows, half_order, axis=0).reshape((2, half_count) + rows.shape[1:])  22.2 us
    all_to_all x2, starting transfers between devices, gather_tp(): gathered = lax.all_to_all(stacked, 'tp', 0, 0, tiled=True)  16.7 us
    all_to_all x1, blocking collectives, on_device(): lax.all_to_all(grouped, 'tp', split_axis=2, concat_axis=1, tiled=True)  16.5 us
    unnamed x75, local copies, waits for them, and re-layouts  15.3 us
    slice x4, local copies, waits for them, and re-layouts, on_device(): out_weight = layer_weights[:, :model_width]  11.9 us
  transfers between devices with their start and end apart: 10, of which 5 were waited for; matrix products, arithmetic and copies ran while one was open for 26% of the time, Pallas kernels for 0%

profile of v12, /device:TPU:0, one launch (start us, length us, event | category | flops | bytes accessed | tf_op | source)
XLA Modules:
  0.0 422.8 jit_solution(8082682090536442543)
XLA Ops:
  8.8 16.5 %all_to_all.60 = bf16[2,8,8,2464]{3,1,0,2:T(8,128)(2,1)S(1)} all-to-all(bf16[2,8,8,2464]{3,1,0,2:T(8,128)(2,1)S(1)} %concatenate.22), channel_id=1, replica_groups=mesh['chip'=8,'core'=2,'tp'=8] {'tp'}, dimensions={2} | all-to-all | bytes 1261568 | tf_op jit(solution)/shard_map/all_to_all | solution.py:106
  38.7 7.7 %all-to-all-start.2 = ((bf16[8,64,384]{2,1,0:T(8,128)(2,1)}), bf16[8,64,384]{2,1,0:T(8,128)(2,1)S(1)}, u32[]{:S(2)}, u32[]{:S(2)}) async-start(bf16[8,64,384]{2,1,0:T(8,128)(2,1)} %broadcast_in_dim.215), calls=%async_computation.2 | async-start | bytes 786432 | tf_op jit(solution)/shard_map/all_to_all | solution.py:120
  47.2 4.5 %gather_fusion.4 = s32[1024]{0:T(1024)S(1)} fusion(s32[1024]{0:T(1024)S(1)} %convert_reduce_fusion.4, s32[1024]{0:T(1024)S(1)} %get-tuple-element.84), kind=kCustom, calls=%fused_computation.3.clone | custom fusion | bytes 12288 | tf_op jit(solution)/shard_map/jit(_take)/gather | solution.py:154
  51.7 4.5 %gather_fusion.7 = s32[1024]{0:T(1024)S(1)} fusion(s32[1024]{0:T(1024)S(1)} %copy-done, s32[1024]{0:T(1024)S(1)} %get-tuple-element.84), kind=kCustom, calls=%fused_computation.13.clone | custom fusion | bytes 12288 | tf_op jit(solution)/shard_map/jit(_take)/gather | solution.py:155
  58.5 4.5 %all-to-all-start = ((bf16[8,128,1024]{2,1,0:T(8,128)(2,1)}), bf16[8,128,1024]{2,1,0:T(8,128)(2,1)}, u32[]{:S(2)}, u32[]{:S(2)}) async-start(bf16[8,128,1024]{2,1,0:T(8,128)(2,1)} %broadcast_in_dim.213), calls=%async_computation | async-start | bytes 4194304 | tf_op jit(solution)/shard_map/all_to_all | solution.py:60
  70.7 22.7 %all-to-all-done = bf16[8,128,1024]{2,1,0:T(8,128)(2,1)} async-done(((bf16[8,128,1024]{2,1,0:T(8,128)(2,1)}), bf16[8,128,1024]{2,1,0:T(8,128)(2,1)}, u32[]{:S(2)}, u32[]{:S(2)}) %all-to-all-start) | async-done | bytes 2097184 | tf_op jit(solution)/shard_map/all_to_all | solution.py:60
  106.0 4.4 %subtract_convert_fusion.3 = (bf16[1024,2,32]{2,1,0:T(2,128)(2,1)S(1)}, bf16[1024,2,32]{2,1,0:T(2,128)(2,1)}, bf16[1024,2,32]{2,1,0:T(2,128)(2,1)S(1)}, bf16[1024,2,32]{2,1,0:T(2,128)(2,1)S(1)}) fusion(f32[1024,2,32]{2,1,0:T(2,128)} %copy.291, f32[1024,2,32]{2,1,0:T(2,128)S(1)} %copy.290, f32[1024,32]{1,0:T(8,128)S(1)} %get-tuple-element.61, ...), kind=kLoop, calls=%fused_computation.66 | loop fusion | flops 1048576 | bytes 1835008 | tf_op jit(solution)/shard_map/convert.7
  124.9 5.5 %broadcast_select_fusion.7 = (bf16[1024,2,64]{2,1,0:T(2,128)(2,1)}, bf16[1024,2,64]{2,1,0:T(2,128)(2,1)}, bf16[1024,2,64]{2,1,0:T(2,128)(2,1)}) fusion(bf16[1024,2,64]{2,1,0:T(2,128)(2,1)S(1)} %gather_fusion.3, pred[1024]{0:T(1024)(128)(4,1)} %get-tuple-element.83, bf16[1024,2,64]{2,1,0:T(2,128)(2,1)S(1)} %gather_fusion.5, ...), kind=kLoop, calls=%fused_computation.75 | loop fusion | flops 393216 | bytes 1573888 | tf_op jit(solution)/shard_map/jit(_take)/select_n | solution.py:199
  130.4 5.6 %fusion.103 = (f32[2,2,512]{2,1,0:T(2,128)S(1)}, f32[2,2,512,512]{2,3,1,0:T(8,128)}) fusion(f32[2]{0:T(128)S(1)} %copy-done.30, f32[2]{0:T(128)S(1)} %copy-done.29, pred[2,512,512]{1,2,0:T(8,128)(4,1)S(1)} %copy-done.17, pred[2,512,512]{1,2,0:T(8,128)(4,1)S(1)} %copy-done.15, bf16[2,512,2,64]{3,2,1,0:T(2,128)(2,1)} %bitcast.145, ...), kind=kOutput, calls=%fused_computation.216 | convolution fusion | flops 140509696 | bytes 5775376 | tf_op jit(solution)/shard_map/sub | solution.py:215
  139.2 3.7 gather_fusion.8
  143.0 3.7 broadcast_select_fusion.1
  161.1 30.8 %all_to_all.61 = bf16[8,128,1024]{2,1,0:T(8,128)(2,1)S(1)} all-to-all(bf16[8,128,1024]{2,1,0:T(8,128)(2,1)S(1)} %broadcast_in_dim.226), channel_id=1, replica_groups=mesh['chip'=8,'core'=2,'tp'=8] {'tp'}, dimensions={0} | all-to-all | bytes 4194304 | tf_op jit(solution)/shard_map/all_to_all | solution.py:60
  195.1 4.0 convolution_convert_fusion.1
  202.8 27.6 %all-to-all-done.5 = bf16[8,128,1024]{2,1,0:T(8,128)(2,1)S(1)} async-done(((bf16[8,128,1024]{2,1,0:T(8,128)(2,1)}), bf16[8,128,1024]{2,1,0:T(8,128)(2,1)S(1)}, u32[]{:S(2)}, u32[]{:S(2)}) %all-to-all-start.5) | async-done | bytes 2097184 | tf_op jit(solution)/shard_map/all_to_all | solution.py:66
  236.7 12.2 %all-to-all-start.6 = ((bf16[8,128,1024]{2,1,0:T(8,128)(2,1)}), bf16[8,128,1024]{2,1,0:T(8,128)(2,1)S(1)}, u32[]{:S(2)}, u32[]{:S(2)}) async-start(bf16[8,128,1024]{2,1,0:T(8,128)(2,1)} %broadcast_in_dim.227), calls=%async_computation.6 | async-start | bytes 4194304 | tf_op jit(solution)/shard_map/all_to_all | solution.py:60
  249.2 27.9 %all-to-all-done.6 = bf16[8,128,1024]{2,1,0:T(8,128)(2,1)S(1)} async-done(((bf16[8,128,1024]{2,1,0:T(8,128)(2,1)}), bf16[8,128,1024]{2,1,0:T(8,128)(2,1)S(1)}, u32[]{:S(2)}, u32[]{:S(2)}) %all-to-all-start.6) | async-done | bytes 2097184 | tf_op jit(solution)/shard_map/all_to_all | solution.py:60
  288.4 4.4 %subtract_convert_fusion.1 = (bf16[1024,2,32]{2,1,0:T(2,128)(2,1)}, bf16[1024,2,32]{2,1,0:T(2,128)(2,1)}, bf16[1024,2,32]{2,1,0:T(2,128)(2,1)S(1)}, bf16[1024,2,32]{2,1,0:T(2,128)(2,1)S(1)}) fusion(f32[1024,2,32]{2,1,0:T(2,128)} %copy.295, f32[1024,2,32]{2,1,0:T(2,128)S(1)} %copy.294, f32[1024,32]{1,0:T(8,128)S(1)} %copy-done.5, ...), kind=kLoop, calls=%fused_computation.61 | loop fusion | flops 1048576 | bytes 1835008 | tf_op jit(solution)/shard_map/convert.2
  307.2 5.1 %broadcast_select_fusion.4 = (bf16[1024,2,64]{2,1,0:T(2,128)(2,1)}, bf16[1024,2,64]{2,1,0:T(2,128)(2,1)}, bf16[1024,2,64]{2,1,0:T(2,128)(2,1)}) fusion(bf16[1024,2,64]{2,1,0:T(2,128)(2,1)S(1)} %gather_fusion.10, pred[1024]{0:T(1024)(128)(4,1)S(1)} %copy-done.23, bf16[1024,2,64]{2,1,0:T(2,128)(2,1)S(1)} %gather_fusion.11, ...), kind=kLoop, calls=%fused_computation.72 | loop fusion | flops 393216 | bytes 1573888 | tf_op jit(solution)/shard_map/jit(_take)/select_n | solution.py:199
  312.3 5.7 %fusion.108 = (f32[2,2,512]{2,1,0:T(2,128)S(1)}, f32[2,2,512,512]{2,3,1,0:T(8,128)}) fusion(f32[2]{0:T(128)S(1)} %get-tuple-element.14, f32[2]{0:T(128)S(1)} %get-tuple-element.13, pred[2,512,512]{1,2,0:T(8,128)(4,1)} %broadcast_compare_fusion, pred[2,512,512]{1,2,0:T(8,128)(4,1)S(1)} %copy-done.16, bf16[2,512,2,64]{3,2,1,0:T(2,128)(2,1)} %bitcast.142, ...), kind=kOutput, calls=%fused_computation.217 | convolution fusion | flops 140509696 | bytes 5775376 | tf_op jit(solution)/shard_map/sub | solution.py:215
  324.9 3.7 broadcast_select_fusion
  343.7 29.2 %all_to_all.62 = bf16[8,128,1024]{2,1,0:T(8,128)(2,1)S(1)} all-to-all(bf16[8,128,1024]{2,1,0:T(8,128)(2,1)S(1)} %broadcast_in_dim.232), channel_id=1, replica_groups=mesh['chip'=8,'core'=2,'tp'=8] {'tp'}, dimensions={0} | all-to-all | bytes 4194304 | tf_op jit(solution)/shard_map/all_to_all | solution.py:60
  376.1 4.1 convolution_convert_fusion
  380.1 3.7 all-to-all-start.9
  383.9 26.2 %all-to-all-done.9 = bf16[8,128,1024]{2,1,0:T(8,128)(2,1)S(1)} async-done(((bf16[8,128,1024]{2,1,0:T(8,128)(2,1)}), bf16[8,128,1024]{2,1,0:T(8,128)(2,1)S(1)}, u32[]{:S(2)}, u32[]{:S(2)}) %all-to-all-start.9) | async-done | bytes 2097184 | tf_op jit(solution)/shard_map/all_to_all | solution.py:66
  (223 shorter events, 137.6 us)
Async XLA Ops:
  6.5 45.2 %copy-start = (s32[1024]{0:T(1024)S(1)}, s32[1024]{0:T(1024)}, u32[]{:S(2)}) copy-start(s32[1024]{0:T(1024)} %param.20) | copy-start | bytes 12292
  6.5 145.7 %all-gather.3.cloned.1.call-start = ((), (), s32[]{:S(2)}) async-start(), calls=%async_computation.10 | async-start | bytes 4734976 | tf_op jit(solution)/shard_map/all_gather | solution.py:116
  8.8 18.1 %copy-start.20 = (f32[2,2,1024]{2,1,0:T(2,128)S(1)}, f32[2,2,1024]{2,1,0:T(2,128)}, u32[]{:S(2)}) copy-start(f32[2,2,1024]{2,1,0:T(2,128)} %param.18) | copy-start | bytes 49156
  38.7 18.1 %all-to-all-start.2 = ((bf16[8,64,384]{2,1,0:T(8,128)(2,1)}), bf16[8,64,384]{2,1,0:T(8,128)(2,1)S(1)}, u32[]{:S(2)}, u32[]{:S(2)}) async-start(bf16[8,64,384]{2,1,0:T(8,128)(2,1)} %broadcast_in_dim.215), calls=%async_computation.2 | async-start | bytes 786432 | tf_op jit(solution)/shard_map/all_to_all | solution.py:120
  58.5 6.3 %copy-start.26 = (f32[2,16,2]{1,2,0:T(2,128)S(1)}, f32[2,16,2]{1,2,0:T(2,128)}, u32[]{:S(2)}) copy-start(f32[2,16,2]{1,2,0:T(2,128)} %param.21) | copy-start | bytes 772
  58.5 34.9 %all-to-all-start = ((bf16[8,128,1024]{2,1,0:T(8,128)(2,1)}), bf16[8,128,1024]{2,1,0:T(8,128)(2,1)}, u32[]{:S(2)}, u32[]{:S(2)}) async-start(bf16[8,128,1024]{2,1,0:T(8,128)(2,1)} %broadcast_in_dim.213), calls=%async_computation | async-start | bytes 4194304 | tf_op jit(solution)/shard_map/all_to_all | solution.py:60
  63.0 186.2 %all-gather.5.cloned.1.call-start = ((), (), s32[]{:S(2)}) async-start(), calls=%async_computation.11 | async-start | bytes 5570560 | tf_op jit(solution)/shard_map/all_gather | solution.py:116
  67.9 2.8 collective-permute-start
  70.7 35.4 %copy-start.2 = (f32[1024,32]{1,0:T(8,128)}, f32[1024,32]{1,0:T(8,128)S(1)}, u32[]{:S(2)}) copy-start(f32[1024,32]{1,0:T(8,128)S(1)} %get-tuple-element.60) | copy-start | bytes 393220
  70.7 35.4 %copy-start.4 = (f32[1024,32]{1,0:T(8,128)}, f32[1024,32]{1,0:T(8,128)S(1)}, u32[]{:S(2)}) copy-start(f32[1024,32]{1,0:T(8,128)S(1)} %get-tuple-element.61) | copy-start | bytes 393220
  121.1 9.3 %copy-start.15 = (pred[2,512,512]{1,2,0:T(8,128)(4,1)S(1)}, pred[2,512,512]{1,2,0:T(8,128)(4,1)}, u32[]{:S(2)}) copy-start(pred[2,512,512]{1,2,0:T(8,128)(4,1)} %broadcast_compare_fusion.1) | copy-start | bytes 1572868
  121.1 9.3 %copy-start.29 = (f32[2]{0:T(128)S(1)}, f32[2]{0:T(128)}, u32[]{:S(2)}) copy-start(f32[2]{0:T(128)} %get-tuple-element.15) | copy-start | bytes 28
  121.2 9.3 %copy-start.30 = (f32[2]{0:T(128)S(1)}, f32[2]{0:T(128)}, u32[]{:S(2)}) copy-start(f32[2]{0:T(128)} %get-tuple-element.16) | copy-start | bytes 28
  136.0 6.9 %copy-start.21 = (pred[1024]{0:T(1024)(128)(4,1)S(1)}, pred[1024]{0:T(1024)(128)(4,1)}, u32[]{:S(2)}) copy-start(pred[1024]{0:T(1024)(128)(4,1)} %get-tuple-element.82) | copy-start | bytes 3076
  147.7 10.6 %all-to-all-start.3 = ((bf16[8,128,128]{2,1,0:T(8,128)(2,1)}), bf16[8,128,128]{2,1,0:T(8,128)(2,1)S(1)}, u32[]{:S(2)}, u32[]{:S(2)}) async-start(bf16[8,128,128]{2,1,0:T(8,128)(2,1)} %reshape.734), calls=%async_computation.3 | async-start | bytes 524288 | tf_op jit(solution)/shard_map/all_to_all | solution.py:73
  199.1 31.4 %all-to-all-start.5 = ((bf16[8,128,1024]{2,1,0:T(8,128)(2,1)}), bf16[8,128,1024]{2,1,0:T(8,128)(2,1)S(1)}, u32[]{:S(2)}, u32[]{:S(2)}) async-start(bf16[8,128,1024]{2,1,0:T(8,128)(2,1)} %bitcast.129), calls=%async_computation.5 | async-start | bytes 4194304 | tf_op jit(solution)/shard_map/all_to_all | solution.py:66
  236.7 12.2 %copy-start.24 = (f32[1,2,2]{1,2,0:T(2,128)S(1)}, f32[1,2,2]{1,2,0:T(2,128)}, u32[]{:S(2)}) copy-start(f32[1,2,2]{1,2,0:T(2,128)} %get-tuple-element.62) | copy-start | bytes 52
  236.7 40.4 %all-to-all-start.6 = ((bf16[8,128,1024]{2,1,0:T(8,128)(2,1)}), bf16[8,128,1024]{2,1,0:T(8,128)(2,1)S(1)}, u32[]{:S(2)}, u32[]{:S(2)}) async-start(bf16[8,128,1024]{2,1,0:T(8,128)(2,1)} %broadcast_in_dim.227), calls=%async_computation.6 | async-start | bytes 4194304 | tf_op jit(solution)/shard_map/all_to_all | solution.py:60
  282.0 6.3 %copy-start.3 = (f32[1024,32]{1,0:T(8,128)S(1)}, f32[1024,32]{1,0:T(8,128)}, u32[]{:S(2)}) copy-start(f32[1024,32]{1,0:T(8,128)} %copy-done.2) | copy-start | bytes 393220
  282.0 6.3 %copy-start.5 = (f32[1024,32]{1,0:T(8,128)S(1)}, f32[1024,32]{1,0:T(8,128)}, u32[]{:S(2)}) copy-start(f32[1024,32]{1,0:T(8,128)} %copy-done.4) | copy-start | bytes 393220
  297.9 9.3 %copy-start.23 = (pred[1024]{0:T(1024)(128)(4,1)S(1)}, pred[1024]{0:T(1024)(128)(4,1)}, u32[]{:S(2)}) copy-start(pred[1024]{0:T(1024)(128)(4,1)} %get-tuple-element.83) | copy-start | bytes 3076
  318.0 6.9 %copy-start.22 = (pred[1024]{0:T(1024)(128)(4,1)S(1)}, pred[1024]{0:T(1024)(128)(4,1)}, u32[]{:S(2)}) copy-start(pred[1024]{0:T(1024)(128)(4,1)} %get-tuple-element.82) | copy-start | bytes 3076
  329.6 10.5 %all-to-all-start.7 = ((bf16[8,128,128]{2,1,0:T(8,128)(2,1)}), bf16[8,128,128]{2,1,0:T(8,128)(2,1)S(1)}, u32[]{:S(2)}, u32[]{:S(2)}) async-start(bf16[8,128,128]{2,1,0:T(8,128)(2,1)} %reshape.735), calls=%async_computation.7 | async-start | bytes 524288 | tf_op jit(solution)/shard_map/all_to_all | solution.py:73
  380.1 30.0 %all-to-all-start.9 = ((bf16[8,128,1024]{2,1,0:T(8,128)(2,1)}), bf16[8,128,1024]{2,1,0:T(8,128)(2,1)S(1)}, u32[]{:S(2)}, u32[]{:S(2)}) async-start(bf16[8,128,1024]{2,1,0:T(8,128)(2,1)} %bitcast.128), calls=%async_computation.9 | async-start | bytes 4194304 | tf_op jit(solution)/shard_map/all_to_all | solution.py:66
  (19 other events, 59.0 us)
Sparse Core Ops, SparseCore 0:
  27.0 81.4 all-gather.2
  111.0 60.5 all-gather.4

commit v13 on v8

--- a/solution.py
+++ b/solution.py
@@ -53,6 +53,13 @@
     return lax.dot_general(
         source, weight, (((1,), (1,)), ((), ())), preferred_element_type=jnp.float32
     )
+
+
+def gather_normed(residual, gain, tp_count):
+    stacked = jnp.broadcast_to(residual[None], (tp_count,) + residual.shape)
+    normed = rms_scaled(stacked, gain).astype(jnp.bfloat16)
+    gathered = lax.all_to_all(normed, "tp", 0, 0, tiled=True)
+    return gathered.reshape((tp_count * residual.shape[0],) + residual.shape[1:])
 
 
 def gather_tp(values, tp_count):
@@ -195,8 +202,9 @@
         )
         head_total = project_owned(mixed_heads, out_weight, tp_count)
         residual = residual + head_total
-        normed_mlp = rms_scaled(residual, gains[layer_index][1]).astype(jnp.bfloat16)
-        hidden = gated_units(gather_tp(normed_mlp, tp_count), weight=gate_up_weight)
+        hidden = gated_units(
+            gather_normed(residual, gains[layer_index][1], tp_count), weight=gate_up_weight
+        )
         unit_total = reduce_tp(
             project_out(source=hidden, weight=down_weight).astype(jnp.bfloat16), tp_count
         )

time: 347 us -> 346 us (level)
  no operation moved by 1% of the time
where the time goes in v13:
time: 346 us; the launch traced here: 345 us
  waiting for transfers between devices  118 us (34%)
  blocking collectives  79.3 us (23%)
  matrix products  48.2 us (14%)
  local copies, waits for them, and re-layouts  37.2 us (11%)
  starting transfers between devices  32.2 us (9%)
  other arithmetic  15.2 us (4%)
  between operations  14.1 us (4%)
    all_to_all x2, blocking collectives, gather_normed(): gathered = lax.all_to_all(normed, 'tp', 0, 0, tiled=True)  62.7 us
    all_to_all x2, waiting for transfers between devices, reduce_tp(): received = lax.all_to_all(pieces, 'tp', 0, 0, tiled=True)  55 us
    all_to_all x2, waiting for transfers between devices, gather_tp(): gathered = lax.all_to_all(stacked, 'tp', 0, 0, tiled=True)  53.8 us
    sub x2, matrix products, on_device(): weights_exp = jnp.exp(scores - row_peak)  18.1 us
    all_to_all x1, blocking collectives, on_device(): lax.all_to_all(grouped, 'tp', split_axis=2, concat_axis=1, tiled=True)  16.6 us
    slice x4, local copies, waits for them, and re-layouts, on_device(): out_weight = layer_weights[:, :model_width]  11.9 us
    all_to_all x1, waiting for transfers between devices, gather_chips(): lax.all_to_all(stacked, CHIP_AXES, 0, 0, tiled=True)  8.9 us
    dot_general x2, matrix products, on_device(): jnp.einsum('hqk,khd->qhd', attn_weights, values, preferred_element_type=j...  8.46 us
  transfers between devices with their start and end apart: 10, of which 7 were waited for; matrix products, arithmetic and copies ran while one was open for 18% of the time, Pallas kernels for 0%

profile of v13, /device:TPU:0, one launch (start us, length us, event | category | flops | bytes accessed | tf_op | source)
XLA Modules:
  0.0 344.7 jit_solution(6158078135604190839)
XLA Ops:
  8.8 16.6 %all_to_all.60 = bf16[2,8,8,2464]{3,1,0,2:T(8,128)(2,1)S(1)} all-to-all(bf16[2,8,8,2464]{3,1,0,2:T(8,128)(2,1)S(1)} %concatenate.22), channel_id=1, replica_groups=mesh['chip'=8,'core'=2,'tp'=8] {'tp'}, dimensions={2} | all-to-all | bytes 1261568 | tf_op jit(solution)/shard_map/all_to_all | solution.py:113
  33.9 7.7 %all-to-all-start.2 = ((bf16[8,64,384]{2,1,0:T(8,128)(2,1)}), bf16[8,64,384]{2,1,0:T(8,128)(2,1)S(1)}, u32[]{:S(2)}, u32[]{:S(2)}) async-start(bf16[8,64,384]{2,1,0:T(8,128)(2,1)} %broadcast_in_dim.204), calls=%async_computation.2 | async-start | bytes 786432 | tf_op jit(solution)/shard_map/all_to_all | solution.py:127
  42.7 8.9 %all-to-all-done.2 = bf16[8,64,384]{2,1,0:T(8,128)(2,1)S(1)} async-done(((bf16[8,64,384]{2,1,0:T(8,128)(2,1)}), bf16[8,64,384]{2,1,0:T(8,128)(2,1)S(1)}, u32[]{:S(2)}, u32[]{:S(2)}) %all-to-all-start.2) | async-done | bytes 393248 | tf_op jit(solution)/shard_map/all_to_all | solution.py:127
  53.2 4.4 %all-to-all-start = ((bf16[8,128,1024]{2,1,0:T(8,128)(2,1)}), bf16[8,128,1024]{2,1,0:T(8,128)(2,1)S(1)}, u32[]{:S(2)}, u32[]{:S(2)}) async-start(bf16[8,128,1024]{2,1,0:T(8,128)(2,1)} %broadcast_in_dim.202), calls=%async_computation | async-start | bytes 4194304 | tf_op jit(solution)/shard_map/all_to_all | solution.py:67
  62.2 25.2 %all-to-all-done = bf16[8,128,1024]{2,1,0:T(8,128)(2,1)S(1)} async-done(((bf16[8,128,1024]{2,1,0:T(8,128)(2,1)}), bf16[8,128,1024]{2,1,0:T(8,128)(2,1)S(1)}, u32[]{:S(2)}, u32[]{:S(2)}) %all-to-all-start) | async-done | bytes 2097184 | tf_op jit(solution)/shard_map/all_to_all | solution.py:67
  91.0 9.2 %fusion.75 = (f32[2,1024]{1,0:T(2,128)}, f32[2,1024,1024]{1,2,0:T(8,128)}) fusion(f32[2]{0:T(128)} %get-tuple-element.12, f32[2]{0:T(128)} %get-tuple-element.11, pred[1024,1024]{0,1:T(8,128)(4,1)S(1)} %copy-done.4, pred[1024,1024]{0,1:T(8,128)(4,1)S(1)} %copy-done.6, bf16[1024,2,32]{0,2,1:T(8,128)(2,1)} %get-tuple-element.40, ...), kind=kOutput, calls=%fused_computation.175 | convolution fusion | flops 282067968 | bytes 11018256 | tf_op jit(solution)/shard_map/sub | solution.py:194
  100.3 4.2 %fusion.25 = bf16[2,64,1024]{2,1,0:T(8,128)(2,1)S(1)} fusion(bf16[1024,2,64]{0,2,1:T(8,128)(2,1)S(1)} %bitcast.139, f32[2,1024,1024]{1,2,0:T(8,128)} %get-tuple-element.53, f32[2,1024]{1,0:T(2,128)} %get-tuple-element.52), kind=kOutput, calls=%fused_computation.49 | convolution fusion | flops 272760832 | bytes 8921088 | tf_op jit(solution)/shard_map/hqk,khd->qhd/dot_general | solution.py:199
  105.5 4.2 %all-to-all-start.3 = ((bf16[8,128,128]{2,1,0:T(8,128)(2,1)}), bf16[8,128,128]{2,1,0:T(8,128)(2,1)S(1)}, u32[]{:S(2)}, u32[]{:S(2)}) async-start(bf16[8,128,128]{2,1,0:T(8,128)(2,1)} %copy.119), calls=%async_computation.3 | async-start | bytes 524288 | tf_op jit(solution)/shard_map/all_to_all | solution.py:80
  110.9 3.1 slice.232
  121.1 33.4 %all_to_all.61 = bf16[8,128,1024]{2,1,0:T(8,128)(2,1)S(1)} all-to-all(bf16[8,128,1024]{2,1,0:T(8,128)(2,1)S(1)} %multiply_convert_fusion.1), channel_id=1, replica_groups=mesh['chip'=8,'core'=2,'tp'=8] {'tp'}, dimensions={0} | all-to-all | bytes 4194304 | tf_op jit(solution)/shard_map/all_to_all | solution.py:61
  154.4 3.2 fusion.20
  157.6 4.0 %convolution_convert_fusion.1 = bf16[1024,1024]{1,0:T(8,128)(2,1)} fusion(bf16[1024,2080]{1,0:T(8,128)(2,1)} %all-gather.3.cloned.1.call-done, f32[1024,704]{0,1:T(8,128)S(1)} %fusion.20), kind=kOutput, calls=%fused_computation.39 | convolution fusion | flops 741408768 | bytes 5767168 | tf_op jit(solution)/shard_map/dot_general | solution.py:53
  161.6 4.7 %all-to-all-start.5 = ((bf16[8,128,1024]{2,1,0:T(8,128)(2,1)}), bf16[8,128,1024]{2,1,0:T(8,128)(2,1)S(1)}, u32[]{:S(2)}, u32[]{:S(2)}) async-start(bf16[8,128,1024]{2,1,0:T(8,128)(2,1)} %bitcast.127), calls=%async_computation.5 | async-start | bytes 4194304 | tf_op jit(solution)/shard_map/all_to_all | solution.py:73
  166.4 29.0 %all-to-all-done.5 = bf16[8,128,1024]{2,1,0:T(8,128)(2,1)S(1)} async-done(((bf16[8,128,1024]{2,1,0:T(8,128)(2,1)}), bf16[8,128,1024]{2,1,0:T(8,128)(2,1)S(1)}, u32[]{:S(2)}, u32[]{:S(2)}) %all-to-all-start.5) | async-done | bytes 2097184 | tf_op jit(solution)/shard_map/all_to_all | solution.py:73
  201.6 3.6 %all-to-all-start.6 = ((bf16[8,128,1024]{2,1,0:T(8,128)(2,1)}), bf16[8,128,1024]{2,1,0:T(8,128)(2,1)S(1)}, u32[]{:S(2)}, u32[]{:S(2)}) async-start(bf16[8,128,1024]{2,1,0:T(8,128)(2,1)} %broadcast_in_dim.216), calls=%async_computation.6 | async-start | bytes 4194304 | tf_op jit(solution)/shard_map/all_to_all | solution.py:67
  205.6 28.6 %all-to-all-done.6 = bf16[8,128,1024]{2,1,0:T(8,128)(2,1)S(1)} async-done(((bf16[8,128,1024]{2,1,0:T(8,128)(2,1)}), bf16[8,128,1024]{2,1,0:T(8,128)(2,1)S(1)}, u32[]{:S(2)}, u32[]{:S(2)}) %all-to-all-start.6) | async-done | bytes 2097184 | tf_op jit(solution)/shard_map/all_to_all | solution.py:67
  238.1 8.8 %fusion.76 = (f32[2,1024]{1,0:T(2,128)S(1)}, f32[2,1024,1024]{1,2,0:T(8,128)}) fusion(f32[2]{0:T(128)S(1)} %get-tuple-element.10, f32[2]{0:T(128)S(1)} %get-tuple-element.9, pred[1024,1024]{0,1:T(8,128)(4,1)S(1)} %copy-done.5, pred[1024,1024]{0,1:T(8,128)(4,1)S(1)} %copy-done.7, bf16[1024,2,32]{0,2,1:T(8,128)(2,1)} %get-tuple-element.38, ...), kind=kOutput, calls=%fused_computation.176 | convolution fusion | flops 282067968 | bytes 11018256 | tf_op jit(solution)/shard_map/sub | solution.py:194
  246.9 4.2 %fusion.24 = bf16[2,64,1024]{2,1,0:T(8,128)(2,1)S(1)} fusion(bf16[1024,2,64]{0,2,1:T(8,128)(2,1)S(1)} %bitcast.138, f32[2,1024,1024]{1,2,0:T(8,128)} %get-tuple-element.55, f32[2,1024]{1,0:T(2,128)S(1)} %get-tuple-element.54), kind=kOutput, calls=%fused_computation.48 | convolution fusion | flops 272760832 | bytes 8921088 | tf_op jit(solution)/shard_map/hqk,khd->qhd/dot_general | solution.py:199
  252.1 3.7 %all-to-all-start.7 = ((bf16[8,128,128]{2,1,0:T(8,128)(2,1)}), bf16[8,128,128]{2,1,0:T(8,128)(2,1)S(1)}, u32[]{:S(2)}, u32[]{:S(2)}) async-start(bf16[8,128,128]{2,1,0:T(8,128)(2,1)} %copy.128), calls=%async_computation.7 | async-start | bytes 524288 | tf_op jit(solution)/shard_map/all_to_all | solution.py:80
  266.0 29.3 %all_to_all.62 = bf16[8,128,1024]{2,1,0:T(8,128)(2,1)S(1)} all-to-all(bf16[8,128,1024]{2,1,0:T(8,128)(2,1)S(1)} %multiply_convert_fusion), channel_id=1, replica_groups=mesh['chip'=8,'core'=2,'tp'=8] {'tp'}, dimensions={0} | all-to-all | bytes 4194304 | tf_op jit(solution)/shard_map/all_to_all | solution.py:61
  295.4 3.2 fusion.18
  298.6 4.0 %convolution_convert_fusion = bf16[1024,1024]{1,0:T(8,128)(2,1)} fusion(bf16[1024,2464]{1,0:T(8,128)(2,1)} %all-gather.5.cloned.1.call-done, f32[1024,704]{0,1:T(8,128)S(1)} %fusion.18), kind=kOutput, calls=%fused_computation.38 | convolution fusion | flops 741408768 | bytes 5767168 | tf_op jit(solution)/shard_map/dot_general | solution.py:53
  302.6 3.7 %all-to-all-start.9 = ((bf16[8,128,1024]{2,1,0:T(8,128)(2,1)}), bf16[8,128,1024]{2,1,0:T(8,128)(2,1)S(1)}, u32[]{:S(2)}, u32[]{:S(2)}) async-start(bf16[8,128,1024]{2,1,0:T(8,128)(2,1)} %bitcast.126), calls=%async_computation.9 | async-start | bytes 4194304 | tf_op jit(solution)/shard_map/all_to_all | solution.py:73
  306.4 26.0 %all-to-all-done.9 = bf16[8,128,1024]{2,1,0:T(8,128)(2,1)S(1)} async-done(((bf16[8,128,1024]{2,1,0:T(8,128)(2,1)}), bf16[8,128,1024]{2,1,0:T(8,128)(2,1)S(1)}, u32[]{:S(2)}, u32[]{:S(2)}) %all-to-all-start.9) | async-done | bytes 2097184 | tf_op jit(solution)/shard_map/all_to_all | solution.py:73
  (151 shorter events, 57.6 us)
Async XLA Ops:
  6.5 104.3 %all-gather.3.cloned.1.call-start = ((), (), s32[]{:S(2)}) async-start(), calls=%async_computation.10 | async-start | bytes 4734976 | tf_op jit(solution)/shard_map/all_gather | solution.py:123
  8.4 18.6 %copy-start.12 = (f32[2,2,1024]{2,1,0:T(2,128)S(1)}, f32[2,2,1024]{2,1,0:T(2,128)}, u32[]{:S(2)}) copy-start(f32[2,2,1024]{2,1,0:T(2,128)} %param.14) | copy-start | bytes 49156
  8.8 18.7 %copy-start.16 = (s32[128]{0:T(128)S(1)}, s32[128]{0:T(128)}, u32[]{:S(2)}) copy-start(s32[128]{0:T(128)} %param.12) | copy-start | bytes 1540
  8.8 20.2 %copy-start.9 = (f32[128,1024]{1,0:T(8,128)S(1)}, f32[128,1024]{1,0:T(8,128)}, u32[]{:S(2)}) copy-start(f32[128,1024]{1,0:T(8,128)} %param.13) | copy-start | bytes 1572868
  33.9 17.6 %all-to-all-start.2 = ((bf16[8,64,384]{2,1,0:T(8,128)(2,1)}), bf16[8,64,384]{2,1,0:T(8,128)(2,1)S(1)}, u32[]{:S(2)}, u32[]{:S(2)}) async-start(bf16[8,64,384]{2,1,0:T(8,128)(2,1)} %broadcast_in_dim.204), calls=%async_computation.2 | async-start | bytes 786432 | tf_op jit(solution)/shard_map/all_to_all | solution.py:127
  42.7 15.0 %copy-start.13 = (f32[2,16,2]{1,2,0:T(2,128)S(1)}, f32[2,16,2]{1,2,0:T(2,128)}, u32[]{:S(2)}) copy-start(f32[2,16,2]{1,2,0:T(2,128)} %param.17) | copy-start | bytes 772
  42.7 15.1 %copy-start.17 = (s32[1,4]{1,0:T(1,128)S(1)}, s32[1,4]{1,0:T(1,128)}, u32[]{:S(2)}) copy-start(s32[1,4]{1,0:T(1,128)} %param.15) | copy-start | bytes 52
  53.2 6.6 %copy-start.11 = (s32[1024]{0:T(1024)S(1)}, s32[1024]{0:T(1024)}, u32[]{:S(2)}) copy-start(s32[1024]{0:T(1024)} %param.16) | copy-start | bytes 12292
  53.2 34.2 %all-to-all-start = ((bf16[8,128,1024]{2,1,0:T(8,128)(2,1)}), bf16[8,128,1024]{2,1,0:T(8,128)(2,1)S(1)}, u32[]{:S(2)}, u32[]{:S(2)}) async-start(bf16[8,128,1024]{2,1,0:T(8,128)(2,1)} %broadcast_in_dim.202), calls=%async_computation | async-start | bytes 4194304 | tf_op jit(solution)/shard_map/all_to_all | solution.py:67
  57.6 148.0 %all-gather.5.cloned.1.call-start = ((), (), s32[]{:S(2)}) async-start(), calls=%async_computation.11 | async-start | bytes 5570560 | tf_op jit(solution)/shard_map/all_gather | solution.py:123
  59.6 2.6 collective-permute-start
  89.4 1.6 copy-start.6
  105.5 11.5 %all-to-all-start.3 = ((bf16[8,128,128]{2,1,0:T(8,128)(2,1)}), bf16[8,128,128]{2,1,0:T(8,128)(2,1)S(1)}, u32[]{:S(2)}, u32[]{:S(2)}) async-start(bf16[8,128,128]{2,1,0:T(8,128)(2,1)} %copy.119), calls=%async_computation.3 | async-start | bytes 524288 | tf_op jit(solution)/shard_map/all_to_all | solution.py:80
  120.6 33.8 %copy-start.2 = (f32[128,1024]{1,0:T(8,128)}, f32[128,1024]{1,0:T(8,128)S(1)}, u32[]{:S(2)}) copy-start(f32[128,1024]{1,0:T(8,128)S(1)} %add.234) | copy-start | bytes 1572868
  161.6 33.8 %all-to-all-start.5 = ((bf16[8,128,1024]{2,1,0:T(8,128)(2,1)}), bf16[8,128,1024]{2,1,0:T(8,128)(2,1)S(1)}, u32[]{:S(2)}, u32[]{:S(2)}) async-start(bf16[8,128,1024]{2,1,0:T(8,128)(2,1)} %bitcast.127), calls=%async_computation.5 | async-start | bytes 4194304 | tf_op jit(solution)/shard_map/all_to_all | solution.py:73
  201.6 32.5 %all-to-all-start.6 = ((bf16[8,128,1024]{2,1,0:T(8,128)(2,1)}), bf16[8,128,1024]{2,1,0:T(8,128)(2,1)S(1)}, u32[]{:S(2)}, u32[]{:S(2)}) async-start(bf16[8,128,1024]{2,1,0:T(8,128)(2,1)} %broadcast_in_dim.216), calls=%async_computation.6 | async-start | bytes 4194304 | tf_op jit(solution)/shard_map/all_to_all | solution.py:67
  236.3 1.8 copy-start.5
  236.3 1.8 copy-start.7
  238.1 8.8 %copy-start.10 = (bf16[1024,128]{0,1:T(8,128)(2,1)S(1)}, bf16[1024,128]{0,1:T(8,128)(2,1)}, u32[]{:S(2)}) copy-start(bf16[1024,128]{0,1:T(8,128)(2,1)} %slice.306) | copy-start | bytes 786436
  252.1 10.3 %all-to-all-start.7 = ((bf16[8,128,128]{2,1,0:T(8,128)(2,1)}), bf16[8,128,128]{2,1,0:T(8,128)(2,1)S(1)}, u32[]{:S(2)}, u32[]{:S(2)}) async-start(bf16[8,128,128]{2,1,0:T(8,128)(2,1)} %copy.128), calls=%async_computation.7 | async-start | bytes 524288 | tf_op jit(solution)/shard_map/all_to_all | solution.py:80
  263.9 1.5 copy-start.1
  263.9 1.5 copy-start.3
  302.6 3.7 %copy-start.15 = (s32[128]{0:T(128)S(1)}, s32[128]{0:T(128)}, u32[]{:S(2)}) copy-start(s32[128]{0:T(128)} %copy-done.14) | copy-start | bytes 1540
  302.6 29.7 %all-to-all-start.9 = ((bf16[8,128,1024]{2,1,0:T(8,128)(2,1)}), bf16[8,128,1024]{2,1,0:T(8,128)(2,1)S(1)}, u32[]{:S(2)}, u32[]{:S(2)}) async-start(bf16[8,128,1024]{2,1,0:T(8,128)(2,1)} %bitcast.126), calls=%async_computation.9 | async-start | bytes 4194304 | tf_op jit(solution)/shard_map/all_to_all | solution.py:73
  (4 other events, 3.3 us)
Sparse Core Ops, SparseCore 0:
  27.2 72.5 all-gather.2
  102.2 69.6 all-gather.4

commit v14 on v13

--- a/solution.py
+++ b/solution.py
@@ -158,20 +158,24 @@
         pair_bias = jnp.where(
             same_variate[None], layer_bias[:, 1][:, None, None], layer_bias[:, 0][:, None, None]
         )
-        normed = rms_scaled(residual, gains[layer_index][0]).astype(jnp.bfloat16)
         piece = regrouped[layer_index, :, 0, :]
         if layer_index == 0:
             qkv_weight = gather_chips(piece[:, : 3 * head_cols])
-            normed = reorder(normed, shard_of_block)
+            qkv_tokens = gather_normed(
+                reorder(residual, shard_of_block),
+                reorder(gains[layer_index][0], shard_of_block),
+                tp_count,
+            )
             layer_weights = gather_seq(piece[:, 3 * head_cols :])
         else:
+            qkv_tokens = gather_normed(residual, gains[layer_index][0], tp_count)
             layer_weights = gather_seq(piece)
             qkv_weight = layer_weights[:, : 3 * head_cols]
             layer_weights = layer_weights[:, 3 * head_cols :]
         out_weight = layer_weights[:, :model_width]
         gate_up_weight = layer_weights[:, model_width : model_width + 2 * unit_cols]
         down_weight = layer_weights[:, model_width + 2 * unit_cols :]
-        projected = project_rows(gather_tp(normed, tp_count), weight=qkv_weight)
+        projected = project_rows(qkv_tokens, weight=qkv_weight)
         queries = rotate(
             projected[:, :head_cols].reshape(token_count, local_heads, head_size), offsets
         ).astype(jnp.bfloat16)

time: 346 us -> 340 us (0.983)
  local copies, waits for them, and re-layouts: 37.2 us -> 32.4 us
where the time goes in v14:
time: 340 us; the launch traced here: 339 us
  waiting for transfers between devices  115 us (34%)
  blocking collectives  78.6 us (23%)
  matrix products  47.5 us (14%)
  starting transfers between devices  32.5 us (10%)
  local copies, waits for them, and re-layouts  32.4 us (10%)
  other arithmetic  18.2 us (5%)
  between operations  14.1 us (4%)
    all_to_all x2, blocking collectives, gather_normed(): gathered = lax.all_to_all(normed, 'tp', 0, 0, tiled=True)  62.1 us
    all_to_all x2, waiting for transfers between devices, reduce_tp(): received = lax.all_to_all(pieces, 'tp', 0, 0, tiled=True)  54.5 us
    all_to_all x2, waiting for transfers between devices, gather_normed(): gathered = lax.all_to_all(normed, 'tp', 0, 0, tiled=True)  51.2 us
    sub x2, matrix products, on_device(): weights_exp = jnp.exp(scores - row_peak)  17.9 us
    all_to_all x1, blocking collectives, on_device(): lax.all_to_all(grouped, 'tp', split_axis=2, concat_axis=1, tiled=True)  16.5 us
    slice x4, local copies, waits for them, and re-layouts, on_device(): out_weight = layer_weights[:, :model_width]  12 us
    all_to_all x2, starting transfers between devices, reduce_tp(): received = lax.all_to_all(pieces, 'tp', 0, 0, tiled=True)  8.69 us
    dot_general x2, matrix products, on_device(): jnp.einsum('hqk,khd->qhd', attn_weights, values, preferred_element_type=j...  8.63 us
  transfers between devices with their start and end apart: 10, of which 7 were waited for; matrix products, arithmetic and copies ran while one was open for 18% of the time, Pallas kernels for 0%

profile of v14, /device:TPU:0, one launch (start us, length us, event | category | flops | bytes accessed | tf_op | source)
XLA Modules:
  0.0 338.5 jit_solution(17647095323207743862)
XLA Ops:
  8.8 16.5 %all_to_all.60 = bf16[2,8,8,2464]{3,1,0,2:T(8,128)(2,1)S(1)} all-to-all(bf16[2,8,8,2464]{3,1,0,2:T(8,128)(2,1)S(1)} %concatenate.22), channel_id=1, replica_groups=mesh['chip'=8,'core'=2,'tp'=8] {'tp'}, dimensions={2} | all-to-all | bytes 1261568 | tf_op jit(solution)/shard_map/all_to_all | solution.py:113
  35.3 7.8 %all-to-all-start.2 = ((bf16[8,64,384]{2,1,0:T(8,128)(2,1)}), bf16[8,64,384]{2,1,0:T(8,128)(2,1)S(1)}, u32[]{:S(2)}, u32[]{:S(2)}) async-start(bf16[8,64,384]{2,1,0:T(8,128)(2,1)} %broadcast_in_dim.201), calls=%async_computation.2 | async-start | bytes 786432 | tf_op jit(solution)/shard_map/all_to_all | solution.py:127
  45.0 8.6 %all-to-all-done.2 = bf16[8,64,384]{2,1,0:T(8,128)(2,1)S(1)} async-done(((bf16[8,64,384]{2,1,0:T(8,128)(2,1)}), bf16[8,64,384]{2,1,0:T(8,128)(2,1)S(1)}, u32[]{:S(2)}, u32[]{:S(2)}) %all-to-all-start.2) | async-done | bytes 393248 | tf_op jit(solution)/shard_map/all_to_all | solution.py:127
  54.3 3.6 %all-to-all-start = ((bf16[8,128,1024]{2,1,0:T(8,128)(2,1)}), bf16[8,128,1024]{2,1,0:T(8,128)(2,1)S(1)}, u32[]{:S(2)}, u32[]{:S(2)}) async-start(bf16[8,128,1024]{2,1,0:T(8,128)(2,1)} %multiply_convert_fusion.3), calls=%async_computation | async-start | bytes 4194304 | tf_op jit(solution)/shard_map/all_to_all | solution.py:61
  62.5 22.9 %all-to-all-done = bf16[8,128,1024]{2,1,0:T(8,128)(2,1)S(1)} async-done(((bf16[8,128,1024]{2,1,0:T(8,128)(2,1)}), bf16[8,128,1024]{2,1,0:T(8,128)(2,1)S(1)}, u32[]{:S(2)}, u32[]{:S(2)}) %all-to-all-start) | async-done | bytes 2097184 | tf_op jit(solution)/shard_map/all_to_all | solution.py:61
  89.3 9.2 %fusion.74 = (f32[2,1024]{1,0:T(2,128)S(1)}, f32[2,1024,1024]{1,2,0:T(8,128)}) fusion(f32[2]{0:T(128)} %get-tuple-element.12, f32[2]{0:T(128)S(1)} %copy-done.13, pred[1024,1024]{0,1:T(8,128)(4,1)S(1)} %copy-done.3, pred[1024,1024]{0,1:T(8,128)(4,1)} %get-tuple-element.64, bf16[1024,2,32]{0,2,1:T(8,128)(2,1)} %get-tuple-element.42, ...), kind=kOutput, calls=%fused_computation.178 | convolution fusion | flops 282067968 | bytes 11018256 | tf_op jit(solution)/shard_map/sub | solution.py:198
  98.5 4.4 %fusion.25 = bf16[2,64,1024]{2,1,0:T(8,128)(2,1)S(1)} fusion(bf16[1024,2,64]{0,2,1:T(8,128)(2,1)S(1)} %bitcast.131, f32[2,1024,1024]{1,2,0:T(8,128)} %get-tuple-element.55, f32[2,1024]{1,0:T(2,128)S(1)} %get-tuple-element.54), kind=kOutput, calls=%fused_computation.52 | convolution fusion | flops 272760832 | bytes 8921088 | tf_op jit(solution)/shard_map/hqk,khd->qhd/dot_general | solution.py:203
  103.9 4.9 %all-to-all-start.3 = ((bf16[8,128,128]{2,1,0:T(8,128)(2,1)}), bf16[8,128,128]{2,1,0:T(8,128)(2,1)}, u32[]{:S(2)}, u32[]{:S(2)}) async-start(bf16[8,128,128]{2,1,0:T(8,128)(2,1)} %copy.119), calls=%async_computation.3 | async-start | bytes 524288 | tf_op jit(solution)/shard_map/all_to_all | solution.py:80
  109.9 3.2 slice.234
  119.7 32.8 %all_to_all.61 = bf16[8,128,1024]{2,1,0:T(8,128)(2,1)S(1)} all-to-all(bf16[8,128,1024]{2,1,0:T(8,128)(2,1)S(1)} %multiply_convert_fusion.2), channel_id=1, replica_groups=mesh['chip'=8,'core'=2,'tp'=8] {'tp'}, dimensions={0} | all-to-all | bytes 4194304 | tf_op jit(solution)/shard_map/all_to_all | solution.py:61
  152.5 3.2 fusion.20
  155.7 4.0 %convolution_convert_fusion.1 = bf16[1024,1024]{1,0:T(8,128)(2,1)} fusion(bf16[1024,2080]{1,0:T(8,128)(2,1)} %all-gather.3.cloned.1.call-done, f32[1024,704]{0,1:T(8,128)S(1)} %fusion.20), kind=kOutput, calls=%fused_computation.42 | convolution fusion | flops 741408768 | bytes 5767168 | tf_op jit(solution)/shard_map/dot_general | solution.py:53
  159.7 5.0 %all-to-all-start.5 = ((bf16[8,128,1024]{2,1,0:T(8,128)(2,1)}), bf16[8,128,1024]{2,1,0:T(8,128)(2,1)S(1)}, u32[]{:S(2)}, u32[]{:S(2)}) async-start(bf16[8,128,1024]{2,1,0:T(8,128)(2,1)} %bitcast.119), calls=%async_computation.5 | async-start | bytes 4194304 | tf_op jit(solution)/shard_map/all_to_all | solution.py:73
  164.8 28.4 %all-to-all-done.5 = bf16[8,128,1024]{2,1,0:T(8,128)(2,1)S(1)} async-done(((bf16[8,128,1024]{2,1,0:T(8,128)(2,1)}), bf16[8,128,1024]{2,1,0:T(8,128)(2,1)S(1)}, u32[]{:S(2)}, u32[]{:S(2)}) %all-to-all-start.5) | async-done | bytes 2097184 | tf_op jit(solution)/shard_map/all_to_all | solution.py:73
  198.3 3.6 %all-to-all-start.6 = ((bf16[8,128,1024]{2,1,0:T(8,128)(2,1)}), bf16[8,128,1024]{2,1,0:T(8,128)(2,1)S(1)}, u32[]{:S(2)}, u32[]{:S(2)}) async-start(bf16[8,128,1024]{2,1,0:T(8,128)(2,1)} %multiply_convert_fusion.1), calls=%async_computation.6 | async-start | bytes 4194304 | tf_op jit(solution)/shard_map/all_to_all | solution.py:61
  202.2 28.3 %all-to-all-done.6 = bf16[8,128,1024]{2,1,0:T(8,128)(2,1)S(1)} async-done(((bf16[8,128,1024]{2,1,0:T(8,128)(2,1)}), bf16[8,128,1024]{2,1,0:T(8,128)(2,1)S(1)}, u32[]{:S(2)}, u32[]{:S(2)}) %all-to-all-start.6) | async-done | bytes 2097184 | tf_op jit(solution)/shard_map/all_to_all | solution.py:61
  234.3 8.6 %fusion.75 = (f32[2,1024]{1,0:T(2,128)S(1)}, f32[2,1024,1024]{1,2,0:T(8,128)}) fusion(f32[2]{0:T(128)S(1)} %get-tuple-element.10, f32[2]{0:T(128)S(1)} %get-tuple-element.9, pred[1024,1024]{0,1:T(8,128)(4,1)S(1)} %copy-done.4, pred[1024,1024]{0,1:T(8,128)(4,1)S(1)} %copy-done.5, bf16[1024,2,32]{0,2,1:T(8,128)(2,1)} %get-tuple-element.40, ...), kind=kOutput, calls=%fused_computation.179 | convolution fusion | flops 282067968 | bytes 11018256 | tf_op jit(solution)/shard_map/sub | solution.py:198
  243.0 4.2 %fusion.24 = bf16[2,64,1024]{2,1,0:T(8,128)(2,1)S(1)} fusion(bf16[1024,2,64]{0,2,1:T(8,128)(2,1)S(1)} %bitcast.130, f32[2,1024,1024]{1,2,0:T(8,128)} %get-tuple-element.57, f32[2,1024]{1,0:T(2,128)S(1)} %get-tuple-element.56), kind=kOutput, calls=%fused_computation.51 | convolution fusion | flops 272760832 | bytes 8921088 | tf_op jit(solution)/shard_map/hqk,khd->qhd/dot_general | solution.py:203
  248.2 3.7 %all-to-all-start.7 = ((bf16[8,128,128]{2,1,0:T(8,128)(2,1)}), bf16[8,128,128]{2,1,0:T(8,128)(2,1)S(1)}, u32[]{:S(2)}, u32[]{:S(2)}) async-start(bf16[8,128,128]{2,1,0:T(8,128)(2,1)} %copy.128), calls=%async_computation.7 | async-start | bytes 524288 | tf_op jit(solution)/shard_map/all_to_all | solution.py:80
  260.9 29.3 %all_to_all.62 = bf16[8,128,1024]{2,1,0:T(8,128)(2,1)S(1)} all-to-all(bf16[8,128,1024]{2,1,0:T(8,128)(2,1)S(1)} %multiply_convert_fusion), channel_id=1, replica_groups=mesh['chip'=8,'core'=2,'tp'=8] {'tp'}, dimensions={0} | all-to-all | bytes 4194304 | tf_op jit(solution)/shard_map/all_to_all | solution.py:61
  290.1 3.2 fusion.18
  293.3 4.0 %convolution_convert_fusion = bf16[1024,1024]{1,0:T(8,128)(2,1)} fusion(bf16[1024,2464]{1,0:T(8,128)(2,1)} %all-gather.5.cloned.1.call-done, f32[1024,704]{0,1:T(8,128)S(1)} %fusion.18), kind=kOutput, calls=%fused_computation.41 | convolution fusion | flops 741408768 | bytes 5767168 | tf_op jit(solution)/shard_map/dot_general | solution.py:53
  297.3 3.7 %all-to-all-start.9 = ((bf16[8,128,1024]{2,1,0:T(8,128)(2,1)}), bf16[8,128,1024]{2,1,0:T(8,128)(2,1)S(1)}, u32[]{:S(2)}, u32[]{:S(2)}) async-start(bf16[8,128,1024]{2,1,0:T(8,128)(2,1)} %bitcast.118), calls=%async_computation.9 | async-start | bytes 4194304 | tf_op jit(solution)/shard_map/all_to_all | solution.py:73
  301.1 26.1 %all-to-all-done.9 = bf16[8,128,1024]{2,1,0:T(8,128)(2,1)S(1)} async-done(((bf16[8,128,1024]{2,1,0:T(8,128)(2,1)}), bf16[8,128,1024]{2,1,0:T(8,128)(2,1)S(1)}, u32[]{:S(2)}, u32[]{:S(2)}) %all-to-all-start.9) | async-done | bytes 2097184 | tf_op jit(solution)/shard_map/all_to_all | solution.py:73
  (148 shorter events, 55.2 us)
Async XLA Ops:
  6.5 103.4 %all-gather.3.cloned.1.call-start = ((), (), s32[]{:S(2)}) async-start(), calls=%async_computation.10 | async-start | bytes 4734976 | tf_op jit(solution)/shard_map/all_gather | solution.py:123
  7.7 19.2 %copy-start.11 = (f32[2,2,1024]{2,1,0:T(2,128)S(1)}, f32[2,2,1024]{2,1,0:T(2,128)}, u32[]{:S(2)}) copy-start(f32[2,2,1024]{2,1,0:T(2,128)} %param.14) | copy-start | bytes 49156
  8.0 19.4 %copy-start.14 = (s32[128]{0:T(128)S(1)}, s32[128]{0:T(128)}, u32[]{:S(2)}) copy-start(s32[128]{0:T(128)} %param.12) | copy-start | bytes 1540
  8.2 20.7 %copy-start.6 = (f32[128,1024]{1,0:T(8,128)S(1)}, f32[128,1024]{1,0:T(8,128)}, u32[]{:S(2)}) copy-start(f32[128,1024]{1,0:T(8,128)} %param.13) | copy-start | bytes 1572868
  35.3 22.7 %copy-start.15 = (s32[1,4]{1,0:T(1,128)S(1)}, s32[1,4]{1,0:T(1,128)}, u32[]{:S(2)}) copy-start(s32[1,4]{1,0:T(1,128)} %param.15) | copy-start | bytes 52
  35.3 22.9 %copy-start.12 = (f32[2,16,2]{1,2,0:T(2,128)S(1)}, f32[2,16,2]{1,2,0:T(2,128)}, u32[]{:S(2)}) copy-start(f32[2,16,2]{1,2,0:T(2,128)} %param.17) | copy-start | bytes 772
  35.3 18.3 %all-to-all-start.2 = ((bf16[8,64,384]{2,1,0:T(8,128)(2,1)}), bf16[8,64,384]{2,1,0:T(8,128)(2,1)S(1)}, u32[]{:S(2)}, u32[]{:S(2)}) async-start(bf16[8,64,384]{2,1,0:T(8,128)(2,1)} %broadcast_in_dim.201), calls=%async_computation.2 | async-start | bytes 786432 | tf_op jit(solution)/shard_map/all_to_all | solution.py:127
  43.1 17.0 %copy-start.10 = (s32[1024]{0:T(1024)S(1)}, s32[1024]{0:T(1024)}, u32[]{:S(2)}) copy-start(s32[1024]{0:T(1024)} %param.16) | copy-start | bytes 12292
  54.3 31.0 %all-to-all-start = ((bf16[8,128,1024]{2,1,0:T(8,128)(2,1)}), bf16[8,128,1024]{2,1,0:T(8,128)(2,1)S(1)}, u32[]{:S(2)}, u32[]{:S(2)}) async-start(bf16[8,128,1024]{2,1,0:T(8,128)(2,1)} %multiply_convert_fusion.3), calls=%async_computation | async-start | bytes 4194304 | tf_op jit(solution)/shard_map/all_to_all | solution.py:61
  57.9 144.3 %all-gather.5.cloned.1.call-start = ((), (), s32[]{:S(2)}) async-start(), calls=%async_computation.11 | async-start | bytes 5570560 | tf_op jit(solution)/shard_map/all_gather | solution.py:123
  59.8 2.6 collective-permute-start
  87.5 1.8 copy-start.3
  87.5 1.8 copy-start.13
  89.3 9.2 %copy-start.8 = (bf16[1024,128]{0,1:T(8,128)(2,1)S(1)}, bf16[1024,128]{0,1:T(8,128)(2,1)}, u32[]{:S(2)}) copy-start(bf16[1024,128]{0,1:T(8,128)(2,1)} %slice.309) | copy-start | bytes 786436
  98.5 11.3 %copy-start.9 = (f32[128,8]{1,0:T(8,128)S(1)}, f32[128,8]{1,0:T(8,128)}, u32[]{:S(2)}) copy-start(f32[128,8]{1,0:T(8,128)} %get-tuple-element.60) | copy-start | bytes 12292
  103.9 12.2 %all-to-all-start.3 = ((bf16[8,128,128]{2,1,0:T(8,128)(2,1)}), bf16[8,128,128]{2,1,0:T(8,128)(2,1)}, u32[]{:S(2)}, u32[]{:S(2)}) async-start(bf16[8,128,128]{2,1,0:T(8,128)(2,1)} %copy.119), calls=%async_computation.3 | async-start | bytes 524288 | tf_op jit(solution)/shard_map/all_to_all | solution.py:80
  118.0 34.5 %copy-start = (f32[128,1024]{0,1:T(8,128)}, f32[128,1024]{0,1:T(8,128)S(1)}, u32[]{:S(2)}) copy-start(f32[128,1024]{0,1:T(8,128)S(1)} %copy.122) | copy-start | bytes 1572868
  119.3 33.2 %copy-start.1 = (f32[128,1024]{1,0:T(8,128)}, f32[128,1024]{1,0:T(8,128)S(1)}, u32[]{:S(2)}) copy-start(f32[128,1024]{1,0:T(8,128)S(1)} %add.230) | copy-start | bytes 1572868
  159.7 33.4 %all-to-all-start.5 = ((bf16[8,128,1024]{2,1,0:T(8,128)(2,1)}), bf16[8,128,1024]{2,1,0:T(8,128)(2,1)S(1)}, u32[]{:S(2)}, u32[]{:S(2)}) async-start(bf16[8,128,1024]{2,1,0:T(8,128)(2,1)} %bitcast.119), calls=%async_computation.5 | async-start | bytes 4194304 | tf_op jit(solution)/shard_map/all_to_all | solution.py:73
  198.3 32.2 %all-to-all-start.6 = ((bf16[8,128,1024]{2,1,0:T(8,128)(2,1)}), bf16[8,128,1024]{2,1,0:T(8,128)(2,1)S(1)}, u32[]{:S(2)}, u32[]{:S(2)}) async-start(bf16[8,128,1024]{2,1,0:T(8,128)(2,1)} %multiply_convert_fusion.1), calls=%async_computation.6 | async-start | bytes 4194304 | tf_op jit(solution)/shard_map/all_to_all | solution.py:61
  232.7 1.6 copy-start.5
  248.2 10.3 %all-to-all-start.7 = ((bf16[8,128,128]{2,1,0:T(8,128)(2,1)}), bf16[8,128,128]{2,1,0:T(8,128)(2,1)S(1)}, u32[]{:S(2)}, u32[]{:S(2)}) async-start(bf16[8,128,128]{2,1,0:T(8,128)(2,1)} %copy.128), calls=%async_computation.7 | async-start | bytes 524288 | tf_op jit(solution)/shard_map/all_to_all | solution.py:80
  297.3 32.3 %copy-start.2 = (f32[128,128,8]{0,2,1:T(8,128)S(1)}, f32[128,128,8]{0,2,1:T(8,128)}, u32[]{:S(2)}) copy-start(f32[128,128,8]{0,2,1:T(8,128)} %get-tuple-element.14) | copy-start | bytes 1572868
  297.3 29.9 %all-to-all-start.9 = ((bf16[8,128,1024]{2,1,0:T(8,128)(2,1)}), bf16[8,128,1024]{2,1,0:T(8,128)(2,1)S(1)}, u32[]{:S(2)}, u32[]{:S(2)}) async-start(bf16[8,128,1024]{2,1,0:T(8,128)(2,1)} %bitcast.118), calls=%async_computation.9 | async-start | bytes 4194304 | tf_op jit(solution)/shard_map/all_to_all | solution.py:73
  (2 other events, 2.0 us)
Sparse Core Ops, SparseCore 0:
  27.0 73.6 all-gather.2
  103.2 69.0 all-gather.4

commit v15 on v14

--- a/solution.py
+++ b/solution.py
@@ -141,7 +141,7 @@
 
     inverse_order = jnp.zeros_like(shard_order).at[shard_order].set(block_index)
 
-    gains = [reorder(norm_gains[i], shard_order) for i in range(layer_count)]
+    gains = reorder(norm_gains, shard_order)
     token_count = variate_ids.shape[0]
     segment, offsets = prompt_layout(prompt_lengths[0], token_count)
     same_prompt = segment[:, None] == segment[None, :]
@@ -163,12 +163,12 @@
             qkv_weight = gather_chips(piece[:, : 3 * head_cols])
             qkv_tokens = gather_normed(
                 reorder(residual, shard_of_block),
-                reorder(gains[layer_index][0], shard_of_block),
+                reorder(gains[layer_index, 0], shard_of_block),
                 tp_count,
             )
             layer_weights = gather_seq(piece[:, 3 * head_cols :])
         else:
-            qkv_tokens = gather_normed(residual, gains[layer_index][0], tp_count)
+            qkv_tokens = gather_normed(residual, gains[layer_index, 0], tp_count)
             layer_weights = gather_seq(piece)
             qkv_weight = layer_weights[:, : 3 * head_cols]
             layer_weights = layer_weights[:, 3 * head_cols :]
@@ -207,7 +207,7 @@
         head_total = project_owned(mixed_heads, out_weight, tp_count)
         residual = residual + head_total
         hidden = gated_units(
-            gather_normed(residual, gains[layer_index][1], tp_count), weight=gate_up_weight
+            gather_normed(residual, gains[layer_index, 1], tp_count), weight=gate_up_weight
         )
         unit_total = reduce_tp(
             project_out(source=hidden, weight=down_weight).astype(jnp.bfloat16), tp_count

time: 340 us -> 330 us (0.971)
  blocking collectives: 78.6 us -> 108 us
  waiting for transfers between devices: 115 us -> 87.1 us
  starting transfers between devices: 32.5 us -> 26.9 us
    all_to_all x0 -> x1, blocking collectives: none -> 29.5 us  [reduce_tp(): received = lax.all_to_all(pieces, 'tp', 0, 0, tiled=True)]
    all_to_all x2 -> x1, waiting for transfers between devices: 54.5 us -> 25.6 us  [reduce_tp(): received = lax.all_to_all(pieces, 'tp', 0, 0, tiled=True)]
    all_to_all x2 -> x1, starting transfers between devices: 8.69 us -> 3.73 us  [reduce_tp(): received = lax.all_to_all(pieces, 'tp', 0, 0, tiled=True)]
  transfers between devices with their start and end apart: 10 -> 9, of which waited for: 7 -> 6; matrix products, arithmetic and copies ran while one was open for 18% -> 17% of each run, Pallas kernels for 0% -> 0%
where the time goes in v15:
time: 330 us; the launch traced here: 329 us
  blocking collectives  108 us (33%)
  waiting for transfers between devices  87.1 us (26%)
  matrix products  46 us (14%)
  local copies, waits for them, and re-layouts  30.7 us (9%)
  starting transfers between devices  26.9 us (8%)
  other arithmetic  16.2 us (5%)
  between operations  14.1 us (4%)
    all_to_all x2, blocking collectives, gather_normed(): gathered = lax.all_to_all(normed, 'tp', 0, 0, tiled=True)  61.8 us
    all_to_all x2, waiting for transfers between devices, gather_normed(): gathered = lax.all_to_all(normed, 'tp', 0, 0, tiled=True)  52 us
    all_to_all x1, blocking collectives, reduce_tp(): received = lax.all_to_all(pieces, 'tp', 0, 0, tiled=True)  29.5 us
    all_to_all x1, waiting for transfers between devices, reduce_tp(): received = lax.all_to_all(pieces, 'tp', 0, 0, tiled=True)  25.6 us
    sub x2, matrix products, on_device(): weights_exp = jnp.exp(scores - row_peak)  17.7 us
    all_to_all x1, blocking collectives, on_device(): lax.all_to_all(grouped, 'tp', split_axis=2, concat_axis=1, tiled=True)  16.5 us
    slice x4, local copies, waits for them, and re-layouts, on_device(): out_weight = layer_weights[:, :model_width]  12 us
    dot_general x2, matrix products, on_device(): jnp.einsum('hqk,khd->qhd', attn_weights, values, preferred_element_type=j...  8.46 us
  transfers between devices with their start and end apart: 9, of which 6 were waited for; matrix products, arithmetic and copies ran while one was open for 17% of the time, Pallas kernels for 0%

profile of v15, /device:TPU:0, one launch (start us, length us, event | category | flops | bytes accessed | tf_op | source)
XLA Modules:
  0.0 328.9 jit_solution(17026155204087439890)
XLA Ops:
  8.8 16.5 %all_to_all.60 = bf16[2,8,8,2464]{3,1,0,2:T(8,128)(2,1)S(1)} all-to-all(bf16[2,8,8,2464]{3,1,0,2:T(8,128)(2,1)S(1)} %concatenate.22), channel_id=1, replica_groups=mesh['chip'=8,'core'=2,'tp'=8] {'tp'}, dimensions={2} | all-to-all | bytes 1261568 | tf_op jit(solution)/shard_map/all_to_all | solution.py:113
  34.4 7.8 %all-to-all-start.2 = ((bf16[8,64,384]{2,1,0:T(8,128)(2,1)}), bf16[8,64,384]{2,1,0:T(8,128)(2,1)S(1)}, u32[]{:S(2)}, u32[]{:S(2)}) async-start(bf16[8,64,384]{2,1,0:T(8,128)(2,1)} %broadcast_in_dim.211), calls=%async_computation.2 | async-start | bytes 786432 | tf_op jit(solution)/shard_map/all_to_all | solution.py:127
  44.0 8.3 %all-to-all-done.2 = bf16[8,64,384]{2,1,0:T(8,128)(2,1)S(1)} async-done(((bf16[8,64,384]{2,1,0:T(8,128)(2,1)}), bf16[8,64,384]{2,1,0:T(8,128)(2,1)S(1)}, u32[]{:S(2)}, u32[]{:S(2)}) %all-to-all-start.2) | async-done | bytes 393248 | tf_op jit(solution)/shard_map/all_to_all | solution.py:127
  53.1 3.6 %all-to-all-start = ((bf16[8,128,1024]{2,1,0:T(8,128)(2,1)}), bf16[8,128,1024]{2,1,0:T(8,128)(2,1)S(1)}, u32[]{:S(2)}, u32[]{:S(2)}) async-start(bf16[8,128,1024]{2,1,0:T(8,128)(2,1)} %multiply_convert_fusion.3), calls=%async_computation | async-start | bytes 4194304 | tf_op jit(solution)/shard_map/all_to_all | solution.py:61
  61.3 24.9 %all-to-all-done = bf16[8,128,1024]{2,1,0:T(8,128)(2,1)S(1)} async-done(((bf16[8,128,1024]{2,1,0:T(8,128)(2,1)}), bf16[8,128,1024]{2,1,0:T(8,128)(2,1)S(1)}, u32[]{:S(2)}, u32[]{:S(2)}) %all-to-all-start) | async-done | bytes 2097184 | tf_op jit(solution)/shard_map/all_to_all | solution.py:61
  90.0 9.1 %fusion.73 = (f32[2,1024]{1,0:T(2,128)S(1)}, f32[2,1024,1024]{1,2,0:T(8,128)}) fusion(f32[2]{0:T(128)} %get-tuple-element.9, f32[2]{0:T(128)} %get-tuple-element.8, pred[1024,1024]{0,1:T(8,128)(4,1)S(1)} %copy-done.1, pred[1024,1024]{0,1:T(8,128)(4,1)} %get-tuple-element.57, bf16[1024,2,32]{0,2,1:T(8,128)(2,1)} %get-tuple-element.39, ...), kind=kOutput, calls=%fused_computation.173 | convolution fusion | flops 282067968 | bytes 11018256 | tf_op jit(solution)/shard_map/sub | solution.py:198
  99.2 4.2 %fusion.25 = bf16[2,64,1024]{2,1,0:T(8,128)(2,1)S(1)} fusion(bf16[1024,2,64]{0,2,1:T(8,128)(2,1)S(1)} %bitcast.132, f32[2,1024,1024]{1,2,0:T(8,128)} %get-tuple-element.50, f32[2,1024]{1,0:T(2,128)S(1)} %get-tuple-element.49), kind=kOutput, calls=%fused_computation.51 | convolution fusion | flops 272760832 | bytes 8921088 | tf_op jit(solution)/shard_map/hqk,khd->qhd/dot_general | solution.py:203
  104.4 4.2 %all-to-all-start.3 = ((bf16[8,128,128]{2,1,0:T(8,128)(2,1)}), bf16[8,128,128]{2,1,0:T(8,128)(2,1)}, u32[]{:S(2)}, u32[]{:S(2)}) async-start(bf16[8,128,128]{2,1,0:T(8,128)(2,1)} %copy.120), calls=%async_computation.3 | async-start | bytes 524288 | tf_op jit(solution)/shard_map/all_to_all | solution.py:80
  109.6 3.1 slice.220
  112.7 2.9 copy.121
  119.3 32.8 %all_to_all.61 = bf16[8,128,1024]{2,1,0:T(8,128)(2,1)S(1)} all-to-all(bf16[8,128,1024]{2,1,0:T(8,128)(2,1)S(1)} %multiply_convert_fusion.2), channel_id=1, replica_groups=mesh['chip'=8,'core'=2,'tp'=8] {'tp'}, dimensions={0} | all-to-all | bytes 4194304 | tf_op jit(solution)/shard_map/all_to_all | solution.py:61
  152.2 3.2 fusion.20
  158.1 29.5 %all_to_all.62 = bf16[8,128,1024]{2,1,0:T(8,128)(2,1)S(1)} all-to-all(bf16[8,128,1024]{2,1,0:T(8,128)(2,1)S(1)} %bitcast.119), channel_id=1, replica_groups=mesh['chip'=8,'core'=2,'tp'=8] {'tp'}, dimensions={0} | all-to-all | bytes 4194304 | tf_op jit(solution)/shard_map/all_to_all | solution.py:73
  190.7 3.6 %all-to-all-start.6 = ((bf16[8,128,1024]{2,1,0:T(8,128)(2,1)}), bf16[8,128,1024]{2,1,0:T(8,128)(2,1)S(1)}, u32[]{:S(2)}, u32[]{:S(2)}) async-start(bf16[8,128,1024]{2,1,0:T(8,128)(2,1)} %multiply_convert_fusion.1), calls=%async_computation.6 | async-start | bytes 4194304 | tf_op jit(solution)/shard_map/all_to_all | solution.py:61
  194.7 27.2 %all-to-all-done.6 = bf16[8,128,1024]{2,1,0:T(8,128)(2,1)S(1)} async-done(((bf16[8,128,1024]{2,1,0:T(8,128)(2,1)}), bf16[8,128,1024]{2,1,0:T(8,128)(2,1)S(1)}, u32[]{:S(2)}, u32[]{:S(2)}) %all-to-all-start.6) | async-done | bytes 2097184 | tf_op jit(solution)/shard_map/all_to_all | solution.py:61
  225.6 8.6 %fusion.74 = (f32[2,1024]{1,0:T(2,128)S(1)}, f32[2,1024,1024]{1,2,0:T(8,128)}) fusion(f32[2]{0:T(128)S(1)} %get-tuple-element.7, f32[2]{0:T(128)S(1)} %get-tuple-element.6, pred[1024,1024]{0,1:T(8,128)(4,1)S(1)} %copy-done.2, pred[1024,1024]{0,1:T(8,128)(4,1)S(1)} %copy-done.3, bf16[1024,2,32]{0,2,1:T(8,128)(2,1)S(1)} %get-tuple-element.37, ...), kind=kOutput, calls=%fused_computation.174 | convolution fusion | flops 282067968 | bytes 11018256 | tf_op jit(solution)/shard_map/sub | solution.py:198
  234.1 4.2 %fusion.24 = bf16[2,64,1024]{2,1,0:T(8,128)(2,1)S(1)} fusion(bf16[1024,2,64]{0,2,1:T(8,128)(2,1)S(1)} %bitcast.131, f32[2,1024,1024]{1,2,0:T(8,128)} %get-tuple-element.52, f32[2,1024]{1,0:T(2,128)S(1)} %get-tuple-element.51), kind=kOutput, calls=%fused_computation.50 | convolution fusion | flops 272760832 | bytes 8921088 | tf_op jit(solution)/shard_map/hqk,khd->qhd/dot_general | solution.py:203
  239.4 3.7 %all-to-all-start.7 = ((bf16[8,128,128]{2,1,0:T(8,128)(2,1)}), bf16[8,128,128]{2,1,0:T(8,128)(2,1)S(1)}, u32[]{:S(2)}, u32[]{:S(2)}) async-start(bf16[8,128,128]{2,1,0:T(8,128)(2,1)} %copy.128), calls=%async_computation.7 | async-start | bytes 524288 | tf_op jit(solution)/shard_map/all_to_all | solution.py:80
  243.0 3.1 slice.236
  252.0 28.9 %all_to_all.63 = bf16[8,128,1024]{2,1,0:T(8,128)(2,1)S(1)} all-to-all(bf16[8,128,1024]{2,1,0:T(8,128)(2,1)S(1)} %multiply_convert_fusion), channel_id=1, replica_groups=mesh['chip'=8,'core'=2,'tp'=8] {'tp'}, dimensions={0} | all-to-all | bytes 4194304 | tf_op jit(solution)/shard_map/all_to_all | solution.py:61
  280.9 3.2 fusion.18
  284.1 4.0 %convolution_convert_fusion = bf16[1024,1024]{1,0:T(8,128)(2,1)} fusion(bf16[1024,2464]{1,0:T(8,128)(2,1)} %all-gather.5.cloned.1.call-done, f32[1024,704]{0,1:T(8,128)S(1)} %fusion.18), kind=kOutput, calls=%fused_computation.40 | convolution fusion | flops 741408768 | bytes 5767168 | tf_op jit(solution)/shard_map/dot_general | solution.py:53
  288.2 3.7 %all-to-all-start.9 = ((bf16[8,128,1024]{2,1,0:T(8,128)(2,1)}), bf16[8,128,1024]{2,1,0:T(8,128)(2,1)S(1)}, u32[]{:S(2)}, u32[]{:S(2)}) async-start(bf16[8,128,1024]{2,1,0:T(8,128)(2,1)} %bitcast.118), calls=%async_computation.9 | async-start | bytes 4194304 | tf_op jit(solution)/shard_map/all_to_all | solution.py:73
  291.9 25.6 %all-to-all-done.9 = bf16[8,128,1024]{2,1,0:T(8,128)(2,1)S(1)} async-done(((bf16[8,128,1024]{2,1,0:T(8,128)(2,1)}), bf16[8,128,1024]{2,1,0:T(8,128)(2,1)S(1)}, u32[]{:S(2)}, u32[]{:S(2)}) %all-to-all-start.9) | async-done | bytes 2097184 | tf_op jit(solution)/shard_map/all_to_all | solution.py:73
  (143 shorter events, 48.6 us)
Async XLA Ops:
  6.5 103.0 %all-gather.3.cloned.1.call-start = ((), (), s32[]{:S(2)}) async-start(), calls=%async_computation.10 | async-start | bytes 4734976 | tf_op jit(solution)/shard_map/all_gather | solution.py:123
  7.7 19.2 %copy-start.4 = (f32[128,1024]{1,0:T(8,128)S(1)}, f32[128,1024]{1,0:T(8,128)}, u32[]{:S(2)}) copy-start(f32[128,1024]{1,0:T(8,128)} %param.11) | copy-start | bytes 1572868
  8.0 19.1 %copy-start.8 = (f32[2,2,1024]{2,1,0:T(2,128)S(1)}, f32[2,2,1024]{2,1,0:T(2,128)}, u32[]{:S(2)}) copy-start(f32[2,2,1024]{2,1,0:T(2,128)} %param.12) | copy-start | bytes 49156
  8.4 19.1 %copy-start.13 = (s32[128]{0:T(128)S(1)}, s32[128]{0:T(128)}, u32[]{:S(2)}) copy-start(s32[128]{0:T(128)} %param.10) | copy-start | bytes 1540
  30.8 1.6 copy-start.11
  34.4 22.4 %copy-start.14 = (s32[1,4]{1,0:T(1,128)S(1)}, s32[1,4]{1,0:T(1,128)}, u32[]{:S(2)}) copy-start(s32[1,4]{1,0:T(1,128)} %param.13) | copy-start | bytes 52
  34.4 22.6 %copy-start.10 = (f32[2,16,2]{1,2,0:T(2,128)S(1)}, f32[2,16,2]{1,2,0:T(2,128)}, u32[]{:S(2)}) copy-start(f32[2,16,2]{1,2,0:T(2,128)} %param.15) | copy-start | bytes 772
  34.4 18.0 %all-to-all-start.2 = ((bf16[8,64,384]{2,1,0:T(8,128)(2,1)}), bf16[8,64,384]{2,1,0:T(8,128)(2,1)S(1)}, u32[]{:S(2)}, u32[]{:S(2)}) async-start(bf16[8,64,384]{2,1,0:T(8,128)(2,1)} %broadcast_in_dim.211), calls=%async_computation.2 | async-start | bytes 786432 | tf_op jit(solution)/shard_map/all_to_all | solution.py:127
  42.2 16.8 %copy-start.7 = (s32[1024]{0:T(1024)S(1)}, s32[1024]{0:T(1024)}, u32[]{:S(2)}) copy-start(s32[1024]{0:T(1024)} %param.14) | copy-start | bytes 12292
  52.4 0.7 copy-start.5
  53.1 33.0 %all-to-all-start = ((bf16[8,128,1024]{2,1,0:T(8,128)(2,1)}), bf16[8,128,1024]{2,1,0:T(8,128)(2,1)S(1)}, u32[]{:S(2)}, u32[]{:S(2)}) async-start(bf16[8,128,1024]{2,1,0:T(8,128)(2,1)} %multiply_convert_fusion.3), calls=%async_computation | async-start | bytes 4194304 | tf_op jit(solution)/shard_map/all_to_all | solution.py:61
  56.7 137.9 %all-gather.5.cloned.1.call-start = ((), (), s32[]{:S(2)}) async-start(), calls=%async_computation.11 | async-start | bytes 5570560 | tf_op jit(solution)/shard_map/all_gather | solution.py:123
  58.7 2.6 collective-permute-start
  88.3 1.7 copy-start.1
  90.0 9.1 %copy-start.6 = (bf16[1024,128]{0,1:T(8,128)(2,1)S(1)}, bf16[1024,128]{0,1:T(8,128)(2,1)}, u32[]{:S(2)}) copy-start(bf16[1024,128]{0,1:T(8,128)(2,1)} %slice.293) | copy-start | bytes 786436
  104.4 11.6 %all-to-all-start.3 = ((bf16[8,128,128]{2,1,0:T(8,128)(2,1)}), bf16[8,128,128]{2,1,0:T(8,128)(2,1)}, u32[]{:S(2)}, u32[]{:S(2)}) async-start(bf16[8,128,128]{2,1,0:T(8,128)(2,1)} %copy.120), calls=%async_computation.3 | async-start | bytes 524288 | tf_op jit(solution)/shard_map/all_to_all | solution.py:80
  190.7 31.1 %all-to-all-start.6 = ((bf16[8,128,1024]{2,1,0:T(8,128)(2,1)}), bf16[8,128,1024]{2,1,0:T(8,128)(2,1)S(1)}, u32[]{:S(2)}, u32[]{:S(2)}) async-start(bf16[8,128,1024]{2,1,0:T(8,128)(2,1)} %multiply_convert_fusion.1), calls=%async_computation.6 | async-start | bytes 4194304 | tf_op jit(solution)/shard_map/all_to_all | solution.py:61
  224.0 1.2 copy-start.2
  224.0 1.6 copy-start.3
  239.4 10.3 %all-to-all-start.7 = ((bf16[8,128,128]{2,1,0:T(8,128)(2,1)}), bf16[8,128,128]{2,1,0:T(8,128)(2,1)S(1)}, u32[]{:S(2)}, u32[]{:S(2)}) async-start(bf16[8,128,128]{2,1,0:T(8,128)(2,1)} %copy.128), calls=%async_computation.7 | async-start | bytes 524288 | tf_op jit(solution)/shard_map/all_to_all | solution.py:80
  288.2 3.7 %copy-start.12 = (s32[128]{0:T(128)S(1)}, s32[128]{0:T(128)}, u32[]{:S(2)}) copy-start(s32[128]{0:T(128)} %copy-done.11) | copy-start | bytes 1540
  288.2 31.8 %copy-start = (f32[128,128,8]{0,2,1:T(8,128)S(1)}, f32[128,128,8]{0,2,1:T(8,128)}, u32[]{:S(2)}) copy-start(f32[128,128,8]{0,2,1:T(8,128)} %get-tuple-element.11) | copy-start | bytes 1572868
  288.2 29.4 %all-to-all-start.9 = ((bf16[8,128,1024]{2,1,0:T(8,128)(2,1)}), bf16[8,128,1024]{2,1,0:T(8,128)(2,1)S(1)}, u32[]{:S(2)}, u32[]{:S(2)}) async-start(bf16[8,128,1024]{2,1,0:T(8,128)(2,1)} %bitcast.118), calls=%async_computation.9 | async-start | bytes 4194304 | tf_op jit(solution)/shard_map/all_to_all | solution.py:73
  320.0 0.8 copy-start.9
Sparse Core Ops, SparseCore 0:
  27.0 72.3 all-gather.2
  101.9 68.8 all-gather.4

commit v16 on v15

--- a/solution.py
+++ b/solution.py
@@ -139,7 +139,9 @@
         blocks = values.reshape(values.shape[:-1] + (block_count, block_rows))
         return jnp.take(blocks, order, axis=-2).reshape(values.shape)
 
-    inverse_order = jnp.zeros_like(shard_order).at[shard_order].set(block_index)
+    inverse_order = jnp.sum(
+        jnp.where(shard_order[None, :] == block_index[:, None], block_index[None, :], 0), axis=1
+    ).astype(shard_order.dtype)
 
     gains = reorder(norm_gains, shard_order)
     token_count = variate_ids.shape[0]

time: 330 us -> 331 us (level)
  no operation moved by 1% of the time
where the time goes in v16:
time: 331 us; the launch traced here: 329 us
  blocking collectives  108 us (33%)
  waiting for transfers between devices  87.6 us (26%)
  matrix products  45.9 us (14%)
  local copies, waits for them, and re-layouts  29.8 us (9%)
  starting transfers between devices  27.5 us (8%)
  other arithmetic  16.4 us (5%)
  between operations  14.1 us (4%)
    all_to_all x2, blocking collectives, gather_normed(): gathered = lax.all_to_all(normed, 'tp', 0, 0, tiled=True)  61.8 us
    all_to_all x2, waiting for transfers between devices, gather_normed(): gathered = lax.all_to_all(normed, 'tp', 0, 0, tiled=True)  52.5 us
    all_to_all x1, blocking collectives, reduce_tp(): received = lax.all_to_all(pieces, 'tp', 0, 0, tiled=True)  29.6 us
    all_to_all x1, waiting for transfers between devices, reduce_tp(): received = lax.all_to_all(pieces, 'tp', 0, 0, tiled=True)  25.6 us
    sub x2, matrix products, on_device(): weights_exp = jnp.exp(scores - row_peak)  17.7 us
    all_to_all x1, blocking collectives, on_device(): lax.all_to_all(grouped, 'tp', split_axis=2, concat_axis=1, tiled=True)  16.5 us
    slice x4, local copies, waits for them, and re-layouts, on_device(): out_weight = layer_weights[:, :model_width]  12 us
    dot_general x2, matrix products, on_device(): jnp.einsum('hqk,khd->qhd', attn_weights, values, preferred_element_type=j...  8.46 us
  transfers between devices with their start and end apart: 9, of which 6 were waited for; matrix products, arithmetic and copies ran while one was open for 17% of the time, Pallas kernels for 0%

profile of v16, /device:TPU:0, one launch (start us, length us, event | category | flops | bytes accessed | tf_op | source)
XLA Modules:
  0.0 329.0 jit_solution(12496902626509922111)
XLA Ops:
  8.8 16.5 %all_to_all.60 = bf16[2,8,8,2464]{3,1,0,2:T(8,128)(2,1)S(1)} all-to-all(bf16[2,8,8,2464]{3,1,0,2:T(8,128)(2,1)S(1)} %concatenate.22), channel_id=1, replica_groups=mesh['chip'=8,'core'=2,'tp'=8] {'tp'}, dimensions={2} | all-to-all | bytes 1261568 | tf_op jit(solution)/shard_map/all_to_all | solution.py:113
  33.5 7.8 %all-to-all-start.2 = ((bf16[8,64,384]{2,1,0:T(8,128)(2,1)}), bf16[8,64,384]{2,1,0:T(8,128)(2,1)S(1)}, u32[]{:S(2)}, u32[]{:S(2)}) async-start(bf16[8,64,384]{2,1,0:T(8,128)(2,1)} %broadcast_in_dim.225), calls=%async_computation.2 | async-start | bytes 786432 | tf_op jit(solution)/shard_map/all_to_all | solution.py:127
  43.1 8.3 %all-to-all-done.2 = bf16[8,64,384]{2,1,0:T(8,128)(2,1)S(1)} async-done(((bf16[8,64,384]{2,1,0:T(8,128)(2,1)}), bf16[8,64,384]{2,1,0:T(8,128)(2,1)S(1)}, u32[]{:S(2)}, u32[]{:S(2)}) %all-to-all-start.2) | async-done | bytes 393248 | tf_op jit(solution)/shard_map/all_to_all | solution.py:127
  52.2 4.2 %all-to-all-start = ((bf16[8,128,1024]{2,1,0:T(8,128)(2,1)}), bf16[8,128,1024]{2,1,0:T(8,128)(2,1)S(1)}, u32[]{:S(2)}, u32[]{:S(2)}) async-start(bf16[8,128,1024]{2,1,0:T(8,128)(2,1)} %multiply_convert_fusion.3), calls=%async_computation | async-start | bytes 4194304 | tf_op jit(solution)/shard_map/all_to_all | solution.py:61
  61.0 25.3 %all-to-all-done = bf16[8,128,1024]{2,1,0:T(8,128)(2,1)S(1)} async-done(((bf16[8,128,1024]{2,1,0:T(8,128)(2,1)}), bf16[8,128,1024]{2,1,0:T(8,128)(2,1)S(1)}, u32[]{:S(2)}, u32[]{:S(2)}) %all-to-all-start) | async-done | bytes 2097184 | tf_op jit(solution)/shard_map/all_to_all | solution.py:61
  90.1 9.1 %fusion.71 = (f32[2,1024]{1,0:T(2,128)S(1)}, f32[2,1024,1024]{1,2,0:T(8,128)}) fusion(f32[2]{0:T(128)} %get-tuple-element.9, f32[2]{0:T(128)} %get-tuple-element.8, pred[1024,1024]{0,1:T(8,128)(4,1)S(1)} %copy-done.1, pred[1024,1024]{0,1:T(8,128)(4,1)} %get-tuple-element.57, bf16[1024,2,32]{0,2,1:T(8,128)(2,1)} %get-tuple-element.39, ...), kind=kOutput, calls=%fused_computation.172 | convolution fusion | flops 282067968 | bytes 11018256 | tf_op jit(solution)/shard_map/sub | solution.py:200
  99.2 4.2 %fusion.25 = bf16[2,64,1024]{2,1,0:T(8,128)(2,1)S(1)} fusion(bf16[1024,2,64]{0,2,1:T(8,128)(2,1)S(1)} %bitcast.132, f32[2,1024,1024]{1,2,0:T(8,128)} %get-tuple-element.50, f32[2,1024]{1,0:T(2,128)S(1)} %get-tuple-element.49), kind=kOutput, calls=%fused_computation.50 | convolution fusion | flops 272760832 | bytes 8921088 | tf_op jit(solution)/shard_map/hqk,khd->qhd/dot_general | solution.py:205
  104.4 4.1 %all-to-all-start.3 = ((bf16[8,128,128]{2,1,0:T(8,128)(2,1)}), bf16[8,128,128]{2,1,0:T(8,128)(2,1)}, u32[]{:S(2)}, u32[]{:S(2)}) async-start(bf16[8,128,128]{2,1,0:T(8,128)(2,1)} %copy.120), calls=%async_computation.3 | async-start | bytes 524288 | tf_op jit(solution)/shard_map/all_to_all | solution.py:80
  109.5 3.1 slice.220
  112.7 2.9 copy.121
  119.3 32.8 %all_to_all.61 = bf16[8,128,1024]{2,1,0:T(8,128)(2,1)S(1)} all-to-all(bf16[8,128,1024]{2,1,0:T(8,128)(2,1)S(1)} %multiply_convert_fusion.2), channel_id=1, replica_groups=mesh['chip'=8,'core'=2,'tp'=8] {'tp'}, dimensions={0} | all-to-all | bytes 4194304 | tf_op jit(solution)/shard_map/all_to_all | solution.py:61
  152.2 3.2 fusion.20
  158.0 29.6 %all_to_all.62 = bf16[8,128,1024]{2,1,0:T(8,128)(2,1)S(1)} all-to-all(bf16[8,128,1024]{2,1,0:T(8,128)(2,1)S(1)} %bitcast.119), channel_id=1, replica_groups=mesh['chip'=8,'core'=2,'tp'=8] {'tp'}, dimensions={0} | all-to-all | bytes 4194304 | tf_op jit(solution)/shard_map/all_to_all | solution.py:73
  190.7 3.6 %all-to-all-start.6 = ((bf16[8,128,1024]{2,1,0:T(8,128)(2,1)}), bf16[8,128,1024]{2,1,0:T(8,128)(2,1)S(1)}, u32[]{:S(2)}, u32[]{:S(2)}) async-start(bf16[8,128,1024]{2,1,0:T(8,128)(2,1)} %multiply_convert_fusion.1), calls=%async_computation.6 | async-start | bytes 4194304 | tf_op jit(solution)/shard_map/all_to_all | solution.py:61
  194.7 27.3 %all-to-all-done.6 = bf16[8,128,1024]{2,1,0:T(8,128)(2,1)S(1)} async-done(((bf16[8,128,1024]{2,1,0:T(8,128)(2,1)}), bf16[8,128,1024]{2,1,0:T(8,128)(2,1)S(1)}, u32[]{:S(2)}, u32[]{:S(2)}) %all-to-all-start.6) | async-done | bytes 2097184 | tf_op jit(solution)/shard_map/all_to_all | solution.py:61
  225.7 8.6 %fusion.72 = (f32[2,1024]{1,0:T(2,128)S(1)}, f32[2,1024,1024]{1,2,0:T(8,128)}) fusion(f32[2]{0:T(128)S(1)} %get-tuple-element.7, f32[2]{0:T(128)S(1)} %get-tuple-element.6, pred[1024,1024]{0,1:T(8,128)(4,1)S(1)} %copy-done.2, pred[1024,1024]{0,1:T(8,128)(4,1)S(1)} %copy-done.3, bf16[1024,2,32]{0,2,1:T(8,128)(2,1)S(1)} %get-tuple-element.37, ...), kind=kOutput, calls=%fused_computation.173 | convolution fusion | flops 282067968 | bytes 11018256 | tf_op jit(solution)/shard_map/sub | solution.py:200
  234.3 4.2 %fusion.24 = bf16[2,64,1024]{2,1,0:T(8,128)(2,1)S(1)} fusion(bf16[1024,2,64]{0,2,1:T(8,128)(2,1)S(1)} %bitcast.131, f32[2,1024,1024]{1,2,0:T(8,128)} %get-tuple-element.52, f32[2,1024]{1,0:T(2,128)S(1)} %get-tuple-element.51), kind=kOutput, calls=%fused_computation.49 | convolution fusion | flops 272760832 | bytes 8921088 | tf_op jit(solution)/shard_map/hqk,khd->qhd/dot_general | solution.py:205
  239.5 3.7 %all-to-all-start.7 = ((bf16[8,128,128]{2,1,0:T(8,128)(2,1)}), bf16[8,128,128]{2,1,0:T(8,128)(2,1)S(1)}, u32[]{:S(2)}, u32[]{:S(2)}) async-start(bf16[8,128,128]{2,1,0:T(8,128)(2,1)} %copy.128), calls=%async_computation.7 | async-start | bytes 524288 | tf_op jit(solution)/shard_map/all_to_all | solution.py:80
  243.2 3.1 slice.236
  252.2 28.9 %all_to_all.63 = bf16[8,128,1024]{2,1,0:T(8,128)(2,1)S(1)} all-to-all(bf16[8,128,1024]{2,1,0:T(8,128)(2,1)S(1)} %multiply_convert_fusion), channel_id=1, replica_groups=mesh['chip'=8,'core'=2,'tp'=8] {'tp'}, dimensions={0} | all-to-all | bytes 4194304 | tf_op jit(solution)/shard_map/all_to_all | solution.py:61
  281.1 3.2 fusion.18
  284.2 4.0 %convolution_convert_fusion = bf16[1024,1024]{1,0:T(8,128)(2,1)} fusion(bf16[1024,2464]{1,0:T(8,128)(2,1)} %all-gather.5.cloned.1.call-done, f32[1024,704]{0,1:T(8,128)S(1)} %fusion.18), kind=kOutput, calls=%fused_computation.39 | convolution fusion | flops 741408768 | bytes 5767168 | tf_op jit(solution)/shard_map/dot_general | solution.py:53
  288.3 3.7 %all-to-all-start.9 = ((bf16[8,128,1024]{2,1,0:T(8,128)(2,1)}), bf16[8,128,1024]{2,1,0:T(8,128)(2,1)S(1)}, u32[]{:S(2)}, u32[]{:S(2)}) async-start(bf16[8,128,1024]{2,1,0:T(8,128)(2,1)} %bitcast.118), calls=%async_computation.9 | async-start | bytes 4194304 | tf_op jit(solution)/shard_map/all_to_all | solution.py:73
  292.1 25.6 %all-to-all-done.9 = bf16[8,128,1024]{2,1,0:T(8,128)(2,1)S(1)} async-done(((bf16[8,128,1024]{2,1,0:T(8,128)(2,1)}), bf16[8,128,1024]{2,1,0:T(8,128)(2,1)S(1)}, u32[]{:S(2)}, u32[]{:S(2)}) %all-to-all-start.9) | async-done | bytes 2097184 | tf_op jit(solution)/shard_map/all_to_all | solution.py:73
  (142 shorter events, 47.7 us)
Async XLA Ops:
  6.5 103.0 %all-gather.3.cloned.1.call-start = ((), (), s32[]{:S(2)}) async-start(), calls=%async_computation.10 | async-start | bytes 4734976 | tf_op jit(solution)/shard_map/all_gather | solution.py:123
  7.7 19.2 %copy-start.4 = (f32[128,1024]{1,0:T(8,128)S(1)}, f32[128,1024]{1,0:T(8,128)}, u32[]{:S(2)}) copy-start(f32[128,1024]{1,0:T(8,128)} %param.11) | copy-start | bytes 1572868
  8.0 19.1 %copy-start.8 = (f32[2,2,1024]{2,1,0:T(2,128)S(1)}, f32[2,2,1024]{2,1,0:T(2,128)}, u32[]{:S(2)}) copy-start(f32[2,2,1024]{2,1,0:T(2,128)} %param.12) | copy-start | bytes 49156
  8.4 19.1 %copy-start.13 = (s32[128]{0:T(128)S(1)}, s32[128]{0:T(128)}, u32[]{:S(2)}) copy-start(s32[128]{0:T(128)} %param.10) | copy-start | bytes 1540
  29.9 0.6 copy-start.11
  33.5 23.0 %copy-start.14 = (s32[1,4]{1,0:T(1,128)S(1)}, s32[1,4]{1,0:T(1,128)}, u32[]{:S(2)}) copy-start(s32[1,4]{1,0:T(1,128)} %param.13) | copy-start | bytes 52
  33.5 23.2 %copy-start.10 = (f32[2,16,2]{1,2,0:T(2,128)S(1)}, f32[2,16,2]{1,2,0:T(2,128)}, u32[]{:S(2)}) copy-start(f32[2,16,2]{1,2,0:T(2,128)} %param.15) | copy-start | bytes 772
  33.5 18.0 %all-to-all-start.2 = ((bf16[8,64,384]{2,1,0:T(8,128)(2,1)}), bf16[8,64,384]{2,1,0:T(8,128)(2,1)S(1)}, u32[]{:S(2)}, u32[]{:S(2)}) async-start(bf16[8,64,384]{2,1,0:T(8,128)(2,1)} %broadcast_in_dim.225), calls=%async_computation.2 | async-start | bytes 786432 | tf_op jit(solution)/shard_map/all_to_all | solution.py:127
  41.3 17.4 %copy-start.7 = (s32[1024]{0:T(1024)S(1)}, s32[1024]{0:T(1024)}, u32[]{:S(2)}) copy-start(s32[1024]{0:T(1024)} %param.14) | copy-start | bytes 12292
  51.4 0.7 copy-start.5
  52.2 34.0 %all-to-all-start = ((bf16[8,128,1024]{2,1,0:T(8,128)(2,1)}), bf16[8,128,1024]{2,1,0:T(8,128)(2,1)S(1)}, u32[]{:S(2)}, u32[]{:S(2)}) async-start(bf16[8,128,1024]{2,1,0:T(8,128)(2,1)} %multiply_convert_fusion.3), calls=%async_computation | async-start | bytes 4194304 | tf_op jit(solution)/shard_map/all_to_all | solution.py:61
  56.4 138.2 %all-gather.5.cloned.1.call-start = ((), (), s32[]{:S(2)}) async-start(), calls=%async_computation.11 | async-start | bytes 5570560 | tf_op jit(solution)/shard_map/all_gather | solution.py:123
  58.4 2.6 collective-permute-start
  88.4 1.7 copy-start.1
  90.1 9.1 %copy-start.6 = (bf16[1024,128]{0,1:T(8,128)(2,1)S(1)}, bf16[1024,128]{0,1:T(8,128)(2,1)}, u32[]{:S(2)}) copy-start(bf16[1024,128]{0,1:T(8,128)(2,1)} %slice.293) | copy-start | bytes 786436
  104.4 11.5 %all-to-all-start.3 = ((bf16[8,128,128]{2,1,0:T(8,128)(2,1)}), bf16[8,128,128]{2,1,0:T(8,128)(2,1)}, u32[]{:S(2)}, u32[]{:S(2)}) async-start(bf16[8,128,128]{2,1,0:T(8,128)(2,1)} %copy.120), calls=%async_computation.3 | async-start | bytes 524288 | tf_op jit(solution)/shard_map/all_to_all | solution.py:80
  190.7 31.2 %all-to-all-start.6 = ((bf16[8,128,1024]{2,1,0:T(8,128)(2,1)}), bf16[8,128,1024]{2,1,0:T(8,128)(2,1)S(1)}, u32[]{:S(2)}, u32[]{:S(2)}) async-start(bf16[8,128,1024]{2,1,0:T(8,128)(2,1)} %multiply_convert_fusion.1), calls=%async_computation.6 | async-start | bytes 4194304 | tf_op jit(solution)/shard_map/all_to_all | solution.py:61
  224.1 1.2 copy-start.2
  224.1 1.6 copy-start.3
  239.5 10.3 %all-to-all-start.7 = ((bf16[8,128,128]{2,1,0:T(8,128)(2,1)}), bf16[8,128,128]{2,1,0:T(8,128)(2,1)S(1)}, u32[]{:S(2)}, u32[]{:S(2)}) async-start(bf16[8,128,128]{2,1,0:T(8,128)(2,1)} %copy.128), calls=%async_computation.7 | async-start | bytes 524288 | tf_op jit(solution)/shard_map/all_to_all | solution.py:80
  288.3 3.7 %copy-start.12 = (s32[128]{0:T(128)S(1)}, s32[128]{0:T(128)}, u32[]{:S(2)}) copy-start(s32[128]{0:T(128)} %copy-done.11) | copy-start | bytes 1540
  288.3 31.8 %copy-start = (f32[128,128,8]{0,2,1:T(8,128)S(1)}, f32[128,128,8]{0,2,1:T(8,128)}, u32[]{:S(2)}) copy-start(f32[128,128,8]{0,2,1:T(8,128)} %get-tuple-element.11) | copy-start | bytes 1572868
  288.3 29.4 %all-to-all-start.9 = ((bf16[8,128,1024]{2,1,0:T(8,128)(2,1)}), bf16[8,128,1024]{2,1,0:T(8,128)(2,1)S(1)}, u32[]{:S(2)}, u32[]{:S(2)}) async-start(bf16[8,128,1024]{2,1,0:T(8,128)(2,1)} %bitcast.118), calls=%async_computation.9 | async-start | bytes 4194304 | tf_op jit(solution)/shard_map/all_to_all | solution.py:73
  320.2 0.8 copy-start.9
Sparse Core Ops, SparseCore 0:
  27.0 71.1 all-gather.2
  100.7 68.7 all-gather.4
